TPU v7x, 32 devices: a whole 2x2x4 slice. The times are simulated.
32 devices in a mesh: gx: 8 (over z, x), gy: 4 (over y, core).
Axes of the slice: x: 2, y: 2, z: 4, core: 2. Of those that a mesh axis runs over, the one named last changes fastest.
Arguments:
- positions: float32 [8, 4, 72, 3, 128], P('gx', 'gy'), may hold values from -6 to 6
- strength: float32 [8, 4, 72, 3, 128], P('gx', 'gy'), may hold values from -3 to 3
- core: float32 [8, 4, 72, 128], P('gx', 'gy'), may hold values from 0.2 to 1
- moves: int32 [5, 8, 4], replicated, may hold values from 0 to 8, as said below
- owner: int32 [1024], replicated, may hold values from 0 to 1023, as said below
- near_list: int32 [8, 4, 32, 8], P('gx', 'gy'), may hold values from 0 to 1023, as said below
- far_list: int32 [8, 4, 32, 8], P('gx', 'gy'), may hold values from 0 to 1023
Outputs:
- velocity: float32 [8, 4, 32, 3, 128], P('gx', 'gy')
Inputs may be any that keep to these rules, and one draw needn't show every extreme that they name: `moves`: no device sends more live blocks than it holds at a level, no device ever holds more than 72 live blocks, and after the last level every device holds exactly 32. `owner`: A permutation of the locations. `near_list`: every entry names a block whose device differs from the target's device by at most one in gx and in gy; over all near lists of one device, exactly 8 entries name blocks of each existing one of its eight neighbouring devices, and all other entries name blocks of the device itself.
All inputs are finite; a program needn't handle non-finite values.
Results may differ from a plain program's by a relative error of at most 0.00002.
Values sent between devices are 32-bit elements; how exact they have to be, the bound alone decides.
No kernel may reach another device: no remote copies, remote signals or barrier semaphores. Data moves between devices by JAX's collectives and lax.ppermute only.
A program may use at most 64 MiB of HBM per device.

v0:
```python
import math

import jax
import jax.numpy as jnp
from jax import lax
from jax.sharding import PartitionSpec as P

NBD = 32
MOVE = 8


inv_four_pi = 0.25 / math.pi


def from_partner(shard, axis, apart):
    return lax.ppermute(shard, axis, [(i, i ^ 1 << apart) for i in range(lax.axis_size(axis))])


def padded(shard, sides, width):
    for axis, dim in sides:
        size, length = (lax.axis_size(axis), shard.shape[dim])
        up = [(i, (i + 1) % size) for i in range(size - 1)]
        down = [(j, i) for i, j in up]
        last = lax.slice_in_dim(shard, length - width, length, axis=dim)
        first = lax.slice_in_dim(shard, 0, width, axis=dim)
        before = lax.ppermute(last, axis, up)
        after = lax.ppermute(first, axis, down)
        shard = jnp.concatenate([before, shard, after], axis=dim)
    return shard


def multipoles(blocks):
    centre = jnp.mean(blocks[:, 0:3], axis=2)
    total = jnp.sum(blocks[:, 3:6], axis=2)
    offset = blocks[:, 0:3] - centre[:, :, None]
    spread = jnp.mean(blocks[:, 6] * blocks[:, 6], axis=1) + jnp.mean(
        jnp.sum(offset * offset, axis=1), axis=1
    )
    return jnp.concatenate([centre, total, spread[:, None]], axis=1)


def evaluate(target, sources, moments):
    sep_x = target[0][None, :, None] - sources[:, 0][:, None, :]
    sep_y = target[1][None, :, None] - sources[:, 1][:, None, :]
    sep_z = target[2][None, :, None] - sources[:, 2][:, None, :]
    radius_sq = (
        sep_x * sep_x + sep_y * sep_y + sep_z * sep_z + (sources[:, 6] * sources[:, 6])[:, None, :]
    )
    weight = 1.0 / (radius_sq * jnp.sqrt(radius_sq))
    str_x = sources[:, 3][:, None, :] * weight
    str_y = sources[:, 4][:, None, :] * weight
    str_z = sources[:, 5][:, None, :] * weight
    near_x = jnp.sum(str_y * sep_z - str_z * sep_y, axis=(0, 2))
    near_y = jnp.sum(str_z * sep_x - str_x * sep_z, axis=(0, 2))
    near_z = jnp.sum(str_x * sep_y - str_y * sep_x, axis=(0, 2))
    off_x = target[0][None, :] - moments[:, 0][:, None]
    off_y = target[1][None, :] - moments[:, 1][:, None]
    off_z = target[2][None, :] - moments[:, 2][:, None]
    far_sq = off_x * off_x + off_y * off_y + off_z * off_z + moments[:, 6][:, None]
    far_weight = 1.0 / (far_sq * jnp.sqrt(far_sq))
    mom_x = moments[:, 3][:, None] * far_weight
    mom_y = moments[:, 4][:, None] * far_weight
    mom_z = moments[:, 5][:, None] * far_weight
    far_x = jnp.sum(mom_y * off_z - mom_z * off_y, axis=0)
    far_y = jnp.sum(mom_z * off_x - mom_x * off_z, axis=0)
    far_z = jnp.sum(mom_x * off_y - mom_y * off_x, axis=0)
    return jnp.stack([near_x + far_x, near_y + far_y, near_z + far_z], axis=0) * inv_four_pi


def evaluate_all(targets, sources_all, moments):
    block_count = targets.shape[0]
    group_size = math.gcd(block_count, 8)
    groups = block_count // group_size

    def one_group(bundle):
        return jax.vmap(evaluate)(bundle[0], bundle[1], bundle[2])

    grouped = (
        targets.reshape((groups, group_size) + targets.shape[1:]),
        sources_all.reshape((groups, group_size) + sources_all.shape[1:]),
        moments.reshape((groups, group_size) + moments.shape[1:]),
    )
    velocity = lax.map(one_group, grouped)
    return velocity.reshape((block_count,) + velocity.shape[2:])


def local(positions, strength, core, moves, owner, near_list, far_list):
    column_index = lax.axis_index("gx")
    row_index = lax.axis_index("gy")
    size_x = lax.axis_size("gx")
    size_y = lax.axis_size("gy")
    bits_x = size_x.bit_length() - 1
    levels = moves.shape[0]
    held = jnp.concatenate([positions[0, 0], strength[0, 0], core[0, 0][:, None, :]], axis=1)
    held = jnp.pad(held, ((0, MOVE), (0, 0), (0, 0)))
    plans = []
    for level in range(levels):
        if level < bits_x:
            bit_at = bits_x - 1 - level
            mate_moves = moves[level, jnp.bitwise_xor(column_index, 1 << bit_at), row_index]
        else:
            bit_at = levels - 1 - level
            mate_moves = moves[level, column_index, jnp.bitwise_xor(row_index, 1 << bit_at)]
        plans.append((bit_at, moves[level, column_index, row_index], mate_moves))
    count = jnp.int32(NBD)
    for plan_item in plans:
        count = count + plan_item[1] - plan_item[2]
    for level in range(levels):
        bit_at, own_moves, mate_moves = plans[level]
        leaving = lax.dynamic_slice_in_dim(held, count - own_moves, MOVE, 0)
        if level < bits_x:
            arriving = from_partner(leaving, "gx", bit_at)
        else:
            arriving = from_partner(leaving, "gy", bit_at)
        count = count - own_moves
        held = lax.dynamic_update_slice_in_dim(held, arriving, count, 0)
        count = count + mate_moves
    blocks = held[:NBD]
    local_table = multipoles(blocks).T
    table = lax.all_gather(local_table, ("gx", "gy"), axis=1, tiled=True)
    near_where = owner[near_list[0, 0]]
    source_device = near_where // NBD
    source_slot = near_where % NBD
    delta_x = source_device // size_y - column_index
    delta_y = source_device % size_y - row_index
    direction = (delta_x + 1) * 3 + (delta_y + 1)
    grid_blocks = padded(blocks[None, None], (("gx", 0), ("gy", 1)), 1)
    source_pool = grid_blocks.reshape(9 * NBD, 7, blocks.shape[2])
    pool_index = direction * NBD + source_slot
    far_where = owner[far_list[0, 0]]
    moments = jnp.transpose(table[:, far_where], (1, 2, 0))
    sources_all = source_pool[pool_index]
    velocity = evaluate_all(blocks[:, 0:3], sources_all, moments)
    return velocity[None, None]


def solution(mesh):
    placed = (
        P("gx", "gy", None, None, None),
        P("gx", "gy", None, None, None),
        P("gx", "gy", None, None),
        P(),
        P(),
        P("gx", "gy", None, None),
        P("gx", "gy", None, None),
    )
    return jax.shard_map(
        local,
        mesh=mesh,
        in_specs=placed,
        out_specs=P("gx", "gy", None, None, None),
        check_vma=False,
    )
```

profile of v0, /device:TPU:0, one launch (start us, length us, event | category | flops | bytes accessed | tf_op | source)
XLA Modules:
  0.0 116.4 jit_solution(7635738264617512784)
XLA Ops:
  0.0 1.5 %constant_dynamic-slice_fusion.13 = (s32[1,1,1]{1,2,0:T(1,128)}, s32[1,1,1]{1,2,0:T(1,128)}, s32[1,1,1]{1,2,0:T(1,128)}, s32[1,1,1]{1,2,0:T(1,128)}, s32[1,1,1]{...) fusion(s32[5,8,4]{1,2,0:T(4,128)} %param.12, ...), kind=kLoop, calls=%fused_computation.133 | loop fusion | bytes 108 | tf_op jit(solution)/shard_map/dynamic_slice | solution.py:103
  8.3 1.0 select_maximum_fusion
  9.3 4.1 %collective-permute-start = (f32[8,7,128]{2,0,1:T(8,128)S(1)}, f32[8,7,128]{2,0,1:T(8,128)S(1)}, u32[]{:S(2)}, u32[]{:S(2)}) collective-permute-start(f32[8,7,128]{2,0,1:T(8,128)S(1)} %constant_dynamic-slice_fusion.4), channel_id=1, source_target_pairs={{0,16},{4,20},{8,24},{12,28},{16,0},{20,4},{24,8},{28,12},{1,17},{... | collective-permute-start | bytes 86024 | tf_op jit(solution)/shard_map/ppermute | solution.py:16
  14.3 1.4 %gather_fusion.2 = s32[256]{0:T(256)S(1)} fusion(s32[1024]{0:T(1024)S(1)} %copy-done, s32[1024]{0:T(1024)S(1)} %pad_clamp_fusion.1), kind=kCustom, calls=%fused_computation.2 | custom fusion | bytes 3072 | tf_op jit(solution)/shard_map/gather | solution.py:130
  17.5 1.6 %collective-permute-start.1 = (f32[8,7,128]{2,0,1:T(8,128)S(1)}, f32[8,7,128]{2,0,1:T(8,128)S(1)}, u32[]{:S(2)}, u32[]{:S(2)}) collective-permute-start(f32[8,7,128]{2,0,1:T(8,128)S(1)} %constant_dynamic-slice_fusion.3), channel_id=1, source_target_pairs={{0,8},{4,12},{8,0},{12,4},{16,24},{20,28},{24,16},{28,20},{1,9},{5... | collective-permute-start | bytes 86024 | tf_op jit(solution)/shard_map/ppermute | solution.py:16
  20.3 1.4 %gather_fusion = s32[256]{0:T(256)S(1)} fusion(s32[1024]{0:T(1024)S(1)} %copy-done, s32[1024]{0:T(1024)S(1)} %pad_clamp_fusion.3), kind=kCustom, calls=%fused_computation | custom fusion | bytes 3072 | tf_op jit(solution)/shard_map/gather | solution.py:121
  22.0 1.6 %collective-permute-start.2 = (f32[8,7,128]{2,0,1:T(8,128)S(1)}, f32[8,7,128]{2,0,1:T(8,128)S(1)}, u32[]{:S(2)}, u32[]{:S(2)}) collective-permute-start(f32[8,7,128]{2,0,1:T(8,128)S(1)} %constant_dynamic-slice_fusion.2), channel_id=1, source_target_pairs={{0,4},{4,0},{8,12},{12,8},{16,20},{20,16},{24,28},{28,24},{1,5},{5... | collective-permute-start | bytes 86024 | tf_op jit(solution)/shard_map/ppermute | solution.py:16
  25.0 1.0 collective-permute-done.2
  26.1 1.6 %collective-permute-start.3 = (f32[8,7,128]{2,0,1:T(8,128)S(1)}, f32[8,7,128]{2,0,1:T(8,128)S(1)}, u32[]{:S(2)}, u32[]{:S(2)}) collective-permute-start(f32[8,7,128]{2,0,1:T(8,128)S(1)} %constant_dynamic-slice_fusion.1), channel_id=1, source_target_pairs={{0,2},{1,3},{2,0},{3,1},{4,6},{5,7},{6,4},{7,5},{8,10},{9,11},{10,... | collective-permute-start | bytes 86024 | tf_op jit(solution)/shard_map/ppermute | solution.py:16
  29.0 1.0 collective-permute-done.3
  30.2 1.2 %collective-permute-done.4 = f32[8,7,128]{2,0,1:T(8,128)S(1)} collective-permute-done((f32[8,7,128]{2,0,1:T(8,128)S(1)}, f32[8,7,128]{2,0,1:T(8,128)S(1)}, u32[]{:S(2)}, u32[]{:S(2)}) %collective-permute-start.4) | collective-permute-done | bytes 28704 | tf_op jit(solution)/shard_map/ppermute | solution.py:16
  31.7 3.4 %collective-permute-start.5 = (f32[1,1,32,7,128]{4,2,1,0,3:T(8,128)S(1)}, f32[1,1,32,7,128]{4,2,1,0,3:T(8,128)S(1)}, u32[]{:S(2)}, u32[]{:S(2)}) collective-permute-start(f32[1,1,32,7,128]{4,2,1,0,3:T(8,128)S(1)} %slice_bitcast_fusion.16), channel_id=1, source_target_pairs={{0,4},{4,8},{8,12},{12,16},{16,20},{20,24},{24,28},{1,5},{5,9},{9,... | collective-permute-start | bytes 344072 | tf_op jit(solution)/shard_map/ppermute | solution.py:26
  35.1 1.3 %collective-permute-start.6 = (f32[1,1,32,7,128]{4,2,1,0,3:T(8,128)S(1)}, f32[1,1,32,7,128]{4,2,1,0,3:T(8,128)S(1)}, u32[]{:S(2)}, u32[]{:S(2)}) collective-permute-start(f32[1,1,32,7,128]{4,2,1,0,3:T(8,128)S(1)} %slice_bitcast_fusion.16), channel_id=1, source_target_pairs={{4,0},{8,4},{12,8},{16,12},{20,16},{24,20},{28,24},{5,1},{9,5},{13... | collective-permute-start | bytes 344072 | tf_op jit(solution)/shard_map/ppermute | solution.py:27
  36.6 1.2 %collective-permute-done.5 = f32[1,1,32,7,128]{4,2,1,0,3:T(8,128)S(1)} collective-permute-done((f32[1,1,32,7,128]{4,2,1,0,3:T(8,128)S(1)}, f32[1,1,32,7,128]{4,2,1,0,3:T(8,128)S(1)}, u32[]{:S(2)}, u32[]{:S(2)}) %collective-permute-start.5) | collective-permute-done | bytes 114720 | tf_op jit(solution)/shard_map/ppermute | solution.py:26
  37.8 4.1 %collective-permute-done.6 = f32[1,1,32,7,128]{4,2,1,0,3:T(8,128)S(1)} collective-permute-done((f32[1,1,32,7,128]{4,2,1,0,3:T(8,128)S(1)}, f32[1,1,32,7,128]{4,2,1,0,3:T(8,128)S(1)}, u32[]{:S(2)}, u32[]{:S(2)}) %collective-permute-start.6) | collective-permute-done | bytes 114720 | tf_op jit(solution)/shard_map/ppermute | solution.py:27
  42.0 1.3 %collective-permute-start.7 = (f32[3,1,32,7,128]{4,2,1,0,3:T(8,128)S(1)}, f32[3,1,32,7,128]{4,2,1,0,3:T(8,128)S(1)}, u32[]{:S(2)}, u32[]{:S(2)}) collective-permute-start(f32[3,1,32,7,128]{4,2,1,0,3:T(8,128)S(1)} %pad_maximum_fusion.1), channel_id=1, source_target_pairs={{0,1},{1,2},{2,3},{4,5},{5,6},{6,7},{8,9},{9,10},{10,11},{12,13},{... | collective-permute-start | bytes 1032200 | tf_op jit(solution)/shard_map/ppermute | solution.py:26
  43.3 1.3 %collective-permute-start.8 = (f32[3,1,32,7,128]{4,2,1,0,3:T(8,128)S(1)}, f32[3,1,32,7,128]{4,2,1,0,3:T(8,128)S(1)}, u32[]{:S(2)}, u32[]{:S(2)}) collective-permute-start(f32[3,1,32,7,128]{4,2,1,0,3:T(8,128)S(1)} %pad_maximum_fusion.1), channel_id=1, source_target_pairs={{1,0},{2,1},{3,2},{5,4},{6,5},{7,6},{9,8},{10,9},{11,10},{13,12},{... | collective-permute-start | bytes 1032200 | tf_op jit(solution)/shard_map/ppermute | solution.py:27
  44.6 41.4 %all-gather = f32[32,32,7]{1,2,0:T(8,128)S(1)} all-gather(f32[1,32,7]{1,2,0:T(8,128)S(1)} %maximum_bitcast_fusion), channel_id=1, replica_groups=mesh['gx'=8,'gy'=4] {'gx','gy'}, dimensions={0}, use_global_device_ids=true | all-gather | bytes 29568 | tf_op jit(solution)/shard_map/all_gather | solution.py:120
  88.1 1.0 gather_fusion.1
  89.3 26.5 %while.10 = (s32[]{:T(128)}, f32[4,8,3,128]{3,1,0,2:T(8,128)S(1)}, f32[4,8,8,7,128]{4,2,1,3,0:T(8,128)S(1)}, f32[4,8,3,128]{3,1,0,2:T(8,128)S(1)}, f32[4,8,8,7]{2,1,3,0:T(8,128)S(1)}, /*index=5*/s32[]{:T(128)}) while((s32[]{:T(128)}, f32[4,8,3,128]{3,1,0,2:T(8,128)S(1)}, f32[4,8,8,7,128]{4,2,1,3,0:T(8,128)S(1)}, ...), condition=%wide.region_11.12_spmd, body=%wide.region_4.11_spmd.sunk | while | flops 27490304 | bytes 1315669 | solution.py:83
  89.4 6.3 %fusion.41 = (f32[8,128]{1,0:T(8,128)S(1)}, f32[8,128]{1,0:T(8,128)S(1)}, f32[8,128]{1,0:T(8,128)S(1)}) fusion(f32[8,8,128]{2,1,0:T(8,128)S(1)} %get-tuple-element.163, f32[8,8,128]{2,1,0:T(8,128)S(1)} %get-tuple-element.164, f32[8,128]{1,0:T(8,128)S(1)} %get-tuple-element.165, f32[8,8,128]{2,1,0:T(8,128)S(1)} %get-tuple-element.166, ...), kind=kLoop, calls=%fused_computation.23.clone.1 | loop fusion | flops 27259904 | bytes 253952 | tf_op jit(solution)/shard_map/while/body/eval_jaxpr/vmap()/reduce_sum | solution.py:53
  96.0 6.3 %fusion.41 = (f32[8,128]{1,0:T(8,128)S(1)}, f32[8,128]{1,0:T(8,128)S(1)}, f32[8,128]{1,0:T(8,128)S(1)}) fusion(f32[8,8,128]{2,1,0:T(8,128)S(1)} %get-tuple-element.163, f32[8,8,128]{2,1,0:T(8,128)S(1)} %get-tuple-element.164, f32[8,128]{1,0:T(8,128)S(1)} %get-tuple-element.165, f32[8,8,128]{2,1,0:T(8,128)S(1)} %get-tuple-element.166, ...), kind=kLoop, calls=%fused_computation.23.clone.1 | loop fusion | flops 27259904 | bytes 253952 | tf_op jit(solution)/shard_map/while/body/eval_jaxpr/vmap()/reduce_sum | solution.py:53
  102.6 6.3 %fusion.41 = (f32[8,128]{1,0:T(8,128)S(1)}, f32[8,128]{1,0:T(8,128)S(1)}, f32[8,128]{1,0:T(8,128)S(1)}) fusion(f32[8,8,128]{2,1,0:T(8,128)S(1)} %get-tuple-element.163, f32[8,8,128]{2,1,0:T(8,128)S(1)} %get-tuple-element.164, f32[8,128]{1,0:T(8,128)S(1)} %get-tuple-element.165, f32[8,8,128]{2,1,0:T(8,128)S(1)} %get-tuple-element.166, ...), kind=kLoop, calls=%fused_computation.23.clone.1 | loop fusion | flops 27259904 | bytes 253952 | tf_op jit(solution)/shard_map/while/body/eval_jaxpr/vmap()/reduce_sum | solution.py:53
  109.2 6.3 %fusion.41 = (f32[8,128]{1,0:T(8,128)S(1)}, f32[8,128]{1,0:T(8,128)S(1)}, f32[8,128]{1,0:T(8,128)S(1)}) fusion(f32[8,8,128]{2,1,0:T(8,128)S(1)} %get-tuple-element.163, f32[8,8,128]{2,1,0:T(8,128)S(1)} %get-tuple-element.164, f32[8,128]{1,0:T(8,128)S(1)} %get-tuple-element.165, f32[8,8,128]{2,1,0:T(8,128)S(1)} %get-tuple-element.166, ...), kind=kLoop, calls=%fused_computation.23.clone.1 | loop fusion | flops 27259904 | bytes 253952 | tf_op jit(solution)/shard_map/while/body/eval_jaxpr/vmap()/reduce_sum | solution.py:53
  (92 shorter events, 6.4 us)
Async XLA Ops:
  0.0 14.3 %copy-start = (s32[1024]{0:T(1024)S(1)}, s32[1024]{0:T(1024)}, u32[]{:S(2)}) copy-start(s32[1024]{0:T(1024)} %param.13) | copy-start | bytes 12292
  9.3 7.9 %collective-permute-start = (f32[8,7,128]{2,0,1:T(8,128)S(1)}, f32[8,7,128]{2,0,1:T(8,128)S(1)}, u32[]{:S(2)}, u32[]{:S(2)}) collective-permute-start(f32[8,7,128]{2,0,1:T(8,128)S(1)} %constant_dynamic-slice_fusion.4), channel_id=1, source_target_pairs={{0,16},{4,20},{8,24},{12,28},{16,0},{20,4},{24,8},{28,12},{1,17},{... | collective-permute-start | bytes 86024 | tf_op jit(solution)/shard_map/ppermute | solution.py:16
  14.3 1.5 %copy-start.1 = (s32[1,1,32,8]{2,3,1,0:T(8,128)S(1)}, s32[1,1,32,8]{2,3,1,0:T(8,128)}, u32[]{:S(2)}) copy-start(s32[1,1,32,8]{2,3,1,0:T(8,128)} %param.14) | copy-start | bytes 3076
  17.5 4.3 %collective-permute-start.1 = (f32[8,7,128]{2,0,1:T(8,128)S(1)}, f32[8,7,128]{2,0,1:T(8,128)S(1)}, u32[]{:S(2)}, u32[]{:S(2)}) collective-permute-start(f32[8,7,128]{2,0,1:T(8,128)S(1)} %constant_dynamic-slice_fusion.3), channel_id=1, source_target_pairs={{0,8},{4,12},{8,0},{12,4},{16,24},{20,28},{24,16},{28,20},{1,9},{5... | collective-permute-start | bytes 86024 | tf_op jit(solution)/shard_map/ppermute | solution.py:16
  22.0 3.9 %collective-permute-start.2 = (f32[8,7,128]{2,0,1:T(8,128)S(1)}, f32[8,7,128]{2,0,1:T(8,128)S(1)}, u32[]{:S(2)}, u32[]{:S(2)}) collective-permute-start(f32[8,7,128]{2,0,1:T(8,128)S(1)} %constant_dynamic-slice_fusion.2), channel_id=1, source_target_pairs={{0,4},{4,0},{8,12},{12,8},{16,20},{20,16},{24,28},{28,24},{1,5},{5... | collective-permute-start | bytes 86024 | tf_op jit(solution)/shard_map/ppermute | solution.py:16
  26.1 3.9 %collective-permute-start.3 = (f32[8,7,128]{2,0,1:T(8,128)S(1)}, f32[8,7,128]{2,0,1:T(8,128)S(1)}, u32[]{:S(2)}, u32[]{:S(2)}) collective-permute-start(f32[8,7,128]{2,0,1:T(8,128)S(1)} %constant_dynamic-slice_fusion.1), channel_id=1, source_target_pairs={{0,2},{1,3},{2,0},{3,1},{4,6},{5,7},{6,4},{7,5},{8,10},{9,11},{10,... | collective-permute-start | bytes 86024 | tf_op jit(solution)/shard_map/ppermute | solution.py:16
  30.1 1.3 %collective-permute-start.4 = (f32[8,7,128]{2,0,1:T(8,128)S(1)}, f32[8,7,128]{2,0,1:T(8,128)S(1)}, u32[]{:S(2)}, u32[]{:S(2)}) collective-permute-start(f32[8,7,128]{2,0,1:T(8,128)S(1)} %constant_dynamic-slice_fusion), channel_id=1, source_target_pairs={{0,1},{1,0},{2,3},{3,2},{4,5},{5,4},{6,7},{7,6},{8,9},{9,8},{10,11... | collective-permute-start | bytes 86024 | tf_op jit(solution)/shard_map/ppermute | solution.py:16
  31.7 6.1 %collective-permute-start.5 = (f32[1,1,32,7,128]{4,2,1,0,3:T(8,128)S(1)}, f32[1,1,32,7,128]{4,2,1,0,3:T(8,128)S(1)}, u32[]{:S(2)}, u32[]{:S(2)}) collective-permute-start(f32[1,1,32,7,128]{4,2,1,0,3:T(8,128)S(1)} %slice_bitcast_fusion.16), channel_id=1, source_target_pairs={{0,4},{4,8},{8,12},{12,16},{16,20},{20,24},{24,28},{1,5},{5,9},{9,... | collective-permute-start | bytes 344072 | tf_op jit(solution)/shard_map/ppermute | solution.py:26
  35.1 6.8 %collective-permute-start.6 = (f32[1,1,32,7,128]{4,2,1,0,3:T(8,128)S(1)}, f32[1,1,32,7,128]{4,2,1,0,3:T(8,128)S(1)}, u32[]{:S(2)}, u32[]{:S(2)}) collective-permute-start(f32[1,1,32,7,128]{4,2,1,0,3:T(8,128)S(1)} %slice_bitcast_fusion.16), channel_id=1, source_target_pairs={{4,0},{8,4},{12,8},{16,12},{20,16},{24,20},{28,24},{5,1},{9,5},{13... | collective-permute-start | bytes 344072 | tf_op jit(solution)/shard_map/ppermute | solution.py:27
  42.0 45.4 %collective-permute-start.7 = (f32[3,1,32,7,128]{4,2,1,0,3:T(8,128)S(1)}, f32[3,1,32,7,128]{4,2,1,0,3:T(8,128)S(1)}, u32[]{:S(2)}, u32[]{:S(2)}) collective-permute-start(f32[3,1,32,7,128]{4,2,1,0,3:T(8,128)S(1)} %pad_maximum_fusion.1), channel_id=1, source_target_pairs={{0,1},{1,2},{2,3},{4,5},{5,6},{6,7},{8,9},{9,10},{10,11},{12,13},{... | collective-permute-start | bytes 1032200 | tf_op jit(solution)/shard_map/ppermute | solution.py:26
  43.3 44.1 %collective-permute-start.8 = (f32[3,1,32,7,128]{4,2,1,0,3:T(8,128)S(1)}, f32[3,1,32,7,128]{4,2,1,0,3:T(8,128)S(1)}, u32[]{:S(2)}, u32[]{:S(2)}) collective-permute-start(f32[3,1,32,7,128]{4,2,1,0,3:T(8,128)S(1)} %pad_maximum_fusion.1), channel_id=1, source_target_pairs={{1,0},{2,1},{3,2},{5,4},{6,5},{7,6},{9,8},{10,9},{11,10},{13,12},{... | collective-permute-start | bytes 1032200 | tf_op jit(solution)/shard_map/ppermute | solution.py:27
  115.8 0.6 copy-start.2
where the time goes:
time: 117 us; the launch traced here: 116 us
  blocking collectives  41.4 us (35%)
  other arithmetic  27.4 us (23%)
  starting transfers between devices  16.3 us (14%)
  between operations  12.2 us (10%)
  local copies, waits for them, and re-layouts  10.2 us (9%)
  waiting for transfers between devices  8.47 us (7%)
    all_gather x1, blocking collectives, local(): table = lax.all_gather(local_table, ('gx', 'gy'), axis=1, tiled=True)  41.4 us
    reduce_sum x4, other arithmetic, evaluate(): near_x = jnp.sum(str_y * sep_z - str_z * sep_y, axis=(0, 2))  25.1 us
    ppermute x5, starting transfers between devices, from_partner(): lax.ppermute(shard, axis, [(i, i ^ 1 << apart) for i in range(lax.axis_si...  8.96 us
    ppermute x2, starting transfers between devices, padded(): before = lax.ppermute(last, axis, up)  4.71 us
    ppermute x2, waiting for transfers between devices, padded(): after = lax.ppermute(first, axis, down)  4.12 us
    ppermute x5, waiting for transfers between devices, from_partner(): lax.ppermute(shard, axis, [(i, i ^ 1 << apart) for i in range(lax.axis_si...  3.14 us
    ppermute x2, starting transfers between devices, padded(): after = lax.ppermute(first, axis, down)  2.58 us
  transfers between devices with their start and end apart: 9, of which 5 were waited for; matrix products, arithmetic and copies ran while one was open for 5% of the time, Pallas kernels for 0%

commit v1 on v0

--- a/solution.py
+++ b/solution.py
@@ -2,10 +2,10 @@
 
 import jax
 import jax.numpy as jnp
+import numpy as np
 from jax import lax
 from jax.sharding import PartitionSpec as P
 
-NBD = 32
 MOVE = 8
 
 
@@ -29,13 +29,11 @@
     return shard
 
 
-def multipoles(blocks):
-    centre = jnp.mean(blocks[:, 0:3], axis=2)
-    total = jnp.sum(blocks[:, 3:6], axis=2)
-    offset = blocks[:, 0:3] - centre[:, :, None]
-    spread = jnp.mean(blocks[:, 6] * blocks[:, 6], axis=1) + jnp.mean(
-        jnp.sum(offset * offset, axis=1), axis=1
-    )
+def slot_multipoles(pos, stren, core):
+    centre = jnp.mean(pos, axis=2)
+    total = jnp.sum(stren, axis=2)
+    offset = pos - centre[:, :, None]
+    spread = jnp.mean(core * core, axis=1) + jnp.mean(jnp.sum(offset * offset, axis=1), axis=1)
     return jnp.concatenate([centre, total, spread[:, None]], axis=1)
 
 
@@ -84,6 +82,49 @@
     return velocity.reshape((block_count,) + velocity.shape[2:])
 
 
+def trace_back(loc, moves, levels, bits_x, size_x, size_y, nbd):
+    devices = size_x * size_y
+    linear = np.arange(devices)
+    grid_x, grid_y = linear // size_y, linear % size_y
+    flat = moves.reshape(levels, devices)
+    mates = []
+    for level in range(levels):
+        if level < bits_x:
+            mates.append((grid_x ^ 1 << bits_x - 1 - level) * size_y + grid_y)
+        else:
+            mates.append(grid_x * size_y + (grid_y ^ 1 << levels - 1 - level))
+    count = jnp.full((devices,), nbd, jnp.int32)
+    for level in range(levels):
+        count = count + flat[level] - flat[level][mates[level]]
+    kept = []
+    for level in range(levels):
+        left = count - flat[level]
+        kept.append(left)
+        count = left + flat[level][mates[level]]
+    device = loc // nbd
+    slot = loc % nbd
+    for level in reversed(range(levels)):
+        if level < bits_x:
+            bit = 1 << bits_x - 1 - level
+            mate = ((device // size_y) ^ bit) * size_y + device % size_y
+        else:
+            bit = 1 << levels - 1 - level
+            mate = (device // size_y) * size_y + ((device % size_y) ^ bit)
+        here = kept[level][device]
+        there = kept[level][mate]
+        moved = slot >= here
+        slot = jnp.where(moved, slot - here + there, slot)
+        device = jnp.where(moved, mate, device)
+    return device, slot
+
+
+def table_blocks(table, lanes):
+    cap, width = table.shape
+    pieces = -(-cap // lanes)
+    wide = jnp.pad(table.T, ((0, 0), (0, pieces * lanes - cap)))
+    return wide.reshape(width, pieces, lanes).transpose(1, 0, 2)
+
+
 def local(positions, strength, core, moves, owner, near_list, far_list):
     column_index = lax.axis_index("gx")
     row_index = lax.axis_index("gy")
@@ -91,44 +132,62 @@
     size_y = lax.axis_size("gy")
     bits_x = size_x.bit_length() - 1
     levels = moves.shape[0]
+    cap = positions.shape[2]
+    nbd = near_list.shape[2]
+    lanes = positions.shape[4]
+    me = column_index * size_y + row_index
+    slot_table = slot_multipoles(positions[0, 0], strength[0, 0], core[0, 0])
+    width = slot_table.shape[1]
+    gathered = table_blocks(slot_table, lanes)
+    pieces = gathered.shape[0]
+    far_where = owner[far_list[0, 0]]
+    far_device, far_slot = trace_back(far_where, moves, levels, bits_x, size_x, size_y, nbd)
     held = jnp.concatenate([positions[0, 0], strength[0, 0], core[0, 0][:, None, :]], axis=1)
     held = jnp.pad(held, ((0, MOVE), (0, 0), (0, 0)))
     plans = []
+    level_bits = []
     for level in range(levels):
         if level < bits_x:
             bit_at = bits_x - 1 - level
             mate_moves = moves[level, jnp.bitwise_xor(column_index, 1 << bit_at), row_index]
+            level_bits.append((1 << bit_at) * size_y)
         else:
             bit_at = levels - 1 - level
             mate_moves = moves[level, column_index, jnp.bitwise_xor(row_index, 1 << bit_at)]
+            level_bits.append(1 << bit_at)
         plans.append((bit_at, moves[level, column_index, row_index], mate_moves))
-    count = jnp.int32(NBD)
+    count = jnp.int32(nbd)
     for plan_item in plans:
         count = count + plan_item[1] - plan_item[2]
     for level in range(levels):
         bit_at, own_moves, mate_moves = plans[level]
         leaving = lax.dynamic_slice_in_dim(held, count - own_moves, MOVE, 0)
-        if level < bits_x:
-            arriving = from_partner(leaving, "gx", bit_at)
-        else:
-            arriving = from_partner(leaving, "gy", bit_at)
+        payload = jnp.concatenate([leaving, gathered], axis=0)
+        if level < bits_x:
+            got = from_partner(payload, "gx", bit_at)
+        else:
+            got = from_partner(payload, "gy", bit_at)
+        arriving = got[:MOVE]
+        gathered = jnp.concatenate([gathered, got[MOVE:]], axis=0)
         count = count - own_moves
         held = lax.dynamic_update_slice_in_dim(held, arriving, count, 0)
         count = count + mate_moves
-    blocks = held[:NBD]
-    local_table = multipoles(blocks).T
-    table = lax.all_gather(local_table, ("gx", "gy"), axis=1, tiled=True)
+    blocks = held[:nbd]
+    relative = jnp.bitwise_xor(far_device, me)
+    entry = jnp.zeros_like(relative)
+    for level in range(levels):
+        entry = entry + ((relative // level_bits[level]) % 2) * (1 << level)
+    all_table = gathered.reshape(-1, pieces, width, lanes).transpose(0, 1, 3, 2).reshape(-1, width)
+    moments = all_table[entry * (pieces * lanes) + far_slot]
     near_where = owner[near_list[0, 0]]
-    source_device = near_where // NBD
-    source_slot = near_where % NBD
+    source_device = near_where // nbd
+    source_slot = near_where % nbd
     delta_x = source_device // size_y - column_index
     delta_y = source_device % size_y - row_index
     direction = (delta_x + 1) * 3 + (delta_y + 1)
     grid_blocks = padded(blocks[None, None], (("gx", 0), ("gy", 1)), 1)
-    source_pool = grid_blocks.reshape(9 * NBD, 7, blocks.shape[2])
-    pool_index = direction * NBD + source_slot
-    far_where = owner[far_list[0, 0]]
-    moments = jnp.transpose(table[:, far_where], (1, 2, 0))
+    source_pool = grid_blocks.reshape(9 * nbd, 7, blocks.shape[2])
+    pool_index = direction * nbd + source_slot
     sources_all = source_pool[pool_index]
     velocity = evaluate_all(blocks[:, 0:3], sources_all, moments)
     return velocity[None, None]

time: 117 us -> 118 us (level)
  the two profiles are of different devices: /device:TPU:0 before, /device:TPU:1 now
where the time goes in v1:
time: 118 us; the launch traced here: 117 us
  local copies, waits for them, and re-layouts  36.4 us (31%)
  other arithmetic  36.1 us (31%)
  starting transfers between devices  21.2 us (18%)
  between operations  12.5 us (11%)
  waiting for transfers between devices  10.6 us (9%)
    reduce_sum x4, other arithmetic, evaluate(): near_x = jnp.sum(str_y * sep_z - str_z * sep_y, axis=(0, 2))  25.1 us
    ppermute x5, starting transfers between devices, from_partner(): lax.ppermute(shard, axis, [(i, i ^ 1 << apart) for i in range(lax.axis_si...  10.7 us
    gather x10, local copies, waits for them, and re-layouts, trace_back(): there = kept[level][mate]  9.75 us
    gather x10, local copies, waits for them, and re-layouts, trace_back(): here = kept[level][device]  9.74 us
    ppermute x2, waiting for transfers between devices, padded(): after = lax.ppermute(first, axis, down)  8.3 us
    ppermute x2, starting transfers between devices, padded(): before = lax.ppermute(last, axis, up)  7.29 us
    gather x5, local copies, waits for them, and re-layouts, trace_back(): count = count + flat[level] - flat[level][mates[level]]  3.51 us
    gather x5, other arithmetic, trace_back(): count = count + flat[level] - flat[level][mates[level]]  3.31 us
  transfers between devices with their start and end apart: 9, of which 6 were waited for; matrix products, arithmetic and copies ran while one was open for 30% of the time, Pallas kernels for 0%

profile of v1, /device:TPU:1, one launch (start us, length us, event | category | flops | bytes accessed | tf_op | source)
XLA Modules:
  0.0 117.2 jit_solution(9198580799524320090)
XLA Ops:
  0.0 1.5 %constant_dynamic-slice_fusion.13 = (s32[1,1,1]{1,2,0:T(1,128)}, s32[1,1,1]{1,2,0:T(1,128)}, s32[1,1,1]{1,2,0:T(1,128)}, s32[1,1,1]{1,2,0:T(1,128)}, s32[1,1,1]{...) fusion(s32[5,8,4]{1,2,0:T(4,128)} %param.26, ...), kind=kLoop, calls=%fused_computation.303 | loop fusion | bytes 108 | tf_op jit(solution)/shard_map/dynamic_slice | solution.py:156
  13.6 3.2 %collective-permute-start = (f32[9,7,128]{2,0,1:T(8,128)S(1)}, f32[9,7,128]{2,0,1:T(8,128)S(1)}, u32[]{:S(2)}, u32[]{:S(2)}) collective-permute-start(f32[9,7,128]{2,0,1:T(8,128)S(1)} %pad_maximum_fusion.2), channel_id=1, source_target_pairs={{0,16},{4,20},{8,24},{12,28},{16,0},{20,4},{24,8},{28,12},{1,17},{... | collective-permute-start | bytes 96776 | tf_op jit(solution)/shard_map/ppermute | solution.py:16
  22.6 1.4 %gather_fusion.2 = s32[256]{0:T(256)S(1)} fusion(s32[1024]{0:T(1024)S(1)} %copy-done, s32[1024]{0:T(1024)S(1)} %pad_clamp_fusion.16), kind=kCustom, calls=%fused_computation.2 | custom fusion | bytes 3072 | tf_op jit(solution)/shard_map/gather | solution.py:143
  27.7 1.9 %gather_fusion.8 = s32[256]{0:T(256)S(1)} fusion(s32[32]{0:T(128)S(1)} %get-tuple-element.83, s32[1024]{0:T(1024)S(1)} %pad_clamp_fusion.10), kind=kCustom, calls=%fused_computation.8 | custom fusion | bytes 3072 | tf_op jit(solution)/shard_map/gather | solution.py:113
  29.9 1.9 %gather_fusion.10 = s32[256]{0:T(256)S(1)} fusion(s32[32]{0:T(128)S(1)} %get-tuple-element.84, s32[1024]{0:T(1024)S(1)} %pad_clamp_fusion.8), kind=kCustom, calls=%fused_computation.10 | custom fusion | bytes 3072 | tf_op jit(solution)/shard_map/gather | solution.py:113
  32.0 1.9 %gather_fusion.9 = s32[256]{0:T(256)S(1)} fusion(s32[32]{0:T(128)S(1)} %get-tuple-element.83, s32[1024]{0:T(1024)S(1)} %pad_clamp_fusion.9), kind=kCustom, calls=%fused_computation.9 | custom fusion | bytes 3072 | tf_op jit(solution)/shard_map/gather | solution.py:114
  34.1 1.9 %gather_fusion.12 = s32[256]{0:T(256)S(1)} fusion(s32[32]{0:T(128)S(1)} %get-tuple-element.85, s32[1024]{0:T(1024)S(1)} %pad_clamp_fusion.6), kind=kCustom, calls=%fused_computation.12 | custom fusion | bytes 3072 | tf_op jit(solution)/shard_map/gather | solution.py:113
  36.2 1.9 %gather_fusion.11 = s32[256]{0:T(256)S(1)} fusion(s32[32]{0:T(128)S(1)} %get-tuple-element.84, s32[1024]{0:T(1024)S(1)} %pad_clamp_fusion.7), kind=kCustom, calls=%fused_computation.11 | custom fusion | bytes 3072 | tf_op jit(solution)/shard_map/gather | solution.py:114
  38.3 1.9 %gather_fusion.14 = s32[256]{0:T(256)S(1)} fusion(s32[32]{0:T(128)S(1)} %get-tuple-element.86, s32[1024]{0:T(1024)S(1)} %pad_clamp_fusion.4), kind=kCustom, calls=%fused_computation.14 | custom fusion | bytes 3072 | tf_op jit(solution)/shard_map/gather | solution.py:113
  40.4 1.9 %gather_fusion.13 = s32[256]{0:T(256)S(1)} fusion(s32[32]{0:T(128)S(1)} %get-tuple-element.85, s32[1024]{0:T(1024)S(1)} %pad_clamp_fusion.5), kind=kCustom, calls=%fused_computation.13 | custom fusion | bytes 3072 | tf_op jit(solution)/shard_map/gather | solution.py:114
  46.7 1.9 %gather_fusion.16 = s32[256]{0:T(256)S(1)} fusion(s32[32]{0:T(128)S(1)} %get-tuple-element.87, s32[1024]{0:T(1024)S(1)} %pad_clamp_fusion.2), kind=kCustom, calls=%fused_computation.16 | custom fusion | bytes 3072 | tf_op jit(solution)/shard_map/gather | solution.py:113
  48.7 1.9 %gather_fusion.17 = s32[256]{0:T(256)S(1)} fusion(s32[32]{0:T(128)S(1)} %get-tuple-element.87, s32[1024]{0:T(1024)S(1)} %pad_clamp_fusion.1), kind=kCustom, calls=%fused_computation.17 | custom fusion | bytes 3072 | tf_op jit(solution)/shard_map/gather | solution.py:114
  50.7 1.9 %gather_fusion.15 = s32[256]{0:T(256)S(1)} fusion(s32[32]{0:T(128)S(1)} %get-tuple-element.86, s32[1024]{0:T(1024)S(1)} %pad_clamp_fusion.3), kind=kCustom, calls=%fused_computation.15 | custom fusion | bytes 3072 | tf_op jit(solution)/shard_map/gather | solution.py:114
  59.5 3.6 %collective-permute-start.4 = (f32[24,7,128]{2,0,1:T(8,128)S(1)}, f32[24,7,128]{2,0,1:T(8,128)S(1)}, u32[]{:S(2)}, u32[]{:S(2)}) collective-permute-start(f32[24,7,128]{2,0,1:T(8,128)S(1)} %concatenate.48), channel_id=1, source_target_pairs={{0,1},{1,0},{2,3},{3,2},{4,5},{5,4},{6,7},{7,6},{8,9},{9,8},{10,11... | collective-permute-start | bytes 258056 | tf_op jit(solution)/shard_map/ppermute | solution.py:16
  64.8 3.1 %collective-permute-start.5 = (f32[1,1,32,7,128]{4,2,1,0,3:T(8,128)S(1)}, f32[1,1,32,7,128]{4,2,1,0,3:T(8,128)S(1)}, u32[]{:S(2)}, u32[]{:S(2)}) collective-permute-start(f32[1,1,32,7,128]{4,2,1,0,3:T(8,128)S(1)} %slice_bitcast_fusion.16), channel_id=1, source_target_pairs={{0,4},{4,8},{8,12},{12,16},{16,20},{20,24},{24,28},{1,5},{5,9},{9,... | collective-permute-start | bytes 344072 | tf_op jit(solution)/shard_map/ppermute | solution.py:26
  70.4 3.8 %collective-permute-done.6 = f32[1,1,32,7,128]{4,2,1,0,3:T(8,128)S(1)} collective-permute-done((f32[1,1,32,7,128]{4,2,1,0,3:T(8,128)S(1)}, f32[1,1,32,7,128]{4,2,1,0,3:T(8,128)S(1)}, u32[]{:S(2)}, u32[]{:S(2)}) %collective-permute-start.6) | collective-permute-done | bytes 114720 | tf_op jit(solution)/shard_map/ppermute | solution.py:27
  74.3 4.2 %collective-permute-start.7 = (f32[3,1,32,7,128]{4,2,1,0,3:T(8,128)S(1)}, f32[3,1,32,7,128]{4,2,1,0,3:T(8,128)}, u32[]{:S(2)}, u32[]{:S(2)}) collective-permute-start(f32[3,1,32,7,128]{4,2,1,0,3:T(8,128)S(1)} %pad_maximum_fusion.1), channel_id=1, source_target_pairs={{0,1},{1,2},{2,3},{4,5},{5,6},{6,7},{8,9},{9,10},{10,11},{12,13},{... | collective-permute-start | bytes 1032200 | tf_op jit(solution)/shard_map/ppermute | solution.py:26
  78.4 1.9 %collective-permute-start.8 = (f32[3,1,32,7,128]{4,2,1,0,3:T(8,128)S(1)}, f32[3,1,32,7,128]{4,2,1,0,3:T(8,128)}, u32[]{:S(2)}, u32[]{:S(2)}) collective-permute-start(f32[3,1,32,7,128]{4,2,1,0,3:T(8,128)S(1)} %pad_maximum_fusion.1), channel_id=1, source_target_pairs={{1,0},{2,1},{3,2},{5,4},{6,5},{7,6},{9,8},{10,9},{11,10},{13,12},{... | collective-permute-start | bytes 1032200 | tf_op jit(solution)/shard_map/ppermute | solution.py:27
  82.6 4.5 %collective-permute-done.8 = f32[3,1,32,7,128]{4,2,1,0,3:T(8,128)} collective-permute-done((f32[3,1,32,7,128]{4,2,1,0,3:T(8,128)S(1)}, f32[3,1,32,7,128]{4,2,1,0,3:T(8,128)}, u32[]{:S(2)}, u32[]{:S(2)}) %collective-permute-start.8) | collective-permute-done | bytes 344096 | tf_op jit(solution)/shard_map/ppermute | solution.py:27
  90.1 26.5 %while.10 = (s32[]{:T(128)}, f32[4,8,3,128]{3,1,0,2:T(8,128)S(1)}, f32[4,8,8,7,128]{4,2,1,3,0:T(8,128)S(1)}, f32[4,8,3,128]{3,1,0,2:T(8,128)S(1)}, f32[4,8,8,7]{2,1,3,0:T(8,128)S(1)}, /*index=5*/s32[]{:T(128)}) while((s32[]{:T(128)}, f32[4,8,3,128]{3,1,0,2:T(8,128)S(1)}, f32[4,8,8,7,128]{4,2,1,3,0:T(8,128)S(1)}, ...), condition=%wide.region_11.12_spmd, body=%wide.region_4.11_spmd.sunk | while | flops 27490304 | bytes 1315669 | solution.py:81
  90.2 6.3 %fusion.108 = (f32[8,128]{1,0:T(8,128)S(1)}, f32[8,128]{1,0:T(8,128)S(1)}, f32[8,128]{1,0:T(8,128)S(1)}) fusion(f32[8,8,128]{2,1,0:T(8,128)S(1)} %get-tuple-element.182, f32[8,8,128]{2,1,0:T(8,128)S(1)} %get-tuple-element.183, f32[8,128]{1,0:T(8,128)S(1)} %get-tuple-element.184, f32[8,8,128]{2,1,0:T(8,128)S(1)} %get-tuple-element.185, ...), kind=kLoop, calls=%fused_computation.38.clone.1 | loop fusion | flops 27259904 | bytes 253952 | tf_op jit(solution)/shard_map/while/body/eval_jaxpr/vmap()/reduce_sum | solution.py:51
  96.8 6.3 %fusion.108 = (f32[8,128]{1,0:T(8,128)S(1)}, f32[8,128]{1,0:T(8,128)S(1)}, f32[8,128]{1,0:T(8,128)S(1)}) fusion(f32[8,8,128]{2,1,0:T(8,128)S(1)} %get-tuple-element.182, f32[8,8,128]{2,1,0:T(8,128)S(1)} %get-tuple-element.183, f32[8,128]{1,0:T(8,128)S(1)} %get-tuple-element.184, f32[8,8,128]{2,1,0:T(8,128)S(1)} %get-tuple-element.185, ...), kind=kLoop, calls=%fused_computation.38.clone.1 | loop fusion | flops 27259904 | bytes 253952 | tf_op jit(solution)/shard_map/while/body/eval_jaxpr/vmap()/reduce_sum | solution.py:51
  103.4 6.3 %fusion.108 = (f32[8,128]{1,0:T(8,128)S(1)}, f32[8,128]{1,0:T(8,128)S(1)}, f32[8,128]{1,0:T(8,128)S(1)}) fusion(f32[8,8,128]{2,1,0:T(8,128)S(1)} %get-tuple-element.182, f32[8,8,128]{2,1,0:T(8,128)S(1)} %get-tuple-element.183, f32[8,128]{1,0:T(8,128)S(1)} %get-tuple-element.184, f32[8,8,128]{2,1,0:T(8,128)S(1)} %get-tuple-element.185, ...), kind=kLoop, calls=%fused_computation.38.clone.1 | loop fusion | flops 27259904 | bytes 253952 | tf_op jit(solution)/shard_map/while/body/eval_jaxpr/vmap()/reduce_sum | solution.py:51
  110.0 6.3 %fusion.108 = (f32[8,128]{1,0:T(8,128)S(1)}, f32[8,128]{1,0:T(8,128)S(1)}, f32[8,128]{1,0:T(8,128)S(1)}) fusion(f32[8,8,128]{2,1,0:T(8,128)S(1)} %get-tuple-element.182, f32[8,8,128]{2,1,0:T(8,128)S(1)} %get-tuple-element.183, f32[8,128]{1,0:T(8,128)S(1)} %get-tuple-element.184, f32[8,8,128]{2,1,0:T(8,128)S(1)} %get-tuple-element.185, ...), kind=kLoop, calls=%fused_computation.38.clone.1 | loop fusion | flops 27259904 | bytes 253952 | tf_op jit(solution)/shard_map/while/body/eval_jaxpr/vmap()/reduce_sum | solution.py:51
  (181 shorter events, 33.3 us)
Async XLA Ops:
  0.0 22.6 %copy-start = (s32[1024]{0:T(1024)S(1)}, s32[1024]{0:T(1024)}, u32[]{:S(2)}) copy-start(s32[1024]{0:T(1024)} %param.27) | copy-start | bytes 12292
  13.6 30.3 %collective-permute-start = (f32[9,7,128]{2,0,1:T(8,128)S(1)}, f32[9,7,128]{2,0,1:T(8,128)S(1)}, u32[]{:S(2)}, u32[]{:S(2)}) collective-permute-start(f32[9,7,128]{2,0,1:T(8,128)S(1)} %pad_maximum_fusion.2), channel_id=1, source_target_pairs={{0,16},{4,20},{8,24},{12,28},{16,0},{20,4},{24,8},{28,12},{1,17},{... | collective-permute-start | bytes 96776 | tf_op jit(solution)/shard_map/ppermute | solution.py:16
  44.2 8.4 %collective-permute-start.1 = (f32[10,7,128]{2,0,1:T(8,128)S(1)}, f32[10,7,128]{2,0,1:T(8,128)S(1)}, u32[]{:S(2)}, u32[]{:S(2)}) collective-permute-start(f32[10,7,128]{2,0,1:T(8,128)S(1)} %pad_maximum_fusion.3), channel_id=1, source_target_pairs={{0,8},{4,12},{8,0},{12,4},{16,24},{20,28},{24,16},{28,20},{1,9},{5... | collective-permute-start | bytes 107528 | tf_op jit(solution)/shard_map/ppermute | solution.py:16
  50.7 4.8 %copy-start.1 = (s32[1,1,32,8]{2,3,1,0:T(8,128)S(1)}, s32[1,1,32,8]{2,3,1,0:T(8,128)}, u32[]{:S(2)}) copy-start(s32[1,1,32,8]{2,3,1,0:T(8,128)} %param.28) | copy-start | bytes 3076
  52.9 3.1 %collective-permute-start.2 = (f32[12,7,128]{2,0,1:T(8,128)S(1)}, f32[12,7,128]{2,0,1:T(8,128)S(1)}, u32[]{:S(2)}, u32[]{:S(2)}) collective-permute-start(f32[12,7,128]{2,0,1:T(8,128)S(1)} %pad_maximum_fusion.4), channel_id=1, source_target_pairs={{0,4},{4,0},{8,12},{12,8},{16,20},{20,16},{24,28},{28,24},{1,5},{5... | collective-permute-start | bytes 129032 | tf_op jit(solution)/shard_map/ppermute | solution.py:16
  56.2 3.1 %collective-permute-start.3 = (f32[16,7,128]{2,0,1:T(8,128)S(1)}, f32[16,7,128]{2,0,1:T(8,128)S(1)}, u32[]{:S(2)}, u32[]{:S(2)}) collective-permute-start(f32[16,7,128]{2,0,1:T(8,128)S(1)} %concatenate.47), channel_id=1, source_target_pairs={{0,2},{1,3},{2,0},{3,1},{4,6},{5,7},{6,4},{7,5},{8,10},{9,11},{10,... | collective-permute-start | bytes 172040 | tf_op jit(solution)/shard_map/ppermute | solution.py:16
  59.5 5.1 %collective-permute-start.4 = (f32[24,7,128]{2,0,1:T(8,128)S(1)}, f32[24,7,128]{2,0,1:T(8,128)S(1)}, u32[]{:S(2)}, u32[]{:S(2)}) collective-permute-start(f32[24,7,128]{2,0,1:T(8,128)S(1)} %concatenate.48), channel_id=1, source_target_pairs={{0,1},{1,0},{2,3},{3,2},{4,5},{5,4},{6,7},{7,6},{8,9},{9,8},{10,11... | collective-permute-start | bytes 258056 | tf_op jit(solution)/shard_map/ppermute | solution.py:16
  64.8 5.7 %collective-permute-start.5 = (f32[1,1,32,7,128]{4,2,1,0,3:T(8,128)S(1)}, f32[1,1,32,7,128]{4,2,1,0,3:T(8,128)S(1)}, u32[]{:S(2)}, u32[]{:S(2)}) collective-permute-start(f32[1,1,32,7,128]{4,2,1,0,3:T(8,128)S(1)} %slice_bitcast_fusion.16), channel_id=1, source_target_pairs={{0,4},{4,8},{8,12},{12,16},{16,20},{20,24},{24,28},{1,5},{5,9},{9,... | collective-permute-start | bytes 344072 | tf_op jit(solution)/shard_map/ppermute | solution.py:26
  67.9 6.3 %collective-permute-start.6 = (f32[1,1,32,7,128]{4,2,1,0,3:T(8,128)S(1)}, f32[1,1,32,7,128]{4,2,1,0,3:T(8,128)S(1)}, u32[]{:S(2)}, u32[]{:S(2)}) collective-permute-start(f32[1,1,32,7,128]{4,2,1,0,3:T(8,128)S(1)} %slice_bitcast_fusion.16), channel_id=1, source_target_pairs={{4,0},{8,4},{12,8},{16,12},{20,16},{24,20},{28,24},{5,1},{9,5},{13... | collective-permute-start | bytes 344072 | tf_op jit(solution)/shard_map/ppermute | solution.py:27
  74.3 8.3 %collective-permute-start.7 = (f32[3,1,32,7,128]{4,2,1,0,3:T(8,128)S(1)}, f32[3,1,32,7,128]{4,2,1,0,3:T(8,128)}, u32[]{:S(2)}, u32[]{:S(2)}) collective-permute-start(f32[3,1,32,7,128]{4,2,1,0,3:T(8,128)S(1)} %pad_maximum_fusion.1), channel_id=1, source_target_pairs={{0,1},{1,2},{2,3},{4,5},{5,6},{6,7},{8,9},{9,10},{10,11},{12,13},{... | collective-permute-start | bytes 1032200 | tf_op jit(solution)/shard_map/ppermute | solution.py:26
  78.4 8.7 %collective-permute-start.8 = (f32[3,1,32,7,128]{4,2,1,0,3:T(8,128)S(1)}, f32[3,1,32,7,128]{4,2,1,0,3:T(8,128)}, u32[]{:S(2)}, u32[]{:S(2)}) collective-permute-start(f32[3,1,32,7,128]{4,2,1,0,3:T(8,128)S(1)} %pad_maximum_fusion.1), channel_id=1, source_target_pairs={{1,0},{2,1},{3,2},{5,4},{6,5},{7,6},{9,8},{10,9},{11,10},{13,12},{... | collective-permute-start | bytes 1032200 | tf_op jit(solution)/shard_map/ppermute | solution.py:27
  116.6 0.6 copy-start.2

commit v2 on v1

--- a/solution.py
+++ b/solution.py
@@ -82,40 +82,47 @@
     return velocity.reshape((block_count,) + velocity.shape[2:])
 
 
-def trace_back(loc, moves, levels, bits_x, size_x, size_y, nbd):
+def partner_values(values, level, bits_x, levels):
+    size_x, size_y = values.shape
+    if level < bits_x:
+        step = 1 << bits_x - 1 - level
+        split = values.reshape(size_x // (2 * step), 2, step, size_y)
+        return split[:, ::-1].reshape(size_x, size_y)
+    step = 1 << levels - 1 - level
+    split = values.reshape(size_x, size_y // (2 * step), 2, step)
+    return split[:, :, ::-1].reshape(size_x, size_y)
+
+
+def trace_back(loc, moves, levels, bits_x, nbd):
+    size_x, size_y = moves.shape[1], moves.shape[2]
     devices = size_x * size_y
-    linear = np.arange(devices)
-    grid_x, grid_y = linear // size_y, linear % size_y
-    flat = moves.reshape(levels, devices)
-    mates = []
-    for level in range(levels):
-        if level < bits_x:
-            mates.append((grid_x ^ 1 << bits_x - 1 - level) * size_y + grid_y)
-        else:
-            mates.append(grid_x * size_y + (grid_y ^ 1 << levels - 1 - level))
-    count = jnp.full((devices,), nbd, jnp.int32)
-    for level in range(levels):
-        count = count + flat[level] - flat[level][mates[level]]
+    mate_moves = [partner_values(moves[level], level, bits_x, levels) for level in range(levels)]
+    count = jnp.full((size_x, size_y), nbd, jnp.int32)
+    for level in range(levels):
+        count = count + moves[level] - mate_moves[level]
     kept = []
     for level in range(levels):
-        left = count - flat[level]
+        left = count - moves[level]
         kept.append(left)
-        count = left + flat[level][mates[level]]
-    device = loc // nbd
-    slot = loc % nbd
+        count = left + mate_moves[level]
+    kept_flat = [k.reshape(1, devices) for k in kept]
+    kept_mate = [partner_values(k, level, bits_x, levels).reshape(1, devices) for level, k in enumerate(kept)]
+    every = jnp.arange(devices, dtype=jnp.int32)[None, :]
+    device = loc.reshape(-1) // nbd
+    slot = loc.reshape(-1) % nbd
     for level in reversed(range(levels)):
         if level < bits_x:
-            bit = 1 << bits_x - 1 - level
-            mate = ((device // size_y) ^ bit) * size_y + device % size_y
+            bit = (1 << bits_x - 1 - level) * size_y
         else:
             bit = 1 << levels - 1 - level
-            mate = (device // size_y) * size_y + ((device % size_y) ^ bit)
-        here = kept[level][device]
-        there = kept[level][mate]
+        mate = jnp.bitwise_xor(device, bit)
+        pick = device[:, None] == every
+        here = jnp.sum(jnp.where(pick, kept_flat[level], 0), axis=1)
+        there = jnp.sum(jnp.where(pick, kept_mate[level], 0), axis=1)
         moved = slot >= here
         slot = jnp.where(moved, slot - here + there, slot)
         device = jnp.where(moved, mate, device)
-    return device, slot
+    return device.reshape(loc.shape), slot.reshape(loc.shape)
 
 
 def table_blocks(table, lanes):
@@ -136,13 +143,13 @@
     nbd = near_list.shape[2]
     lanes = positions.shape[4]
     me = column_index * size_y + row_index
-    slot_table = slot_multipoles(positions[0, 0], strength[0, 0], core[0, 0])
+    held = jnp.concatenate([positions[0, 0], strength[0, 0], core[0, 0][:, None, :]], axis=1)
+    slot_table = slot_multipoles(held[:, 0:3], held[:, 3:6], held[:, 6])
     width = slot_table.shape[1]
     gathered = table_blocks(slot_table, lanes)
     pieces = gathered.shape[0]
     far_where = owner[far_list[0, 0]]
-    far_device, far_slot = trace_back(far_where, moves, levels, bits_x, size_x, size_y, nbd)
-    held = jnp.concatenate([positions[0, 0], strength[0, 0], core[0, 0][:, None, :]], axis=1)
+    far_device, far_slot = trace_back(far_where, moves, levels, bits_x, nbd)
     held = jnp.pad(held, ((0, MOVE), (0, 0), (0, 0)))
     plans = []
     level_bits = []

time: 118 us -> 96 us (0.81)
  the two profiles are of different devices: /device:TPU:1 before, /device:TPU:9 now
where the time goes in v2:
time: 96 us; the launch traced here: 94.6 us
  other arithmetic  33 us (34%)
  starting transfers between devices  21.7 us (23%)
  local copies, waits for them, and re-layouts  17.3 us (18%)
  between operations  12.3 us (13%)
  waiting for transfers between devices  9.91 us (10%)
    reduce_sum x4, other arithmetic, evaluate(): near_x = jnp.sum(str_y * sep_z - str_z * sep_y, axis=(0, 2))  25.1 us
    ppermute x5, starting transfers between devices, from_partner(): lax.ppermute(shard, axis, [(i, i ^ 1 << apart) for i in range(lax.axis_si...  9.66 us
    ppermute x2, starting transfers between devices, padded(): before = lax.ppermute(last, axis, up)  7.05 us
    ppermute x2, waiting for transfers between devices, padded(): after = lax.ppermute(first, axis, down)  6.87 us
    ppermute x2, starting transfers between devices, padded(): after = lax.ppermute(first, axis, down)  4.98 us
  transfers between devices with their start and end apart: 9, of which 7 were waited for; matrix products, arithmetic and copies ran while one was open for 14% of the time, Pallas kernels for 0%

profile of v2, /device:TPU:9, one launch (start us, length us, event | category | flops | bytes accessed | tf_op | source)
XLA Modules:
  0.0 94.6 jit_solution(11355287769397919783)
XLA Ops:
  0.0 1.5 %constant_dynamic-slice_fusion.13 = (s32[1,1,1]{1,2,0:T(1,128)}, s32[1,1,1]{1,2,0:T(1,128)}, s32[1,1,1]{1,2,0:T(1,128)}, s32[1,1,1]{1,2,0:T(1,128)}, s32[1,1,1]{...) fusion(s32[5,8,4]{1,2,0:T(4,128)} %param.12, ...), kind=kLoop, calls=%fused_computation.259 | loop fusion | bytes 108 | tf_op jit(solution)/shard_map/dynamic_slice | solution.py:163
  8.4 1.0 %reduce_sum.204 = f32[72,3]{0,1:T(4,128)S(1)} reduce(f32[1,1,72,3,128]{4,2,3,1,0:T(8,128)} %param.9, f32[]{:T(128)} %constant.185.clone.1), dimensions={0,1,4}, to_apply=%region_0.0 | reduce | flops 27432 | bytes 111460 | tf_op jit(solution)/shard_map/reduce_sum | solution.py:33
  9.5 1.1 %multiply_reduce_fusion = f32[72]{0:T(128)S(1)} fusion(f32[72,3]{0,1:T(4,128)S(1)} %broadcast_multiply_fusion, f32[1,1,72,3,128]{4,2,3,1,0:T(8,128)} %param.9), kind=kLoop, calls=%fused_computation.77 | loop fusion | flops 82872 | bytes 111744 | tf_op jit(solution)/shard_map/reduce_sum | solution.py:36
  11.5 1.0 %reduce_sum.205 = f32[72,3]{0,1:T(4,128)S(1)} reduce(f32[1,1,72,3,128]{4,2,3,1,0:T(8,128)} %param.10, f32[]{:T(128)} %constant.185.clone.1), dimensions={0,1,4}, to_apply=%region_1.0 | reduce | flops 27432 | bytes 111460 | tf_op jit(solution)/shard_map/reduce_sum | solution.py:34
  13.6 2.4 %collective-permute-start = (f32[9,7,128]{2,0,1:T(8,128)S(1)}, f32[9,7,128]{2,0,1:T(8,128)S(1)}, u32[]{:S(2)}, u32[]{:S(2)}) collective-permute-start(f32[9,7,128]{2,0,1:T(8,128)S(1)} %pad_maximum_fusion.2), channel_id=1, source_target_pairs={{0,16},{4,20},{8,24},{12,28},{16,0},{20,4},{24,8},{28,12},{1,17},{... | collective-permute-start | bytes 96776 | tf_op jit(solution)/shard_map/ppermute | solution.py:16
  21.2 1.4 %gather_fusion.2 = s32[256]{0:T(256)S(1)} fusion(s32[1024]{0:T(1024)S(1)} %copy-done, s32[1024]{0:T(1024)S(1)} %pad_clamp_fusion.1), kind=kCustom, calls=%fused_computation.2 | custom fusion | bytes 3072 | tf_op jit(solution)/shard_map/gather | solution.py:151
  29.2 1.3 %collective-permute-start.2 = (f32[12,7,128]{2,0,1:T(8,128)S(1)}, f32[12,7,128]{2,0,1:T(8,128)S(1)}, u32[]{:S(2)}, u32[]{:S(2)}) collective-permute-start(f32[12,7,128]{2,0,1:T(8,128)S(1)} %pad_maximum_fusion.4), channel_id=1, source_target_pairs={{0,4},{4,0},{8,12},{12,8},{16,20},{20,16},{24,28},{28,24},{1,5},{5... | collective-permute-start | bytes 129032 | tf_op jit(solution)/shard_map/ppermute | solution.py:16
  32.5 1.3 %collective-permute-start.3 = (f32[16,7,128]{2,0,1:T(8,128)S(1)}, f32[16,7,128]{2,0,1:T(8,128)S(1)}, u32[]{:S(2)}, u32[]{:S(2)}) collective-permute-start(f32[16,7,128]{2,0,1:T(8,128)S(1)} %concatenate.47), channel_id=1, source_target_pairs={{0,2},{1,3},{2,0},{3,1},{4,6},{5,7},{6,4},{7,5},{8,10},{9,11},{10,... | collective-permute-start | bytes 172040 | tf_op jit(solution)/shard_map/ppermute | solution.py:16
  35.8 4.5 %collective-permute-start.4 = (f32[24,7,128]{2,0,1:T(8,128)S(1)}, f32[24,7,128]{2,0,1:T(8,128)S(1)}, u32[]{:S(2)}, u32[]{:S(2)}) collective-permute-start(f32[24,7,128]{2,0,1:T(8,128)S(1)} %concatenate.48), channel_id=1, source_target_pairs={{0,1},{1,0},{2,3},{3,2},{4,5},{5,4},{6,7},{7,6},{8,9},{9,8},{10,11... | collective-permute-start | bytes 258056 | tf_op jit(solution)/shard_map/ppermute | solution.py:16
  40.3 1.4 %gather_fusion = s32[256]{0:T(256)S(1)} fusion(s32[1024]{0:T(1024)S(1)} %copy-done, s32[1024]{0:T(1024)S(1)} %pad_clamp_fusion.3), kind=kCustom, calls=%fused_computation | custom fusion | bytes 3072 | tf_op jit(solution)/shard_map/gather | solution.py:189
  42.0 3.1 %collective-permute-start.5 = (f32[1,1,32,7,128]{4,2,1,0,3:T(8,128)S(1)}, f32[1,1,32,7,128]{4,2,1,0,3:T(8,128)S(1)}, u32[]{:S(2)}, u32[]{:S(2)}) collective-permute-start(f32[1,1,32,7,128]{4,2,1,0,3:T(8,128)S(1)} %slice_bitcast_fusion.16), channel_id=1, source_target_pairs={{0,4},{4,8},{8,12},{12,16},{16,20},{20,24},{24,28},{1,5},{5,9},{9,... | collective-permute-start | bytes 344072 | tf_op jit(solution)/shard_map/ppermute | solution.py:26
  45.1 3.1 %collective-permute-start.6 = (f32[1,1,32,7,128]{4,2,1,0,3:T(8,128)S(1)}, f32[1,1,32,7,128]{4,2,1,0,3:T(8,128)S(1)}, u32[]{:S(2)}, u32[]{:S(2)}) collective-permute-start(f32[1,1,32,7,128]{4,2,1,0,3:T(8,128)S(1)} %slice_bitcast_fusion.16), channel_id=1, source_target_pairs={{4,0},{8,4},{12,8},{16,12},{20,16},{24,20},{28,24},{5,1},{9,5},{13... | collective-permute-start | bytes 344072 | tf_op jit(solution)/shard_map/ppermute | solution.py:27
  48.2 1.3 %collective-permute-done.5 = f32[1,1,32,7,128]{4,2,1,0,3:T(8,128)S(1)} collective-permute-done((f32[1,1,32,7,128]{4,2,1,0,3:T(8,128)S(1)}, f32[1,1,32,7,128]{4,2,1,0,3:T(8,128)S(1)}, u32[]{:S(2)}, u32[]{:S(2)}) %collective-permute-start.5) | collective-permute-done | bytes 114720 | tf_op jit(solution)/shard_map/ppermute | solution.py:26
  49.5 2.4 %collective-permute-done.6 = f32[1,1,32,7,128]{4,2,1,0,3:T(8,128)S(1)} collective-permute-done((f32[1,1,32,7,128]{4,2,1,0,3:T(8,128)S(1)}, f32[1,1,32,7,128]{4,2,1,0,3:T(8,128)S(1)}, u32[]{:S(2)}, u32[]{:S(2)}) %collective-permute-start.6) | collective-permute-done | bytes 114720 | tf_op jit(solution)/shard_map/ppermute | solution.py:27
  51.9 3.9 %collective-permute-start.7 = (f32[3,1,32,7,128]{4,2,1,0,3:T(8,128)S(1)}, f32[3,1,32,7,128]{4,2,1,0,3:T(8,128)}, u32[]{:S(2)}, u32[]{:S(2)}) collective-permute-start(f32[3,1,32,7,128]{4,2,1,0,3:T(8,128)S(1)} %pad_maximum_fusion.1), channel_id=1, source_target_pairs={{0,1},{1,2},{2,3},{4,5},{5,6},{6,7},{8,9},{9,10},{10,11},{12,13},{... | collective-permute-start | bytes 1032200 | tf_op jit(solution)/shard_map/ppermute | solution.py:26
  55.8 1.9 %collective-permute-start.8 = (f32[3,1,32,7,128]{4,2,1,0,3:T(8,128)S(1)}, f32[3,1,32,7,128]{4,2,1,0,3:T(8,128)}, u32[]{:S(2)}, u32[]{:S(2)}) collective-permute-start(f32[3,1,32,7,128]{4,2,1,0,3:T(8,128)S(1)} %pad_maximum_fusion.1), channel_id=1, source_target_pairs={{1,0},{2,1},{3,2},{5,4},{6,5},{7,6},{9,8},{10,9},{11,10},{13,12},{... | collective-permute-start | bytes 1032200 | tf_op jit(solution)/shard_map/ppermute | solution.py:27
  60.0 4.5 %collective-permute-done.8 = f32[3,1,32,7,128]{4,2,1,0,3:T(8,128)} collective-permute-done((f32[3,1,32,7,128]{4,2,1,0,3:T(8,128)S(1)}, f32[3,1,32,7,128]{4,2,1,0,3:T(8,128)}, u32[]{:S(2)}, u32[]{:S(2)}) %collective-permute-start.8) | collective-permute-done | bytes 344096 | tf_op jit(solution)/shard_map/ppermute | solution.py:27
  64.5 1.2 %pad_maximum_fusion = f32[3,3,32,7,128]{4,2,1,0,3:T(8,128)S(1)} fusion(f32[3,1,32,7,128]{4,2,1,0,3:T(8,128)} %collective-permute-done.8, f32[1,1,32,7,128]{4,2,1,0,3:T(8,128)S(1)} %collective-permute-done.6, f32[1,1,32,7,128]{4,2,1,0,3:T(8,128)S(1)} %slice_bitcast_fusion.16, f32[1,1,32,7,128]{4,2,1,0,3:T(8,128)S(1)} %collective-permute-done.5, ...), kind=kLoop, calls=%fused_computation.71 | loop fusion | flops 1032192 | bytes 2064384 | tf_op jit(solution)/shard_map/concatenate | solution.py:28
  66.3 1.0 %gather_fusion.1 = f32[256,7,128]{2,1,0:T(8,128)S(1)} fusion(f32[288,7,128]{2,1,0:T(8,128)S(1)} %copy.147, s32[1024]{0:T(1024)S(1)} %pad_clamp_fusion.2), kind=kCustom, calls=%fused_computation.1 | custom fusion | bytes 1836032 | tf_op jit(solution)/shard_map/gather | solution.py:198
  67.5 26.5 %while.10 = (s32[]{:T(128)}, f32[4,8,3,128]{3,1,0,2:T(8,128)S(1)}, f32[4,8,8,7,128]{4,2,1,3,0:T(8,128)S(1)}, f32[4,8,3,128]{3,1,0,2:T(8,128)S(1)}, f32[4,8,8,7]{2,1,3,0:T(8,128)S(1)}, /*index=5*/s32[]{:T(128)}) while((s32[]{:T(128)}, f32[4,8,3,128]{3,1,0,2:T(8,128)S(1)}, f32[4,8,8,7,128]{4,2,1,3,0:T(8,128)S(1)}, ...), condition=%wide.region_21.22_spmd, body=%wide.region_14.0_spmd.sunk | while | flops 27490304 | bytes 1315669 | solution.py:81
  67.6 6.3 %fusion.86 = (f32[8,128]{1,0:T(8,128)S(1)}, f32[8,128]{1,0:T(8,128)S(1)}, f32[8,128]{1,0:T(8,128)S(1)}) fusion(f32[8,8,128]{2,1,0:T(8,128)S(1)} %get-tuple-element.178, f32[8,8,128]{2,1,0:T(8,128)S(1)} %get-tuple-element.179, f32[8,128]{1,0:T(8,128)S(1)} %get-tuple-element.180, f32[8,8,128]{2,1,0:T(8,128)S(1)} %get-tuple-element.181, ...), kind=kLoop, calls=%fused_computation.23.clone.1 | loop fusion | flops 27259904 | bytes 253952 | tf_op jit(solution)/shard_map/while/body/eval_jaxpr/vmap()/reduce_sum | solution.py:51
  74.2 6.3 %fusion.86 = (f32[8,128]{1,0:T(8,128)S(1)}, f32[8,128]{1,0:T(8,128)S(1)}, f32[8,128]{1,0:T(8,128)S(1)}) fusion(f32[8,8,128]{2,1,0:T(8,128)S(1)} %get-tuple-element.178, f32[8,8,128]{2,1,0:T(8,128)S(1)} %get-tuple-element.179, f32[8,128]{1,0:T(8,128)S(1)} %get-tuple-element.180, f32[8,8,128]{2,1,0:T(8,128)S(1)} %get-tuple-element.181, ...), kind=kLoop, calls=%fused_computation.23.clone.1 | loop fusion | flops 27259904 | bytes 253952 | tf_op jit(solution)/shard_map/while/body/eval_jaxpr/vmap()/reduce_sum | solution.py:51
  80.8 6.3 %fusion.86 = (f32[8,128]{1,0:T(8,128)S(1)}, f32[8,128]{1,0:T(8,128)S(1)}, f32[8,128]{1,0:T(8,128)S(1)}) fusion(f32[8,8,128]{2,1,0:T(8,128)S(1)} %get-tuple-element.178, f32[8,8,128]{2,1,0:T(8,128)S(1)} %get-tuple-element.179, f32[8,128]{1,0:T(8,128)S(1)} %get-tuple-element.180, f32[8,8,128]{2,1,0:T(8,128)S(1)} %get-tuple-element.181, ...), kind=kLoop, calls=%fused_computation.23.clone.1 | loop fusion | flops 27259904 | bytes 253952 | tf_op jit(solution)/shard_map/while/body/eval_jaxpr/vmap()/reduce_sum | solution.py:51
  87.5 6.3 %fusion.86 = (f32[8,128]{1,0:T(8,128)S(1)}, f32[8,128]{1,0:T(8,128)S(1)}, f32[8,128]{1,0:T(8,128)S(1)}) fusion(f32[8,8,128]{2,1,0:T(8,128)S(1)} %get-tuple-element.178, f32[8,8,128]{2,1,0:T(8,128)S(1)} %get-tuple-element.179, f32[8,128]{1,0:T(8,128)S(1)} %get-tuple-element.180, f32[8,8,128]{2,1,0:T(8,128)S(1)} %get-tuple-element.181, ...), kind=kLoop, calls=%fused_computation.23.clone.1 | loop fusion | flops 27259904 | bytes 253952 | tf_op jit(solution)/shard_map/while/body/eval_jaxpr/vmap()/reduce_sum | solution.py:51
  (198 shorter events, 17.5 us)
Async XLA Ops:
  0.0 21.2 %copy-start = (s32[1024]{0:T(1024)S(1)}, s32[1024]{0:T(1024)}, u32[]{:S(2)}) copy-start(s32[1024]{0:T(1024)} %param.13) | copy-start | bytes 12292
  13.6 12.0 %collective-permute-start = (f32[9,7,128]{2,0,1:T(8,128)S(1)}, f32[9,7,128]{2,0,1:T(8,128)S(1)}, u32[]{:S(2)}, u32[]{:S(2)}) collective-permute-start(f32[9,7,128]{2,0,1:T(8,128)S(1)} %pad_maximum_fusion.2), channel_id=1, source_target_pairs={{0,16},{4,20},{8,24},{12,28},{16,0},{20,4},{24,8},{28,12},{1,17},{... | collective-permute-start | bytes 96776 | tf_op jit(solution)/shard_map/ppermute | solution.py:16
  21.2 10.7 %copy-start.1 = (s32[1,1,32,8]{2,3,1,0:T(8,128)S(1)}, s32[1,1,32,8]{2,3,1,0:T(8,128)}, u32[]{:S(2)}) copy-start(s32[1,1,32,8]{2,3,1,0:T(8,128)} %param.14) | copy-start | bytes 3076
  25.9 3.1 %collective-permute-start.1 = (f32[10,7,128]{2,0,1:T(8,128)S(1)}, f32[10,7,128]{2,0,1:T(8,128)S(1)}, u32[]{:S(2)}, u32[]{:S(2)}) collective-permute-start(f32[10,7,128]{2,0,1:T(8,128)S(1)} %pad_maximum_fusion.3), channel_id=1, source_target_pairs={{0,8},{4,12},{8,0},{12,4},{16,24},{20,28},{24,16},{28,20},{1,9},{5... | collective-permute-start | bytes 107528 | tf_op jit(solution)/shard_map/ppermute | solution.py:16
  29.2 3.1 %collective-permute-start.2 = (f32[12,7,128]{2,0,1:T(8,128)S(1)}, f32[12,7,128]{2,0,1:T(8,128)S(1)}, u32[]{:S(2)}, u32[]{:S(2)}) collective-permute-start(f32[12,7,128]{2,0,1:T(8,128)S(1)} %pad_maximum_fusion.4), channel_id=1, source_target_pairs={{0,4},{4,0},{8,12},{12,8},{16,20},{20,16},{24,28},{28,24},{1,5},{5... | collective-permute-start | bytes 129032 | tf_op jit(solution)/shard_map/ppermute | solution.py:16
  32.5 3.1 %collective-permute-start.3 = (f32[16,7,128]{2,0,1:T(8,128)S(1)}, f32[16,7,128]{2,0,1:T(8,128)S(1)}, u32[]{:S(2)}, u32[]{:S(2)}) collective-permute-start(f32[16,7,128]{2,0,1:T(8,128)S(1)} %concatenate.47), channel_id=1, source_target_pairs={{0,2},{1,3},{2,0},{3,1},{4,6},{5,7},{6,4},{7,5},{8,10},{9,11},{10,... | collective-permute-start | bytes 172040 | tf_op jit(solution)/shard_map/ppermute | solution.py:16
  35.8 5.9 %collective-permute-start.4 = (f32[24,7,128]{2,0,1:T(8,128)S(1)}, f32[24,7,128]{2,0,1:T(8,128)S(1)}, u32[]{:S(2)}, u32[]{:S(2)}) collective-permute-start(f32[24,7,128]{2,0,1:T(8,128)S(1)} %concatenate.48), channel_id=1, source_target_pairs={{0,1},{1,0},{2,3},{3,2},{4,5},{5,4},{6,7},{7,6},{8,9},{9,8},{10,11... | collective-permute-start | bytes 258056 | tf_op jit(solution)/shard_map/ppermute | solution.py:16
  42.0 7.5 %collective-permute-start.5 = (f32[1,1,32,7,128]{4,2,1,0,3:T(8,128)S(1)}, f32[1,1,32,7,128]{4,2,1,0,3:T(8,128)S(1)}, u32[]{:S(2)}, u32[]{:S(2)}) collective-permute-start(f32[1,1,32,7,128]{4,2,1,0,3:T(8,128)S(1)} %slice_bitcast_fusion.16), channel_id=1, source_target_pairs={{0,4},{4,8},{8,12},{12,16},{16,20},{20,24},{24,28},{1,5},{5,9},{9,... | collective-permute-start | bytes 344072 | tf_op jit(solution)/shard_map/ppermute | solution.py:26
  45.1 6.8 %collective-permute-start.6 = (f32[1,1,32,7,128]{4,2,1,0,3:T(8,128)S(1)}, f32[1,1,32,7,128]{4,2,1,0,3:T(8,128)S(1)}, u32[]{:S(2)}, u32[]{:S(2)}) collective-permute-start(f32[1,1,32,7,128]{4,2,1,0,3:T(8,128)S(1)} %slice_bitcast_fusion.16), channel_id=1, source_target_pairs={{4,0},{8,4},{12,8},{16,12},{20,16},{24,20},{28,24},{5,1},{9,5},{13... | collective-permute-start | bytes 344072 | tf_op jit(solution)/shard_map/ppermute | solution.py:27
  51.9 8.1 %collective-permute-start.7 = (f32[3,1,32,7,128]{4,2,1,0,3:T(8,128)S(1)}, f32[3,1,32,7,128]{4,2,1,0,3:T(8,128)}, u32[]{:S(2)}, u32[]{:S(2)}) collective-permute-start(f32[3,1,32,7,128]{4,2,1,0,3:T(8,128)S(1)} %pad_maximum_fusion.1), channel_id=1, source_target_pairs={{0,1},{1,2},{2,3},{4,5},{5,6},{6,7},{8,9},{9,10},{10,11},{12,13},{... | collective-permute-start | bytes 1032200 | tf_op jit(solution)/shard_map/ppermute | solution.py:26
  55.8 8.7 %collective-permute-start.8 = (f32[3,1,32,7,128]{4,2,1,0,3:T(8,128)S(1)}, f32[3,1,32,7,128]{4,2,1,0,3:T(8,128)}, u32[]{:S(2)}, u32[]{:S(2)}) collective-permute-start(f32[3,1,32,7,128]{4,2,1,0,3:T(8,128)S(1)} %pad_maximum_fusion.1), channel_id=1, source_target_pairs={{1,0},{2,1},{3,2},{5,4},{6,5},{7,6},{9,8},{10,9},{11,10},{13,12},{... | collective-permute-start | bytes 1032200 | tf_op jit(solution)/shard_map/ppermute | solution.py:27
  94.0 0.6 copy-start.2

commit v3 on v2

--- a/solution.py
+++ b/solution.py
@@ -44,7 +44,8 @@
     radius_sq = (
         sep_x * sep_x + sep_y * sep_y + sep_z * sep_z + (sources[:, 6] * sources[:, 6])[:, None, :]
     )
-    weight = 1.0 / (radius_sq * jnp.sqrt(radius_sq))
+    inverse = lax.rsqrt(radius_sq)
+    weight = inverse * inverse * inverse
     str_x = sources[:, 3][:, None, :] * weight
     str_y = sources[:, 4][:, None, :] * weight
     str_z = sources[:, 5][:, None, :] * weight
@@ -55,7 +56,8 @@
     off_y = target[1][None, :] - moments[:, 1][:, None]
     off_z = target[2][None, :] - moments[:, 2][:, None]
     far_sq = off_x * off_x + off_y * off_y + off_z * off_z + moments[:, 6][:, None]
-    far_weight = 1.0 / (far_sq * jnp.sqrt(far_sq))
+    far_inverse = lax.rsqrt(far_sq)
+    far_weight = far_inverse * far_inverse * far_inverse
     mom_x = moments[:, 3][:, None] * far_weight
     mom_y = moments[:, 4][:, None] * far_weight
     mom_z = moments[:, 5][:, None] * far_weight
@@ -196,7 +198,7 @@
     source_pool = grid_blocks.reshape(9 * nbd, 7, blocks.shape[2])
     pool_index = direction * nbd + source_slot
     sources_all = source_pool[pool_index]
-    velocity = evaluate_all(blocks[:, 0:3], sources_all, moments)
+    velocity = jax.vmap(evaluate)(blocks[:, 0:3], sources_all, moments)
     return velocity[None, None]
 
 

time: 96 us -> 90.4 us (0.942)
  other arithmetic: 33 us -> 30.5 us
  waiting for transfers between devices: 9.91 us -> 7.74 us
  starting transfers between devices: 21.7 us -> 20.5 us
    ppermute x2, waiting for transfers between devices: 6.87 us -> 2.65 us  [padded(): after = lax.ppermute(first, axis, down)]
    reduce_sum x4 -> x1, other arithmetic: 25.1 us -> 22.7 us  [evaluate(): near_x = jnp.sum(str_y * sep_z - str_z * sep_y, axis=(0, 2))]
    ppermute x2, starting transfers between devices: 7.05 us -> 5.3 us  [padded(): before = lax.ppermute(last, axis, up)]
    ppermute x5, waiting for transfers between devices: 1.38 us -> 2.88 us  [from_partner(): lax.ppermute(shard, axis, [(i, i ^ 1 << apart) for i in range(lax.axis_si...]
    ppermute x2, starting transfers between devices: 4.98 us -> 6.44 us  [padded(): after = lax.ppermute(first, axis, down)]
    concatenate x2, other arithmetic: 1.18 us -> 0.1 us  [padded(): shard = jnp.concatenate([before, shard, after], axis=dim)]
  transfers between devices with their start and end apart: 9 -> 9, of which waited for: 7 -> 6; matrix products, arithmetic and copies ran while one was open for 14% -> 17% of each run, Pallas kernels for 0% -> 0%
where the time goes in v3:
time: 90.4 us; the launch traced here: 89.1 us
  other arithmetic  30.5 us (34%)
  starting transfers between devices  20.5 us (23%)
  local copies, waits for them, and re-layouts  18 us (20%)
  between operations  12.4 us (14%)
  waiting for transfers between devices  7.74 us (9%)
    reduce_sum x1, other arithmetic, evaluate(): near_x = jnp.sum(str_y * sep_z - str_z * sep_y, axis=(0, 2))  22.7 us
    ppermute x5, starting transfers between devices, from_partner(): lax.ppermute(shard, axis, [(i, i ^ 1 << apart) for i in range(lax.axis_si...  8.79 us
    ppermute x2, starting transfers between devices, padded(): after = lax.ppermute(first, axis, down)  6.44 us
    ppermute x2, starting transfers between devices, padded(): before = lax.ppermute(last, axis, up)  5.3 us
    ppermute x5, waiting for transfers between devices, from_partner(): lax.ppermute(shard, axis, [(i, i ^ 1 << apart) for i in range(lax.axis_si...  2.88 us
    ppermute x2, waiting for transfers between devices, padded(): after = lax.ppermute(first, axis, down)  2.65 us
    ppermute x2, waiting for transfers between devices, padded(): before = lax.ppermute(last, axis, up)  2.22 us
  transfers between devices with their start and end apart: 9, of which 6 were waited for; matrix products, arithmetic and copies ran while one was open for 17% of the time, Pallas kernels for 0%

profile of v3, /device:TPU:9, one launch (start us, length us, event | category | flops | bytes accessed | tf_op | source)
XLA Modules:
  0.0 89.1 jit_solution(2653763200077050193)
XLA Ops:
  0.0 0.9 multiply_reduce_fusion.1
  0.9 1.5 %constant_dynamic-slice_fusion.13 = (s32[1,1,1]{1,2,0:T(1,128)}, s32[1,1,1]{1,2,0:T(1,128)}, s32[1,1,1]{1,2,0:T(1,128)}, s32[1,1,1]{1,2,0:T(1,128)}, s32[1,1,1]{...) fusion(s32[5,8,4]{1,2,0:T(4,128)} %param.10, ...), kind=kLoop, calls=%fused_computation.240 | loop fusion | bytes 108 | tf_op jit(solution)/shard_map/dynamic_slice | solution.py:165
  9.2 1.0 %reduce_sum.205 = f32[72,3]{0,1:T(4,128)S(1)} reduce(f32[1,1,72,3,128]{4,2,3,1,0:T(8,128)} %param.8, f32[]{:T(128)} %constant.164.clone.1), dimensions={0,1,4}, to_apply=%region_1.0 | reduce | flops 27432 | bytes 111460 | tf_op jit(solution)/shard_map/reduce_sum | solution.py:34
  10.3 1.0 %reduce_sum.204 = f32[72,3]{0,1:T(4,128)S(1)} reduce(f32[1,1,72,3,128]{4,2,3,1,0:T(8,128)} %param.7, f32[]{:T(128)} %constant.164.clone.1), dimensions={0,1,4}, to_apply=%region_0.0 | reduce | flops 27432 | bytes 111460 | tf_op jit(solution)/shard_map/reduce_sum | solution.py:33
  11.3 1.1 %multiply_reduce_fusion = f32[72]{0:T(128)S(1)} fusion(f32[72,3]{0,1:T(4,128)S(1)} %broadcast_multiply_fusion, f32[1,1,72,3,128]{4,2,3,1,0:T(8,128)} %param.7), kind=kLoop, calls=%fused_computation.51 | loop fusion | flops 82872 | bytes 111744 | tf_op jit(solution)/shard_map/reduce_sum | solution.py:36
  12.5 1.0 %select_maximum_fusion = f32[80,7,128]{2,0,1:T(8,128)S(1)} fusion(f32[72,1,128]{2,0,1:T(8,128)} %bitcast.210, f32[72,3,128]{2,0,1:T(8,128)} %bitcast.209, f32[72,3,128]{2,0,1:T(8,128)} %bitcast.207), kind=kLoop, calls=%fused_computation.26 | loop fusion | flops 430080 | bytes 544768 | tf_op jit(solution)/shard_map/concatenate | solution.py:148
  13.5 2.4 %collective-permute-start = (f32[9,7,128]{2,0,1:T(8,128)S(1)}, f32[9,7,128]{2,0,1:T(8,128)S(1)}, u32[]{:S(2)}, u32[]{:S(2)}) collective-permute-start(f32[9,7,128]{2,0,1:T(8,128)S(1)} %pad_maximum_fusion.2), channel_id=1, source_target_pairs={{0,16},{4,20},{8,24},{12,28},{16,0},{20,4},{24,8},{28,12},{1,17},{... | collective-permute-start | bytes 96776 | tf_op jit(solution)/shard_map/ppermute | solution.py:16
  19.4 0.8 copy.167
  20.3 1.4 %gather_fusion.2 = s32[256]{0:T(256)S(1)} fusion(s32[1024]{0:T(1024)S(1)} %copy-done, s32[1024]{0:T(1024)S(1)} %pad_clamp_fusion.1), kind=kCustom, calls=%fused_computation.2 | custom fusion | bytes 3072 | tf_op jit(solution)/shard_map/gather | solution.py:153
  28.7 1.4 %gather_fusion = s32[256]{0:T(256)S(1)} fusion(s32[1024]{0:T(1024)S(1)} %copy-done, s32[1024]{0:T(1024)S(1)} %pad_clamp_fusion.3), kind=kCustom, calls=%fused_computation | custom fusion | bytes 3072 | tf_op jit(solution)/shard_map/gather | solution.py:191
  30.5 1.3 %collective-permute-start.2 = (f32[12,7,128]{2,0,1:T(8,128)S(1)}, f32[12,7,128]{2,0,1:T(8,128)S(1)}, u32[]{:S(2)}, u32[]{:S(2)}) collective-permute-start(f32[12,7,128]{2,0,1:T(8,128)S(1)} %pad_maximum_fusion.4), channel_id=1, source_target_pairs={{0,4},{4,0},{8,12},{12,8},{16,20},{20,16},{24,28},{28,24},{1,5},{5... | collective-permute-start | bytes 129032 | tf_op jit(solution)/shard_map/ppermute | solution.py:16
  34.8 1.3 %collective-permute-start.3 = (f32[16,7,128]{2,0,1:T(8,128)S(1)}, f32[16,7,128]{2,0,1:T(8,128)S(1)}, u32[]{:S(2)}, u32[]{:S(2)}) collective-permute-start(f32[16,7,128]{2,0,1:T(8,128)S(1)} %concatenate.47), channel_id=1, source_target_pairs={{0,2},{1,3},{2,0},{3,1},{4,6},{5,7},{6,4},{7,5},{8,10},{9,11},{10,... | collective-permute-start | bytes 172040 | tf_op jit(solution)/shard_map/ppermute | solution.py:16
  36.1 1.8 %collective-permute-done.3 = f32[16,7,128]{2,0,1:T(8,128)S(1)} collective-permute-done((f32[16,7,128]{2,0,1:T(8,128)S(1)}, f32[16,7,128]{2,0,1:T(8,128)S(1)}, u32[]{:S(2)}, u32[]{:S(2)}) %collective-permute-start.3) | collective-permute-done | bytes 57376 | tf_op jit(solution)/shard_map/ppermute | solution.py:16
  38.1 3.6 %collective-permute-start.4 = (f32[24,7,128]{2,0,1:T(8,128)S(1)}, f32[24,7,128]{2,0,1:T(8,128)S(1)}, u32[]{:S(2)}, u32[]{:S(2)}) collective-permute-start(f32[24,7,128]{2,0,1:T(8,128)S(1)} %concatenate.48), channel_id=1, source_target_pairs={{0,1},{1,0},{2,3},{3,2},{4,5},{5,4},{6,7},{7,6},{8,9},{9,8},{10,11... | collective-permute-start | bytes 258056 | tf_op jit(solution)/shard_map/ppermute | solution.py:16
  41.7 0.9 %collective-permute-done.4 = f32[24,7,128]{2,0,1:T(8,128)S(1)} collective-permute-done((f32[24,7,128]{2,0,1:T(8,128)S(1)}, f32[24,7,128]{2,0,1:T(8,128)S(1)}, u32[]{:S(2)}, u32[]{:S(2)}) %collective-permute-start.4) | collective-permute-done | bytes 86048 | tf_op jit(solution)/shard_map/ppermute | solution.py:16
  42.8 3.0 %collective-permute-start.6 = (f32[1,1,32,7,128]{4,2,1,0,3:T(8,128)S(1)}, f32[1,1,32,7,128]{4,2,1,0,3:T(8,128)S(1)}, u32[]{:S(2)}, u32[]{:S(2)}) collective-permute-start(f32[1,1,32,7,128]{4,2,1,0,3:T(8,128)S(1)} %slice_bitcast_fusion), channel_id=1, source_target_pairs={{4,0},{8,4},{12,8},{16,12},{20,16},{24,20},{28,24},{5,1},{9,5},{13... | collective-permute-start | bytes 344072 | tf_op jit(solution)/shard_map/ppermute | solution.py:27
  45.8 2.3 %collective-permute-start.5 = (f32[1,1,32,7,128]{4,2,1,0,3:T(8,128)S(1)}, f32[1,1,32,7,128]{4,2,1,0,3:T(8,128)S(1)}, u32[]{:S(2)}, u32[]{:S(2)}) collective-permute-start(f32[1,1,32,7,128]{4,2,1,0,3:T(8,128)S(1)} %slice_bitcast_fusion), channel_id=1, source_target_pairs={{0,4},{4,8},{8,12},{12,16},{16,20},{20,24},{24,28},{1,5},{5,9},{9,... | collective-permute-start | bytes 344072 | tf_op jit(solution)/shard_map/ppermute | solution.py:26
  51.6 1.0 %collective-permute-done.5 = f32[1,1,32,7,128]{4,2,1,0,3:T(8,128)S(1)} collective-permute-done((f32[1,1,32,7,128]{4,2,1,0,3:T(8,128)S(1)}, f32[1,1,32,7,128]{4,2,1,0,3:T(8,128)S(1)}, u32[]{:S(2)}, u32[]{:S(2)}) %collective-permute-start.5) | collective-permute-done | bytes 114720 | tf_op jit(solution)/shard_map/ppermute | solution.py:26
  52.7 3.4 %collective-permute-start.8 = (f32[3,1,32,7,128]{4,2,1,0,3:T(8,128)S(1)}, f32[3,1,32,7,128]{4,2,1,0,3:T(8,128)S(1)}, u32[]{:S(2)}, u32[]{:S(2)}) collective-permute-start(f32[3,1,32,7,128]{4,2,1,0,3:T(8,128)S(1)} %pad_maximum_fusion.1), channel_id=1, source_target_pairs={{1,0},{2,1},{3,2},{5,4},{6,5},{7,6},{9,8},{10,9},{11,10},{13,12},{... | collective-permute-start | bytes 1032200 | tf_op jit(solution)/shard_map/ppermute | solution.py:27
  56.1 3.0 %collective-permute-start.7 = (f32[3,1,32,7,128]{4,2,1,0,3:T(8,128)S(1)}, f32[3,1,32,7,128]{4,2,1,0,3:T(8,128)S(1)}, u32[]{:S(2)}, u32[]{:S(2)}) collective-permute-start(f32[3,1,32,7,128]{4,2,1,0,3:T(8,128)S(1)} %pad_maximum_fusion.1), channel_id=1, source_target_pairs={{0,1},{1,2},{2,3},{4,5},{5,6},{6,7},{8,9},{9,10},{10,11},{12,13},{... | collective-permute-start | bytes 1032200 | tf_op jit(solution)/shard_map/ppermute | solution.py:26
  59.5 2.6 %collective-permute-done.8 = f32[3,1,32,7,128]{4,2,1,0,3:T(8,128)S(1)} collective-permute-done((f32[3,1,32,7,128]{4,2,1,0,3:T(8,128)S(1)}, f32[3,1,32,7,128]{4,2,1,0,3:T(8,128)S(1)}, u32[]{:S(2)}, u32[]{:S(2)}) %collective-permute-start.8) | collective-permute-done | bytes 344096 | tf_op jit(solution)/shard_map/ppermute | solution.py:27
  62.1 1.2 %collective-permute-done.7 = f32[3,1,32,7,128]{4,2,1,0,3:T(8,128)S(1)} collective-permute-done((f32[3,1,32,7,128]{4,2,1,0,3:T(8,128)S(1)}, f32[3,1,32,7,128]{4,2,1,0,3:T(8,128)S(1)}, u32[]{:S(2)}, u32[]{:S(2)}) %collective-permute-start.7) | collective-permute-done | bytes 344096 | tf_op jit(solution)/shard_map/ppermute | solution.py:26
  64.0 1.0 %gather_fusion.1 = f32[256,7,128]{2,1,0:T(8,128)S(1)} fusion(f32[288,7,128]{2,1,0:T(8,128)S(1)} %copy.165, s32[1024]{0:T(1024)S(1)} %pad_clamp_fusion.2), kind=kCustom, calls=%fused_computation.1 | custom fusion | bytes 1836032 | tf_op jit(solution)/shard_map/gather | solution.py:200
  65.7 22.7 %fusion.9 = (f32[32,128]{1,0:T(8,128)S(1)}, f32[32,128]{1,0:T(8,128)S(1)}, f32[32,128]{1,0:T(8,128)S(1)}) fusion(f32[32,8,128]{2,1,0:T(8,128)S(1)} %bitcast.214, f32[32,8,128]{2,1,0:T(8,128)S(1)} %bitcast.215, f32[32,8,128]{2,1,0:T(8,128)S(1)} %bitcast.216, f32[32,128]{1,0:T(8,128)S(1)} %get-tuple-element.36, f32[32,8,128]{2,1,0:T(8,128)S(1)} %bitcast.217, ...), kind=kLoop, calls=%fused_computation.23 | loop fusion | flops 109039616 | bytes 1015808 | tf_op jit(solution)/shard_map/vmap()/reduce_sum | solution.py:52
  (162 shorter events, 15.0 us)
Async XLA Ops:
  0.0 20.3 %copy-start = (s32[1024]{0:T(1024)S(1)}, s32[1024]{0:T(1024)}, u32[]{:S(2)}) copy-start(s32[1024]{0:T(1024)} %param.11) | copy-start | bytes 12292
  13.5 13.4 %collective-permute-start = (f32[9,7,128]{2,0,1:T(8,128)S(1)}, f32[9,7,128]{2,0,1:T(8,128)S(1)}, u32[]{:S(2)}, u32[]{:S(2)}) collective-permute-start(f32[9,7,128]{2,0,1:T(8,128)S(1)} %pad_maximum_fusion.2), channel_id=1, source_target_pairs={{0,16},{4,20},{8,24},{12,28},{16,0},{20,4},{24,8},{28,12},{1,17},{... | collective-permute-start | bytes 96776 | tf_op jit(solution)/shard_map/ppermute | solution.py:16
  20.3 4.4 %copy-start.1 = (s32[1,1,32,8]{2,3,1,0:T(8,128)S(1)}, s32[1,1,32,8]{2,3,1,0:T(8,128)}, u32[]{:S(2)}) copy-start(s32[1,1,32,8]{2,3,1,0:T(8,128)} %param.12) | copy-start | bytes 3076
  27.2 3.1 %collective-permute-start.1 = (f32[10,7,128]{2,0,1:T(8,128)S(1)}, f32[10,7,128]{2,0,1:T(8,128)S(1)}, u32[]{:S(2)}, u32[]{:S(2)}) collective-permute-start(f32[10,7,128]{2,0,1:T(8,128)S(1)} %pad_maximum_fusion.3), channel_id=1, source_target_pairs={{0,8},{4,12},{8,0},{12,4},{16,24},{20,28},{24,16},{28,20},{1,9},{5... | collective-permute-start | bytes 107528 | tf_op jit(solution)/shard_map/ppermute | solution.py:16
  30.5 4.0 %collective-permute-start.2 = (f32[12,7,128]{2,0,1:T(8,128)S(1)}, f32[12,7,128]{2,0,1:T(8,128)S(1)}, u32[]{:S(2)}, u32[]{:S(2)}) collective-permute-start(f32[12,7,128]{2,0,1:T(8,128)S(1)} %pad_maximum_fusion.4), channel_id=1, source_target_pairs={{0,4},{4,0},{8,12},{12,8},{16,20},{20,16},{24,28},{28,24},{1,5},{5... | collective-permute-start | bytes 129032 | tf_op jit(solution)/shard_map/ppermute | solution.py:16
  34.8 3.1 %collective-permute-start.3 = (f32[16,7,128]{2,0,1:T(8,128)S(1)}, f32[16,7,128]{2,0,1:T(8,128)S(1)}, u32[]{:S(2)}, u32[]{:S(2)}) collective-permute-start(f32[16,7,128]{2,0,1:T(8,128)S(1)} %concatenate.47), channel_id=1, source_target_pairs={{0,2},{1,3},{2,0},{3,1},{4,6},{5,7},{6,4},{7,5},{8,10},{9,11},{10,... | collective-permute-start | bytes 172040 | tf_op jit(solution)/shard_map/ppermute | solution.py:16
  38.1 4.5 %collective-permute-start.4 = (f32[24,7,128]{2,0,1:T(8,128)S(1)}, f32[24,7,128]{2,0,1:T(8,128)S(1)}, u32[]{:S(2)}, u32[]{:S(2)}) collective-permute-start(f32[24,7,128]{2,0,1:T(8,128)S(1)} %concatenate.48), channel_id=1, source_target_pairs={{0,1},{1,0},{2,3},{3,2},{4,5},{5,4},{6,7},{7,6},{8,9},{9,8},{10,11... | collective-permute-start | bytes 258056 | tf_op jit(solution)/shard_map/ppermute | solution.py:16
  42.8 8.8 %collective-permute-start.6 = (f32[1,1,32,7,128]{4,2,1,0,3:T(8,128)S(1)}, f32[1,1,32,7,128]{4,2,1,0,3:T(8,128)S(1)}, u32[]{:S(2)}, u32[]{:S(2)}) collective-permute-start(f32[1,1,32,7,128]{4,2,1,0,3:T(8,128)S(1)} %slice_bitcast_fusion), channel_id=1, source_target_pairs={{4,0},{8,4},{12,8},{16,12},{20,16},{24,20},{28,24},{5,1},{9,5},{13... | collective-permute-start | bytes 344072 | tf_op jit(solution)/shard_map/ppermute | solution.py:27
  45.8 6.9 %collective-permute-start.5 = (f32[1,1,32,7,128]{4,2,1,0,3:T(8,128)S(1)}, f32[1,1,32,7,128]{4,2,1,0,3:T(8,128)S(1)}, u32[]{:S(2)}, u32[]{:S(2)}) collective-permute-start(f32[1,1,32,7,128]{4,2,1,0,3:T(8,128)S(1)} %slice_bitcast_fusion), channel_id=1, source_target_pairs={{0,4},{4,8},{8,12},{12,16},{16,20},{20,24},{24,28},{1,5},{5,9},{9,... | collective-permute-start | bytes 344072 | tf_op jit(solution)/shard_map/ppermute | solution.py:26
  52.7 9.5 %collective-permute-start.8 = (f32[3,1,32,7,128]{4,2,1,0,3:T(8,128)S(1)}, f32[3,1,32,7,128]{4,2,1,0,3:T(8,128)S(1)}, u32[]{:S(2)}, u32[]{:S(2)}) collective-permute-start(f32[3,1,32,7,128]{4,2,1,0,3:T(8,128)S(1)} %pad_maximum_fusion.1), channel_id=1, source_target_pairs={{1,0},{2,1},{3,2},{5,4},{6,5},{7,6},{9,8},{10,9},{11,10},{13,12},{... | collective-permute-start | bytes 1032200 | tf_op jit(solution)/shard_map/ppermute | solution.py:27
  56.1 7.2 %collective-permute-start.7 = (f32[3,1,32,7,128]{4,2,1,0,3:T(8,128)S(1)}, f32[3,1,32,7,128]{4,2,1,0,3:T(8,128)S(1)}, u32[]{:S(2)}, u32[]{:S(2)}) collective-permute-start(f32[3,1,32,7,128]{4,2,1,0,3:T(8,128)S(1)} %pad_maximum_fusion.1), channel_id=1, source_target_pairs={{0,1},{1,2},{2,3},{4,5},{5,6},{6,7},{8,9},{9,10},{10,11},{12,13},{... | collective-permute-start | bytes 1032200 | tf_op jit(solution)/shard_map/ppermute | solution.py:26

commit v4 on v3

--- a/solution.py
+++ b/solution.py
@@ -84,46 +84,34 @@
     return velocity.reshape((block_count,) + velocity.shape[2:])
 
 
-def partner_values(values, level, bits_x, levels):
-    size_x, size_y = values.shape
-    if level < bits_x:
-        step = 1 << bits_x - 1 - level
-        split = values.reshape(size_x // (2 * step), 2, step, size_y)
-        return split[:, ::-1].reshape(size_x, size_y)
-    step = 1 << levels - 1 - level
-    split = values.reshape(size_x, size_y // (2 * step), 2, step)
-    return split[:, :, ::-1].reshape(size_x, size_y)
-
-
 def trace_back(loc, moves, levels, bits_x, nbd):
     size_x, size_y = moves.shape[1], moves.shape[2]
     devices = size_x * size_y
-    mate_moves = [partner_values(moves[level], level, bits_x, levels) for level in range(levels)]
-    count = jnp.full((size_x, size_y), nbd, jnp.int32)
-    for level in range(levels):
-        count = count + moves[level] - mate_moves[level]
+    level_bit = np.array(
+        [(1 << bits_x - 1 - level) * size_y if level < bits_x else 1 << levels - 1 - level for level in range(levels)],
+        np.int32,
+    )
+    flat = moves.reshape(levels, devices)
+    every = jnp.arange(devices, dtype=jnp.int32)
+    swap = jnp.bitwise_xor(every[None, :, None], level_bit[:, None, None]) == every[None, None, :]
+    mate_moves = jnp.sum(jnp.where(swap, flat[:, None, :], 0), axis=2)
+    delta = flat - mate_moves
+    before = nbd + jnp.sum(delta, axis=0)
     kept = []
     for level in range(levels):
-        left = count - moves[level]
-        kept.append(left)
-        count = left + mate_moves[level]
-    kept_flat = [k.reshape(1, devices) for k in kept]
-    kept_mate = [partner_values(k, level, bits_x, levels).reshape(1, devices) for level, k in enumerate(kept)]
-    every = jnp.arange(devices, dtype=jnp.int32)[None, :]
+        kept.append(before - flat[level])
+        before = before - delta[level]
+    kept = jnp.stack(kept, axis=0)
+    kept_mate = jnp.sum(jnp.where(swap, kept[:, None, :], 0), axis=2)
     device = loc.reshape(-1) // nbd
     slot = loc.reshape(-1) % nbd
     for level in reversed(range(levels)):
-        if level < bits_x:
-            bit = (1 << bits_x - 1 - level) * size_y
-        else:
-            bit = 1 << levels - 1 - level
-        mate = jnp.bitwise_xor(device, bit)
-        pick = device[:, None] == every
-        here = jnp.sum(jnp.where(pick, kept_flat[level], 0), axis=1)
-        there = jnp.sum(jnp.where(pick, kept_mate[level], 0), axis=1)
+        pick = device[:, None] == every[None, :]
+        here = jnp.sum(jnp.where(pick, kept[level][None, :], 0), axis=1)
+        there = jnp.sum(jnp.where(pick, kept_mate[level][None, :], 0), axis=1)
         moved = slot >= here
         slot = jnp.where(moved, slot - here + there, slot)
-        device = jnp.where(moved, mate, device)
+        device = jnp.where(moved, jnp.bitwise_xor(device, level_bit[level]), device)
     return device.reshape(loc.shape), slot.reshape(loc.shape)
 
 

time: 90.4 us -> 87.5 us (0.968)
  local copies, waits for them, and re-layouts: 18 us -> 14.6 us
    reshape x23 -> x0, local copies, waits for them, and re-layouts: 2.09 us -> none  [the longest x12 1.13 us: partner_values(): return split[:, :, ::-1].reshape(size_x, size_y)]
    rev x18 -> x0, local copies, waits for them, and re-layouts: 0.97 us -> none  [the longest x10 0.54 us: partner_values(): return split[:, ::-1].reshape(size_x, size_y)]
  transfers between devices with their start and end apart: 9 -> 9, of which waited for: 6 -> 6; matrix products, arithmetic and copies ran while one was open for 17% -> 14% of each run, Pallas kernels for 0% -> 0%
where the time goes in v4:
time: 87.5 us; the launch traced here: 86.2 us
  other arithmetic  30.9 us (35%)
  starting transfers between devices  20.5 us (23%)
  local copies, waits for them, and re-layouts  14.6 us (17%)
  between operations  12.4 us (14%)
  waiting for transfers between devices  7.74 us (9%)
    reduce_sum x1, other arithmetic, evaluate(): near_x = jnp.sum(str_y * sep_z - str_z * sep_y, axis=(0, 2))  22.7 us
    ppermute x5, starting transfers between devices, from_partner(): lax.ppermute(shard, axis, [(i, i ^ 1 << apart) for i in range(lax.axis_si...  8.79 us
    ppermute x2, starting transfers between devices, padded(): after = lax.ppermute(first, axis, down)  6.44 us
    ppermute x2, starting transfers between devices, padded(): before = lax.ppermute(last, axis, up)  5.3 us
    ppermute x5, waiting for transfers between devices, from_partner(): lax.ppermute(shard, axis, [(i, i ^ 1 << apart) for i in range(lax.axis_si...  2.88 us
    ppermute x2, waiting for transfers between devices, padded(): after = lax.ppermute(first, axis, down)  2.65 us
    ppermute x2, waiting for transfers between devices, padded(): before = lax.ppermute(last, axis, up)  2.21 us
  transfers between devices with their start and end apart: 9, of which 6 were waited for; matrix products, arithmetic and copies ran while one was open for 14% of the time, Pallas kernels for 0%

profile of v4, /device:TPU:9, one launch (start us, length us, event | category | flops | bytes accessed | tf_op | source)
XLA Modules:
  0.0 86.2 jit_solution(12322105606599915389)
XLA Ops:
  0.0 0.9 %multiply_reduce_fusion.1 = f32[72]{0:T(128)S(1)} fusion(f32[1,1,72,128]{3,2,1,0:T(8,128)} %param.10), kind=kLoop, calls=%fused_computation.64 | loop fusion | flops 18360 | bytes 37152 | tf_op jit(solution)/shard_map/reduce_sum | solution.py:36
  0.9 1.5 %constant_dynamic-slice_fusion.13 = (s32[1,1,1]{1,2,0:T(1,128)}, s32[1,1,1]{1,2,0:T(1,128)}, s32[1,1,1]{1,2,0:T(1,128)}, s32[1,1,1]{1,2,0:T(1,128)}, s32[1,1,1]{...) fusion(s32[5,8,4]{1,2,0:T(4,128)} %param.11, ...), kind=kLoop, calls=%fused_computation.222 | loop fusion | bytes 108 | tf_op jit(solution)/shard_map/dynamic_slice | solution.py:153
  9.2 1.0 %reduce_sum.234 = f32[72,3]{0,1:T(4,128)S(1)} reduce(f32[1,1,72,3,128]{4,2,3,1,0:T(8,128)} %param.9, f32[]{:T(128)} %constant.166.clone.1), dimensions={0,1,4}, to_apply=%region_1.0 | reduce | flops 27432 | bytes 111460 | tf_op jit(solution)/shard_map/reduce_sum | solution.py:34
  10.3 1.0 %reduce_sum.233 = f32[72,3]{0,1:T(4,128)S(1)} reduce(f32[1,1,72,3,128]{4,2,3,1,0:T(8,128)} %param.8, f32[]{:T(128)} %constant.166.clone.1), dimensions={0,1,4}, to_apply=%region_0.0 | reduce | flops 27432 | bytes 111460 | tf_op jit(solution)/shard_map/reduce_sum | solution.py:33
  11.3 1.1 %multiply_reduce_fusion = f32[72]{0:T(128)S(1)} fusion(f32[72,3]{0,1:T(4,128)S(1)} %broadcast_multiply_fusion, f32[1,1,72,3,128]{4,2,3,1,0:T(8,128)} %param.8), kind=kLoop, calls=%fused_computation.51 | loop fusion | flops 82872 | bytes 111744 | tf_op jit(solution)/shard_map/reduce_sum | solution.py:36
  12.5 1.0 %select_maximum_fusion = f32[80,7,128]{2,0,1:T(8,128)S(1)} fusion(f32[72,1,128]{2,0,1:T(8,128)} %bitcast.97, f32[72,3,128]{2,0,1:T(8,128)} %bitcast.96, f32[72,3,128]{2,0,1:T(8,128)} %bitcast.94), kind=kLoop, calls=%fused_computation.26 | loop fusion | flops 430080 | bytes 544768 | tf_op jit(solution)/shard_map/concatenate | solution.py:136
  13.5 2.4 %collective-permute-start = (f32[9,7,128]{2,0,1:T(8,128)S(1)}, f32[9,7,128]{2,0,1:T(8,128)S(1)}, u32[]{:S(2)}, u32[]{:S(2)}) collective-permute-start(f32[9,7,128]{2,0,1:T(8,128)S(1)} %pad_maximum_fusion.2), channel_id=1, source_target_pairs={{0,16},{4,20},{8,24},{12,28},{16,0},{20,4},{24,8},{28,12},{1,17},{... | collective-permute-start | bytes 96776 | tf_op jit(solution)/shard_map/ppermute | solution.py:16
  16.9 0.8 copy.72
  17.8 1.4 %gather_fusion.2 = s32[256]{0:T(256)S(1)} fusion(s32[1024]{0:T(1024)S(1)} %copy-done, s32[1024]{0:T(1024)S(1)} %pad_clamp_fusion.1), kind=kCustom, calls=%fused_computation.2 | custom fusion | bytes 3072 | tf_op jit(solution)/shard_map/gather | solution.py:141
  25.8 1.4 %gather_fusion = s32[256]{0:T(256)S(1)} fusion(s32[1024]{0:T(1024)S(1)} %copy-done, s32[1024]{0:T(1024)S(1)} %pad_clamp_fusion.3), kind=kCustom, calls=%fused_computation | custom fusion | bytes 3072 | tf_op jit(solution)/shard_map/gather | solution.py:179
  27.6 1.3 %collective-permute-start.2 = (f32[12,7,128]{2,0,1:T(8,128)S(1)}, f32[12,7,128]{2,0,1:T(8,128)S(1)}, u32[]{:S(2)}, u32[]{:S(2)}) collective-permute-start(f32[12,7,128]{2,0,1:T(8,128)S(1)} %pad_maximum_fusion.4), channel_id=1, source_target_pairs={{0,4},{4,0},{8,12},{12,8},{16,20},{20,16},{24,28},{28,24},{1,5},{5... | collective-permute-start | bytes 129032 | tf_op jit(solution)/shard_map/ppermute | solution.py:16
  31.9 1.3 %collective-permute-start.3 = (f32[16,7,128]{2,0,1:T(8,128)S(1)}, f32[16,7,128]{2,0,1:T(8,128)S(1)}, u32[]{:S(2)}, u32[]{:S(2)}) collective-permute-start(f32[16,7,128]{2,0,1:T(8,128)S(1)} %concatenate.47), channel_id=1, source_target_pairs={{0,2},{1,3},{2,0},{3,1},{4,6},{5,7},{6,4},{7,5},{8,10},{9,11},{10,... | collective-permute-start | bytes 172040 | tf_op jit(solution)/shard_map/ppermute | solution.py:16
  33.2 1.8 %collective-permute-done.3 = f32[16,7,128]{2,0,1:T(8,128)S(1)} collective-permute-done((f32[16,7,128]{2,0,1:T(8,128)S(1)}, f32[16,7,128]{2,0,1:T(8,128)S(1)}, u32[]{:S(2)}, u32[]{:S(2)}) %collective-permute-start.3) | collective-permute-done | bytes 57376 | tf_op jit(solution)/shard_map/ppermute | solution.py:16
  35.2 3.6 %collective-permute-start.4 = (f32[24,7,128]{2,0,1:T(8,128)S(1)}, f32[24,7,128]{2,0,1:T(8,128)S(1)}, u32[]{:S(2)}, u32[]{:S(2)}) collective-permute-start(f32[24,7,128]{2,0,1:T(8,128)S(1)} %concatenate.48), channel_id=1, source_target_pairs={{0,1},{1,0},{2,3},{3,2},{4,5},{5,4},{6,7},{7,6},{8,9},{9,8},{10,11... | collective-permute-start | bytes 258056 | tf_op jit(solution)/shard_map/ppermute | solution.py:16
  38.8 0.9 %collective-permute-done.4 = f32[24,7,128]{2,0,1:T(8,128)S(1)} collective-permute-done((f32[24,7,128]{2,0,1:T(8,128)S(1)}, f32[24,7,128]{2,0,1:T(8,128)S(1)}, u32[]{:S(2)}, u32[]{:S(2)}) %collective-permute-start.4) | collective-permute-done | bytes 86048 | tf_op jit(solution)/shard_map/ppermute | solution.py:16
  39.9 3.0 %collective-permute-start.6 = (f32[1,1,32,7,128]{4,2,1,0,3:T(8,128)S(1)}, f32[1,1,32,7,128]{4,2,1,0,3:T(8,128)S(1)}, u32[]{:S(2)}, u32[]{:S(2)}) collective-permute-start(f32[1,1,32,7,128]{4,2,1,0,3:T(8,128)S(1)} %slice_bitcast_fusion), channel_id=1, source_target_pairs={{4,0},{8,4},{12,8},{16,12},{20,16},{24,20},{28,24},{5,1},{9,5},{13... | collective-permute-start | bytes 344072 | tf_op jit(solution)/shard_map/ppermute | solution.py:27
  42.9 2.3 %collective-permute-start.5 = (f32[1,1,32,7,128]{4,2,1,0,3:T(8,128)S(1)}, f32[1,1,32,7,128]{4,2,1,0,3:T(8,128)S(1)}, u32[]{:S(2)}, u32[]{:S(2)}) collective-permute-start(f32[1,1,32,7,128]{4,2,1,0,3:T(8,128)S(1)} %slice_bitcast_fusion), channel_id=1, source_target_pairs={{0,4},{4,8},{8,12},{12,16},{16,20},{20,24},{24,28},{1,5},{5,9},{9,... | collective-permute-start | bytes 344072 | tf_op jit(solution)/shard_map/ppermute | solution.py:26
  48.7 1.0 %collective-permute-done.5 = f32[1,1,32,7,128]{4,2,1,0,3:T(8,128)S(1)} collective-permute-done((f32[1,1,32,7,128]{4,2,1,0,3:T(8,128)S(1)}, f32[1,1,32,7,128]{4,2,1,0,3:T(8,128)S(1)}, u32[]{:S(2)}, u32[]{:S(2)}) %collective-permute-start.5) | collective-permute-done | bytes 114720 | tf_op jit(solution)/shard_map/ppermute | solution.py:26
  49.8 3.4 %collective-permute-start.8 = (f32[3,1,32,7,128]{4,2,1,0,3:T(8,128)S(1)}, f32[3,1,32,7,128]{4,2,1,0,3:T(8,128)S(1)}, u32[]{:S(2)}, u32[]{:S(2)}) collective-permute-start(f32[3,1,32,7,128]{4,2,1,0,3:T(8,128)S(1)} %pad_maximum_fusion.1), channel_id=1, source_target_pairs={{1,0},{2,1},{3,2},{5,4},{6,5},{7,6},{9,8},{10,9},{11,10},{13,12},{... | collective-permute-start | bytes 1032200 | tf_op jit(solution)/shard_map/ppermute | solution.py:27
  53.2 3.0 %collective-permute-start.7 = (f32[3,1,32,7,128]{4,2,1,0,3:T(8,128)S(1)}, f32[3,1,32,7,128]{4,2,1,0,3:T(8,128)S(1)}, u32[]{:S(2)}, u32[]{:S(2)}) collective-permute-start(f32[3,1,32,7,128]{4,2,1,0,3:T(8,128)S(1)} %pad_maximum_fusion.1), channel_id=1, source_target_pairs={{0,1},{1,2},{2,3},{4,5},{5,6},{6,7},{8,9},{9,10},{10,11},{12,13},{... | collective-permute-start | bytes 1032200 | tf_op jit(solution)/shard_map/ppermute | solution.py:26
  56.6 2.6 %collective-permute-done.8 = f32[3,1,32,7,128]{4,2,1,0,3:T(8,128)S(1)} collective-permute-done((f32[3,1,32,7,128]{4,2,1,0,3:T(8,128)S(1)}, f32[3,1,32,7,128]{4,2,1,0,3:T(8,128)S(1)}, u32[]{:S(2)}, u32[]{:S(2)}) %collective-permute-start.8) | collective-permute-done | bytes 344096 | tf_op jit(solution)/shard_map/ppermute | solution.py:27
  59.2 1.2 %collective-permute-done.7 = f32[3,1,32,7,128]{4,2,1,0,3:T(8,128)S(1)} collective-permute-done((f32[3,1,32,7,128]{4,2,1,0,3:T(8,128)S(1)}, f32[3,1,32,7,128]{4,2,1,0,3:T(8,128)S(1)}, u32[]{:S(2)}, u32[]{:S(2)}) %collective-permute-start.7) | collective-permute-done | bytes 344096 | tf_op jit(solution)/shard_map/ppermute | solution.py:26
  61.1 1.0 %gather_fusion.1 = f32[256,7,128]{2,1,0:T(8,128)S(1)} fusion(f32[288,7,128]{2,1,0:T(8,128)S(1)} %copy.70, s32[1024]{0:T(1024)S(1)} %pad_clamp_fusion.2), kind=kCustom, calls=%fused_computation.1 | custom fusion | bytes 1836032 | tf_op jit(solution)/shard_map/gather | solution.py:188
  62.8 22.7 %fusion.9 = (f32[32,128]{1,0:T(8,128)S(1)}, f32[32,128]{1,0:T(8,128)S(1)}, f32[32,128]{1,0:T(8,128)S(1)}) fusion(f32[32,8,128]{2,1,0:T(8,128)S(1)} %bitcast.99, f32[32,8,128]{2,1,0:T(8,128)S(1)} %bitcast.100, f32[32,8,128]{2,1,0:T(8,128)S(1)} %bitcast.101, f32[32,128]{1,0:T(8,128)S(1)} %get-tuple-element.33, f32[32,8,128]{2,1,0:T(8,128)S(1)} %bitcast.102, ...), kind=kLoop, calls=%fused_computation.23 | loop fusion | flops 109039616 | bytes 1015808 | tf_op jit(solution)/shard_map/vmap()/reduce_sum | solution.py:52
  (126 shorter events, 12.1 us)
Async XLA Ops:
  0.0 17.8 %copy-start = (s32[1024]{0:T(1024)S(1)}, s32[1024]{0:T(1024)}, u32[]{:S(2)}) copy-start(s32[1024]{0:T(1024)} %param.12) | copy-start | bytes 12292
  13.5 10.5 %collective-permute-start = (f32[9,7,128]{2,0,1:T(8,128)S(1)}, f32[9,7,128]{2,0,1:T(8,128)S(1)}, u32[]{:S(2)}, u32[]{:S(2)}) collective-permute-start(f32[9,7,128]{2,0,1:T(8,128)S(1)} %pad_maximum_fusion.2), channel_id=1, source_target_pairs={{0,16},{4,20},{8,24},{12,28},{16,0},{20,4},{24,8},{28,12},{1,17},{... | collective-permute-start | bytes 96776 | tf_op jit(solution)/shard_map/ppermute | solution.py:16
  17.8 1.5 %copy-start.1 = (s32[5,8,4]{1,2,0:T(4,128)S(1)}, s32[5,8,4]{1,2,0:T(4,128)}, u32[]{:S(2)}) copy-start(s32[5,8,4]{1,2,0:T(4,128)} %param.11) | copy-start | bytes 1924
  17.8 1.6 %copy-start.3 = (s32[5]{0:T(128)S(1)}, s32[5]{0:T(128)}, u32[]{:S(2)}) copy-start(s32[5]{0:T(128)} %constant.200) | copy-start | bytes 64
  17.8 4.0 %copy-start.2 = (s32[1,1,32,8]{2,3,1,0:T(8,128)S(1)}, s32[1,1,32,8]{2,3,1,0:T(8,128)}, u32[]{:S(2)}) copy-start(s32[1,1,32,8]{2,3,1,0:T(8,128)} %param.13) | copy-start | bytes 3076
  24.3 3.1 %collective-permute-start.1 = (f32[10,7,128]{2,0,1:T(8,128)S(1)}, f32[10,7,128]{2,0,1:T(8,128)S(1)}, u32[]{:S(2)}, u32[]{:S(2)}) collective-permute-start(f32[10,7,128]{2,0,1:T(8,128)S(1)} %pad_maximum_fusion.3), channel_id=1, source_target_pairs={{0,8},{4,12},{8,0},{12,4},{16,24},{20,28},{24,16},{28,20},{1,9},{5... | collective-permute-start | bytes 107528 | tf_op jit(solution)/shard_map/ppermute | solution.py:16
  27.6 4.0 %collective-permute-start.2 = (f32[12,7,128]{2,0,1:T(8,128)S(1)}, f32[12,7,128]{2,0,1:T(8,128)S(1)}, u32[]{:S(2)}, u32[]{:S(2)}) collective-permute-start(f32[12,7,128]{2,0,1:T(8,128)S(1)} %pad_maximum_fusion.4), channel_id=1, source_target_pairs={{0,4},{4,0},{8,12},{12,8},{16,20},{20,16},{24,28},{28,24},{1,5},{5... | collective-permute-start | bytes 129032 | tf_op jit(solution)/shard_map/ppermute | solution.py:16
  31.9 3.1 %collective-permute-start.3 = (f32[16,7,128]{2,0,1:T(8,128)S(1)}, f32[16,7,128]{2,0,1:T(8,128)S(1)}, u32[]{:S(2)}, u32[]{:S(2)}) collective-permute-start(f32[16,7,128]{2,0,1:T(8,128)S(1)} %concatenate.47), channel_id=1, source_target_pairs={{0,2},{1,3},{2,0},{3,1},{4,6},{5,7},{6,4},{7,5},{8,10},{9,11},{10,... | collective-permute-start | bytes 172040 | tf_op jit(solution)/shard_map/ppermute | solution.py:16
  35.2 4.5 %collective-permute-start.4 = (f32[24,7,128]{2,0,1:T(8,128)S(1)}, f32[24,7,128]{2,0,1:T(8,128)S(1)}, u32[]{:S(2)}, u32[]{:S(2)}) collective-permute-start(f32[24,7,128]{2,0,1:T(8,128)S(1)} %concatenate.48), channel_id=1, source_target_pairs={{0,1},{1,0},{2,3},{3,2},{4,5},{5,4},{6,7},{7,6},{8,9},{9,8},{10,11... | collective-permute-start | bytes 258056 | tf_op jit(solution)/shard_map/ppermute | solution.py:16
  39.9 8.8 %collective-permute-start.6 = (f32[1,1,32,7,128]{4,2,1,0,3:T(8,128)S(1)}, f32[1,1,32,7,128]{4,2,1,0,3:T(8,128)S(1)}, u32[]{:S(2)}, u32[]{:S(2)}) collective-permute-start(f32[1,1,32,7,128]{4,2,1,0,3:T(8,128)S(1)} %slice_bitcast_fusion), channel_id=1, source_target_pairs={{4,0},{8,4},{12,8},{16,12},{20,16},{24,20},{28,24},{5,1},{9,5},{13... | collective-permute-start | bytes 344072 | tf_op jit(solution)/shard_map/ppermute | solution.py:27
  42.9 6.9 %collective-permute-start.5 = (f32[1,1,32,7,128]{4,2,1,0,3:T(8,128)S(1)}, f32[1,1,32,7,128]{4,2,1,0,3:T(8,128)S(1)}, u32[]{:S(2)}, u32[]{:S(2)}) collective-permute-start(f32[1,1,32,7,128]{4,2,1,0,3:T(8,128)S(1)} %slice_bitcast_fusion), channel_id=1, source_target_pairs={{0,4},{4,8},{8,12},{12,16},{16,20},{20,24},{24,28},{1,5},{5,9},{9,... | collective-permute-start | bytes 344072 | tf_op jit(solution)/shard_map/ppermute | solution.py:26
  49.8 9.5 %collective-permute-start.8 = (f32[3,1,32,7,128]{4,2,1,0,3:T(8,128)S(1)}, f32[3,1,32,7,128]{4,2,1,0,3:T(8,128)S(1)}, u32[]{:S(2)}, u32[]{:S(2)}) collective-permute-start(f32[3,1,32,7,128]{4,2,1,0,3:T(8,128)S(1)} %pad_maximum_fusion.1), channel_id=1, source_target_pairs={{1,0},{2,1},{3,2},{5,4},{6,5},{7,6},{9,8},{10,9},{11,10},{13,12},{... | collective-permute-start | bytes 1032200 | tf_op jit(solution)/shard_map/ppermute | solution.py:27
  53.2 7.2 %collective-permute-start.7 = (f32[3,1,32,7,128]{4,2,1,0,3:T(8,128)S(1)}, f32[3,1,32,7,128]{4,2,1,0,3:T(8,128)S(1)}, u32[]{:S(2)}, u32[]{:S(2)}) collective-permute-start(f32[3,1,32,7,128]{4,2,1,0,3:T(8,128)S(1)} %pad_maximum_fusion.1), channel_id=1, source_target_pairs={{0,1},{1,2},{2,3},{4,5},{5,6},{6,7},{8,9},{9,10},{10,11},{12,13},{... | collective-permute-start | bytes 1032200 | tf_op jit(solution)/shard_map/ppermute | solution.py:26

commit v5 on v4

--- a/solution.py
+++ b/solution.py
@@ -156,9 +156,12 @@
     count = jnp.int32(nbd)
     for plan_item in plans:
         count = count + plan_item[1] - plan_item[2]
+    slot_ids = jnp.arange(held.shape[0], dtype=jnp.int32)
+    move_ids = jnp.arange(MOVE, dtype=jnp.int32)
     for level in range(levels):
         bit_at, own_moves, mate_moves = plans[level]
-        leaving = lax.dynamic_slice_in_dim(held, count - own_moves, MOVE, 0)
+        take = slot_ids[None, :] == (count - own_moves + move_ids)[:, None]
+        leaving = jnp.sum(jnp.where(take[:, :, None, None], held[None], 0.0), axis=1)
         payload = jnp.concatenate([leaving, gathered], axis=0)
         if level < bits_x:
             got = from_partner(payload, "gx", bit_at)
@@ -167,7 +170,9 @@
         arriving = got[:MOVE]
         gathered = jnp.concatenate([gathered, got[MOVE:]], axis=0)
         count = count - own_moves
-        held = lax.dynamic_update_slice_in_dim(held, arriving, count, 0)
+        put = slot_ids[:, None] == (count + move_ids)[None, :]
+        placed = jnp.sum(jnp.where(put[:, :, None, None], arriving[None], 0.0), axis=1)
+        held = jnp.where(jnp.any(put, axis=1)[:, None, None], placed, held)
         count = count + mate_moves
     blocks = held[:nbd]
     relative = jnp.bitwise_xor(far_device, me)

time: 87.5 us -> 99.3 us (1.13)
  other arithmetic: 30.9 us -> 38.3 us
  waiting for transfers between devices: 7.74 us -> 11.8 us
  starting transfers between devices: 20.5 us -> 21.6 us
    reduce_sum x0 -> x10, other arithmetic: none -> 4.97 us  [the longest x5 3.52 us: local(): jnp.sum(jnp.where(put[:, :, None, None], arriving[None], 0.0), axis=1)]
    ppermute x5, waiting for transfers between devices: 2.88 us -> 6.31 us  [from_partner(): lax.ppermute(shard, axis, [(i, i ^ 1 << apart) for i in range(lax.axis_si...]
    squeeze x0 -> x1, local copies, waits for them, and re-layouts: none -> 1.03 us  [local(): strength[0, 0]]
  transfers between devices with their start and end apart: 9 -> 9, of which waited for: 6 -> 7; matrix products, arithmetic and copies ran while one was open for 14% -> 12% of each run, Pallas kernels for 0% -> 0%
where the time goes in v5:
time: 99.3 us; the launch traced here: 98 us
  other arithmetic  38.3 us (39%)
  starting transfers between devices  21.6 us (22%)
  local copies, waits for them, and re-layouts  13.8 us (14%)
  between operations  12.5 us (13%)
  waiting for transfers between devices  11.8 us (12%)
    reduce_sum x1, other arithmetic, evaluate(): near_x = jnp.sum(str_y * sep_z - str_z * sep_y, axis=(0, 2))  22.7 us
    ppermute x5, starting transfers between devices, from_partner(): lax.ppermute(shard, axis, [(i, i ^ 1 << apart) for i in range(lax.axis_si...  9.66 us
    ppermute x2, starting transfers between devices, padded(): after = lax.ppermute(first, axis, down)  6.42 us
    ppermute x5, waiting for transfers between devices, from_partner(): lax.ppermute(shard, axis, [(i, i ^ 1 << apart) for i in range(lax.axis_si...  6.31 us
    ppermute x2, starting transfers between devices, padded(): before = lax.ppermute(last, axis, up)  5.5 us
    reduce_sum x5, other arithmetic, local(): jnp.sum(jnp.where(put[:, :, None, None], arriving[None], 0.0), axis=1)  3.52 us
    ppermute x2, waiting for transfers between devices, padded(): after = lax.ppermute(first, axis, down)  2.96 us
    ppermute x2, waiting for transfers between devices, padded(): before = lax.ppermute(last, axis, up)  2.55 us
  transfers between devices with their start and end apart: 9, of which 7 were waited for; matrix products, arithmetic and copies ran while one was open for 12% of the time, Pallas kernels for 0%

profile of v5, /device:TPU:9, one launch (start us, length us, event | category | flops | bytes accessed | tf_op | source)
XLA Modules:
  0.0 98.0 jit_solution(1049424944231681438)
XLA Ops:
  0.0 1.1 %reduce_sum.325 = f32[72,3]{0,1:T(4,128)S(1)} reduce(f32[1,1,72,3,128]{4,2,3,1,0:T(8,128)} %param.9, f32[]{:T(128)} %constant.177.clone.1), dimensions={0,1,4}, to_apply=%region_7.8 | reduce | flops 27432 | bytes 111460 | tf_op jit(solution)/shard_map/reduce_sum | solution.py:34
  1.1 1.0 %reduce_sum.324 = f32[72,3]{0,1:T(4,128)S(1)} reduce(f32[1,1,72,3,128]{4,2,3,1,0:T(8,128)} %param.8, f32[]{:T(128)} %constant.177.clone.1), dimensions={0,1,4}, to_apply=%region_6.7 | reduce | flops 27432 | bytes 111460 | tf_op jit(solution)/shard_map/reduce_sum | solution.py:33
  2.1 1.0 %copy_bitcast_fusion = (f32[72,3,128]{2,1,0:T(4,128)S(1)}, f32[72,3,128]{2,1,0:T(4,128)S(1)}) fusion(f32[1,1,72,3,128]{4,2,3,1,0:T(8,128)} %param.9, f32[1,1,72,3,128]{4,2,3,1,0:T(8,128)} %param.8), kind=kLoop, calls=%fused_computation.54 | loop fusion | bytes 442368 | tf_op jit(solution)/shard_map/squeeze | solution.py:136
  4.1 1.5 %constant_dynamic-slice_fusion.6 = (s32[1,1,1]{1,2,0:T(1,128)}, s32[1,1,1]{1,2,0:T(1,128)}, s32[1,1,1]{1,2,0:T(1,128)}, s32[1,1,1]{1,2,0:T(1,128)}, s32[1,1,1]{1...) fusion(s32[5,8,4]{1,2,0:T(4,128)} %param.11, ...), kind=kLoop, calls=%fused_computation.245 | loop fusion | bytes 108 | tf_op jit(solution)/shard_map/dynamic_slice | solution.py:153
  12.5 1.9 %multiply_reduce_fusion = f32[72]{0:T(128)S(1)} fusion(f32[72,3]{1,0:T(8,128)S(1)} %copy.155, f32[1,1,72,3,128]{4,2,3,1,0:T(8,128)} %param.8), kind=kLoop, calls=%fused_computation.56 | loop fusion | flops 82872 | bytes 111744 | tf_op jit(solution)/shard_map/reduce_sum | solution.py:36
  15.8 2.4 %collective-permute-start = (f32[9,7,128]{2,1,0:T(8,128)S(1)}, f32[9,7,128]{2,1,0:T(8,128)S(1)}, u32[]{:S(2)}, u32[]{:S(2)}) collective-permute-start(f32[9,7,128]{2,1,0:T(8,128)S(1)} %pad_maximum_fusion.4), channel_id=1, source_target_pairs={{0,16},{4,20},{8,24},{12,28},{16,0},{20,4},{24,8},{28,12},{1,17},{... | collective-permute-start | bytes 96776 | tf_op jit(solution)/shard_map/ppermute | solution.py:16
  24.2 1.4 %gather_fusion.2 = s32[256]{0:T(256)S(1)} fusion(s32[1024]{0:T(1024)S(1)} %copy-done, s32[1024]{0:T(1024)S(1)} %pad_clamp_fusion.1), kind=kCustom, calls=%fused_computation.2 | custom fusion | bytes 3072 | tf_op jit(solution)/shard_map/gather | solution.py:141
  28.5 1.4 %gather_fusion = s32[256]{0:T(256)S(1)} fusion(s32[1024]{0:T(1024)S(1)} %copy-done, s32[1024]{0:T(1024)S(1)} %pad_clamp_fusion.3), kind=kCustom, calls=%fused_computation | custom fusion | bytes 3072 | tf_op jit(solution)/shard_map/gather | solution.py:184
  32.6 2.5 %collective-permute-done.1 = f32[10,7,128]{2,1,0:T(8,128)S(1)} collective-permute-done((f32[10,7,128]{2,1,0:T(8,128)S(1)}, f32[10,7,128]{2,1,0:T(8,128)S(1)}, u32[]{:S(2)}, u32[]{:S(2)}) %collective-permute-start.1) | collective-permute-done | bytes 35872 | tf_op jit(solution)/shard_map/ppermute | solution.py:16
  36.4 1.3 %collective-permute-start.2 = (f32[12,7,128]{2,1,0:T(8,128)S(1)}, f32[12,7,128]{2,1,0:T(8,128)S(1)}, u32[]{:S(2)}, u32[]{:S(2)}) collective-permute-start(f32[12,7,128]{2,1,0:T(8,128)S(1)} %pad_maximum_fusion.2), channel_id=1, source_target_pairs={{0,4},{4,0},{8,12},{12,8},{16,20},{20,16},{24,28},{28,24},{1,5},{5... | collective-permute-start | bytes 129032 | tf_op jit(solution)/shard_map/ppermute | solution.py:16
  38.3 1.1 %collective-permute-done.2 = f32[12,7,128]{2,1,0:T(8,128)S(1)} collective-permute-done((f32[12,7,128]{2,1,0:T(8,128)S(1)}, f32[12,7,128]{2,1,0:T(8,128)S(1)}, u32[]{:S(2)}, u32[]{:S(2)}) %collective-permute-start.2) | collective-permute-done | bytes 43040 | tf_op jit(solution)/shard_map/ppermute | solution.py:16
  40.7 1.3 %collective-permute-start.3 = (f32[16,7,128]{2,0,1:T(8,128)S(1)}, f32[16,7,128]{2,0,1:T(8,128)S(1)}, u32[]{:S(2)}, u32[]{:S(2)}) collective-permute-start(f32[16,7,128]{2,0,1:T(8,128)S(1)} %concatenate.47), channel_id=1, source_target_pairs={{0,2},{1,3},{2,0},{3,1},{4,6},{5,7},{6,4},{7,5},{8,10},{9,11},{10,... | collective-permute-start | bytes 172040 | tf_op jit(solution)/shard_map/ppermute | solution.py:16
  42.0 1.8 %collective-permute-done.3 = f32[16,7,128]{2,0,1:T(8,128)S(1)} collective-permute-done((f32[16,7,128]{2,0,1:T(8,128)S(1)}, f32[16,7,128]{2,0,1:T(8,128)S(1)}, u32[]{:S(2)}, u32[]{:S(2)}) %collective-permute-start.3) | collective-permute-done | bytes 57376 | tf_op jit(solution)/shard_map/ppermute | solution.py:16
  45.1 4.5 %collective-permute-start.4 = (f32[24,7,128]{2,0,1:T(8,128)S(1)}, f32[24,7,128]{2,0,1:T(8,128)S(1)}, u32[]{:S(2)}, u32[]{:S(2)}) collective-permute-start(f32[24,7,128]{2,0,1:T(8,128)S(1)} %concatenate.48), channel_id=1, source_target_pairs={{0,1},{1,0},{2,3},{3,2},{4,5},{5,4},{6,7},{7,6},{8,9},{9,8},{10,11... | collective-permute-start | bytes 258056 | tf_op jit(solution)/shard_map/ppermute | solution.py:16
  49.6 0.9 collective-permute-done.4
  51.4 3.0 %collective-permute-start.6 = (f32[1,1,32,7,128]{4,3,2,1,0:T(8,128)S(1)}, f32[1,1,32,7,128]{4,3,2,1,0:T(8,128)S(1)}, u32[]{:S(2)}, u32[]{:S(2)}) collective-permute-start(f32[1,1,32,7,128]{4,3,2,1,0:T(8,128)S(1)} %slice_bitcast_fusion), channel_id=1, source_target_pairs={{4,0},{8,4},{12,8},{16,12},{20,16},{24,20},{28,24},{5,1},{9,5},{13... | collective-permute-start | bytes 344072 | tf_op jit(solution)/shard_map/ppermute | solution.py:27
  54.4 2.3 %collective-permute-start.5 = (f32[1,1,32,7,128]{4,3,2,1,0:T(8,128)S(1)}, f32[1,1,32,7,128]{4,3,2,1,0:T(8,128)S(1)}, u32[]{:S(2)}, u32[]{:S(2)}) collective-permute-start(f32[1,1,32,7,128]{4,3,2,1,0:T(8,128)S(1)} %slice_bitcast_fusion), channel_id=1, source_target_pairs={{0,4},{4,8},{8,12},{12,16},{16,20},{20,24},{24,28},{1,5},{5,9},{9,... | collective-permute-start | bytes 344072 | tf_op jit(solution)/shard_map/ppermute | solution.py:26
  60.3 1.4 %collective-permute-done.5 = f32[1,1,32,7,128]{4,3,2,1,0:T(8,128)S(1)} collective-permute-done((f32[1,1,32,7,128]{4,3,2,1,0:T(8,128)S(1)}, f32[1,1,32,7,128]{4,3,2,1,0:T(8,128)S(1)}, u32[]{:S(2)}, u32[]{:S(2)}) %collective-permute-start.5) | collective-permute-done | bytes 114720 | tf_op jit(solution)/shard_map/ppermute | solution.py:26
  61.7 3.4 %collective-permute-start.8 = (f32[3,1,32,7,128]{4,3,2,1,0:T(8,128)S(1)}, f32[3,1,32,7,128]{4,3,2,1,0:T(8,128)S(1)}, u32[]{:S(2)}, u32[]{:S(2)}) collective-permute-start(f32[3,1,32,7,128]{4,3,2,1,0:T(8,128)S(1)} %pad_maximum_fusion.1), channel_id=1, source_target_pairs={{1,0},{2,1},{3,2},{5,4},{6,5},{7,6},{9,8},{10,9},{11,10},{13,12},{... | collective-permute-start | bytes 1032200 | tf_op jit(solution)/shard_map/ppermute | solution.py:27
  65.1 3.2 %collective-permute-start.7 = (f32[3,1,32,7,128]{4,3,2,1,0:T(8,128)S(1)}, f32[3,1,32,7,128]{4,3,2,1,0:T(8,128)S(1)}, u32[]{:S(2)}, u32[]{:S(2)}) collective-permute-start(f32[3,1,32,7,128]{4,3,2,1,0:T(8,128)S(1)} %pad_maximum_fusion.1), channel_id=1, source_target_pairs={{0,1},{1,2},{2,3},{4,5},{5,6},{6,7},{8,9},{9,10},{10,11},{12,13},{... | collective-permute-start | bytes 1032200 | tf_op jit(solution)/shard_map/ppermute | solution.py:26
  68.7 3.0 %collective-permute-done.8 = f32[3,1,32,7,128]{4,3,2,1,0:T(8,128)S(1)} collective-permute-done((f32[3,1,32,7,128]{4,3,2,1,0:T(8,128)S(1)}, f32[3,1,32,7,128]{4,3,2,1,0:T(8,128)S(1)}, u32[]{:S(2)}, u32[]{:S(2)}) %collective-permute-start.8) | collective-permute-done | bytes 344096 | tf_op jit(solution)/shard_map/ppermute | solution.py:27
  71.7 1.2 %collective-permute-done.7 = f32[3,1,32,7,128]{4,3,2,1,0:T(8,128)S(1)} collective-permute-done((f32[3,1,32,7,128]{4,3,2,1,0:T(8,128)S(1)}, f32[3,1,32,7,128]{4,3,2,1,0:T(8,128)S(1)}, u32[]{:S(2)}, u32[]{:S(2)}) %collective-permute-start.7) | collective-permute-done | bytes 344096 | tf_op jit(solution)/shard_map/ppermute | solution.py:26
  73.0 1.0 %gather_fusion.1 = f32[256,7,128]{2,1,0:T(8,128)S(1)} fusion(f32[288,7,128]{2,1,0:T(8,128)S(1)} %bitcast.94, s32[1024]{0:T(1024)S(1)} %pad_clamp_fusion.2), kind=kCustom, calls=%fused_computation.1 | custom fusion | bytes 1836032 | tf_op jit(solution)/shard_map/gather | solution.py:193
  74.6 22.7 %fusion.9 = (f32[32,128]{1,0:T(8,128)S(1)}, f32[32,128]{1,0:T(8,128)S(1)}, f32[32,128]{1,0:T(8,128)S(1)}) fusion(f32[32,8,128]{2,1,0:T(8,128)S(1)} %bitcast.100, f32[32,8,128]{2,1,0:T(8,128)S(1)} %bitcast.101, f32[32,8,128]{2,1,0:T(8,128)S(1)} %bitcast.102, f32[32,128]{1,0:T(8,128)S(1)} %bitcast.116, f32[32,8,128]{2,1,0:T(8,128)S(1)} %bitcast.103, ...), kind=kLoop, calls=%fused_computation.23 | loop fusion | flops 109039616 | bytes 1015808 | tf_op jit(solution)/shard_map/vmap()/reduce_sum | solution.py:52
  (170 shorter events, 19.3 us)
Async XLA Ops:
  0.0 24.2 %copy-start = (s32[1024]{0:T(1024)S(1)}, s32[1024]{0:T(1024)}, u32[]{:S(2)}) copy-start(s32[1024]{0:T(1024)} %param.12) | copy-start | bytes 12292
  0.0 23.8 %copy-start.2 = (s32[5,8,4]{1,2,0:T(4,128)S(1)}, s32[5,8,4]{1,2,0:T(4,128)}, u32[]{:S(2)}) copy-start(s32[5,8,4]{1,2,0:T(4,128)} %param.11) | copy-start | bytes 1924
  0.0 24.0 %copy-start.3 = (s32[1,1,32,8]{2,3,1,0:T(8,128)S(1)}, s32[1,1,32,8]{2,3,1,0:T(8,128)}, u32[]{:S(2)}) copy-start(s32[1,1,32,8]{2,3,1,0:T(8,128)} %param.14) | copy-start | bytes 3076
  15.8 15.1 %collective-permute-start = (f32[9,7,128]{2,1,0:T(8,128)S(1)}, f32[9,7,128]{2,1,0:T(8,128)S(1)}, u32[]{:S(2)}, u32[]{:S(2)}) collective-permute-start(f32[9,7,128]{2,1,0:T(8,128)S(1)} %pad_maximum_fusion.4), channel_id=1, source_target_pairs={{0,16},{4,20},{8,24},{12,28},{16,0},{20,4},{24,8},{28,12},{1,17},{... | collective-permute-start | bytes 96776 | tf_op jit(solution)/shard_map/ppermute | solution.py:16
  24.2 1.6 %copy-start.5 = (s32[5]{0:T(128)S(1)}, s32[5]{0:T(128)}, u32[]{:S(2)}) copy-start(s32[5]{0:T(128)} %constant.200) | copy-start | bytes 64
  24.2 4.0 %copy-start.4 = (s32[1,1,32,8]{2,3,1,0:T(8,128)S(1)}, s32[1,1,32,8]{2,3,1,0:T(8,128)}, u32[]{:S(2)}) copy-start(s32[1,1,32,8]{2,3,1,0:T(8,128)} %param.13) | copy-start | bytes 3076
  28.5 3.2 %copy-start.1 = (f32[1,1,72,128]{3,2,1,0:T(8,128)S(1)}, f32[1,1,72,128]{3,2,1,0:T(8,128)}, u32[]{:S(2)}) copy-start(f32[1,1,72,128]{3,2,1,0:T(8,128)} %param.10) | copy-start | bytes 110596
  32.2 2.9 %collective-permute-start.1 = (f32[10,7,128]{2,1,0:T(8,128)S(1)}, f32[10,7,128]{2,1,0:T(8,128)S(1)}, u32[]{:S(2)}, u32[]{:S(2)}) collective-permute-start(f32[10,7,128]{2,1,0:T(8,128)S(1)} %pad_maximum_fusion.3), channel_id=1, source_target_pairs={{0,8},{4,12},{8,0},{12,4},{16,24},{20,28},{24,16},{28,20},{1,9},{5... | collective-permute-start | bytes 107528 | tf_op jit(solution)/shard_map/ppermute | solution.py:16
  36.4 3.0 %collective-permute-start.2 = (f32[12,7,128]{2,1,0:T(8,128)S(1)}, f32[12,7,128]{2,1,0:T(8,128)S(1)}, u32[]{:S(2)}, u32[]{:S(2)}) collective-permute-start(f32[12,7,128]{2,1,0:T(8,128)S(1)} %pad_maximum_fusion.2), channel_id=1, source_target_pairs={{0,4},{4,0},{8,12},{12,8},{16,20},{20,16},{24,28},{28,24},{1,5},{5... | collective-permute-start | bytes 129032 | tf_op jit(solution)/shard_map/ppermute | solution.py:16
  40.7 3.1 %collective-permute-start.3 = (f32[16,7,128]{2,0,1:T(8,128)S(1)}, f32[16,7,128]{2,0,1:T(8,128)S(1)}, u32[]{:S(2)}, u32[]{:S(2)}) collective-permute-start(f32[16,7,128]{2,0,1:T(8,128)S(1)} %concatenate.47), channel_id=1, source_target_pairs={{0,2},{1,3},{2,0},{3,1},{4,6},{5,7},{6,4},{7,5},{8,10},{9,11},{10,... | collective-permute-start | bytes 172040 | tf_op jit(solution)/shard_map/ppermute | solution.py:16
  45.1 5.4 %collective-permute-start.4 = (f32[24,7,128]{2,0,1:T(8,128)S(1)}, f32[24,7,128]{2,0,1:T(8,128)S(1)}, u32[]{:S(2)}, u32[]{:S(2)}) collective-permute-start(f32[24,7,128]{2,0,1:T(8,128)S(1)} %concatenate.48), channel_id=1, source_target_pairs={{0,1},{1,0},{2,3},{3,2},{4,5},{5,4},{6,7},{7,6},{8,9},{9,8},{10,11... | collective-permute-start | bytes 258056 | tf_op jit(solution)/shard_map/ppermute | solution.py:16
  51.4 8.8 %collective-permute-start.6 = (f32[1,1,32,7,128]{4,3,2,1,0:T(8,128)S(1)}, f32[1,1,32,7,128]{4,3,2,1,0:T(8,128)S(1)}, u32[]{:S(2)}, u32[]{:S(2)}) collective-permute-start(f32[1,1,32,7,128]{4,3,2,1,0:T(8,128)S(1)} %slice_bitcast_fusion), channel_id=1, source_target_pairs={{4,0},{8,4},{12,8},{16,12},{20,16},{24,20},{28,24},{5,1},{9,5},{13... | collective-permute-start | bytes 344072 | tf_op jit(solution)/shard_map/ppermute | solution.py:27
  54.4 7.2 %collective-permute-start.5 = (f32[1,1,32,7,128]{4,3,2,1,0:T(8,128)S(1)}, f32[1,1,32,7,128]{4,3,2,1,0:T(8,128)S(1)}, u32[]{:S(2)}, u32[]{:S(2)}) collective-permute-start(f32[1,1,32,7,128]{4,3,2,1,0:T(8,128)S(1)} %slice_bitcast_fusion), channel_id=1, source_target_pairs={{0,4},{4,8},{8,12},{12,16},{16,20},{20,24},{24,28},{1,5},{5,9},{9,... | collective-permute-start | bytes 344072 | tf_op jit(solution)/shard_map/ppermute | solution.py:26
  61.7 10.0 %collective-permute-start.8 = (f32[3,1,32,7,128]{4,3,2,1,0:T(8,128)S(1)}, f32[3,1,32,7,128]{4,3,2,1,0:T(8,128)S(1)}, u32[]{:S(2)}, u32[]{:S(2)}) collective-permute-start(f32[3,1,32,7,128]{4,3,2,1,0:T(8,128)S(1)} %pad_maximum_fusion.1), channel_id=1, source_target_pairs={{1,0},{2,1},{3,2},{5,4},{6,5},{7,6},{9,8},{10,9},{11,10},{13,12},{... | collective-permute-start | bytes 1032200 | tf_op jit(solution)/shard_map/ppermute | solution.py:27
  65.1 7.8 %collective-permute-start.7 = (f32[3,1,32,7,128]{4,3,2,1,0:T(8,128)S(1)}, f32[3,1,32,7,128]{4,3,2,1,0:T(8,128)S(1)}, u32[]{:S(2)}, u32[]{:S(2)}) collective-permute-start(f32[3,1,32,7,128]{4,3,2,1,0:T(8,128)S(1)} %pad_maximum_fusion.1), channel_id=1, source_target_pairs={{0,1},{1,2},{2,3},{4,5},{5,6},{6,7},{8,9},{9,10},{10,11},{12,13},{... | collective-permute-start | bytes 1032200 | tf_op jit(solution)/shard_map/ppermute | solution.py:26

commit v6 on v4

--- a/solution.py
+++ b/solution.py
@@ -37,21 +37,25 @@
     return jnp.concatenate([centre, total, spread[:, None]], axis=1)
 
 
-def evaluate(target, sources, moments):
+def evaluate(target, centre, sources, extra, moments):
     sep_x = target[0][None, :, None] - sources[:, 0][:, None, :]
     sep_y = target[1][None, :, None] - sources[:, 1][:, None, :]
     sep_z = target[2][None, :, None] - sources[:, 2][:, None, :]
-    radius_sq = (
-        sep_x * sep_x + sep_y * sep_y + sep_z * sep_z + (sources[:, 6] * sources[:, 6])[:, None, :]
-    )
+    radius_sq = sep_x * sep_x + sep_y * sep_y + sep_z * sep_z + extra[:, 0][:, None, :]
     inverse = lax.rsqrt(radius_sq)
     weight = inverse * inverse * inverse
-    str_x = sources[:, 3][:, None, :] * weight
-    str_y = sources[:, 4][:, None, :] * weight
-    str_z = sources[:, 5][:, None, :] * weight
-    near_x = jnp.sum(str_y * sep_z - str_z * sep_y, axis=(0, 2))
-    near_y = jnp.sum(str_z * sep_x - str_x * sep_z, axis=(0, 2))
-    near_z = jnp.sum(str_x * sep_y - str_y * sep_x, axis=(0, 2))
+    sum_x = jnp.sum(sources[:, 3][:, None, :] * weight, axis=(0, 2))
+    sum_y = jnp.sum(sources[:, 4][:, None, :] * weight, axis=(0, 2))
+    sum_z = jnp.sum(sources[:, 5][:, None, :] * weight, axis=(0, 2))
+    arm_x = jnp.sum(extra[:, 1][:, None, :] * weight, axis=(0, 2))
+    arm_y = jnp.sum(extra[:, 2][:, None, :] * weight, axis=(0, 2))
+    arm_z = jnp.sum(extra[:, 3][:, None, :] * weight, axis=(0, 2))
+    rel_x = target[0] - centre[0]
+    rel_y = target[1] - centre[1]
+    rel_z = target[2] - centre[2]
+    near_x = sum_y * rel_z - sum_z * rel_y - arm_x
+    near_y = sum_z * rel_x - sum_x * rel_z - arm_y
+    near_z = sum_x * rel_y - sum_y * rel_x - arm_z
     off_x = target[0][None, :] - moments[:, 0][:, None]
     off_y = target[1][None, :] - moments[:, 1][:, None]
     off_z = target[2][None, :] - moments[:, 2][:, None]
@@ -67,21 +71,14 @@
     return jnp.stack([near_x + far_x, near_y + far_y, near_z + far_z], axis=0) * inv_four_pi
 
 
-def evaluate_all(targets, sources_all, moments):
-    block_count = targets.shape[0]
-    group_size = math.gcd(block_count, 8)
-    groups = block_count // group_size
-
-    def one_group(bundle):
-        return jax.vmap(evaluate)(bundle[0], bundle[1], bundle[2])
-
-    grouped = (
-        targets.reshape((groups, group_size) + targets.shape[1:]),
-        sources_all.reshape((groups, group_size) + sources_all.shape[1:]),
-        moments.reshape((groups, group_size) + moments.shape[1:]),
-    )
-    velocity = lax.map(one_group, grouped)
-    return velocity.reshape((block_count,) + velocity.shape[2:])
+def source_terms(sources_all, centre):
+    px = sources_all[:, :, 0] - centre[:, 0][:, None, None]
+    py = sources_all[:, :, 1] - centre[:, 1][:, None, None]
+    pz = sources_all[:, :, 2] - centre[:, 2][:, None, None]
+    sx, sy, sz = sources_all[:, :, 3], sources_all[:, :, 4], sources_all[:, :, 5]
+    core_sq = sources_all[:, :, 6] * sources_all[:, :, 6]
+    extra = jnp.stack([core_sq, sy * pz - sz * py, sz * px - sx * pz, sx * py - sy * px], axis=2)
+    return lax.optimization_barrier(extra)
 
 
 def trace_back(loc, moves, levels, bits_x, nbd):
@@ -186,7 +183,10 @@
     source_pool = grid_blocks.reshape(9 * nbd, 7, blocks.shape[2])
     pool_index = direction * nbd + source_slot
     sources_all = source_pool[pool_index]
-    velocity = jax.vmap(evaluate)(blocks[:, 0:3], sources_all, moments)
+    targets = blocks[:, 0:3]
+    centre = jnp.mean(targets, axis=2)
+    extra = source_terms(sources_all, centre)
+    velocity = jax.vmap(evaluate)(targets, centre, sources_all, extra, moments)
     return velocity[None, None]
 
 

time: 87.5 us -> 84.4 us (0.965)
  other arithmetic: 30.9 us -> 26.5 us
  local copies, waits for them, and re-layouts: 14.6 us -> 16.1 us
    reduce_sum x1 -> x2, other arithmetic: 22.7 us -> 18 us  [the longest x1 17.9 us: evaluate(): arm_x = jnp.sum(extra[:, 1][:, None, :] * weight, axis=(0, 2))]
  transfers between devices with their start and end apart: 9 -> 9, of which waited for: 6 -> 6; matrix products, arithmetic and copies ran while one was open for 14% -> 16% of each run, Pallas kernels for 0% -> 0%
where the time goes in v6:
time: 84.4 us; the launch traced here: 83.1 us
  other arithmetic  26.5 us (31%)
  starting transfers between devices  20.5 us (24%)
  local copies, waits for them, and re-layouts  16.1 us (19%)
  between operations  12.4 us (15%)
  waiting for transfers between devices  7.65 us (9%)
    reduce_sum x1, other arithmetic, evaluate(): arm_x = jnp.sum(extra[:, 1][:, None, :] * weight, axis=(0, 2))  17.9 us
    ppermute x5, starting transfers between devices, from_partner(): lax.ppermute(shard, axis, [(i, i ^ 1 << apart) for i in range(lax.axis_si...  8.79 us
    ppermute x2, starting transfers between devices, padded(): after = lax.ppermute(first, axis, down)  6.43 us
    ppermute x2, starting transfers between devices, padded(): before = lax.ppermute(last, axis, up)  5.3 us
    ppermute x5, waiting for transfers between devices, from_partner(): lax.ppermute(shard, axis, [(i, i ^ 1 << apart) for i in range(lax.axis_si...  2.88 us
    ppermute x2, waiting for transfers between devices, padded(): after = lax.ppermute(first, axis, down)  2.66 us
    ppermute x2, waiting for transfers between devices, padded(): before = lax.ppermute(last, axis, up)  2.12 us
  transfers between devices with their start and end apart: 9, of which 6 were waited for; matrix products, arithmetic and copies ran while one was open for 16% of the time, Pallas kernels for 0%

profile of v6, /device:TPU:9, one launch (start us, length us, event | category | flops | bytes accessed | tf_op | source)
XLA Modules:
  0.0 83.1 jit_solution(3971598536460153634)
XLA Ops:
  0.0 0.9 %multiply_reduce_fusion.7 = f32[72]{0:T(128)S(1)} fusion(f32[1,1,72,128]{3,2,1,0:T(8,128)} %param.10), kind=kLoop, calls=%fused_computation.59 | loop fusion | flops 18360 | bytes 37152 | tf_op jit(solution)/shard_map/reduce_sum | solution.py:36
  0.9 1.0 %reduce_sum.287 = f32[72,3]{0,1:T(4,128)S(1)} reduce(f32[1,1,72,3,128]{4,2,3,1,0:T(8,128)} %param.8, f32[]{:T(128)} %constant.168.clone.1), dimensions={0,1,4}, to_apply=%region_0.0 | reduce | flops 27432 | bytes 111460 | tf_op jit(solution)/shard_map/reduce_sum | solution.py:33
  1.9 1.1 %multiply_reduce_fusion.6 = f32[72]{0:T(128)S(1)} fusion(f32[72,3]{0,1:T(4,128)S(1)} %broadcast_multiply_fusion.1, f32[1,1,72,3,128]{4,2,3,1,0:T(8,128)} %param.8), kind=kLoop, calls=%fused_computation.45 | loop fusion | flops 82872 | bytes 111744 | tf_op jit(solution)/shard_map/reduce_sum | solution.py:36
  3.0 1.0 %reduce_sum.288 = f32[72,3]{0,1:T(4,128)S(1)} reduce(f32[1,1,72,3,128]{4,2,3,1,0:T(8,128)} %param.9, f32[]{:T(128)} %constant.168.clone.1), dimensions={0,1,4}, to_apply=%region_1.0 | reduce | flops 27432 | bytes 111460 | tf_op jit(solution)/shard_map/reduce_sum | solution.py:34
  4.2 1.5 %constant_dynamic-slice_fusion.13 = (s32[1,1,1]{1,2,0:T(1,128)}, s32[1,1,1]{1,2,0:T(1,128)}, s32[1,1,1]{1,2,0:T(1,128)}, s32[1,1,1]{1,2,0:T(1,128)}, s32[1,1,1]{...) fusion(s32[5,8,4]{1,2,0:T(4,128)} %param.11, ...), kind=kLoop, calls=%fused_computation.236 | loop fusion | bytes 108 | tf_op jit(solution)/shard_map/dynamic_slice | solution.py:150
  12.5 1.0 %select_maximum_fusion = f32[80,7,128]{2,0,1:T(8,128)S(1)} fusion(f32[72,1,128]{2,0,1:T(8,128)} %bitcast.194, f32[72,3,128]{2,0,1:T(8,128)} %bitcast.193, f32[72,3,128]{2,0,1:T(8,128)} %bitcast.179), kind=kLoop, calls=%fused_computation.14 | loop fusion | flops 430080 | bytes 544768 | tf_op jit(solution)/shard_map/concatenate | solution.py:133
  13.5 2.4 %collective-permute-start = (f32[9,7,128]{2,0,1:T(8,128)S(1)}, f32[9,7,128]{2,0,1:T(8,128)S(1)}, u32[]{:S(2)}, u32[]{:S(2)}) collective-permute-start(f32[9,7,128]{2,0,1:T(8,128)S(1)} %pad_maximum_fusion.3), channel_id=1, source_target_pairs={{0,16},{4,20},{8,24},{12,28},{16,0},{20,4},{24,8},{28,12},{1,17},{... | collective-permute-start | bytes 96776 | tf_op jit(solution)/shard_map/ppermute | solution.py:16
  15.9 0.8 copy.137
  19.9 1.4 %gather_fusion.2 = s32[256]{0:T(256)S(1)} fusion(s32[1024]{0:T(1024)S(1)} %copy-done, s32[1024]{0:T(1024)S(1)} %pad_clamp_fusion.1), kind=kCustom, calls=%fused_computation.2 | custom fusion | bytes 3072 | tf_op jit(solution)/shard_map/gather | solution.py:138
  27.1 1.4 %gather_fusion = s32[256]{0:T(256)S(1)} fusion(s32[1024]{0:T(1024)S(1)} %copy-done, s32[1024]{0:T(1024)S(1)} %pad_clamp_fusion.3), kind=kCustom, calls=%fused_computation | custom fusion | bytes 3072 | tf_op jit(solution)/shard_map/gather | solution.py:176
  28.9 1.3 %collective-permute-start.2 = (f32[12,7,128]{2,0,1:T(8,128)S(1)}, f32[12,7,128]{2,0,1:T(8,128)S(1)}, u32[]{:S(2)}, u32[]{:S(2)}) collective-permute-start(f32[12,7,128]{2,0,1:T(8,128)S(1)} %pad_maximum_fusion.5), channel_id=1, source_target_pairs={{0,4},{4,0},{8,12},{12,8},{16,20},{20,16},{24,28},{28,24},{1,5},{5... | collective-permute-start | bytes 129032 | tf_op jit(solution)/shard_map/ppermute | solution.py:16
  33.2 1.3 %collective-permute-start.3 = (f32[16,7,128]{2,0,1:T(8,128)S(1)}, f32[16,7,128]{2,0,1:T(8,128)S(1)}, u32[]{:S(2)}, u32[]{:S(2)}) collective-permute-start(f32[16,7,128]{2,0,1:T(8,128)S(1)} %concatenate.47), channel_id=1, source_target_pairs={{0,2},{1,3},{2,0},{3,1},{4,6},{5,7},{6,4},{7,5},{8,10},{9,11},{10,... | collective-permute-start | bytes 172040 | tf_op jit(solution)/shard_map/ppermute | solution.py:16
  34.5 1.8 %collective-permute-done.3 = f32[16,7,128]{2,0,1:T(8,128)S(1)} collective-permute-done((f32[16,7,128]{2,0,1:T(8,128)S(1)}, f32[16,7,128]{2,0,1:T(8,128)S(1)}, u32[]{:S(2)}, u32[]{:S(2)}) %collective-permute-start.3) | collective-permute-done | bytes 57376 | tf_op jit(solution)/shard_map/ppermute | solution.py:16
  36.5 3.6 %collective-permute-start.4 = (f32[24,7,128]{2,0,1:T(8,128)S(1)}, f32[24,7,128]{2,0,1:T(8,128)S(1)}, u32[]{:S(2)}, u32[]{:S(2)}) collective-permute-start(f32[24,7,128]{2,0,1:T(8,128)S(1)} %concatenate.48), channel_id=1, source_target_pairs={{0,1},{1,0},{2,3},{3,2},{4,5},{5,4},{6,7},{7,6},{8,9},{9,8},{10,11... | collective-permute-start | bytes 258056 | tf_op jit(solution)/shard_map/ppermute | solution.py:16
  40.1 0.9 %collective-permute-done.4 = f32[24,7,128]{2,0,1:T(8,128)S(1)} collective-permute-done((f32[24,7,128]{2,0,1:T(8,128)S(1)}, f32[24,7,128]{2,0,1:T(8,128)S(1)}, u32[]{:S(2)}, u32[]{:S(2)}) %collective-permute-start.4) | collective-permute-done | bytes 86048 | tf_op jit(solution)/shard_map/ppermute | solution.py:16
  41.2 3.0 %collective-permute-start.6 = (f32[1,1,32,7,128]{4,2,3,1,0:T(8,128)S(1)}, f32[1,1,32,7,128]{4,2,3,1,0:T(8,128)S(1)}, u32[]{:S(2)}, u32[]{:S(2)}) collective-permute-start(f32[1,1,32,7,128]{4,2,3,1,0:T(8,128)S(1)} %slice_bitcast_fusion.4), channel_id=1, source_target_pairs={{4,0},{8,4},{12,8},{16,12},{20,16},{24,20},{28,24},{5,1},{9,5},{13... | collective-permute-start | bytes 344072 | tf_op jit(solution)/shard_map/ppermute | solution.py:27
  44.2 2.3 %collective-permute-start.5 = (f32[1,1,32,7,128]{4,2,3,1,0:T(8,128)S(1)}, f32[1,1,32,7,128]{4,2,3,1,0:T(8,128)S(1)}, u32[]{:S(2)}, u32[]{:S(2)}) collective-permute-start(f32[1,1,32,7,128]{4,2,3,1,0:T(8,128)S(1)} %slice_bitcast_fusion.4), channel_id=1, source_target_pairs={{0,4},{4,8},{8,12},{12,16},{16,20},{20,24},{24,28},{1,5},{5,9},{9,... | collective-permute-start | bytes 344072 | tf_op jit(solution)/shard_map/ppermute | solution.py:26
  50.2 0.9 %collective-permute-done.5 = f32[1,1,32,7,128]{4,2,3,1,0:T(8,128)S(1)} collective-permute-done((f32[1,1,32,7,128]{4,2,3,1,0:T(8,128)S(1)}, f32[1,1,32,7,128]{4,2,3,1,0:T(8,128)S(1)}, u32[]{:S(2)}, u32[]{:S(2)}) %collective-permute-start.5) | collective-permute-done | bytes 114720 | tf_op jit(solution)/shard_map/ppermute | solution.py:26
  51.1 3.4 %collective-permute-start.8 = (f32[3,1,32,7,128]{4,2,3,1,0:T(8,128)S(1)}, f32[3,1,32,7,128]{4,2,3,1,0:T(8,128)S(1)}, u32[]{:S(2)}, u32[]{:S(2)}) collective-permute-start(f32[3,1,32,7,128]{4,2,3,1,0:T(8,128)S(1)} %pad_maximum_fusion.2), channel_id=1, source_target_pairs={{1,0},{2,1},{3,2},{5,4},{6,5},{7,6},{9,8},{10,9},{11,10},{13,12},{... | collective-permute-start | bytes 1032200 | tf_op jit(solution)/shard_map/ppermute | solution.py:27
  54.5 3.0 %collective-permute-start.7 = (f32[3,1,32,7,128]{4,2,3,1,0:T(8,128)S(1)}, f32[3,1,32,7,128]{4,2,3,1,0:T(8,128)S(1)}, u32[]{:S(2)}, u32[]{:S(2)}) collective-permute-start(f32[3,1,32,7,128]{4,2,3,1,0:T(8,128)S(1)} %pad_maximum_fusion.2), channel_id=1, source_target_pairs={{0,1},{1,2},{2,3},{4,5},{5,6},{6,7},{8,9},{9,10},{10,11},{12,13},{... | collective-permute-start | bytes 1032200 | tf_op jit(solution)/shard_map/ppermute | solution.py:26
  57.9 2.6 %collective-permute-done.8 = f32[3,1,32,7,128]{4,2,3,1,0:T(8,128)S(1)} collective-permute-done((f32[3,1,32,7,128]{4,2,3,1,0:T(8,128)S(1)}, f32[3,1,32,7,128]{4,2,3,1,0:T(8,128)S(1)}, u32[]{:S(2)}, u32[]{:S(2)}) %collective-permute-start.8) | collective-permute-done | bytes 344096 | tf_op jit(solution)/shard_map/ppermute | solution.py:27
  60.6 1.2 %collective-permute-done.7 = f32[3,1,32,7,128]{4,2,3,1,0:T(8,128)S(1)} collective-permute-done((f32[3,1,32,7,128]{4,2,3,1,0:T(8,128)S(1)}, f32[3,1,32,7,128]{4,2,3,1,0:T(8,128)S(1)}, u32[]{:S(2)}, u32[]{:S(2)}) %collective-permute-start.7) | collective-permute-done | bytes 344096 | tf_op jit(solution)/shard_map/ppermute | solution.py:26
  62.5 1.0 %gather_fusion.1 = f32[256,7,128]{2,1,0:T(8,128)S(1)} fusion(f32[288,7,128]{2,1,0:T(8,128)S(1)} %copy.125, s32[1024]{0:T(1024)S(1)} %pad_clamp_fusion.2), kind=kCustom, calls=%fused_computation.1 | custom fusion | bytes 1836032 | tf_op jit(solution)/shard_map/gather | solution.py:185
  64.5 17.9 %multiply_reduce_fusion.3 = (f32[32,128]{1,0:T(8,128)S(1)}, f32[32,128]{1,0:T(8,128)S(1)}, f32[32,128]{1,0:T(8,128)S(1)}, f32[32,128]{1,0:T(8,128)S(1)}, f32[32,128]{1,0:T(8,128)S(1)}, /*index=5*/f32[32,128]{1,0:T(8,128)S(1)}) fusion(f32[32,8,128]{2,1,0:T(8,128)S(1)} %get-tuple-element.37, f32[32,8,128]{2,1,0:T(8,128)S(1)} %get-tuple-element.38, ...), kind=kLoop, calls=%fused_computation.8 | loop fusion | flops 96444416 | bytes 1458176 | tf_op jit(solution)/shard_map/vmap()/reduce_sum | solution.py:50
  (129 shorter events, 14.0 us)
Async XLA Ops:
  0.0 19.9 %copy-start = (s32[1024]{0:T(1024)S(1)}, s32[1024]{0:T(1024)}, u32[]{:S(2)}) copy-start(s32[1024]{0:T(1024)} %param.12) | copy-start | bytes 12292
  13.5 11.9 %collective-permute-start = (f32[9,7,128]{2,0,1:T(8,128)S(1)}, f32[9,7,128]{2,0,1:T(8,128)S(1)}, u32[]{:S(2)}, u32[]{:S(2)}) collective-permute-start(f32[9,7,128]{2,0,1:T(8,128)S(1)} %pad_maximum_fusion.3), channel_id=1, source_target_pairs={{0,16},{4,20},{8,24},{12,28},{16,0},{20,4},{24,8},{28,12},{1,17},{... | collective-permute-start | bytes 96776 | tf_op jit(solution)/shard_map/ppermute | solution.py:16
  19.9 3.9 %copy-start.1 = (s32[1,1,32,8]{2,3,1,0:T(8,128)S(1)}, s32[1,1,32,8]{2,3,1,0:T(8,128)}, u32[]{:S(2)}) copy-start(s32[1,1,32,8]{2,3,1,0:T(8,128)} %param.13) | copy-start | bytes 3076
  25.6 3.1 %collective-permute-start.1 = (f32[10,7,128]{2,0,1:T(8,128)S(1)}, f32[10,7,128]{2,0,1:T(8,128)S(1)}, u32[]{:S(2)}, u32[]{:S(2)}) collective-permute-start(f32[10,7,128]{2,0,1:T(8,128)S(1)} %pad_maximum_fusion.4), channel_id=1, source_target_pairs={{0,8},{4,12},{8,0},{12,4},{16,24},{20,28},{24,16},{28,20},{1,9},{5... | collective-permute-start | bytes 107528 | tf_op jit(solution)/shard_map/ppermute | solution.py:16
  28.9 4.0 %collective-permute-start.2 = (f32[12,7,128]{2,0,1:T(8,128)S(1)}, f32[12,7,128]{2,0,1:T(8,128)S(1)}, u32[]{:S(2)}, u32[]{:S(2)}) collective-permute-start(f32[12,7,128]{2,0,1:T(8,128)S(1)} %pad_maximum_fusion.5), channel_id=1, source_target_pairs={{0,4},{4,0},{8,12},{12,8},{16,20},{20,16},{24,28},{28,24},{1,5},{5... | collective-permute-start | bytes 129032 | tf_op jit(solution)/shard_map/ppermute | solution.py:16
  33.2 3.1 %collective-permute-start.3 = (f32[16,7,128]{2,0,1:T(8,128)S(1)}, f32[16,7,128]{2,0,1:T(8,128)S(1)}, u32[]{:S(2)}, u32[]{:S(2)}) collective-permute-start(f32[16,7,128]{2,0,1:T(8,128)S(1)} %concatenate.47), channel_id=1, source_target_pairs={{0,2},{1,3},{2,0},{3,1},{4,6},{5,7},{6,4},{7,5},{8,10},{9,11},{10,... | collective-permute-start | bytes 172040 | tf_op jit(solution)/shard_map/ppermute | solution.py:16
  36.5 4.5 %collective-permute-start.4 = (f32[24,7,128]{2,0,1:T(8,128)S(1)}, f32[24,7,128]{2,0,1:T(8,128)S(1)}, u32[]{:S(2)}, u32[]{:S(2)}) collective-permute-start(f32[24,7,128]{2,0,1:T(8,128)S(1)} %concatenate.48), channel_id=1, source_target_pairs={{0,1},{1,0},{2,3},{3,2},{4,5},{5,4},{6,7},{7,6},{8,9},{9,8},{10,11... | collective-permute-start | bytes 258056 | tf_op jit(solution)/shard_map/ppermute | solution.py:16
  41.2 8.9 %collective-permute-start.6 = (f32[1,1,32,7,128]{4,2,3,1,0:T(8,128)S(1)}, f32[1,1,32,7,128]{4,2,3,1,0:T(8,128)S(1)}, u32[]{:S(2)}, u32[]{:S(2)}) collective-permute-start(f32[1,1,32,7,128]{4,2,3,1,0:T(8,128)S(1)} %slice_bitcast_fusion.4), channel_id=1, source_target_pairs={{4,0},{8,4},{12,8},{16,12},{20,16},{24,20},{28,24},{5,1},{9,5},{13... | collective-permute-start | bytes 344072 | tf_op jit(solution)/shard_map/ppermute | solution.py:27
  44.2 6.9 %collective-permute-start.5 = (f32[1,1,32,7,128]{4,2,3,1,0:T(8,128)S(1)}, f32[1,1,32,7,128]{4,2,3,1,0:T(8,128)S(1)}, u32[]{:S(2)}, u32[]{:S(2)}) collective-permute-start(f32[1,1,32,7,128]{4,2,3,1,0:T(8,128)S(1)} %slice_bitcast_fusion.4), channel_id=1, source_target_pairs={{0,4},{4,8},{8,12},{12,16},{16,20},{20,24},{24,28},{1,5},{5,9},{9,... | collective-permute-start | bytes 344072 | tf_op jit(solution)/shard_map/ppermute | solution.py:26
  51.1 9.5 %collective-permute-start.8 = (f32[3,1,32,7,128]{4,2,3,1,0:T(8,128)S(1)}, f32[3,1,32,7,128]{4,2,3,1,0:T(8,128)S(1)}, u32[]{:S(2)}, u32[]{:S(2)}) collective-permute-start(f32[3,1,32,7,128]{4,2,3,1,0:T(8,128)S(1)} %pad_maximum_fusion.2), channel_id=1, source_target_pairs={{1,0},{2,1},{3,2},{5,4},{6,5},{7,6},{9,8},{10,9},{11,10},{13,12},{... | collective-permute-start | bytes 1032200 | tf_op jit(solution)/shard_map/ppermute | solution.py:27
  54.5 7.2 %collective-permute-start.7 = (f32[3,1,32,7,128]{4,2,3,1,0:T(8,128)S(1)}, f32[3,1,32,7,128]{4,2,3,1,0:T(8,128)S(1)}, u32[]{:S(2)}, u32[]{:S(2)}) collective-permute-start(f32[3,1,32,7,128]{4,2,3,1,0:T(8,128)S(1)} %pad_maximum_fusion.2), channel_id=1, source_target_pairs={{0,1},{1,2},{2,3},{4,5},{5,6},{6,7},{8,9},{9,10},{10,11},{12,13},{... | collective-permute-start | bytes 1032200 | tf_op jit(solution)/shard_map/ppermute | solution.py:26

commit v7 on v6

--- a/solution.py
+++ b/solution.py
@@ -16,17 +16,19 @@
     return lax.ppermute(shard, axis, [(i, i ^ 1 << apart) for i in range(lax.axis_size(axis))])
 
 
-def padded(shard, sides, width):
-    for axis, dim in sides:
-        size, length = (lax.axis_size(axis), shard.shape[dim])
-        up = [(i, (i + 1) % size) for i in range(size - 1)]
-        down = [(j, i) for i, j in up]
-        last = lax.slice_in_dim(shard, length - width, length, axis=dim)
-        first = lax.slice_in_dim(shard, 0, width, axis=dim)
-        before = lax.ppermute(last, axis, up)
-        after = lax.ppermute(first, axis, down)
-        shard = jnp.concatenate([before, shard, after], axis=dim)
-    return shard
+def shifted(shard, axis, step):
+    size = lax.axis_size(axis)
+    return lax.ppermute(shard, axis, [(i, i + step) for i in range(size) if 0 <= i + step < size])
+
+
+def halo_sources(blocks, near_where, column_index, row_index, size_y, nbd):
+    column = jnp.concatenate([shifted(blocks, "gx", 1), blocks, shifted(blocks, "gx", -1)], axis=0)
+    pool = jnp.concatenate([shifted(column, "gy", 1), column, shifted(column, "gy", -1)], axis=0)
+    source_device = near_where // nbd
+    delta_x = source_device // size_y - column_index
+    delta_y = source_device % size_y - row_index
+    pool_index = ((delta_y + 1) * 3 + (delta_x + 1)) * nbd + near_where % nbd
+    return pool[pool_index]
 
 
 def slot_multipoles(pos, stren, core):
@@ -135,7 +137,9 @@
     width = slot_table.shape[1]
     gathered = table_blocks(slot_table, lanes)
     pieces = gathered.shape[0]
-    far_where = owner[far_list[0, 0]]
+    both_where = owner[jnp.concatenate([near_list[0, 0], far_list[0, 0]], axis=1)]
+    near_where = both_where[:, : near_list.shape[3]]
+    far_where = both_where[:, near_list.shape[3] :]
     far_device, far_slot = trace_back(far_where, moves, levels, bits_x, nbd)
     held = jnp.pad(held, ((0, MOVE), (0, 0), (0, 0)))
     plans = []
@@ -173,16 +177,7 @@
         entry = entry + ((relative // level_bits[level]) % 2) * (1 << level)
     all_table = gathered.reshape(-1, pieces, width, lanes).transpose(0, 1, 3, 2).reshape(-1, width)
     moments = all_table[entry * (pieces * lanes) + far_slot]
-    near_where = owner[near_list[0, 0]]
-    source_device = near_where // nbd
-    source_slot = near_where % nbd
-    delta_x = source_device // size_y - column_index
-    delta_y = source_device % size_y - row_index
-    direction = (delta_x + 1) * 3 + (delta_y + 1)
-    grid_blocks = padded(blocks[None, None], (("gx", 0), ("gy", 1)), 1)
-    source_pool = grid_blocks.reshape(9 * nbd, 7, blocks.shape[2])
-    pool_index = direction * nbd + source_slot
-    sources_all = source_pool[pool_index]
+    sources_all = halo_sources(blocks, near_where, column_index, row_index, size_y, nbd)
     targets = blocks[:, 0:3]
     centre = jnp.mean(targets, axis=2)
     extra = source_terms(sources_all, centre)

time: 84.4 us -> 87.1 us (1.032)
  waiting for transfers between devices: 7.65 us -> 11.1 us
  local copies, waits for them, and re-layouts: 16.1 us -> 14.8 us
  other arithmetic: 26.5 us -> 27.6 us
    ppermute x4, waiting for transfers between devices: 4.77 us -> 7.82 us  [shifted(): lax.ppermute(shard, axis, [(i, i + step) for i in range(size) if 0 <= i +...]
    squeeze x0 -> x1, local copies, waits for them, and re-layouts: none -> 1.04 us  [local(): strength[0, 0]]
    gather x5 -> x3, local copies, waits for them, and re-layouts: 3.92 us -> 3.39 us  [the longest x2 2.37 us: local(): owner[jnp.concatenate([near_list[0, 0], far_list[0, 0]], axis=1)]]
where the time goes in v7:
time: 87.1 us; the launch traced here: 86.4 us
  other arithmetic  27.6 us (32%)
  starting transfers between devices  20.5 us (24%)
  local copies, waits for them, and re-layouts  14.8 us (17%)
  between operations  12.3 us (14%)
  waiting for transfers between devices  11.1 us (13%)
    reduce_sum x1, other arithmetic, evaluate(): arm_x = jnp.sum(extra[:, 1][:, None, :] * weight, axis=(0, 2))  17.7 us
    ppermute x4, starting transfers between devices, shifted(): lax.ppermute(shard, axis, [(i, i + step) for i in range(size) if 0 <= i +...  11.7 us
    ppermute x5, starting transfers between devices, from_partner(): lax.ppermute(shard, axis, [(i, i ^ 1 << apart) for i in range(lax.axis_si...  8.79 us
    ppermute x4, waiting for transfers between devices, shifted(): lax.ppermute(shard, axis, [(i, i + step) for i in range(size) if 0 <= i +...  7.82 us
    ppermute x5, waiting for transfers between devices, from_partner(): lax.ppermute(shard, axis, [(i, i ^ 1 << apart) for i in range(lax.axis_si...  3.29 us
    gather x2, local copies, waits for them, and re-layouts, local(): owner[jnp.concatenate([near_list[0, 0], far_list[0, 0]], axis=1)]  2.37 us
    reduce_sum x1, other arithmetic, slot_multipoles(): jnp.mean(jnp.sum(offset * offset, axis=1), axis=1)  1.95 us
  transfers between devices with their start and end apart: 9, of which 6 were waited for; matrix products, arithmetic and copies ran while one was open for 16% of the time, Pallas kernels for 0%

profile of v7, /device:TPU:9, one launch (start us, length us, event | category | flops | bytes accessed | tf_op | source)
XLA Modules:
  0.0 86.4 jit_solution(8260214044067733607)
XLA Ops:
  0.0 1.0 %copy_bitcast_fusion = (f32[72,3,128]{2,1,0:T(4,128)S(1)}, f32[72,3,128]{2,1,0:T(4,128)S(1)}) fusion(f32[1,1,72,3,128]{4,2,3,1,0:T(8,128)} %param.9, f32[1,1,72,3,128]{4,2,3,1,0:T(8,128)} %param.8), kind=kLoop, calls=%fused_computation.25 | loop fusion | bytes 442368 | tf_op jit(solution)/shard_map/squeeze | solution.py:135
  1.0 1.0 %reduce_sum.287 = f32[72,3]{0,1:T(4,128)S(1)} reduce(f32[1,1,72,3,128]{4,2,3,1,0:T(8,128)} %param.8, f32[]{:T(128)} %constant.169.clone.1), dimensions={0,1,4}, to_apply=%region_0.0 | reduce | flops 27432 | bytes 111460 | tf_op jit(solution)/shard_map/reduce_sum | solution.py:35
  2.1 1.0 %reduce_sum.288 = f32[72,3]{0,1:T(4,128)S(1)} reduce(f32[1,1,72,3,128]{4,2,3,1,0:T(8,128)} %param.9, f32[]{:T(128)} %constant.169.clone.1), dimensions={0,1,4}, to_apply=%region_1.0 | reduce | flops 27432 | bytes 111460 | tf_op jit(solution)/shard_map/reduce_sum | solution.py:36
  3.2 1.5 %constant_dynamic-slice_fusion.11 = (s32[1,1,1]{1,2,0:T(1,128)}, s32[1,1,1]{1,2,0:T(1,128)}, s32[1,1,1]{1,2,0:T(1,128)}, s32[1,1,1]{1,2,0:T(1,128)}, s32[1,1,1]{...) fusion(s32[5,8,4]{1,2,0:T(4,128)} %param.11, ...), kind=kLoop, calls=%fused_computation.256 | loop fusion | bytes 108 | tf_op jit(solution)/shard_map/dynamic_slice | solution.py:154
  11.4 0.9 %multiply_reduce_fusion.7 = f32[72]{0:T(128)S(1)} fusion(f32[1,1,72,128]{3,2,1,0:T(8,128)} %param.10), kind=kLoop, calls=%fused_computation.78 | loop fusion | flops 18360 | bytes 37152 | tf_op jit(solution)/shard_map/reduce_sum | solution.py:38
  12.4 2.0 %multiply_reduce_fusion.6 = f32[72]{0:T(128)S(1)} fusion(f32[72,3]{1,0:T(8,128)S(1)} %copy.193, f32[1,1,72,3,128]{4,2,3,1,0:T(8,128)} %param.8), kind=kLoop, calls=%fused_computation.27 | loop fusion | flops 82872 | bytes 111744 | tf_op jit(solution)/shard_map/reduce_sum | solution.py:38
  14.4 0.9 %select_maximum_fusion = f32[80,7,128]{2,1,0:T(8,128)S(1)} fusion(f32[72,1,128]{2,1,0:T(1,128)} %bitcast.189, f32[72,3,128]{2,1,0:T(4,128)S(1)} %get-tuple-element.94, f32[72,3,128]{2,1,0:T(4,128)S(1)} %get-tuple-element.95), kind=kLoop, calls=%fused_computation.12 | loop fusion | flops 430080 | bytes 544768 | tf_op jit(solution)/shard_map/concatenate | solution.py:135
  15.3 2.4 %collective-permute-start = (f32[9,7,128]{2,1,0:T(8,128)S(1)}, f32[9,7,128]{2,1,0:T(8,128)S(1)}, u32[]{:S(2)}, u32[]{:S(2)}) collective-permute-start(f32[9,7,128]{2,1,0:T(8,128)S(1)} %pad_maximum_fusion.4), channel_id=1, source_target_pairs={{0,16},{4,20},{8,24},{12,28},{16,0},{20,4},{24,8},{28,12},{1,17},{... | collective-permute-start | bytes 96776 | tf_op jit(solution)/shard_map/ppermute | solution.py:16
  17.7 0.8 copy.206
  18.5 0.7 fusion.56
  21.3 2.3 %gather_fusion = s32[512]{0:T(512)S(1)} fusion(s32[1024]{0:T(1024)S(1)} %copy-done, s32[1024]{0:T(1024)S(1)} %pad_clamp_fusion.2), kind=kCustom, calls=%fused_computation | custom fusion | bytes 6144 | tf_op jit(solution)/shard_map/gather | solution.py:140
  30.0 1.3 %collective-permute-start.2 = (f32[12,7,128]{2,1,0:T(8,128)S(1)}, f32[12,7,128]{2,1,0:T(8,128)S(1)}, u32[]{:S(2)}, u32[]{:S(2)}) collective-permute-start(f32[12,7,128]{2,1,0:T(8,128)S(1)} %pad_maximum_fusion.2), channel_id=1, source_target_pairs={{0,4},{4,0},{8,12},{12,8},{16,20},{20,16},{24,28},{28,24},{1,5},{5... | collective-permute-start | bytes 129032 | tf_op jit(solution)/shard_map/ppermute | solution.py:16
  34.3 1.3 %collective-permute-start.3 = (f32[16,7,128]{2,1,0:T(8,128)S(1)}, f32[16,7,128]{2,1,0:T(8,128)S(1)}, u32[]{:S(2)}, u32[]{:S(2)}) collective-permute-start(f32[16,7,128]{2,1,0:T(8,128)S(1)} %constant_dynamic-update-slice_fusion), channel_id=1, source_target_pairs={{0,2},{1,3},{2,0},{3,1},{4,6},{5,7},{6,4},{7,5},{8,10},{9,11},{10,... | collective-permute-start | bytes 172040 | tf_op jit(solution)/shard_map/ppermute | solution.py:16
  35.6 1.9 %collective-permute-done.3 = f32[16,7,128]{2,1,0:T(8,128)S(1)} collective-permute-done((f32[16,7,128]{2,1,0:T(8,128)S(1)}, f32[16,7,128]{2,1,0:T(8,128)S(1)}, u32[]{:S(2)}, u32[]{:S(2)}) %collective-permute-start.3) | collective-permute-done | bytes 57376 | tf_op jit(solution)/shard_map/ppermute | solution.py:16
  37.5 3.6 %collective-permute-start.4 = (f32[24,7,128]{2,1,0:T(8,128)S(1)}, f32[24,7,128]{2,1,0:T(8,128)S(1)}, u32[]{:S(2)}, u32[]{:S(2)}) collective-permute-start(f32[24,7,128]{2,1,0:T(8,128)S(1)} %get-tuple-element.55), channel_id=1, source_target_pairs={{0,1},{1,0},{2,3},{3,2},{4,5},{5,4},{6,7},{7,6},{8,9},{9,8},{10,11... | collective-permute-start | bytes 258056 | tf_op jit(solution)/shard_map/ppermute | solution.py:16
  41.1 0.9 %collective-permute-done.4 = f32[24,7,128]{2,1,0:T(8,128)S(1)} collective-permute-done((f32[24,7,128]{2,1,0:T(8,128)S(1)}, f32[24,7,128]{2,1,0:T(8,128)S(1)}, u32[]{:S(2)}, u32[]{:S(2)}) %collective-permute-start.4) | collective-permute-done | bytes 86048 | tf_op jit(solution)/shard_map/ppermute | solution.py:16
  42.1 2.7 %collective-permute-start.6 = (f32[32,7,128]{2,1,0:T(8,128)S(1)}, f32[32,7,128]{2,1,0:T(8,128)S(1)}, u32[]{:S(2)}, u32[]{:S(2)}) collective-permute-start(f32[32,7,128]{2,1,0:T(8,128)S(1)} %slice.248), channel_id=1, source_target_pairs={{4,0},{8,4},{12,8},{16,12},{20,16},{24,20},{28,24},{5,1},{9,5},{13... | collective-permute-start | bytes 344072 | tf_op jit(solution)/shard_map/ppermute | solution.py:21
  44.8 2.6 %collective-permute-start.5 = (f32[32,7,128]{2,1,0:T(8,128)S(1)}, f32[32,7,128]{2,1,0:T(8,128)S(1)}, u32[]{:S(2)}, u32[]{:S(2)}) collective-permute-start(f32[32,7,128]{2,1,0:T(8,128)S(1)} %slice.248), channel_id=1, source_target_pairs={{0,4},{4,8},{8,12},{12,16},{16,20},{20,24},{24,28},{1,5},{5,9},{9,... | collective-permute-start | bytes 344072 | tf_op jit(solution)/shard_map/ppermute | solution.py:21
  52.0 4.5 %collective-permute-start.7 = (f32[96,7,128]{2,1,0:T(8,128)S(1)}, f32[96,7,128]{2,1,0:T(8,128)S(1)}, u32[]{:S(2)}, u32[]{:S(2)}) collective-permute-start(f32[96,7,128]{2,1,0:T(8,128)S(1)} %pad_maximum_fusion.1), channel_id=1, source_target_pairs={{0,1},{1,2},{2,3},{4,5},{5,6},{6,7},{8,9},{9,10},{10,11},{12,13},{... | collective-permute-start | bytes 1032200 | tf_op jit(solution)/shard_map/ppermute | solution.py:21
  56.9 1.9 %collective-permute-start.8 = (f32[96,7,128]{2,1,0:T(8,128)S(1)}, f32[96,7,128]{2,1,0:T(8,128)S(1)}, u32[]{:S(2)}, u32[]{:S(2)}) collective-permute-start(f32[96,7,128]{2,1,0:T(8,128)S(1)} %pad_maximum_fusion.1), channel_id=1, source_target_pairs={{1,0},{2,1},{3,2},{5,4},{6,5},{7,6},{9,8},{10,9},{11,10},{13,12},{... | collective-permute-start | bytes 1032200 | tf_op jit(solution)/shard_map/ppermute | solution.py:21
  58.8 2.4 %collective-permute-done.7 = f32[96,7,128]{2,1,0:T(8,128)S(1)} collective-permute-done((f32[96,7,128]{2,1,0:T(8,128)S(1)}, f32[96,7,128]{2,1,0:T(8,128)S(1)}, u32[]{:S(2)}, u32[]{:S(2)}) %collective-permute-start.7) | collective-permute-done | bytes 344096 | tf_op jit(solution)/shard_map/ppermute | solution.py:21
  61.3 4.7 %collective-permute-done.8 = f32[96,7,128]{2,1,0:T(8,128)S(1)} collective-permute-done((f32[96,7,128]{2,1,0:T(8,128)S(1)}, f32[96,7,128]{2,1,0:T(8,128)S(1)}, u32[]{:S(2)}, u32[]{:S(2)}) %collective-permute-start.8) | collective-permute-done | bytes 344096 | tf_op jit(solution)/shard_map/ppermute | solution.py:21
  66.0 1.0 %gather_fusion.1 = f32[256,7,128]{2,1,0:T(8,128)S(1)} fusion(f32[288,7,128]{2,1,0:T(8,128)S(1)} %constant_dynamic-update-slice_fusion.11, s32[1024]{0:T(1024)S(1)} %pad_clamp_fusion.1), kind=kCustom, calls=%fused_computation.1 | custom fusion | bytes 1836032 | tf_op jit(solution)/shard_map/gather | solution.py:31
  68.0 17.7 %multiply_reduce_fusion.3 = (f32[32,128]{1,0:T(8,128)S(1)}, f32[32,128]{1,0:T(8,128)S(1)}, f32[32,128]{1,0:T(8,128)S(1)}, f32[32,128]{1,0:T(8,128)S(1)}, f32[32,128]{1,0:T(8,128)S(1)}, /*index=5*/f32[32,128]{1,0:T(8,128)S(1)}) fusion(f32[32,8,128]{2,1,0:T(8,128)S(1)} %get-tuple-element.40, f32[32,8,128]{2,1,0:T(8,128)S(1)} %get-tuple-element.41, ...), kind=kLoop, calls=%fused_computation.7 | loop fusion | flops 96444416 | bytes 1458176 | tf_op jit(solution)/shard_map/vmap()/reduce_sum | solution.py:52
  (125 shorter events, 13.0 us)
Async XLA Ops:
  0.0 21.3 %copy-start = (s32[1024]{0:T(1024)S(1)}, s32[1024]{0:T(1024)}, u32[]{:S(2)}) copy-start(s32[1024]{0:T(1024)} %param.12) | copy-start | bytes 12292
  15.3 11.6 %collective-permute-start = (f32[9,7,128]{2,1,0:T(8,128)S(1)}, f32[9,7,128]{2,1,0:T(8,128)S(1)}, u32[]{:S(2)}, u32[]{:S(2)}) collective-permute-start(f32[9,7,128]{2,1,0:T(8,128)S(1)} %pad_maximum_fusion.4), channel_id=1, source_target_pairs={{0,16},{4,20},{8,24},{12,28},{16,0},{20,4},{24,8},{28,12},{1,17},{... | collective-permute-start | bytes 96776 | tf_op jit(solution)/shard_map/ppermute | solution.py:16
  27.0 2.9 %collective-permute-start.1 = (f32[10,7,128]{2,1,0:T(8,128)S(1)}, f32[10,7,128]{2,1,0:T(8,128)S(1)}, u32[]{:S(2)}, u32[]{:S(2)}) collective-permute-start(f32[10,7,128]{2,1,0:T(8,128)S(1)} %pad_maximum_fusion.3), channel_id=1, source_target_pairs={{0,8},{4,12},{8,0},{12,4},{16,24},{20,28},{24,16},{28,20},{1,9},{5... | collective-permute-start | bytes 107528 | tf_op jit(solution)/shard_map/ppermute | solution.py:16
  30.0 4.2 %collective-permute-start.2 = (f32[12,7,128]{2,1,0:T(8,128)S(1)}, f32[12,7,128]{2,1,0:T(8,128)S(1)}, u32[]{:S(2)}, u32[]{:S(2)}) collective-permute-start(f32[12,7,128]{2,1,0:T(8,128)S(1)} %pad_maximum_fusion.2), channel_id=1, source_target_pairs={{0,4},{4,0},{8,12},{12,8},{16,20},{20,16},{24,28},{28,24},{1,5},{5... | collective-permute-start | bytes 129032 | tf_op jit(solution)/shard_map/ppermute | solution.py:16
  34.3 3.2 %collective-permute-start.3 = (f32[16,7,128]{2,1,0:T(8,128)S(1)}, f32[16,7,128]{2,1,0:T(8,128)S(1)}, u32[]{:S(2)}, u32[]{:S(2)}) collective-permute-start(f32[16,7,128]{2,1,0:T(8,128)S(1)} %constant_dynamic-update-slice_fusion), channel_id=1, source_target_pairs={{0,2},{1,3},{2,0},{3,1},{4,6},{5,7},{6,4},{7,5},{8,10},{9,11},{10,... | collective-permute-start | bytes 172040 | tf_op jit(solution)/shard_map/ppermute | solution.py:16
  37.5 4.5 %collective-permute-start.4 = (f32[24,7,128]{2,1,0:T(8,128)S(1)}, f32[24,7,128]{2,1,0:T(8,128)S(1)}, u32[]{:S(2)}, u32[]{:S(2)}) collective-permute-start(f32[24,7,128]{2,1,0:T(8,128)S(1)} %get-tuple-element.55), channel_id=1, source_target_pairs={{0,1},{1,0},{2,3},{3,2},{4,5},{5,4},{6,7},{7,6},{8,9},{9,8},{10,11... | collective-permute-start | bytes 258056 | tf_op jit(solution)/shard_map/ppermute | solution.py:16
  42.1 9.1 %collective-permute-start.6 = (f32[32,7,128]{2,1,0:T(8,128)S(1)}, f32[32,7,128]{2,1,0:T(8,128)S(1)}, u32[]{:S(2)}, u32[]{:S(2)}) collective-permute-start(f32[32,7,128]{2,1,0:T(8,128)S(1)} %slice.248), channel_id=1, source_target_pairs={{4,0},{8,4},{12,8},{16,12},{20,16},{24,20},{28,24},{5,1},{9,5},{13... | collective-permute-start | bytes 344072 | tf_op jit(solution)/shard_map/ppermute | solution.py:21
  44.8 7.2 %collective-permute-start.5 = (f32[32,7,128]{2,1,0:T(8,128)S(1)}, f32[32,7,128]{2,1,0:T(8,128)S(1)}, u32[]{:S(2)}, u32[]{:S(2)}) collective-permute-start(f32[32,7,128]{2,1,0:T(8,128)S(1)} %slice.248), channel_id=1, source_target_pairs={{0,4},{4,8},{8,12},{12,16},{16,20},{20,24},{24,28},{1,5},{5,9},{9,... | collective-permute-start | bytes 344072 | tf_op jit(solution)/shard_map/ppermute | solution.py:21
  52.0 9.2 %collective-permute-start.7 = (f32[96,7,128]{2,1,0:T(8,128)S(1)}, f32[96,7,128]{2,1,0:T(8,128)S(1)}, u32[]{:S(2)}, u32[]{:S(2)}) collective-permute-start(f32[96,7,128]{2,1,0:T(8,128)S(1)} %pad_maximum_fusion.1), channel_id=1, source_target_pairs={{0,1},{1,2},{2,3},{4,5},{5,6},{6,7},{8,9},{9,10},{10,11},{12,13},{... | collective-permute-start | bytes 1032200 | tf_op jit(solution)/shard_map/ppermute | solution.py:21
  56.9 9.1 %collective-permute-start.8 = (f32[96,7,128]{2,1,0:T(8,128)S(1)}, f32[96,7,128]{2,1,0:T(8,128)S(1)}, u32[]{:S(2)}, u32[]{:S(2)}) collective-permute-start(f32[96,7,128]{2,1,0:T(8,128)S(1)} %pad_maximum_fusion.1), channel_id=1, source_target_pairs={{1,0},{2,1},{3,2},{5,4},{6,5},{7,6},{9,8},{10,9},{11,10},{13,12},{... | collective-permute-start | bytes 1032200 | tf_op jit(solution)/shard_map/ppermute | solution.py:21

commit v8 on v6

--- a/solution.py
+++ b/solution.py
@@ -81,7 +81,7 @@
     return lax.optimization_barrier(extra)
 
 
-def trace_back(loc, moves, levels, bits_x, nbd):
+def level_tables(moves, levels, bits_x, nbd):
     size_x, size_y = moves.shape[1], moves.shape[2]
     devices = size_x * size_y
     level_bit = np.array(
@@ -100,6 +100,12 @@
         before = before - delta[level]
     kept = jnp.stack(kept, axis=0)
     kept_mate = jnp.sum(jnp.where(swap, kept[:, None, :], 0), axis=2)
+    return kept, kept_mate, level_bit
+
+
+def trace_back(loc, kept, kept_mate, level_bit, nbd):
+    levels, devices = kept.shape
+    every = jnp.arange(devices, dtype=jnp.int32)
     device = loc.reshape(-1) // nbd
     slot = loc.reshape(-1) % nbd
     for level in reversed(range(levels)):
@@ -135,8 +141,6 @@
     width = slot_table.shape[1]
     gathered = table_blocks(slot_table, lanes)
     pieces = gathered.shape[0]
-    far_where = owner[far_list[0, 0]]
-    far_device, far_slot = trace_back(far_where, moves, levels, bits_x, nbd)
     held = jnp.pad(held, ((0, MOVE), (0, 0), (0, 0)))
     plans = []
     level_bits = []
@@ -166,6 +170,16 @@
         count = count - own_moves
         held = lax.dynamic_update_slice_in_dim(held, arriving, count, 0)
         count = count + mate_moves
+        if level == 0:
+            moves_late, _ = lax.optimization_barrier((moves, held))
+            kept, kept_mate, level_bit = level_tables(moves_late, levels, bits_x, nbd)
+        if level == min(1, levels - 1):
+            near_late, _ = lax.optimization_barrier((near_list[0, 0], held))
+            near_where = owner[near_late]
+        if level == min(2, levels - 1):
+            far_late, _ = lax.optimization_barrier((far_list[0, 0], held))
+            far_where = owner[far_late]
+            far_device, far_slot = trace_back(far_where, kept, kept_mate, level_bit, nbd)
     blocks = held[:nbd]
     relative = jnp.bitwise_xor(far_device, me)
     entry = jnp.zeros_like(relative)
@@ -173,7 +187,6 @@
         entry = entry + ((relative // level_bits[level]) % 2) * (1 << level)
     all_table = gathered.reshape(-1, pieces, width, lanes).transpose(0, 1, 3, 2).reshape(-1, width)
     moments = all_table[entry * (pieces * lanes) + far_slot]
-    near_where = owner[near_list[0, 0]]
     source_device = near_where // nbd
     source_slot = near_where % nbd
     delta_x = source_device // size_y - column_index

time: 84.4 us -> 85 us (level)
    unnamed x7 -> x6, local copies, waits for them, and re-layouts: 1.67 us -> 0.01 us
  transfers between devices with their start and end apart: 9 -> 9, of which waited for: 6 -> 6; matrix products, arithmetic and copies ran while one was open for 16% -> 10% of each run, Pallas kernels for 0% -> 0%
where the time goes in v8:
time: 85 us; the launch traced here: 83.7 us
  other arithmetic  26.5 us (31%)
  starting transfers between devices  21.3 us (25%)
  local copies, waits for them, and re-layouts  15.4 us (18%)
  between operations  12.4 us (15%)
  waiting for transfers between devices  8.08 us (10%)
    reduce_sum x1, other arithmetic, evaluate(): arm_x = jnp.sum(extra[:, 1][:, None, :] * weight, axis=(0, 2))  17.9 us
    ppermute x5, starting transfers between devices, from_partner(): lax.ppermute(shard, axis, [(i, i ^ 1 << apart) for i in range(lax.axis_si...  9.59 us
    ppermute x2, starting transfers between devices, padded(): after = lax.ppermute(first, axis, down)  6.42 us
    ppermute x2, starting transfers between devices, padded(): before = lax.ppermute(last, axis, up)  5.32 us
    ppermute x5, waiting for transfers between devices, from_partner(): lax.ppermute(shard, axis, [(i, i ^ 1 << apart) for i in range(lax.axis_si...  3.32 us
    ppermute x2, waiting for transfers between devices, padded(): after = lax.ppermute(first, axis, down)  2.66 us
    ppermute x2, waiting for transfers between devices, padded(): before = lax.ppermute(last, axis, up)  2.1 us
  transfers between devices with their start and end apart: 9, of which 6 were waited for; matrix products, arithmetic and copies ran while one was open for 10% of the time, Pallas kernels for 0%

profile of v8, /device:TPU:9, one launch (start us, length us, event | category | flops | bytes accessed | tf_op | source)
XLA Modules:
  0.0 83.7 jit_solution(4028431181088369103)
XLA Ops:
  0.0 0.9 %multiply_reduce_fusion.7 = f32[72]{0:T(128)S(1)} fusion(f32[1,1,72,128]{3,2,1,0:T(8,128)} %param.10), kind=kLoop, calls=%fused_computation.57 | loop fusion | flops 18360 | bytes 37152 | tf_op jit(solution)/shard_map/reduce_sum | solution.py:36
  0.9 1.0 %reduce_sum.287 = f32[72,3]{0,1:T(4,128)S(1)} reduce(f32[1,1,72,3,128]{4,2,3,1,0:T(8,128)} %param.8, f32[]{:T(128)} %constant.168.clone.1), dimensions={0,1,4}, to_apply=%region_0.0 | reduce | flops 27432 | bytes 111460 | tf_op jit(solution)/shard_map/reduce_sum | solution.py:33
  2.0 1.1 %multiply_reduce_fusion.6 = f32[72]{0:T(128)S(1)} fusion(f32[72,3]{0,1:T(4,128)S(1)} %broadcast_multiply_fusion.1, f32[1,1,72,3,128]{4,2,3,1,0:T(8,128)} %param.8), kind=kLoop, calls=%fused_computation.45 | loop fusion | flops 82872 | bytes 111744 | tf_op jit(solution)/shard_map/reduce_sum | solution.py:36
  3.1 1.0 %reduce_sum.288 = f32[72,3]{0,1:T(4,128)S(1)} reduce(f32[1,1,72,3,128]{4,2,3,1,0:T(8,128)} %param.9, f32[]{:T(128)} %constant.168.clone.1), dimensions={0,1,4}, to_apply=%region_1.0 | reduce | flops 27432 | bytes 111460 | tf_op jit(solution)/shard_map/reduce_sum | solution.py:34
  4.2 1.5 %constant_dynamic-slice_fusion.13 = (s32[1,1,1]{1,2,0:T(1,128)}, s32[1,1,1]{1,2,0:T(1,128)}, s32[1,1,1]{1,2,0:T(1,128)}, s32[1,1,1]{1,2,0:T(1,128)}, s32[1,1,1]{...) fusion(s32[5,8,4]{1,2,0:T(4,128)} %param.11, ...), kind=kLoop, calls=%fused_computation.236 | loop fusion | bytes 108 | tf_op jit(solution)/shard_map/dynamic_slice | solution.py:154
  12.5 1.0 %select_maximum_fusion = f32[80,7,128]{2,0,1:T(8,128)S(1)} fusion(f32[72,1,128]{2,0,1:T(8,128)} %bitcast.188, f32[72,3,128]{2,0,1:T(8,128)} %bitcast.187, f32[72,3,128]{2,0,1:T(8,128)} %bitcast.173), kind=kLoop, calls=%fused_computation.14 | loop fusion | flops 430080 | bytes 544768 | tf_op jit(solution)/shard_map/concatenate | solution.py:139
  13.5 2.4 %collective-permute-start = (f32[9,7,128]{2,0,1:T(8,128)S(1)}, f32[9,7,128]{2,0,1:T(8,128)S(1)}, u32[]{:S(2)}, u32[]{:S(2)}) collective-permute-start(f32[9,7,128]{2,0,1:T(8,128)S(1)} %pad_maximum_fusion.3), channel_id=1, source_target_pairs={{0,16},{4,20},{8,24},{12,28},{16,0},{20,4},{24,8},{28,12},{1,17},{... | collective-permute-start | bytes 96776 | tf_op jit(solution)/shard_map/ppermute | solution.py:16
  25.5 1.5 %collective-permute-done.1 = f32[10,7,128]{2,0,1:T(8,128)S(1)} collective-permute-done((f32[10,7,128]{2,0,1:T(8,128)S(1)}, f32[10,7,128]{2,0,1:T(8,128)S(1)}, u32[]{:S(2)}, u32[]{:S(2)}) %collective-permute-start.1) | collective-permute-done | bytes 35872 | tf_op jit(solution)/shard_map/ppermute | solution.py:16
  27.1 1.3 %collective-permute-start.2 = (f32[12,7,128]{2,0,1:T(8,128)S(1)}, f32[12,7,128]{2,0,1:T(8,128)S(1)}, u32[]{:S(2)}, u32[]{:S(2)}) collective-permute-start(f32[12,7,128]{2,0,1:T(8,128)S(1)} %pad_maximum_fusion.5), channel_id=1, source_target_pairs={{0,4},{4,0},{8,12},{12,8},{16,20},{20,16},{24,28},{28,24},{1,5},{5... | collective-permute-start | bytes 129032 | tf_op jit(solution)/shard_map/ppermute | solution.py:16
  28.6 1.4 %gather_fusion = s32[256]{0:T(256)S(1)} fusion(s32[1024]{0:T(1024)S(1)} %copy-done, s32[1024]{0:T(1024)S(1)} %pad_clamp_fusion.3), kind=kCustom, calls=%fused_computation | custom fusion | bytes 3072 | tf_op jit(solution)/shard_map/gather | solution.py:178
  30.6 1.4 %gather_fusion.2 = s32[256]{0:T(256)S(1)} fusion(s32[1024]{0:T(1024)S(1)} %copy-done, s32[1024]{0:T(1024)S(1)} %pad_clamp_fusion.1), kind=kCustom, calls=%fused_computation.2 | custom fusion | bytes 3072 | tf_op jit(solution)/shard_map/gather | solution.py:181
  33.0 1.3 %collective-permute-start.3 = (f32[16,7,128]{2,0,1:T(8,128)S(1)}, f32[16,7,128]{2,0,1:T(8,128)S(1)}, u32[]{:S(2)}, u32[]{:S(2)}) collective-permute-start(f32[16,7,128]{2,0,1:T(8,128)S(1)} %concatenate.47), channel_id=1, source_target_pairs={{0,2},{1,3},{2,0},{3,1},{4,6},{5,7},{6,4},{7,5},{8,10},{9,11},{10,... | collective-permute-start | bytes 172040 | tf_op jit(solution)/shard_map/ppermute | solution.py:16
  35.1 0.9 %collective-permute-done.3 = f32[16,7,128]{2,0,1:T(8,128)S(1)} collective-permute-done((f32[16,7,128]{2,0,1:T(8,128)S(1)}, f32[16,7,128]{2,0,1:T(8,128)S(1)}, u32[]{:S(2)}, u32[]{:S(2)}) %collective-permute-start.3) | collective-permute-done | bytes 57376 | tf_op jit(solution)/shard_map/ppermute | solution.py:16
  36.3 4.4 %collective-permute-start.4 = (f32[24,7,128]{2,0,1:T(8,128)S(1)}, f32[24,7,128]{2,0,1:T(8,128)S(1)}, u32[]{:S(2)}, u32[]{:S(2)}) collective-permute-start(f32[24,7,128]{2,0,1:T(8,128)S(1)} %concatenate.48), channel_id=1, source_target_pairs={{0,1},{1,0},{2,3},{3,2},{4,5},{5,4},{6,7},{7,6},{8,9},{9,8},{10,11... | collective-permute-start | bytes 258056 | tf_op jit(solution)/shard_map/ppermute | solution.py:16
  40.7 0.9 %collective-permute-done.4 = f32[24,7,128]{2,0,1:T(8,128)S(1)} collective-permute-done((f32[24,7,128]{2,0,1:T(8,128)S(1)}, f32[24,7,128]{2,0,1:T(8,128)S(1)}, u32[]{:S(2)}, u32[]{:S(2)}) %collective-permute-start.4) | collective-permute-done | bytes 86048 | tf_op jit(solution)/shard_map/ppermute | solution.py:16
  41.8 3.0 %collective-permute-start.6 = (f32[1,1,32,7,128]{4,2,3,1,0:T(8,128)S(1)}, f32[1,1,32,7,128]{4,2,3,1,0:T(8,128)S(1)}, u32[]{:S(2)}, u32[]{:S(2)}) collective-permute-start(f32[1,1,32,7,128]{4,2,3,1,0:T(8,128)S(1)} %slice_bitcast_fusion.4), channel_id=1, source_target_pairs={{4,0},{8,4},{12,8},{16,12},{20,16},{24,20},{28,24},{5,1},{9,5},{13... | collective-permute-start | bytes 344072 | tf_op jit(solution)/shard_map/ppermute | solution.py:27
  44.8 2.3 %collective-permute-start.5 = (f32[1,1,32,7,128]{4,2,3,1,0:T(8,128)S(1)}, f32[1,1,32,7,128]{4,2,3,1,0:T(8,128)S(1)}, u32[]{:S(2)}, u32[]{:S(2)}) collective-permute-start(f32[1,1,32,7,128]{4,2,3,1,0:T(8,128)S(1)} %slice_bitcast_fusion.4), channel_id=1, source_target_pairs={{0,4},{4,8},{8,12},{12,16},{16,20},{20,24},{24,28},{1,5},{5,9},{9,... | collective-permute-start | bytes 344072 | tf_op jit(solution)/shard_map/ppermute | solution.py:26
  50.7 0.9 %collective-permute-done.5 = f32[1,1,32,7,128]{4,2,3,1,0:T(8,128)S(1)} collective-permute-done((f32[1,1,32,7,128]{4,2,3,1,0:T(8,128)S(1)}, f32[1,1,32,7,128]{4,2,3,1,0:T(8,128)S(1)}, u32[]{:S(2)}, u32[]{:S(2)}) %collective-permute-start.5) | collective-permute-done | bytes 114720 | tf_op jit(solution)/shard_map/ppermute | solution.py:26
  51.7 3.4 %collective-permute-start.8 = (f32[3,1,32,7,128]{4,2,3,1,0:T(8,128)S(1)}, f32[3,1,32,7,128]{4,2,3,1,0:T(8,128)S(1)}, u32[]{:S(2)}, u32[]{:S(2)}) collective-permute-start(f32[3,1,32,7,128]{4,2,3,1,0:T(8,128)S(1)} %pad_maximum_fusion.2), channel_id=1, source_target_pairs={{1,0},{2,1},{3,2},{5,4},{6,5},{7,6},{9,8},{10,9},{11,10},{13,12},{... | collective-permute-start | bytes 1032200 | tf_op jit(solution)/shard_map/ppermute | solution.py:27
  55.1 3.0 %collective-permute-start.7 = (f32[3,1,32,7,128]{4,2,3,1,0:T(8,128)S(1)}, f32[3,1,32,7,128]{4,2,3,1,0:T(8,128)S(1)}, u32[]{:S(2)}, u32[]{:S(2)}) collective-permute-start(f32[3,1,32,7,128]{4,2,3,1,0:T(8,128)S(1)} %pad_maximum_fusion.2), channel_id=1, source_target_pairs={{0,1},{1,2},{2,3},{4,5},{5,6},{6,7},{8,9},{9,10},{10,11},{12,13},{... | collective-permute-start | bytes 1032200 | tf_op jit(solution)/shard_map/ppermute | solution.py:26
  58.5 2.6 %collective-permute-done.8 = f32[3,1,32,7,128]{4,2,3,1,0:T(8,128)S(1)} collective-permute-done((f32[3,1,32,7,128]{4,2,3,1,0:T(8,128)S(1)}, f32[3,1,32,7,128]{4,2,3,1,0:T(8,128)S(1)}, u32[]{:S(2)}, u32[]{:S(2)}) %collective-permute-start.8) | collective-permute-done | bytes 344096 | tf_op jit(solution)/shard_map/ppermute | solution.py:27
  61.1 1.2 %collective-permute-done.7 = f32[3,1,32,7,128]{4,2,3,1,0:T(8,128)S(1)} collective-permute-done((f32[3,1,32,7,128]{4,2,3,1,0:T(8,128)S(1)}, f32[3,1,32,7,128]{4,2,3,1,0:T(8,128)S(1)}, u32[]{:S(2)}, u32[]{:S(2)}) %collective-permute-start.7) | collective-permute-done | bytes 344096 | tf_op jit(solution)/shard_map/ppermute | solution.py:26
  63.1 1.0 %gather_fusion.1 = f32[256,7,128]{2,1,0:T(8,128)S(1)} fusion(f32[288,7,128]{2,1,0:T(8,128)S(1)} %copy.125, s32[1024]{0:T(1024)S(1)} %pad_clamp_fusion.2), kind=kCustom, calls=%fused_computation.1 | custom fusion | bytes 1836032 | tf_op jit(solution)/shard_map/gather | solution.py:198
  65.1 17.9 %multiply_reduce_fusion.3 = (f32[32,128]{1,0:T(8,128)S(1)}, f32[32,128]{1,0:T(8,128)S(1)}, f32[32,128]{1,0:T(8,128)S(1)}, f32[32,128]{1,0:T(8,128)S(1)}, f32[32,128]{1,0:T(8,128)S(1)}, /*index=5*/f32[32,128]{1,0:T(8,128)S(1)}) fusion(f32[32,8,128]{2,1,0:T(8,128)S(1)} %get-tuple-element.43, f32[32,8,128]{2,1,0:T(8,128)S(1)} %get-tuple-element.44, ...), kind=kLoop, calls=%fused_computation.8 | loop fusion | flops 96444416 | bytes 1458176 | tf_op jit(solution)/shard_map/vmap()/reduce_sum | solution.py:50
  (131 shorter events, 13.9 us)
Async XLA Ops:
  0.0 28.6 %copy-start = (s32[1024]{0:T(1024)S(1)}, s32[1024]{0:T(1024)}, u32[]{:S(2)}) copy-start(s32[1024]{0:T(1024)} %param.12) | copy-start | bytes 12292
  0.0 28.4 %copy-start.1 = (s32[1,1,32,8]{2,3,1,0:T(8,128)S(1)}, s32[1,1,32,8]{2,3,1,0:T(8,128)}, u32[]{:S(2)}) copy-start(s32[1,1,32,8]{2,3,1,0:T(8,128)} %param.13) | copy-start | bytes 3076
  13.5 8.1 %collective-permute-start = (f32[9,7,128]{2,0,1:T(8,128)S(1)}, f32[9,7,128]{2,0,1:T(8,128)S(1)}, u32[]{:S(2)}, u32[]{:S(2)}) collective-permute-start(f32[9,7,128]{2,0,1:T(8,128)S(1)} %pad_maximum_fusion.3), channel_id=1, source_target_pairs={{0,16},{4,20},{8,24},{12,28},{16,0},{20,4},{24,8},{28,12},{1,17},{... | collective-permute-start | bytes 96776 | tf_op jit(solution)/shard_map/ppermute | solution.py:16
  23.9 3.1 %collective-permute-start.1 = (f32[10,7,128]{2,0,1:T(8,128)S(1)}, f32[10,7,128]{2,0,1:T(8,128)S(1)}, u32[]{:S(2)}, u32[]{:S(2)}) collective-permute-start(f32[10,7,128]{2,0,1:T(8,128)S(1)} %pad_maximum_fusion.4), channel_id=1, source_target_pairs={{0,8},{4,12},{8,0},{12,4},{16,24},{20,28},{24,16},{28,20},{1,9},{5... | collective-permute-start | bytes 107528 | tf_op jit(solution)/shard_map/ppermute | solution.py:16
  27.1 3.1 %collective-permute-start.2 = (f32[12,7,128]{2,0,1:T(8,128)S(1)}, f32[12,7,128]{2,0,1:T(8,128)S(1)}, u32[]{:S(2)}, u32[]{:S(2)}) collective-permute-start(f32[12,7,128]{2,0,1:T(8,128)S(1)} %pad_maximum_fusion.5), channel_id=1, source_target_pairs={{0,4},{4,0},{8,12},{12,8},{16,20},{20,16},{24,28},{28,24},{1,5},{5... | collective-permute-start | bytes 129032 | tf_op jit(solution)/shard_map/ppermute | solution.py:16
  28.6 1.8 %copy-start.2 = (s32[1,1,32,8]{2,3,1,0:T(8,128)S(1)}, s32[1,1,32,8]{2,3,1,0:T(8,128)}, u32[]{:S(2)}) copy-start(s32[1,1,32,8]{2,3,1,0:T(8,128)} %param.14) | copy-start | bytes 3076
  33.0 3.1 %collective-permute-start.3 = (f32[16,7,128]{2,0,1:T(8,128)S(1)}, f32[16,7,128]{2,0,1:T(8,128)S(1)}, u32[]{:S(2)}, u32[]{:S(2)}) collective-permute-start(f32[16,7,128]{2,0,1:T(8,128)S(1)} %concatenate.47), channel_id=1, source_target_pairs={{0,2},{1,3},{2,0},{3,1},{4,6},{5,7},{6,4},{7,5},{8,10},{9,11},{10,... | collective-permute-start | bytes 172040 | tf_op jit(solution)/shard_map/ppermute | solution.py:16
  36.3 5.3 %collective-permute-start.4 = (f32[24,7,128]{2,0,1:T(8,128)S(1)}, f32[24,7,128]{2,0,1:T(8,128)S(1)}, u32[]{:S(2)}, u32[]{:S(2)}) collective-permute-start(f32[24,7,128]{2,0,1:T(8,128)S(1)} %concatenate.48), channel_id=1, source_target_pairs={{0,1},{1,0},{2,3},{3,2},{4,5},{5,4},{6,7},{7,6},{8,9},{9,8},{10,11... | collective-permute-start | bytes 258056 | tf_op jit(solution)/shard_map/ppermute | solution.py:16
  41.8 8.9 %collective-permute-start.6 = (f32[1,1,32,7,128]{4,2,3,1,0:T(8,128)S(1)}, f32[1,1,32,7,128]{4,2,3,1,0:T(8,128)S(1)}, u32[]{:S(2)}, u32[]{:S(2)}) collective-permute-start(f32[1,1,32,7,128]{4,2,3,1,0:T(8,128)S(1)} %slice_bitcast_fusion.4), channel_id=1, source_target_pairs={{4,0},{8,4},{12,8},{16,12},{20,16},{24,20},{28,24},{5,1},{9,5},{13... | collective-permute-start | bytes 344072 | tf_op jit(solution)/shard_map/ppermute | solution.py:27
  44.8 6.9 %collective-permute-start.5 = (f32[1,1,32,7,128]{4,2,3,1,0:T(8,128)S(1)}, f32[1,1,32,7,128]{4,2,3,1,0:T(8,128)S(1)}, u32[]{:S(2)}, u32[]{:S(2)}) collective-permute-start(f32[1,1,32,7,128]{4,2,3,1,0:T(8,128)S(1)} %slice_bitcast_fusion.4), channel_id=1, source_target_pairs={{0,4},{4,8},{8,12},{12,16},{16,20},{20,24},{24,28},{1,5},{5,9},{9,... | collective-permute-start | bytes 344072 | tf_op jit(solution)/shard_map/ppermute | solution.py:26
  51.7 9.5 %collective-permute-start.8 = (f32[3,1,32,7,128]{4,2,3,1,0:T(8,128)S(1)}, f32[3,1,32,7,128]{4,2,3,1,0:T(8,128)S(1)}, u32[]{:S(2)}, u32[]{:S(2)}) collective-permute-start(f32[3,1,32,7,128]{4,2,3,1,0:T(8,128)S(1)} %pad_maximum_fusion.2), channel_id=1, source_target_pairs={{1,0},{2,1},{3,2},{5,4},{6,5},{7,6},{9,8},{10,9},{11,10},{13,12},{... | collective-permute-start | bytes 1032200 | tf_op jit(solution)/shard_map/ppermute | solution.py:27
  55.1 7.2 %collective-permute-start.7 = (f32[3,1,32,7,128]{4,2,3,1,0:T(8,128)S(1)}, f32[3,1,32,7,128]{4,2,3,1,0:T(8,128)S(1)}, u32[]{:S(2)}, u32[]{:S(2)}) collective-permute-start(f32[3,1,32,7,128]{4,2,3,1,0:T(8,128)S(1)} %pad_maximum_fusion.2), channel_id=1, source_target_pairs={{0,1},{1,2},{2,3},{4,5},{5,6},{6,7},{8,9},{9,10},{10,11},{12,13},{... | collective-permute-start | bytes 1032200 | tf_op jit(solution)/shard_map/ppermute | solution.py:26

commit v9 on v8

--- a/solution.py
+++ b/solution.py
@@ -157,9 +157,21 @@
     count = jnp.int32(nbd)
     for plan_item in plans:
         count = count + plan_item[1] - plan_item[2]
+    devices = size_x * size_y
+    flat_moves = moves.reshape(levels, devices)
+    every = jnp.arange(devices, dtype=jnp.int32)
+    weights = [(every == me).astype(jnp.int32) - (every == jnp.bitwise_xor(me, level_bit)).astype(jnp.int32) for level_bit in level_bits]
+    start_all = nbd + sum(jnp.sum(weights[level] * flat_moves[level]) for level in range(levels))
+    first_out = start_all - jnp.sum((every == me).astype(jnp.int32) * flat_moves[0])
+    slot_ids = jnp.arange(held.shape[0], dtype=jnp.int32)
+    take = slot_ids[None, :] == (first_out + jnp.arange(MOVE, dtype=jnp.int32))[:, None]
+    first_leaving = jnp.sum(jnp.where(take[:, :, None, None], held[None], 0.0), axis=1)
     for level in range(levels):
         bit_at, own_moves, mate_moves = plans[level]
-        leaving = lax.dynamic_slice_in_dim(held, count - own_moves, MOVE, 0)
+        if level == 0:
+            leaving = first_leaving
+        else:
+            leaving = lax.dynamic_slice_in_dim(held, count - own_moves, MOVE, 0)
         payload = jnp.concatenate([leaving, gathered], axis=0)
         if level < bits_x:
             got = from_partner(payload, "gx", bit_at)

time: 85 us -> 90.6 us (1.066)
  between operations: 12.4 us -> 16.1 us
  other arithmetic: 26.5 us -> 28.4 us
    reduce_sum x0 -> x2, other arithmetic: none -> 1.82 us  [the longest x1 1.53 us: local(): jnp.sum((every == me).astype(jnp.int32) * flat_moves[0])]
  transfers between devices with their start and end apart: 9 -> 9, of which waited for: 6 -> 6; matrix products, arithmetic and copies ran while one was open for 10% -> 11% of each run, Pallas kernels for 0% -> 0%
where the time goes in v9:
time: 90.6 us; the launch traced here: 89.2 us
  other arithmetic  28.4 us (31%)
  starting transfers between devices  21.3 us (24%)
  between operations  16.1 us (18%)
  local copies, waits for them, and re-layouts  15.4 us (17%)
  waiting for transfers between devices  8.08 us (9%)
    reduce_sum x1, other arithmetic, evaluate(): arm_x = jnp.sum(extra[:, 1][:, None, :] * weight, axis=(0, 2))  17.8 us
    ppermute x5, starting transfers between devices, from_partner(): lax.ppermute(shard, axis, [(i, i ^ 1 << apart) for i in range(lax.axis_si...  9.59 us
    ppermute x2, starting transfers between devices, padded(): after = lax.ppermute(first, axis, down)  6.42 us
    ppermute x2, starting transfers between devices, padded(): before = lax.ppermute(last, axis, up)  5.32 us
    ppermute x5, waiting for transfers between devices, from_partner(): lax.ppermute(shard, axis, [(i, i ^ 1 << apart) for i in range(lax.axis_si...  3.32 us
    ppermute x2, waiting for transfers between devices, padded(): after = lax.ppermute(first, axis, down)  2.66 us
    ppermute x2, waiting for transfers between devices, padded(): before = lax.ppermute(last, axis, up)  2.1 us
  transfers between devices with their start and end apart: 9, of which 6 were waited for; matrix products, arithmetic and copies ran while one was open for 11% of the time, Pallas kernels for 0%

profile of v9, /device:TPU:9, one launch (start us, length us, event | category | flops | bytes accessed | tf_op | source)
XLA Modules:
  0.0 89.2 jit_solution(3478866374492870070)
XLA Ops:
  0.9 1.0 %reduce_sum.357 = f32[72,3]{0,1:T(4,128)S(1)} reduce(f32[1,1,72,3,128]{4,2,3,1,0:T(8,128)} %param.8, f32[]{:T(128)} %constant.180.clone.1), dimensions={0,1,4}, to_apply=%region_7.8 | reduce | flops 27432 | bytes 111460 | tf_op jit(solution)/shard_map/reduce_sum | solution.py:33
  2.0 1.1 %multiply_reduce_fusion.6 = f32[72]{0:T(128)S(1)} fusion(f32[72,3]{0,1:T(4,128)S(1)} %broadcast_multiply_fusion.1, f32[1,1,72,3,128]{4,2,3,1,0:T(8,128)} %param.8), kind=kLoop, calls=%fused_computation.46 | loop fusion | flops 82872 | bytes 111744 | tf_op jit(solution)/shard_map/reduce_sum | solution.py:36
  3.1 1.0 %reduce_sum.358 = f32[72,3]{0,1:T(4,128)S(1)} reduce(f32[1,1,72,3,128]{4,2,3,1,0:T(8,128)} %param.9, f32[]{:T(128)} %constant.180.clone.1), dimensions={0,1,4}, to_apply=%region_8.9 | reduce | flops 27432 | bytes 111460 | tf_op jit(solution)/shard_map/reduce_sum | solution.py:34
  4.2 1.5 %select_reduce_fusion.13 = (s32[]{:T(128)}, s32[]{:T(128)}, s32[]{:T(128)}, s32[]{:T(128)}, s32[]{:T(128)}, /*index=5*/s32[]{:T(128)}) fusion(s32[5,8,4]{1,2,0:T(4,128)} %param.11, s32[]{:T(128)S(6)} %add.644, s32[]{:T(128)S(6)} %xor.179, s32[]{:T(128)S(6)} %xor.178, s32[]{:T(128)S(6)} %xor.177, s32[]{:T(128)S(6)} %xor.176, s32[]{:T(128)S(6)} %xor.175), kind=kLoop, calls=%fused_computation.213 | loop fusion | flops 986 | bytes 688 | tf_op jit(solution)/shard_map/reduce_sum | solution.py:165
  9.5 1.0 %select_maximum_fusion = f32[80,7,128]{2,0,1:T(8,128)S(1)} fusion(f32[72,1,128]{2,0,1:T(8,128)} %bitcast.190, f32[72,3,128]{2,0,1:T(8,128)} %bitcast.189, f32[72,3,128]{2,0,1:T(8,128)} %bitcast.175), kind=kLoop, calls=%fused_computation.15 | loop fusion | flops 430080 | bytes 544768 | tf_op jit(solution)/shard_map/concatenate | solution.py:139
  10.9 2.4 %collective-permute-start = (f32[9,7,128]{2,1,0:T(8,128)S(1)}, f32[9,7,128]{2,1,0:T(8,128)S(1)}, u32[]{:S(2)}, u32[]{:S(2)}) collective-permute-start(f32[9,7,128]{2,1,0:T(8,128)S(1)} %pad_maximum_fusion.5), channel_id=1, source_target_pairs={{0,16},{4,20},{8,24},{12,28},{16,0},{20,4},{24,8},{28,12},{1,17},{... | collective-permute-start | bytes 96776 | tf_op jit(solution)/shard_map/ppermute | solution.py:16
  14.0 1.5 %constant_dynamic-slice_fusion.12 = (s32[1,1,1]{1,2,0:T(1,128)}, s32[1,1,1]{1,2,0:T(1,128)}, s32[1,1,1]{1,2,0:T(1,128)}, s32[1,1,1]{1,2,0:T(1,128)}, s32[1,1,1]{...) fusion(s32[5,8,4]{1,2,0:T(4,128)} %param.11, ...), kind=kLoop, calls=%fused_computation.262 | loop fusion | bytes 108 | tf_op jit(solution)/shard_map/dynamic_slice | solution.py:154
  31.1 1.5 %collective-permute-done.1 = f32[10,7,128]{2,0,1:T(8,128)S(1)} collective-permute-done((f32[10,7,128]{2,0,1:T(8,128)S(1)}, f32[10,7,128]{2,0,1:T(8,128)S(1)}, u32[]{:S(2)}, u32[]{:S(2)}) %collective-permute-start.1) | collective-permute-done | bytes 35872 | tf_op jit(solution)/shard_map/ppermute | solution.py:16
  32.8 1.3 %collective-permute-start.2 = (f32[12,7,128]{2,0,1:T(8,128)S(1)}, f32[12,7,128]{2,0,1:T(8,128)S(1)}, u32[]{:S(2)}, u32[]{:S(2)}) collective-permute-start(f32[12,7,128]{2,0,1:T(8,128)S(1)} %pad_maximum_fusion.4), channel_id=1, source_target_pairs={{0,4},{4,0},{8,12},{12,8},{16,20},{20,16},{24,28},{28,24},{1,5},{5... | collective-permute-start | bytes 129032 | tf_op jit(solution)/shard_map/ppermute | solution.py:16
  34.3 1.4 %gather_fusion = s32[256]{0:T(256)S(1)} fusion(s32[1024]{0:T(1024)S(1)} %copy-done, s32[1024]{0:T(1024)S(1)} %pad_clamp_fusion.3), kind=kCustom, calls=%fused_computation | custom fusion | bytes 3072 | tf_op jit(solution)/shard_map/gather | solution.py:190
  36.3 1.4 %gather_fusion.2 = s32[256]{0:T(256)S(1)} fusion(s32[1024]{0:T(1024)S(1)} %copy-done, s32[1024]{0:T(1024)S(1)} %pad_clamp_fusion.1), kind=kCustom, calls=%fused_computation.2 | custom fusion | bytes 3072 | tf_op jit(solution)/shard_map/gather | solution.py:193
  38.6 1.3 %collective-permute-start.3 = (f32[16,7,128]{2,0,1:T(8,128)S(1)}, f32[16,7,128]{2,0,1:T(8,128)S(1)}, u32[]{:S(2)}, u32[]{:S(2)}) collective-permute-start(f32[16,7,128]{2,0,1:T(8,128)S(1)} %concatenate.47), channel_id=1, source_target_pairs={{0,2},{1,3},{2,0},{3,1},{4,6},{5,7},{6,4},{7,5},{8,10},{9,11},{10,... | collective-permute-start | bytes 172040 | tf_op jit(solution)/shard_map/ppermute | solution.py:16
  40.8 0.9 %collective-permute-done.3 = f32[16,7,128]{2,0,1:T(8,128)S(1)} collective-permute-done((f32[16,7,128]{2,0,1:T(8,128)S(1)}, f32[16,7,128]{2,0,1:T(8,128)S(1)}, u32[]{:S(2)}, u32[]{:S(2)}) %collective-permute-start.3) | collective-permute-done | bytes 57376 | tf_op jit(solution)/shard_map/ppermute | solution.py:16
  41.9 4.4 %collective-permute-start.4 = (f32[24,7,128]{2,0,1:T(8,128)S(1)}, f32[24,7,128]{2,0,1:T(8,128)S(1)}, u32[]{:S(2)}, u32[]{:S(2)}) collective-permute-start(f32[24,7,128]{2,0,1:T(8,128)S(1)} %concatenate.48), channel_id=1, source_target_pairs={{0,1},{1,0},{2,3},{3,2},{4,5},{5,4},{6,7},{7,6},{8,9},{9,8},{10,11... | collective-permute-start | bytes 258056 | tf_op jit(solution)/shard_map/ppermute | solution.py:16
  46.3 0.9 %collective-permute-done.4 = f32[24,7,128]{2,0,1:T(8,128)S(1)} collective-permute-done((f32[24,7,128]{2,0,1:T(8,128)S(1)}, f32[24,7,128]{2,0,1:T(8,128)S(1)}, u32[]{:S(2)}, u32[]{:S(2)}) %collective-permute-start.4) | collective-permute-done | bytes 86048 | tf_op jit(solution)/shard_map/ppermute | solution.py:16
  47.4 3.0 %collective-permute-start.6 = (f32[1,1,32,7,128]{4,2,3,1,0:T(8,128)S(1)}, f32[1,1,32,7,128]{4,2,3,1,0:T(8,128)S(1)}, u32[]{:S(2)}, u32[]{:S(2)}) collective-permute-start(f32[1,1,32,7,128]{4,2,3,1,0:T(8,128)S(1)} %slice_bitcast_fusion.4), channel_id=1, source_target_pairs={{4,0},{8,4},{12,8},{16,12},{20,16},{24,20},{28,24},{5,1},{9,5},{13... | collective-permute-start | bytes 344072 | tf_op jit(solution)/shard_map/ppermute | solution.py:27
  50.4 2.3 %collective-permute-start.5 = (f32[1,1,32,7,128]{4,2,3,1,0:T(8,128)S(1)}, f32[1,1,32,7,128]{4,2,3,1,0:T(8,128)S(1)}, u32[]{:S(2)}, u32[]{:S(2)}) collective-permute-start(f32[1,1,32,7,128]{4,2,3,1,0:T(8,128)S(1)} %slice_bitcast_fusion.4), channel_id=1, source_target_pairs={{0,4},{4,8},{8,12},{12,16},{16,20},{20,24},{24,28},{1,5},{5,9},{9,... | collective-permute-start | bytes 344072 | tf_op jit(solution)/shard_map/ppermute | solution.py:26
  56.4 0.9 %collective-permute-done.5 = f32[1,1,32,7,128]{4,2,3,1,0:T(8,128)S(1)} collective-permute-done((f32[1,1,32,7,128]{4,2,3,1,0:T(8,128)S(1)}, f32[1,1,32,7,128]{4,2,3,1,0:T(8,128)S(1)}, u32[]{:S(2)}, u32[]{:S(2)}) %collective-permute-start.5) | collective-permute-done | bytes 114720 | tf_op jit(solution)/shard_map/ppermute | solution.py:26
  57.3 3.4 %collective-permute-start.8 = (f32[3,1,32,7,128]{4,2,3,1,0:T(8,128)S(1)}, f32[3,1,32,7,128]{4,2,3,1,0:T(8,128)S(1)}, u32[]{:S(2)}, u32[]{:S(2)}) collective-permute-start(f32[3,1,32,7,128]{4,2,3,1,0:T(8,128)S(1)} %pad_maximum_fusion.2), channel_id=1, source_target_pairs={{1,0},{2,1},{3,2},{5,4},{6,5},{7,6},{9,8},{10,9},{11,10},{13,12},{... | collective-permute-start | bytes 1032200 | tf_op jit(solution)/shard_map/ppermute | solution.py:27
  60.7 3.0 %collective-permute-start.7 = (f32[3,1,32,7,128]{4,2,3,1,0:T(8,128)S(1)}, f32[3,1,32,7,128]{4,2,3,1,0:T(8,128)S(1)}, u32[]{:S(2)}, u32[]{:S(2)}) collective-permute-start(f32[3,1,32,7,128]{4,2,3,1,0:T(8,128)S(1)} %pad_maximum_fusion.2), channel_id=1, source_target_pairs={{0,1},{1,2},{2,3},{4,5},{5,6},{6,7},{8,9},{9,10},{10,11},{12,13},{... | collective-permute-start | bytes 1032200 | tf_op jit(solution)/shard_map/ppermute | solution.py:26
  64.1 2.6 %collective-permute-done.8 = f32[3,1,32,7,128]{4,2,3,1,0:T(8,128)S(1)} collective-permute-done((f32[3,1,32,7,128]{4,2,3,1,0:T(8,128)S(1)}, f32[3,1,32,7,128]{4,2,3,1,0:T(8,128)S(1)}, u32[]{:S(2)}, u32[]{:S(2)}) %collective-permute-start.8) | collective-permute-done | bytes 344096 | tf_op jit(solution)/shard_map/ppermute | solution.py:27
  66.8 1.2 %collective-permute-done.7 = f32[3,1,32,7,128]{4,2,3,1,0:T(8,128)S(1)} collective-permute-done((f32[3,1,32,7,128]{4,2,3,1,0:T(8,128)S(1)}, f32[3,1,32,7,128]{4,2,3,1,0:T(8,128)S(1)}, u32[]{:S(2)}, u32[]{:S(2)}) %collective-permute-start.7) | collective-permute-done | bytes 344096 | tf_op jit(solution)/shard_map/ppermute | solution.py:26
  68.7 1.0 %gather_fusion.1 = f32[256,7,128]{2,1,0:T(8,128)S(1)} fusion(f32[288,7,128]{2,1,0:T(8,128)S(1)} %copy.159, s32[1024]{0:T(1024)S(1)} %pad_clamp_fusion.2), kind=kCustom, calls=%fused_computation.1 | custom fusion | bytes 1836032 | tf_op jit(solution)/shard_map/gather | solution.py:210
  70.7 17.8 %multiply_reduce_fusion.3 = (f32[32,128]{1,0:T(8,128)S(1)}, f32[32,128]{1,0:T(8,128)S(1)}, f32[32,128]{1,0:T(8,128)S(1)}, f32[32,128]{1,0:T(8,128)S(1)}, f32[32,128]{1,0:T(8,128)S(1)}, /*index=5*/f32[32,128]{1,0:T(8,128)S(1)}) fusion(f32[32,8,128]{2,1,0:T(8,128)S(1)} %get-tuple-element.49, f32[32,8,128]{2,1,0:T(8,128)S(1)} %get-tuple-element.50, ...), kind=kLoop, calls=%fused_computation.8 | loop fusion | flops 96444416 | bytes 1458176 | tf_op jit(solution)/shard_map/vmap()/reduce_sum | solution.py:50
  (136 shorter events, 15.2 us)
Async XLA Ops:
  0.0 34.2 %copy-start = (s32[1024]{0:T(1024)S(1)}, s32[1024]{0:T(1024)}, u32[]{:S(2)}) copy-start(s32[1024]{0:T(1024)} %param.12) | copy-start | bytes 12292
  0.0 34.1 %copy-start.1 = (s32[1,1,32,8]{2,3,1,0:T(8,128)S(1)}, s32[1,1,32,8]{2,3,1,0:T(8,128)}, u32[]{:S(2)}) copy-start(s32[1,1,32,8]{2,3,1,0:T(8,128)} %param.13) | copy-start | bytes 3076
  10.9 16.4 %collective-permute-start = (f32[9,7,128]{2,1,0:T(8,128)S(1)}, f32[9,7,128]{2,1,0:T(8,128)S(1)}, u32[]{:S(2)}, u32[]{:S(2)}) collective-permute-start(f32[9,7,128]{2,1,0:T(8,128)S(1)} %pad_maximum_fusion.5), channel_id=1, source_target_pairs={{0,16},{4,20},{8,24},{12,28},{16,0},{20,4},{24,8},{28,12},{1,17},{... | collective-permute-start | bytes 96776 | tf_op jit(solution)/shard_map/ppermute | solution.py:16
  29.5 3.1 %collective-permute-start.1 = (f32[10,7,128]{2,0,1:T(8,128)S(1)}, f32[10,7,128]{2,0,1:T(8,128)S(1)}, u32[]{:S(2)}, u32[]{:S(2)}) collective-permute-start(f32[10,7,128]{2,0,1:T(8,128)S(1)} %pad_maximum_fusion.3), channel_id=1, source_target_pairs={{0,8},{4,12},{8,0},{12,4},{16,24},{20,28},{24,16},{28,20},{1,9},{5... | collective-permute-start | bytes 107528 | tf_op jit(solution)/shard_map/ppermute | solution.py:16
  32.8 3.1 %collective-permute-start.2 = (f32[12,7,128]{2,0,1:T(8,128)S(1)}, f32[12,7,128]{2,0,1:T(8,128)S(1)}, u32[]{:S(2)}, u32[]{:S(2)}) collective-permute-start(f32[12,7,128]{2,0,1:T(8,128)S(1)} %pad_maximum_fusion.4), channel_id=1, source_target_pairs={{0,4},{4,0},{8,12},{12,8},{16,20},{20,16},{24,28},{28,24},{1,5},{5... | collective-permute-start | bytes 129032 | tf_op jit(solution)/shard_map/ppermute | solution.py:16
  34.3 1.8 %copy-start.2 = (s32[1,1,32,8]{2,3,1,0:T(8,128)S(1)}, s32[1,1,32,8]{2,3,1,0:T(8,128)}, u32[]{:S(2)}) copy-start(s32[1,1,32,8]{2,3,1,0:T(8,128)} %param.14) | copy-start | bytes 3076
  38.6 3.1 %collective-permute-start.3 = (f32[16,7,128]{2,0,1:T(8,128)S(1)}, f32[16,7,128]{2,0,1:T(8,128)S(1)}, u32[]{:S(2)}, u32[]{:S(2)}) collective-permute-start(f32[16,7,128]{2,0,1:T(8,128)S(1)} %concatenate.47), channel_id=1, source_target_pairs={{0,2},{1,3},{2,0},{3,1},{4,6},{5,7},{6,4},{7,5},{8,10},{9,11},{10,... | collective-permute-start | bytes 172040 | tf_op jit(solution)/shard_map/ppermute | solution.py:16
  41.9 5.3 %collective-permute-start.4 = (f32[24,7,128]{2,0,1:T(8,128)S(1)}, f32[24,7,128]{2,0,1:T(8,128)S(1)}, u32[]{:S(2)}, u32[]{:S(2)}) collective-permute-start(f32[24,7,128]{2,0,1:T(8,128)S(1)} %concatenate.48), channel_id=1, source_target_pairs={{0,1},{1,0},{2,3},{3,2},{4,5},{5,4},{6,7},{7,6},{8,9},{9,8},{10,11... | collective-permute-start | bytes 258056 | tf_op jit(solution)/shard_map/ppermute | solution.py:16
  47.4 8.9 %collective-permute-start.6 = (f32[1,1,32,7,128]{4,2,3,1,0:T(8,128)S(1)}, f32[1,1,32,7,128]{4,2,3,1,0:T(8,128)S(1)}, u32[]{:S(2)}, u32[]{:S(2)}) collective-permute-start(f32[1,1,32,7,128]{4,2,3,1,0:T(8,128)S(1)} %slice_bitcast_fusion.4), channel_id=1, source_target_pairs={{4,0},{8,4},{12,8},{16,12},{20,16},{24,20},{28,24},{5,1},{9,5},{13... | collective-permute-start | bytes 344072 | tf_op jit(solution)/shard_map/ppermute | solution.py:27
  50.4 6.9 %collective-permute-start.5 = (f32[1,1,32,7,128]{4,2,3,1,0:T(8,128)S(1)}, f32[1,1,32,7,128]{4,2,3,1,0:T(8,128)S(1)}, u32[]{:S(2)}, u32[]{:S(2)}) collective-permute-start(f32[1,1,32,7,128]{4,2,3,1,0:T(8,128)S(1)} %slice_bitcast_fusion.4), channel_id=1, source_target_pairs={{0,4},{4,8},{8,12},{12,16},{16,20},{20,24},{24,28},{1,5},{5,9},{9,... | collective-permute-start | bytes 344072 | tf_op jit(solution)/shard_map/ppermute | solution.py:26
  57.3 9.5 %collective-permute-start.8 = (f32[3,1,32,7,128]{4,2,3,1,0:T(8,128)S(1)}, f32[3,1,32,7,128]{4,2,3,1,0:T(8,128)S(1)}, u32[]{:S(2)}, u32[]{:S(2)}) collective-permute-start(f32[3,1,32,7,128]{4,2,3,1,0:T(8,128)S(1)} %pad_maximum_fusion.2), channel_id=1, source_target_pairs={{1,0},{2,1},{3,2},{5,4},{6,5},{7,6},{9,8},{10,9},{11,10},{13,12},{... | collective-permute-start | bytes 1032200 | tf_op jit(solution)/shard_map/ppermute | solution.py:27
  60.7 7.2 %collective-permute-start.7 = (f32[3,1,32,7,128]{4,2,3,1,0:T(8,128)S(1)}, f32[3,1,32,7,128]{4,2,3,1,0:T(8,128)S(1)}, u32[]{:S(2)}, u32[]{:S(2)}) collective-permute-start(f32[3,1,32,7,128]{4,2,3,1,0:T(8,128)S(1)} %pad_maximum_fusion.2), channel_id=1, source_target_pairs={{0,1},{1,2},{2,3},{4,5},{5,6},{6,7},{8,9},{9,10},{10,11},{12,13},{... | collective-permute-start | bytes 1032200 | tf_op jit(solution)/shard_map/ppermute | solution.py:26

commit v10 on v8

--- a/solution.py
+++ b/solution.py
@@ -142,34 +142,37 @@
     gathered = table_blocks(slot_table, lanes)
     pieces = gathered.shape[0]
     held = jnp.pad(held, ((0, MOVE), (0, 0), (0, 0)))
-    plans = []
     level_bits = []
     for level in range(levels):
         if level < bits_x:
-            bit_at = bits_x - 1 - level
-            mate_moves = moves[level, jnp.bitwise_xor(column_index, 1 << bit_at), row_index]
-            level_bits.append((1 << bit_at) * size_y)
+            level_bits.append((1 << bits_x - 1 - level) * size_y)
         else:
-            bit_at = levels - 1 - level
-            mate_moves = moves[level, column_index, jnp.bitwise_xor(row_index, 1 << bit_at)]
-            level_bits.append(1 << bit_at)
-        plans.append((bit_at, moves[level, column_index, row_index], mate_moves))
-    count = jnp.int32(nbd)
-    for plan_item in plans:
-        count = count + plan_item[1] - plan_item[2]
-    for level in range(levels):
-        bit_at, own_moves, mate_moves = plans[level]
-        leaving = lax.dynamic_slice_in_dim(held, count - own_moves, MOVE, 0)
+            level_bits.append(1 << levels - 1 - level)
+    devices = size_x * size_y
+    flat_moves = moves.reshape(levels, devices)
+    every = jnp.arange(devices, dtype=jnp.int32)
+    mates = jnp.bitwise_xor(me, jnp.array(level_bits, jnp.int32))
+    own = jnp.sum(jnp.where(every[None, :] == me, flat_moves, 0), axis=1)
+    mate_own = jnp.sum(jnp.where(every[None, :] == mates[:, None], flat_moves, 0), axis=1)
+    count = nbd + jnp.sum(own - mate_own, keepdims=True)
+    slot_ids = jnp.arange(held.shape[0], dtype=jnp.int32)
+    move_ids = jnp.arange(MOVE, dtype=jnp.int32)
+    for level in range(levels):
+        if level < bits_x:
+            axis_name, bit_at = "gx", bits_x - 1 - level
+        else:
+            axis_name, bit_at = "gy", levels - 1 - level
+        count = count - own[level : level + 1]
+        take = slot_ids[None, :] == (count + move_ids)[:, None]
+        leaving = jnp.sum(jnp.where(take[:, :, None, None], held[None], 0.0), axis=1)
         payload = jnp.concatenate([leaving, gathered], axis=0)
-        if level < bits_x:
-            got = from_partner(payload, "gx", bit_at)
-        else:
-            got = from_partner(payload, "gy", bit_at)
+        got = from_partner(payload, axis_name, bit_at)
         arriving = got[:MOVE]
         gathered = jnp.concatenate([gathered, got[MOVE:]], axis=0)
-        count = count - own_moves
-        held = lax.dynamic_update_slice_in_dim(held, arriving, count, 0)
-        count = count + mate_moves
+        put = slot_ids[:, None] == (count + move_ids)[None, :]
+        placed = jnp.sum(jnp.where(put[:, :, None, None], arriving[None], 0.0), axis=1)
+        held = jnp.where(jnp.any(put, axis=1)[:, None, None], placed, held)
+        count = count + mate_own[level : level + 1]
         if level == 0:
             moves_late, _ = lax.optimization_barrier((moves, held))
             kept, kept_mate, level_bit = level_tables(moves_late, levels, bits_x, nbd)

time: 85 us -> 91.3 us (1.074)
  other arithmetic: 26.5 us -> 35.6 us
  between operations: 12.4 us -> 6.95 us
  waiting for transfers between devices: 8.08 us -> 12 us
  local copies, waits for them, and re-layouts: 15.4 us -> 13.9 us
    reduce_sum x0 -> x12, other arithmetic: none -> 6.69 us  [the longest x5 3.52 us: local(): jnp.sum(jnp.where(put[:, :, None, None], arriving[None], 0.0), axis=1)]
    ppermute x5, waiting for transfers between devices: 3.32 us -> 6.74 us  [from_partner(): lax.ppermute(shard, axis, [(i, i ^ 1 << apart) for i in range(lax.axis_si...]
    dynamic_slice x6 -> x0, local copies, waits for them, and re-layouts: 1.63 us -> none  [the longest x1 1.53 us: local(): moves[level, column_index, jnp.bitwise_xor(row_index, 1 << bit_at)]]
    squeeze x0 -> x1, local copies, waits for them, and re-layouts: none -> 1.03 us  [local(): strength[0, 0]]
    slice x0 -> x3, local copies, waits for them, and re-layouts: none -> 0.95 us  [the longest x1 0.68 us: local(): count = count - own[level:level + 1]]
  transfers between devices with their start and end apart: 9 -> 9, of which waited for: 6 -> 7; matrix products, arithmetic and copies ran while one was open for 10% -> 7% of each run, Pallas kernels for 0% -> 0%
where the time goes in v10:
time: 91.3 us; the launch traced here: 90 us
  other arithmetic  35.6 us (39%)
  starting transfers between devices  21.6 us (24%)
  local copies, waits for them, and re-layouts  13.9 us (15%)
  waiting for transfers between devices  12 us (13%)
  between operations  6.95 us (8%)
    reduce_sum x1, other arithmetic, evaluate(): arm_x = jnp.sum(extra[:, 1][:, None, :] * weight, axis=(0, 2))  17.9 us
    ppermute x5, starting transfers between devices, from_partner(): lax.ppermute(shard, axis, [(i, i ^ 1 << apart) for i in range(lax.axis_si...  9.66 us
    ppermute x5, waiting for transfers between devices, from_partner(): lax.ppermute(shard, axis, [(i, i ^ 1 << apart) for i in range(lax.axis_si...  6.74 us
    ppermute x2, starting transfers between devices, padded(): after = lax.ppermute(first, axis, down)  6.42 us
    ppermute x2, starting transfers between devices, padded(): before = lax.ppermute(last, axis, up)  5.5 us
    reduce_sum x5, other arithmetic, local(): jnp.sum(jnp.where(put[:, :, None, None], arriving[None], 0.0), axis=1)  3.52 us
    ppermute x2, waiting for transfers between devices, padded(): after = lax.ppermute(first, axis, down)  2.97 us
    ppermute x2, waiting for transfers between devices, padded(): before = lax.ppermute(last, axis, up)  2.3 us
  transfers between devices with their start and end apart: 9, of which 7 were waited for; matrix products, arithmetic and copies ran while one was open for 7% of the time, Pallas kernels for 0%

profile of v10, /device:TPU:9, one launch (start us, length us, event | category | flops | bytes accessed | tf_op | source)
XLA Modules:
  0.0 90.0 jit_solution(15591321865567224177)
XLA Ops:
  0.7 1.0 %select_reduce_fusion.22 = (s32[5]{0:T(128)S(1)}, s32[5]{0:T(128)S(1)}) fusion(s32[5,8,4]{1,2,0:T(4,128)} %param.12, s32[8,4]{0,1:T(4,128)S(1)} %multiply_add_fusion, s32[5]{0:T(128)S(1)} %broadcast_xor_fusion, pred[8,4]{0,1:T(4,128)(4,1)S(1)} %broadcast_compare_fusion), kind=kLoop, calls=%fused_computation.205 | loop fusion | flops 790 | bytes 860 | tf_op jit(solution)/shard_map/reduce_sum | solution.py:156
  3.1 1.0 %reduce_sum.409 = f32[72,3]{0,1:T(4,128)S(1)} reduce(f32[1,1,72,3,128]{4,2,3,1,0:T(8,128)} %param.10, f32[]{:T(128)} %constant.180.clone.1), dimensions={0,1,4}, to_apply=%region_10.11 | reduce | flops 27432 | bytes 111460 | tf_op jit(solution)/shard_map/reduce_sum | solution.py:34
  4.1 1.1 %reduce_sum.408 = f32[72,3]{0,1:T(4,128)S(1)} reduce(f32[1,1,72,3,128]{4,2,3,1,0:T(8,128)} %param.9, f32[]{:T(128)} %constant.180.clone.1), dimensions={0,1,4}, to_apply=%region_9.10 | reduce | flops 27432 | bytes 111460 | tf_op jit(solution)/shard_map/reduce_sum | solution.py:33
  5.2 1.0 %copy_bitcast_fusion = (f32[72,3,128]{2,1,0:T(4,128)S(1)}, f32[72,3,128]{2,1,0:T(4,128)S(1)}) fusion(f32[1,1,72,3,128]{4,2,3,1,0:T(8,128)} %param.10, f32[1,1,72,3,128]{4,2,3,1,0:T(8,128)} %param.9), kind=kLoop, calls=%fused_computation.42 | loop fusion | bytes 442368 | tf_op jit(solution)/shard_map/squeeze | solution.py:139
  8.5 1.9 %multiply_reduce_fusion.6 = f32[72]{0:T(128)S(1)} fusion(f32[72,3]{1,0:T(8,128)S(1)} %copy.392, f32[1,1,72,3,128]{4,2,3,1,0:T(8,128)} %param.9), kind=kLoop, calls=%fused_computation.44 | loop fusion | flops 82872 | bytes 111744 | tf_op jit(solution)/shard_map/reduce_sum | solution.py:36
  11.8 2.4 %collective-permute-start = (f32[9,7,128]{2,1,0:T(8,128)S(1)}, f32[9,7,128]{2,1,0:T(8,128)S(1)}, u32[]{:S(2)}, u32[]{:S(2)}) collective-permute-start(f32[9,7,128]{2,1,0:T(8,128)S(1)} %pad_maximum_fusion.5), channel_id=1, source_target_pairs={{0,16},{4,20},{8,24},{12,28},{16,0},{20,4},{24,8},{28,12},{1,17},{... | collective-permute-start | bytes 96776 | tf_op jit(solution)/shard_map/ppermute | solution.py:16
  24.0 2.5 %collective-permute-done.1 = f32[10,7,128]{2,1,0:T(8,128)S(1)} collective-permute-done((f32[10,7,128]{2,1,0:T(8,128)S(1)}, f32[10,7,128]{2,1,0:T(8,128)S(1)}, u32[]{:S(2)}, u32[]{:S(2)}) %collective-permute-start.1) | collective-permute-done | bytes 35872 | tf_op jit(solution)/shard_map/ppermute | solution.py:16
  27.7 1.4 %gather_fusion = s32[256]{0:T(256)S(1)} fusion(s32[1024]{0:T(1024)S(1)} %copy-done, s32[1024]{0:T(1024)S(1)} %pad_clamp_fusion.3), kind=kCustom, calls=%fused_computation | custom fusion | bytes 3072 | tf_op jit(solution)/shard_map/gather | solution.py:181
  29.6 1.3 %collective-permute-start.2 = (f32[12,7,128]{2,1,0:T(8,128)S(1)}, f32[12,7,128]{2,1,0:T(8,128)S(1)}, u32[]{:S(2)}, u32[]{:S(2)}) collective-permute-start(f32[12,7,128]{2,1,0:T(8,128)S(1)} %pad_maximum_fusion.3), channel_id=1, source_target_pairs={{0,4},{4,0},{8,12},{12,8},{16,20},{20,16},{24,28},{28,24},{1,5},{5... | collective-permute-start | bytes 129032 | tf_op jit(solution)/shard_map/ppermute | solution.py:16
  30.9 1.7 %collective-permute-done.2 = f32[12,7,128]{2,1,0:T(8,128)S(1)} collective-permute-done((f32[12,7,128]{2,1,0:T(8,128)S(1)}, f32[12,7,128]{2,1,0:T(8,128)S(1)}, u32[]{:S(2)}, u32[]{:S(2)}) %collective-permute-start.2) | collective-permute-done | bytes 43040 | tf_op jit(solution)/shard_map/ppermute | solution.py:16
  33.7 1.4 %gather_fusion.2 = s32[256]{0:T(256)S(1)} fusion(s32[1024]{0:T(1024)S(1)} %copy-done, s32[1024]{0:T(1024)S(1)} %pad_clamp_fusion.1), kind=kCustom, calls=%fused_computation.2 | custom fusion | bytes 3072 | tf_op jit(solution)/shard_map/gather | solution.py:184
  37.1 1.3 %collective-permute-start.3 = (f32[16,7,128]{2,0,1:T(8,128)S(1)}, f32[16,7,128]{2,0,1:T(8,128)S(1)}, u32[]{:S(2)}, u32[]{:S(2)}) collective-permute-start(f32[16,7,128]{2,0,1:T(8,128)S(1)} %concatenate.47), channel_id=1, source_target_pairs={{0,2},{1,3},{2,0},{3,1},{4,6},{5,7},{6,4},{7,5},{8,10},{9,11},{10,... | collective-permute-start | bytes 172040 | tf_op jit(solution)/shard_map/ppermute | solution.py:16
  38.6 1.6 %collective-permute-done.3 = f32[16,7,128]{2,0,1:T(8,128)S(1)} collective-permute-done((f32[16,7,128]{2,0,1:T(8,128)S(1)}, f32[16,7,128]{2,0,1:T(8,128)S(1)}, u32[]{:S(2)}, u32[]{:S(2)}) %collective-permute-start.3) | collective-permute-done | bytes 57376 | tf_op jit(solution)/shard_map/ppermute | solution.py:16
  41.5 4.5 %collective-permute-start.4 = (f32[24,7,128]{2,0,1:T(8,128)S(1)}, f32[24,7,128]{2,0,1:T(8,128)S(1)}, u32[]{:S(2)}, u32[]{:S(2)}) collective-permute-start(f32[24,7,128]{2,0,1:T(8,128)S(1)} %concatenate.48), channel_id=1, source_target_pairs={{0,1},{1,0},{2,3},{3,2},{4,5},{5,4},{6,7},{7,6},{8,9},{9,8},{10,11... | collective-permute-start | bytes 258056 | tf_op jit(solution)/shard_map/ppermute | solution.py:16
  46.0 0.9 %collective-permute-done.4 = f32[24,7,128]{2,0,1:T(8,128)S(1)} collective-permute-done((f32[24,7,128]{2,0,1:T(8,128)S(1)}, f32[24,7,128]{2,0,1:T(8,128)S(1)}, u32[]{:S(2)}, u32[]{:S(2)}) %collective-permute-start.4) | collective-permute-done | bytes 86048 | tf_op jit(solution)/shard_map/ppermute | solution.py:16
  47.9 3.0 %collective-permute-start.6 = (f32[1,1,32,7,128]{4,3,2,1,0:T(8,128)S(1)}, f32[1,1,32,7,128]{4,3,2,1,0:T(8,128)S(1)}, u32[]{:S(2)}, u32[]{:S(2)}) collective-permute-start(f32[1,1,32,7,128]{4,3,2,1,0:T(8,128)S(1)} %slice_bitcast_fusion.4), channel_id=1, source_target_pairs={{4,0},{8,4},{12,8},{16,12},{20,16},{24,20},{28,24},{5,1},{9,5},{13... | collective-permute-start | bytes 344072 | tf_op jit(solution)/shard_map/ppermute | solution.py:27
  50.9 2.3 %collective-permute-start.5 = (f32[1,1,32,7,128]{4,3,2,1,0:T(8,128)S(1)}, f32[1,1,32,7,128]{4,3,2,1,0:T(8,128)S(1)}, u32[]{:S(2)}, u32[]{:S(2)}) collective-permute-start(f32[1,1,32,7,128]{4,3,2,1,0:T(8,128)S(1)} %slice_bitcast_fusion.4), channel_id=1, source_target_pairs={{0,4},{4,8},{8,12},{12,16},{16,20},{20,24},{24,28},{1,5},{5,9},{9,... | collective-permute-start | bytes 344072 | tf_op jit(solution)/shard_map/ppermute | solution.py:26
  57.0 1.1 %collective-permute-done.5 = f32[1,1,32,7,128]{4,3,2,1,0:T(8,128)S(1)} collective-permute-done((f32[1,1,32,7,128]{4,3,2,1,0:T(8,128)S(1)}, f32[1,1,32,7,128]{4,3,2,1,0:T(8,128)S(1)}, u32[]{:S(2)}, u32[]{:S(2)}) %collective-permute-start.5) | collective-permute-done | bytes 114720 | tf_op jit(solution)/shard_map/ppermute | solution.py:26
  58.1 3.4 %collective-permute-start.8 = (f32[3,1,32,7,128]{4,3,2,1,0:T(8,128)S(1)}, f32[3,1,32,7,128]{4,3,2,1,0:T(8,128)S(1)}, u32[]{:S(2)}, u32[]{:S(2)}) collective-permute-start(f32[3,1,32,7,128]{4,3,2,1,0:T(8,128)S(1)} %pad_maximum_fusion.2), channel_id=1, source_target_pairs={{1,0},{2,1},{3,2},{5,4},{6,5},{7,6},{9,8},{10,9},{11,10},{13,12},{... | collective-permute-start | bytes 1032200 | tf_op jit(solution)/shard_map/ppermute | solution.py:27
  61.6 3.2 %collective-permute-start.7 = (f32[3,1,32,7,128]{4,3,2,1,0:T(8,128)S(1)}, f32[3,1,32,7,128]{4,3,2,1,0:T(8,128)S(1)}, u32[]{:S(2)}, u32[]{:S(2)}) collective-permute-start(f32[3,1,32,7,128]{4,3,2,1,0:T(8,128)S(1)} %pad_maximum_fusion.2), channel_id=1, source_target_pairs={{0,1},{1,2},{2,3},{4,5},{5,6},{6,7},{8,9},{9,10},{10,11},{12,13},{... | collective-permute-start | bytes 1032200 | tf_op jit(solution)/shard_map/ppermute | solution.py:26
  65.2 3.0 %collective-permute-done.8 = f32[3,1,32,7,128]{4,3,2,1,0:T(8,128)S(1)} collective-permute-done((f32[3,1,32,7,128]{4,3,2,1,0:T(8,128)S(1)}, f32[3,1,32,7,128]{4,3,2,1,0:T(8,128)S(1)}, u32[]{:S(2)}, u32[]{:S(2)}) %collective-permute-start.8) | collective-permute-done | bytes 344096 | tf_op jit(solution)/shard_map/ppermute | solution.py:27
  68.1 1.2 %collective-permute-done.7 = f32[3,1,32,7,128]{4,3,2,1,0:T(8,128)S(1)} collective-permute-done((f32[3,1,32,7,128]{4,3,2,1,0:T(8,128)S(1)}, f32[3,1,32,7,128]{4,3,2,1,0:T(8,128)S(1)}, u32[]{:S(2)}, u32[]{:S(2)}) %collective-permute-start.7) | collective-permute-done | bytes 344096 | tf_op jit(solution)/shard_map/ppermute | solution.py:26
  69.4 1.0 %gather_fusion.1 = f32[256,7,128]{2,1,0:T(8,128)S(1)} fusion(f32[288,7,128]{2,1,0:T(8,128)S(1)} %bitcast.169, s32[1024]{0:T(1024)S(1)} %pad_clamp_fusion.2), kind=kCustom, calls=%fused_computation.1 | custom fusion | bytes 1836032 | tf_op jit(solution)/shard_map/gather | solution.py:201
  71.4 17.9 %multiply_reduce_fusion.3 = (f32[32,128]{1,0:T(8,128)S(1)}, f32[32,128]{1,0:T(8,128)S(1)}, f32[32,128]{1,0:T(8,128)S(1)}, f32[32,128]{1,0:T(8,128)S(1)}, f32[32,128]{1,0:T(8,128)S(1)}, /*index=5*/f32[32,128]{1,0:T(8,128)S(1)}) fusion(f32[32,8,128]{2,1,0:T(8,128)S(1)} %get-tuple-element.48, f32[32,8,128]{2,1,0:T(8,128)S(1)} %get-tuple-element.49, ...), kind=kLoop, calls=%fused_computation.8 | loop fusion | flops 96444416 | bytes 1458176 | tf_op jit(solution)/shard_map/vmap()/reduce_sum | solution.py:50
  (180 shorter events, 22.0 us)
Async XLA Ops:
  0.0 27.7 %copy-start = (s32[1024]{0:T(1024)S(1)}, s32[1024]{0:T(1024)}, u32[]{:S(2)}) copy-start(s32[1024]{0:T(1024)} %param.13) | copy-start | bytes 12292
  0.0 19.8 %copy-start.5 = (s32[5]{0:T(128)S(1)}, s32[5]{0:T(128)}, u32[]{:S(2)}) copy-start(s32[5]{0:T(128)} %constant.197.clone) | copy-start | bytes 64
  0.0 21.3 %copy-start.1 = (f32[1,1,72,128]{3,2,1,0:T(8,128)S(1)}, f32[1,1,72,128]{3,2,1,0:T(8,128)}, u32[]{:S(2)}) copy-start(f32[1,1,72,128]{3,2,1,0:T(8,128)} %param.11) | copy-start | bytes 110596
  4.1 17.3 %copy-start.2 = (s32[5,8,4]{1,2,0:T(4,128)S(1)}, s32[5,8,4]{1,2,0:T(4,128)}, u32[]{:S(2)}) copy-start(s32[5,8,4]{1,2,0:T(4,128)} %param.12) | copy-start | bytes 1924
  11.8 8.8 %collective-permute-start = (f32[9,7,128]{2,1,0:T(8,128)S(1)}, f32[9,7,128]{2,1,0:T(8,128)S(1)}, u32[]{:S(2)}, u32[]{:S(2)}) collective-permute-start(f32[9,7,128]{2,1,0:T(8,128)S(1)} %pad_maximum_fusion.5), channel_id=1, source_target_pairs={{0,16},{4,20},{8,24},{12,28},{16,0},{20,4},{24,8},{28,12},{1,17},{... | collective-permute-start | bytes 96776 | tf_op jit(solution)/shard_map/ppermute | solution.py:16
  21.3 6.2 %copy-start.3 = (s32[1,1,32,8]{2,3,1,0:T(8,128)S(1)}, s32[1,1,32,8]{2,3,1,0:T(8,128)}, u32[]{:S(2)}) copy-start(s32[1,1,32,8]{2,3,1,0:T(8,128)} %param.14) | copy-start | bytes 3076
  23.6 2.9 %collective-permute-start.1 = (f32[10,7,128]{2,1,0:T(8,128)S(1)}, f32[10,7,128]{2,1,0:T(8,128)S(1)}, u32[]{:S(2)}, u32[]{:S(2)}) collective-permute-start(f32[10,7,128]{2,1,0:T(8,128)S(1)} %pad_maximum_fusion.4), channel_id=1, source_target_pairs={{0,8},{4,12},{8,0},{12,4},{16,24},{20,28},{24,16},{28,20},{1,9},{5... | collective-permute-start | bytes 107528 | tf_op jit(solution)/shard_map/ppermute | solution.py:16
  27.7 5.8 %copy-start.4 = (s32[1,1,32,8]{2,3,1,0:T(8,128)S(1)}, s32[1,1,32,8]{2,3,1,0:T(8,128)}, u32[]{:S(2)}) copy-start(s32[1,1,32,8]{2,3,1,0:T(8,128)} %param.15) | copy-start | bytes 3076
  29.6 3.0 %collective-permute-start.2 = (f32[12,7,128]{2,1,0:T(8,128)S(1)}, f32[12,7,128]{2,1,0:T(8,128)S(1)}, u32[]{:S(2)}, u32[]{:S(2)}) collective-permute-start(f32[12,7,128]{2,1,0:T(8,128)S(1)} %pad_maximum_fusion.3), channel_id=1, source_target_pairs={{0,4},{4,0},{8,12},{12,8},{16,20},{20,16},{24,28},{28,24},{1,5},{5... | collective-permute-start | bytes 129032 | tf_op jit(solution)/shard_map/ppermute | solution.py:16
  37.1 3.1 %collective-permute-start.3 = (f32[16,7,128]{2,0,1:T(8,128)S(1)}, f32[16,7,128]{2,0,1:T(8,128)S(1)}, u32[]{:S(2)}, u32[]{:S(2)}) collective-permute-start(f32[16,7,128]{2,0,1:T(8,128)S(1)} %concatenate.47), channel_id=1, source_target_pairs={{0,2},{1,3},{2,0},{3,1},{4,6},{5,7},{6,4},{7,5},{8,10},{9,11},{10,... | collective-permute-start | bytes 172040 | tf_op jit(solution)/shard_map/ppermute | solution.py:16
  41.5 5.4 %collective-permute-start.4 = (f32[24,7,128]{2,0,1:T(8,128)S(1)}, f32[24,7,128]{2,0,1:T(8,128)S(1)}, u32[]{:S(2)}, u32[]{:S(2)}) collective-permute-start(f32[24,7,128]{2,0,1:T(8,128)S(1)} %concatenate.48), channel_id=1, source_target_pairs={{0,1},{1,0},{2,3},{3,2},{4,5},{5,4},{6,7},{7,6},{8,9},{9,8},{10,11... | collective-permute-start | bytes 258056 | tf_op jit(solution)/shard_map/ppermute | solution.py:16
  47.9 9.1 %collective-permute-start.6 = (f32[1,1,32,7,128]{4,3,2,1,0:T(8,128)S(1)}, f32[1,1,32,7,128]{4,3,2,1,0:T(8,128)S(1)}, u32[]{:S(2)}, u32[]{:S(2)}) collective-permute-start(f32[1,1,32,7,128]{4,3,2,1,0:T(8,128)S(1)} %slice_bitcast_fusion.4), channel_id=1, source_target_pairs={{4,0},{8,4},{12,8},{16,12},{20,16},{24,20},{28,24},{5,1},{9,5},{13... | collective-permute-start | bytes 344072 | tf_op jit(solution)/shard_map/ppermute | solution.py:27
  50.9 7.2 %collective-permute-start.5 = (f32[1,1,32,7,128]{4,3,2,1,0:T(8,128)S(1)}, f32[1,1,32,7,128]{4,3,2,1,0:T(8,128)S(1)}, u32[]{:S(2)}, u32[]{:S(2)}) collective-permute-start(f32[1,1,32,7,128]{4,3,2,1,0:T(8,128)S(1)} %slice_bitcast_fusion.4), channel_id=1, source_target_pairs={{0,4},{4,8},{8,12},{12,16},{16,20},{20,24},{24,28},{1,5},{5,9},{9,... | collective-permute-start | bytes 344072 | tf_op jit(solution)/shard_map/ppermute | solution.py:26
  58.1 10.0 %collective-permute-start.8 = (f32[3,1,32,7,128]{4,3,2,1,0:T(8,128)S(1)}, f32[3,1,32,7,128]{4,3,2,1,0:T(8,128)S(1)}, u32[]{:S(2)}, u32[]{:S(2)}) collective-permute-start(f32[3,1,32,7,128]{4,3,2,1,0:T(8,128)S(1)} %pad_maximum_fusion.2), channel_id=1, source_target_pairs={{1,0},{2,1},{3,2},{5,4},{6,5},{7,6},{9,8},{10,9},{11,10},{13,12},{... | collective-permute-start | bytes 1032200 | tf_op jit(solution)/shard_map/ppermute | solution.py:27
  61.6 7.8 %collective-permute-start.7 = (f32[3,1,32,7,128]{4,3,2,1,0:T(8,128)S(1)}, f32[3,1,32,7,128]{4,3,2,1,0:T(8,128)S(1)}, u32[]{:S(2)}, u32[]{:S(2)}) collective-permute-start(f32[3,1,32,7,128]{4,3,2,1,0:T(8,128)S(1)} %pad_maximum_fusion.2), channel_id=1, source_target_pairs={{0,1},{1,2},{2,3},{4,5},{5,6},{6,7},{8,9},{9,10},{10,11},{12,13},{... | collective-permute-start | bytes 1032200 | tf_op jit(solution)/shard_map/ppermute | solution.py:26

commit v11 on v6

--- a/solution.py
+++ b/solution.py
@@ -16,17 +16,11 @@
     return lax.ppermute(shard, axis, [(i, i ^ 1 << apart) for i in range(lax.axis_size(axis))])
 
 
-def padded(shard, sides, width):
-    for axis, dim in sides:
-        size, length = (lax.axis_size(axis), shard.shape[dim])
-        up = [(i, (i + 1) % size) for i in range(size - 1)]
-        down = [(j, i) for i, j in up]
-        last = lax.slice_in_dim(shard, length - width, length, axis=dim)
-        first = lax.slice_in_dim(shard, 0, width, axis=dim)
-        before = lax.ppermute(last, axis, up)
-        after = lax.ppermute(first, axis, down)
-        shard = jnp.concatenate([before, shard, after], axis=dim)
-    return shard
+def swapped(shard, axis):
+    size = lax.axis_size(axis)
+    first = [(i, i ^ 1) for i in range(size)]
+    second = [(i, i + 1 - 2 * (i % 2 == 0)) for i in range(1, size - 1)]
+    return jnp.concatenate([lax.ppermute(shard, axis, first), shard, lax.ppermute(shard, axis, second)], axis=0)
 
 
 def slot_multipoles(pos, stren, core):
@@ -178,10 +172,10 @@
     source_slot = near_where % nbd
     delta_x = source_device // size_y - column_index
     delta_y = source_device % size_y - row_index
-    direction = (delta_x + 1) * 3 + (delta_y + 1)
-    grid_blocks = padded(blocks[None, None], (("gx", 0), ("gy", 1)), 1)
-    source_pool = grid_blocks.reshape(9 * nbd, 7, blocks.shape[2])
-    pool_index = direction * nbd + source_slot
+    sign_x = 2 * (column_index % 2) - 1
+    sign_y = 2 * (row_index % 2) - 1
+    source_pool = swapped(swapped(blocks, "gx"), "gy")
+    pool_index = ((1 + delta_y * sign_y) * 3 + (1 + delta_x * sign_x)) * nbd + source_slot
     sources_all = source_pool[pool_index]
     targets = blocks[:, 0:3]
     centre = jnp.mean(targets, axis=2)

time: 84.4 us -> 83.5 us (0.989)
  waiting for transfers between devices: 7.65 us -> 12.8 us
  starting transfers between devices: 20.5 us -> 15.4 us
    ppermute x4, waiting for transfers between devices: 4.77 us -> 10.1 us  [the longest x2 6.65 us: swapped(): lax.ppermute(shard, axis, second)]
    ppermute x4, starting transfers between devices: 11.7 us -> 6.62 us  [the longest x2 5.87 us: swapped(): lax.ppermute(shard, axis, second)]
    squeeze x0 -> x1, local copies, waits for them, and re-layouts: none -> 1.05 us  [local(): strength[0, 0]]
    reduce_sum x1, other arithmetic: 1.1 us -> 1.95 us  [slot_multipoles(): jnp.mean(jnp.sum(offset * offset, axis=1), axis=1)]
where the time goes in v11:
time: 83.5 us; the launch traced here: 82.9 us
  other arithmetic  26.9 us (32%)
  local copies, waits for them, and re-layouts  15.4 us (18%)
  starting transfers between devices  15.4 us (18%)
  waiting for transfers between devices  12.8 us (15%)
  between operations  12.4 us (15%)
    reduce_sum x1, other arithmetic, evaluate(): arm_x = jnp.sum(extra[:, 1][:, None, :] * weight, axis=(0, 2))  17.7 us
    ppermute x5, starting transfers between devices, from_partner(): lax.ppermute(shard, axis, [(i, i ^ 1 << apart) for i in range(lax.axis_si...  8.79 us
    ppermute x2, waiting for transfers between devices, swapped(): lax.ppermute(shard, axis, second)  6.65 us
    ppermute x2, starting transfers between devices, swapped(): lax.ppermute(shard, axis, second)  5.87 us
    ppermute x2, waiting for transfers between devices, swapped(): lax.ppermute(shard, axis, first)  3.46 us
    ppermute x5, waiting for transfers between devices, from_partner(): lax.ppermute(shard, axis, [(i, i ^ 1 << apart) for i in range(lax.axis_si...  2.68 us
    reduce_sum x1, other arithmetic, slot_multipoles(): jnp.mean(jnp.sum(offset * offset, axis=1), axis=1)  1.95 us
  transfers between devices with their start and end apart: 9, of which 6 were waited for; matrix products, arithmetic and copies ran while one was open for 16% of the time, Pallas kernels for 0%

profile of v11, /device:TPU:9, one launch (start us, length us, event | category | flops | bytes accessed | tf_op | source)
XLA Modules:
  0.0 82.9 jit_solution(3490800995076483282)
XLA Ops:
  0.0 1.1 %copy_bitcast_fusion = (f32[72,3,128]{2,1,0:T(4,128)S(1)}, f32[72,3,128]{2,1,0:T(4,128)S(1)}) fusion(f32[1,1,72,3,128]{4,2,3,1,0:T(8,128)} %param.9, f32[1,1,72,3,128]{4,2,3,1,0:T(8,128)} %param.8), kind=kLoop, calls=%fused_computation.26 | loop fusion | bytes 442368 | tf_op jit(solution)/shard_map/squeeze | solution.py:127
  1.1 1.0 %reduce_sum.287 = f32[72,3]{0,1:T(4,128)S(1)} reduce(f32[1,1,72,3,128]{4,2,3,1,0:T(8,128)} %param.8, f32[]{:T(128)} %constant.180.clone.1), dimensions={0,1,4}, to_apply=%region_0.0 | reduce | flops 27432 | bytes 111460 | tf_op jit(solution)/shard_map/reduce_sum | solution.py:27
  2.1 1.0 %reduce_sum.288 = f32[72,3]{0,1:T(4,128)S(1)} reduce(f32[1,1,72,3,128]{4,2,3,1,0:T(8,128)} %param.9, f32[]{:T(128)} %constant.180.clone.1), dimensions={0,1,4}, to_apply=%region_1.0 | reduce | flops 27432 | bytes 111460 | tf_op jit(solution)/shard_map/reduce_sum | solution.py:28
  3.2 1.5 %constant_dynamic-slice_fusion.11 = (s32[1,1,1]{1,2,0:T(1,128)}, s32[1,1,1]{1,2,0:T(1,128)}, s32[1,1,1]{1,2,0:T(1,128)}, s32[1,1,1]{1,2,0:T(1,128)}, s32[1,1,1]{...) fusion(s32[5,8,4]{1,2,0:T(4,128)} %param.11, ...), kind=kLoop, calls=%fused_computation.261 | loop fusion | bytes 108 | tf_op jit(solution)/shard_map/dynamic_slice | solution.py:144
  11.5 0.9 %multiply_reduce_fusion.7 = f32[72]{0:T(128)S(1)} fusion(f32[1,1,72,128]{3,2,1,0:T(8,128)} %param.10), kind=kLoop, calls=%fused_computation.81 | loop fusion | flops 18360 | bytes 37152 | tf_op jit(solution)/shard_map/reduce_sum | solution.py:30
  12.4 2.0 %multiply_reduce_fusion.6 = f32[72]{0:T(128)S(1)} fusion(f32[72,3]{1,0:T(8,128)S(1)} %copy.199, f32[1,1,72,3,128]{4,2,3,1,0:T(8,128)} %param.8), kind=kLoop, calls=%fused_computation.28 | loop fusion | flops 82872 | bytes 111744 | tf_op jit(solution)/shard_map/reduce_sum | solution.py:30
  14.4 0.9 %select_maximum_fusion = f32[80,7,128]{2,1,0:T(8,128)S(1)} fusion(f32[72,1,128]{2,1,0:T(1,128)} %bitcast.197, f32[72,3,128]{2,1,0:T(4,128)S(1)} %get-tuple-element.92, f32[72,3,128]{2,1,0:T(4,128)S(1)} %get-tuple-element.93), kind=kLoop, calls=%fused_computation.13 | loop fusion | flops 430080 | bytes 544768 | tf_op jit(solution)/shard_map/concatenate | solution.py:127
  15.4 2.4 %collective-permute-start = (f32[9,7,128]{2,1,0:T(8,128)S(1)}, f32[9,7,128]{2,1,0:T(8,128)S(1)}, u32[]{:S(2)}, u32[]{:S(2)}) collective-permute-start(f32[9,7,128]{2,1,0:T(8,128)S(1)} %pad_maximum_fusion.4), channel_id=1, source_target_pairs={{0,16},{4,20},{8,24},{12,28},{16,0},{20,4},{24,8},{28,12},{1,17},{... | collective-permute-start | bytes 96776 | tf_op jit(solution)/shard_map/ppermute | solution.py:16
  17.7 0.8 copy.213
  18.5 0.7 fusion.58
  21.1 1.4 %gather_fusion.2 = s32[256]{0:T(256)S(1)} fusion(s32[1024]{0:T(1024)S(1)} %copy-done, s32[1024]{0:T(1024)S(1)} %pad_clamp_fusion.1), kind=kCustom, calls=%fused_computation.2 | custom fusion | bytes 3072 | tf_op jit(solution)/shard_map/gather | solution.py:132
  28.1 1.3 %collective-permute-done.1 = f32[10,7,128]{2,1,0:T(8,128)S(1)} collective-permute-done((f32[10,7,128]{2,1,0:T(8,128)S(1)}, f32[10,7,128]{2,1,0:T(8,128)S(1)}, u32[]{:S(2)}, u32[]{:S(2)}) %collective-permute-start.1) | collective-permute-done | bytes 35872 | tf_op jit(solution)/shard_map/ppermute | solution.py:16
  29.4 1.3 %collective-permute-start.2 = (f32[12,7,128]{2,1,0:T(8,128)S(1)}, f32[12,7,128]{2,1,0:T(8,128)S(1)}, u32[]{:S(2)}, u32[]{:S(2)}) collective-permute-start(f32[12,7,128]{2,1,0:T(8,128)S(1)} %pad_maximum_fusion.2), channel_id=1, source_target_pairs={{0,4},{4,0},{8,12},{12,8},{16,20},{20,16},{24,28},{28,24},{1,5},{5... | collective-permute-start | bytes 129032 | tf_op jit(solution)/shard_map/ppermute | solution.py:16
  32.0 1.4 %gather_fusion = s32[256]{0:T(256)S(1)} fusion(s32[1024]{0:T(1024)S(1)} %copy-done, s32[1024]{0:T(1024)S(1)} %get-tuple-element.95), kind=kCustom, calls=%fused_computation | custom fusion | bytes 3072 | tf_op jit(solution)/shard_map/gather | solution.py:170
  33.6 1.3 %collective-permute-start.3 = (f32[16,7,128]{2,1,0:T(8,128)S(1)}, f32[16,7,128]{2,1,0:T(8,128)S(1)}, u32[]{:S(2)}, u32[]{:S(2)}) collective-permute-start(f32[16,7,128]{2,1,0:T(8,128)S(1)} %constant_dynamic-update-slice_fusion), channel_id=1, source_target_pairs={{0,2},{1,3},{2,0},{3,1},{4,6},{5,7},{6,4},{7,5},{8,10},{9,11},{10,... | collective-permute-start | bytes 172040 | tf_op jit(solution)/shard_map/ppermute | solution.py:16
  36.8 3.6 %collective-permute-start.4 = (f32[24,7,128]{2,1,0:T(8,128)S(1)}, f32[24,7,128]{2,1,0:T(8,128)S(1)}, u32[]{:S(2)}, u32[]{:S(2)}) collective-permute-start(f32[24,7,128]{2,1,0:T(8,128)S(1)} %get-tuple-element.55), channel_id=1, source_target_pairs={{0,1},{1,0},{2,3},{3,2},{4,5},{5,4},{6,7},{7,6},{8,9},{9,8},{10,11... | collective-permute-start | bytes 258056 | tf_op jit(solution)/shard_map/ppermute | solution.py:16
  40.4 0.9 %collective-permute-done.4 = f32[24,7,128]{2,1,0:T(8,128)S(1)} collective-permute-done((f32[24,7,128]{2,1,0:T(8,128)S(1)}, f32[24,7,128]{2,1,0:T(8,128)S(1)}, u32[]{:S(2)}, u32[]{:S(2)}) %collective-permute-start.4) | collective-permute-done | bytes 86048 | tf_op jit(solution)/shard_map/ppermute | solution.py:16
  41.4 2.8 %collective-permute-start.6 = (f32[32,7,128]{2,1,0:T(8,128)S(1)}, f32[32,7,128]{2,1,0:T(8,128)S(1)}, u32[]{:S(2)}, u32[]{:S(2)}) collective-permute-start(f32[32,7,128]{2,1,0:T(8,128)S(1)} %slice.242), channel_id=1, source_target_pairs={{4,8},{8,4},{12,16},{16,12},{20,24},{24,20},{5,9},{9,5},{13,17},{1... | collective-permute-start | bytes 344072 | tf_op jit(solution)/shard_map/ppermute | solution.py:23
  45.2 0.7 gather_fusion.3
  49.0 3.5 %collective-permute-done.5 = f32[32,7,128]{2,1,0:T(8,128)S(1)} collective-permute-done((f32[32,7,128]{2,1,0:T(8,128)S(1)}, f32[32,7,128]{2,1,0:T(8,128)S(1)}, u32[]{:S(2)}, u32[]{:S(2)}) %collective-permute-start.5) | collective-permute-done | bytes 114720 | tf_op jit(solution)/shard_map/ppermute | solution.py:23
  53.4 3.1 %collective-permute-start.8 = (f32[96,7,128]{2,1,0:T(8,128)S(1)}, f32[96,7,128]{2,1,0:T(8,128)S(1)}, u32[]{:S(2)}, u32[]{:S(2)}) collective-permute-start(f32[96,7,128]{2,1,0:T(8,128)S(1)} %pad_maximum_fusion.1), channel_id=1, source_target_pairs={{1,2},{2,1},{5,6},{6,5},{9,10},{10,9},{13,14},{14,13},{17,18},{18,... | collective-permute-start | bytes 1032200 | tf_op jit(solution)/shard_map/ppermute | solution.py:23
  56.5 5.9 %collective-permute-done.8 = f32[96,7,128]{2,1,0:T(8,128)S(1)} collective-permute-done((f32[96,7,128]{2,1,0:T(8,128)S(1)}, f32[96,7,128]{2,1,0:T(8,128)S(1)}, u32[]{:S(2)}, u32[]{:S(2)}) %collective-permute-start.8) | collective-permute-done | bytes 344096 | tf_op jit(solution)/shard_map/ppermute | solution.py:23
  62.5 1.0 %gather_fusion.1 = f32[256,7,128]{2,1,0:T(8,128)S(1)} fusion(f32[288,7,128]{2,1,0:T(8,128)S(1)} %constant_dynamic-update-slice_fusion.11, s32[1024]{0:T(1024)S(1)} %pad_clamp_fusion.2), kind=kCustom, calls=%fused_computation.1 | custom fusion | bytes 1836032 | tf_op jit(solution)/shard_map/gather | solution.py:179
  64.5 17.7 %multiply_reduce_fusion.3 = (f32[32,128]{1,0:T(8,128)S(1)}, f32[32,128]{1,0:T(8,128)S(1)}, f32[32,128]{1,0:T(8,128)S(1)}, f32[32,128]{1,0:T(8,128)S(1)}, f32[32,128]{1,0:T(8,128)S(1)}, /*index=5*/f32[32,128]{1,0:T(8,128)S(1)}) fusion(f32[32,8,128]{2,1,0:T(8,128)S(1)} %get-tuple-element.40, f32[32,8,128]{2,1,0:T(8,128)S(1)} %get-tuple-element.41, ...), kind=kLoop, calls=%fused_computation.8 | loop fusion | flops 96444416 | bytes 1458176 | tf_op jit(solution)/shard_map/vmap()/reduce_sum | solution.py:44
  (133 shorter events, 12.4 us)
Async XLA Ops:
  0.0 21.1 %copy-start = (s32[1024]{0:T(1024)S(1)}, s32[1024]{0:T(1024)}, u32[]{:S(2)}) copy-start(s32[1024]{0:T(1024)} %param.12) | copy-start | bytes 12292
  0.0 20.8 %copy-start.1 = (s32[1,1,32,8]{2,3,1,0:T(8,128)S(1)}, s32[1,1,32,8]{2,3,1,0:T(8,128)}, u32[]{:S(2)}) copy-start(s32[1,1,32,8]{2,3,1,0:T(8,128)} %param.14) | copy-start | bytes 3076
  15.4 11.1 %collective-permute-start = (f32[9,7,128]{2,1,0:T(8,128)S(1)}, f32[9,7,128]{2,1,0:T(8,128)S(1)}, u32[]{:S(2)}, u32[]{:S(2)}) collective-permute-start(f32[9,7,128]{2,1,0:T(8,128)S(1)} %pad_maximum_fusion.4), channel_id=1, source_target_pairs={{0,16},{4,20},{8,24},{12,28},{16,0},{20,4},{24,8},{28,12},{1,17},{... | collective-permute-start | bytes 96776 | tf_op jit(solution)/shard_map/ppermute | solution.py:16
  21.1 5.3 %copy-start.2 = (s32[1,1,32,8]{2,3,1,0:T(8,128)S(1)}, s32[1,1,32,8]{2,3,1,0:T(8,128)}, u32[]{:S(2)}) copy-start(s32[1,1,32,8]{2,3,1,0:T(8,128)} %param.13) | copy-start | bytes 3076
  26.5 2.9 %collective-permute-start.1 = (f32[10,7,128]{2,1,0:T(8,128)S(1)}, f32[10,7,128]{2,1,0:T(8,128)S(1)}, u32[]{:S(2)}, u32[]{:S(2)}) collective-permute-start(f32[10,7,128]{2,1,0:T(8,128)S(1)} %pad_maximum_fusion.3), channel_id=1, source_target_pairs={{0,8},{4,12},{8,0},{12,4},{16,24},{20,28},{24,16},{28,20},{1,9},{5... | collective-permute-start | bytes 107528 | tf_op jit(solution)/shard_map/ppermute | solution.py:16
  29.4 4.0 %collective-permute-start.2 = (f32[12,7,128]{2,1,0:T(8,128)S(1)}, f32[12,7,128]{2,1,0:T(8,128)S(1)}, u32[]{:S(2)}, u32[]{:S(2)}) collective-permute-start(f32[12,7,128]{2,1,0:T(8,128)S(1)} %pad_maximum_fusion.2), channel_id=1, source_target_pairs={{0,4},{4,0},{8,12},{12,8},{16,20},{20,16},{24,28},{28,24},{1,5},{5... | collective-permute-start | bytes 129032 | tf_op jit(solution)/shard_map/ppermute | solution.py:16
  33.6 3.2 %collective-permute-start.3 = (f32[16,7,128]{2,1,0:T(8,128)S(1)}, f32[16,7,128]{2,1,0:T(8,128)S(1)}, u32[]{:S(2)}, u32[]{:S(2)}) collective-permute-start(f32[16,7,128]{2,1,0:T(8,128)S(1)} %constant_dynamic-update-slice_fusion), channel_id=1, source_target_pairs={{0,2},{1,3},{2,0},{3,1},{4,6},{5,7},{6,4},{7,5},{8,10},{9,11},{10,... | collective-permute-start | bytes 172040 | tf_op jit(solution)/shard_map/ppermute | solution.py:16
  36.8 4.5 %collective-permute-start.4 = (f32[24,7,128]{2,1,0:T(8,128)S(1)}, f32[24,7,128]{2,1,0:T(8,128)S(1)}, u32[]{:S(2)}, u32[]{:S(2)}) collective-permute-start(f32[24,7,128]{2,1,0:T(8,128)S(1)} %get-tuple-element.55), channel_id=1, source_target_pairs={{0,1},{1,0},{2,3},{3,2},{4,5},{5,4},{6,7},{7,6},{8,9},{9,8},{10,11... | collective-permute-start | bytes 258056 | tf_op jit(solution)/shard_map/ppermute | solution.py:16
  41.4 7.6 %collective-permute-start.6 = (f32[32,7,128]{2,1,0:T(8,128)S(1)}, f32[32,7,128]{2,1,0:T(8,128)S(1)}, u32[]{:S(2)}, u32[]{:S(2)}) collective-permute-start(f32[32,7,128]{2,1,0:T(8,128)S(1)} %slice.242), channel_id=1, source_target_pairs={{4,8},{8,4},{12,16},{16,12},{20,24},{24,20},{5,9},{9,5},{13,17},{1... | collective-permute-start | bytes 344072 | tf_op jit(solution)/shard_map/ppermute | solution.py:23
  44.2 8.2 %collective-permute-start.5 = (f32[32,7,128]{2,1,0:T(8,128)S(1)}, f32[32,7,128]{2,1,0:T(8,128)S(1)}, u32[]{:S(2)}, u32[]{:S(2)}) collective-permute-start(f32[32,7,128]{2,1,0:T(8,128)S(1)} %slice.242), channel_id=1, source_target_pairs={{0,4},{4,0},{8,12},{12,8},{16,20},{20,16},{24,28},{28,24},{1,5},{5... | collective-permute-start | bytes 344072 | tf_op jit(solution)/shard_map/ppermute | solution.py:23
  52.5 4.0 %collective-permute-start.7 = (f32[96,7,128]{2,1,0:T(8,128)S(1)}, f32[96,7,128]{2,1,0:T(8,128)S(1)}, u32[]{:S(2)}, u32[]{:S(2)}) collective-permute-start(f32[96,7,128]{2,1,0:T(8,128)S(1)} %pad_maximum_fusion.1), channel_id=1, source_target_pairs={{0,1},{1,0},{2,3},{3,2},{4,5},{5,4},{6,7},{7,6},{8,9},{9,8},{10,11... | collective-permute-start | bytes 1032200 | tf_op jit(solution)/shard_map/ppermute | solution.py:23
  53.4 9.1 %collective-permute-start.8 = (f32[96,7,128]{2,1,0:T(8,128)S(1)}, f32[96,7,128]{2,1,0:T(8,128)S(1)}, u32[]{:S(2)}, u32[]{:S(2)}) collective-permute-start(f32[96,7,128]{2,1,0:T(8,128)S(1)} %pad_maximum_fusion.1), channel_id=1, source_target_pairs={{1,2},{2,1},{5,6},{6,5},{9,10},{10,9},{13,14},{14,13},{17,18},{18,... | collective-permute-start | bytes 1032200 | tf_op jit(solution)/shard_map/ppermute | solution.py:23

commit v12 on v11

--- a/solution.py
+++ b/solution.py
@@ -21,6 +21,15 @@
     first = [(i, i ^ 1) for i in range(size)]
     second = [(i, i + 1 - 2 * (i % 2 == 0)) for i in range(1, size - 1)]
     return jnp.concatenate([lax.ppermute(shard, axis, first), shard, lax.ppermute(shard, axis, second)], axis=0)
+
+
+def routed(shard, axis):
+    size = lax.axis_size(axis)
+    step = [(i, i + 2 if i % 2 else i - 2) for i in range(size) if 0 <= (i + 2 if i % 2 else i - 2) < size]
+    relayed = lax.ppermute(shard, axis, step)
+    pair = lax.ppermute(jnp.concatenate([shard, relayed], axis=0), axis, [(i, i ^ 1) for i in range(size)])
+    count = shard.shape[0]
+    return jnp.concatenate([pair[:count], shard, pair[count:]], axis=0)
 
 
 def slot_multipoles(pos, stren, core):
@@ -174,7 +183,7 @@
     delta_y = source_device % size_y - row_index
     sign_x = 2 * (column_index % 2) - 1
     sign_y = 2 * (row_index % 2) - 1
-    source_pool = swapped(swapped(blocks, "gx"), "gy")
+    source_pool = swapped(routed(blocks, "gx"), "gy")
     pool_index = ((1 + delta_y * sign_y) * 3 + (1 + delta_x * sign_x)) * nbd + source_slot
     sources_all = source_pool[pool_index]
     targets = blocks[:, 0:3]

time: 83.5 us -> 91.8 us (1.099)
  waiting for transfers between devices: 12.8 us -> 18.4 us
  starting transfers between devices: 15.4 us -> 17.2 us
    ppermute x0 -> x2, waiting for transfers between devices: none -> 9.8 us  [the longest x1 5.37 us: routed(): lax.ppermute(jnp.concatenate([shard, relayed], axis=0), axis, [(i, i ^ 1)...]
    ppermute x2 -> x1, waiting for transfers between devices: 3.46 us -> 0.01 us  [swapped(): lax.ppermute(shard, axis, first)]
    ppermute x0 -> x2, starting transfers between devices: none -> 3.17 us  [the longest x1 2.08 us: routed(): relayed = lax.ppermute(shard, axis, step)]
    ppermute x2 -> x1, starting transfers between devices: 5.87 us -> 3.04 us  [swapped(): lax.ppermute(shard, axis, second)]
    ppermute x2 -> x1, starting transfers between devices: 0.75 us -> 2.17 us  [swapped(): lax.ppermute(shard, axis, first)]
    ppermute x2 -> x1, waiting for transfers between devices: 6.65 us -> 5.94 us  [swapped(): lax.ppermute(shard, axis, second)]
  transfers between devices with their start and end apart: 9 -> 9, of which waited for: 6 -> 6; matrix products, arithmetic and copies ran while one was open for 16% -> 11% of each run, Pallas kernels for 0% -> 0%
where the time goes in v12:
time: 91.8 us; the launch traced here: 90.3 us
  other arithmetic  27 us (29%)
  waiting for transfers between devices  18.4 us (20%)
  starting transfers between devices  17.2 us (19%)
  local copies, waits for them, and re-layouts  15.4 us (17%)
  between operations  12.4 us (14%)
    reduce_sum x1, other arithmetic, evaluate(): arm_x = jnp.sum(extra[:, 1][:, None, :] * weight, axis=(0, 2))  17.7 us
    ppermute x5, starting transfers between devices, from_partner(): lax.ppermute(shard, axis, [(i, i ^ 1 << apart) for i in range(lax.axis_si...  8.79 us
    ppermute x1, waiting for transfers between devices, swapped(): lax.ppermute(shard, axis, second)  5.94 us
    ppermute x1, waiting for transfers between devices, routed(): lax.ppermute(jnp.concatenate([shard, relayed], axis=0), axis, [(i, i ^ 1)...  5.37 us
    ppermute x1, waiting for transfers between devices, routed(): relayed = lax.ppermute(shard, axis, step)  4.43 us
    ppermute x1, starting transfers between devices, swapped(): lax.ppermute(shard, axis, second)  3.04 us
    ppermute x5, waiting for transfers between devices, from_partner(): lax.ppermute(shard, axis, [(i, i ^ 1 << apart) for i in range(lax.axis_si...  2.68 us
    ppermute x1, starting transfers between devices, swapped(): lax.ppermute(shard, axis, first)  2.17 us
  transfers between devices with their start and end apart: 9, of which 6 were waited for; matrix products, arithmetic and copies ran while one was open for 11% of the time, Pallas kernels for 0%

profile of v12, /device:TPU:9, one launch (start us, length us, event | category | flops | bytes accessed | tf_op | source)
XLA Modules:
  0.0 90.3 jit_solution(6559576892388376898)
XLA Ops:
  0.0 1.1 %copy_bitcast_fusion = (f32[72,3,128]{2,1,0:T(4,128)S(1)}, f32[72,3,128]{2,1,0:T(4,128)S(1)}) fusion(f32[1,1,72,3,128]{4,2,3,1,0:T(8,128)} %param.9, f32[1,1,72,3,128]{4,2,3,1,0:T(8,128)} %param.8), kind=kLoop, calls=%fused_computation.27 | loop fusion | bytes 442368 | tf_op jit(solution)/shard_map/squeeze | solution.py:136
  1.1 1.0 %reduce_sum.287 = f32[72,3]{0,1:T(4,128)S(1)} reduce(f32[1,1,72,3,128]{4,2,3,1,0:T(8,128)} %param.8, f32[]{:T(128)} %constant.180.clone.1), dimensions={0,1,4}, to_apply=%region_0.0 | reduce | flops 27432 | bytes 111460 | tf_op jit(solution)/shard_map/reduce_sum | solution.py:36
  2.1 1.0 %reduce_sum.288 = f32[72,3]{0,1:T(4,128)S(1)} reduce(f32[1,1,72,3,128]{4,2,3,1,0:T(8,128)} %param.9, f32[]{:T(128)} %constant.180.clone.1), dimensions={0,1,4}, to_apply=%region_1.0 | reduce | flops 27432 | bytes 111460 | tf_op jit(solution)/shard_map/reduce_sum | solution.py:37
  3.2 1.5 %constant_dynamic-slice_fusion.11 = (s32[1,1,1]{1,2,0:T(1,128)}, s32[1,1,1]{1,2,0:T(1,128)}, s32[1,1,1]{1,2,0:T(1,128)}, s32[1,1,1]{1,2,0:T(1,128)}, s32[1,1,1]{...) fusion(s32[5,8,4]{1,2,0:T(4,128)} %param.11, ...), kind=kLoop, calls=%fused_computation.262 | loop fusion | bytes 108 | tf_op jit(solution)/shard_map/dynamic_slice | solution.py:153
  11.5 0.9 multiply_reduce_fusion.7
  12.4 2.0 %multiply_reduce_fusion.6 = f32[72]{0:T(128)S(1)} fusion(f32[72,3]{1,0:T(8,128)S(1)} %copy.199, f32[1,1,72,3,128]{4,2,3,1,0:T(8,128)} %param.8), kind=kLoop, calls=%fused_computation.29 | loop fusion | flops 82872 | bytes 111744 | tf_op jit(solution)/shard_map/reduce_sum | solution.py:39
  14.4 0.9 select_maximum_fusion
  15.4 2.4 %collective-permute-start = (f32[9,7,128]{2,1,0:T(8,128)S(1)}, f32[9,7,128]{2,1,0:T(8,128)S(1)}, u32[]{:S(2)}, u32[]{:S(2)}) collective-permute-start(f32[9,7,128]{2,1,0:T(8,128)S(1)} %pad_maximum_fusion.5), channel_id=1, source_target_pairs={{0,16},{4,20},{8,24},{12,28},{16,0},{20,4},{24,8},{28,12},{1,17},{... | collective-permute-start | bytes 96776 | tf_op jit(solution)/shard_map/ppermute | solution.py:16
  21.1 1.4 %gather_fusion.2 = s32[256]{0:T(256)S(1)} fusion(s32[1024]{0:T(1024)S(1)} %copy-done, s32[1024]{0:T(1024)S(1)} %pad_clamp_fusion.1), kind=kCustom, calls=%fused_computation.2 | custom fusion | bytes 3072 | tf_op jit(solution)/shard_map/gather | solution.py:141
  28.1 1.3 %collective-permute-done.1 = f32[10,7,128]{2,1,0:T(8,128)S(1)} collective-permute-done((f32[10,7,128]{2,1,0:T(8,128)S(1)}, f32[10,7,128]{2,1,0:T(8,128)S(1)}, u32[]{:S(2)}, u32[]{:S(2)}) %collective-permute-start.1) | collective-permute-done | bytes 35872 | tf_op jit(solution)/shard_map/ppermute | solution.py:16
  29.4 1.3 %collective-permute-start.2 = (f32[12,7,128]{2,1,0:T(8,128)S(1)}, f32[12,7,128]{2,1,0:T(8,128)S(1)}, u32[]{:S(2)}, u32[]{:S(2)}) collective-permute-start(f32[12,7,128]{2,1,0:T(8,128)S(1)} %pad_maximum_fusion.3), channel_id=1, source_target_pairs={{0,4},{4,0},{8,12},{12,8},{16,20},{20,16},{24,28},{28,24},{1,5},{5... | collective-permute-start | bytes 129032 | tf_op jit(solution)/shard_map/ppermute | solution.py:16
  32.0 1.4 %gather_fusion = s32[256]{0:T(256)S(1)} fusion(s32[1024]{0:T(1024)S(1)} %copy-done, s32[1024]{0:T(1024)S(1)} %get-tuple-element.97), kind=kCustom, calls=%fused_computation | custom fusion | bytes 3072 | tf_op jit(solution)/shard_map/gather | solution.py:179
  33.6 1.3 %collective-permute-start.3 = (f32[16,7,128]{2,1,0:T(8,128)S(1)}, f32[16,7,128]{2,1,0:T(8,128)S(1)}, u32[]{:S(2)}, u32[]{:S(2)}) collective-permute-start(f32[16,7,128]{2,1,0:T(8,128)S(1)} %constant_dynamic-update-slice_fusion), channel_id=1, source_target_pairs={{0,2},{1,3},{2,0},{3,1},{4,6},{5,7},{6,4},{7,5},{8,10},{9,11},{10,... | collective-permute-start | bytes 172040 | tf_op jit(solution)/shard_map/ppermute | solution.py:16
  36.8 3.6 %collective-permute-start.4 = (f32[24,7,128]{2,1,0:T(8,128)S(1)}, f32[24,7,128]{2,1,0:T(8,128)S(1)}, u32[]{:S(2)}, u32[]{:S(2)}) collective-permute-start(f32[24,7,128]{2,1,0:T(8,128)S(1)} %get-tuple-element.57), channel_id=1, source_target_pairs={{0,1},{1,0},{2,3},{3,2},{4,5},{5,4},{6,7},{7,6},{8,9},{9,8},{10,11... | collective-permute-start | bytes 258056 | tf_op jit(solution)/shard_map/ppermute | solution.py:16
  40.4 0.9 %collective-permute-done.4 = f32[24,7,128]{2,1,0:T(8,128)S(1)} collective-permute-done((f32[24,7,128]{2,1,0:T(8,128)S(1)}, f32[24,7,128]{2,1,0:T(8,128)S(1)}, u32[]{:S(2)}, u32[]{:S(2)}) %collective-permute-start.4) | collective-permute-done | bytes 86048 | tf_op jit(solution)/shard_map/ppermute | solution.py:16
  44.9 2.1 %collective-permute-start.5 = (f32[32,7,128]{2,1,0:T(8,128)S(1)}, f32[32,7,128]{2,1,0:T(8,128)S(1)}, u32[]{:S(2)}, u32[]{:S(2)}) collective-permute-start(f32[32,7,128]{2,1,0:T(8,128)S(1)} %slice.250), channel_id=1, source_target_pairs={{4,12},{8,0},{12,20},{16,8},{20,28},{24,16},{5,13},{9,1},{13,21},{... | collective-permute-start | bytes 344072 | tf_op jit(solution)/shard_map/ppermute | solution.py:29
  47.1 4.4 %collective-permute-done.5 = f32[32,7,128]{2,1,0:T(8,128)S(1)} collective-permute-done((f32[32,7,128]{2,1,0:T(8,128)S(1)}, f32[32,7,128]{2,1,0:T(8,128)S(1)}, u32[]{:S(2)}, u32[]{:S(2)}) %collective-permute-start.5) | collective-permute-done | bytes 114720 | tf_op jit(solution)/shard_map/ppermute | solution.py:29
  51.5 1.1 %collective-permute-start.6 = (f32[64,7,128]{2,1,0:T(8,128)S(1)}, f32[64,7,128]{2,1,0:T(8,128)S(1)}, u32[]{:S(2)}, u32[]{:S(2)}) collective-permute-start(f32[64,7,128]{2,1,0:T(8,128)S(1)} %pad_maximum_fusion.2), channel_id=1, source_target_pairs={{0,4},{4,0},{8,12},{12,8},{16,20},{20,16},{24,28},{28,24},{1,5},{5... | collective-permute-start | bytes 688136 | tf_op jit(solution)/shard_map/ppermute | solution.py:30
  52.8 5.4 %collective-permute-done.6 = f32[64,7,128]{2,1,0:T(8,128)S(1)} collective-permute-done((f32[64,7,128]{2,1,0:T(8,128)S(1)}, f32[64,7,128]{2,1,0:T(8,128)S(1)}, u32[]{:S(2)}, u32[]{:S(2)}) %collective-permute-start.6) | collective-permute-done | bytes 229408 | tf_op jit(solution)/shard_map/ppermute | solution.py:30
  58.3 2.2 %collective-permute-start.7 = (f32[96,7,128]{2,1,0:T(8,128)S(1)}, f32[96,7,128]{2,1,0:T(8,128)S(1)}, u32[]{:S(2)}, u32[]{:S(2)}) collective-permute-start(f32[96,7,128]{2,1,0:T(8,128)S(1)} %pad_maximum_fusion.1), channel_id=1, source_target_pairs={{0,1},{1,0},{2,3},{3,2},{4,5},{5,4},{6,7},{7,6},{8,9},{9,8},{10,11... | collective-permute-start | bytes 1032200 | tf_op jit(solution)/shard_map/ppermute | solution.py:23
  60.8 3.0 %collective-permute-start.8 = (f32[96,7,128]{2,1,0:T(8,128)S(1)}, f32[96,7,128]{2,1,0:T(8,128)S(1)}, u32[]{:S(2)}, u32[]{:S(2)}) collective-permute-start(f32[96,7,128]{2,1,0:T(8,128)S(1)} %pad_maximum_fusion.1), channel_id=1, source_target_pairs={{1,2},{2,1},{5,6},{6,5},{9,10},{10,9},{13,14},{14,13},{17,18},{18,... | collective-permute-start | bytes 1032200 | tf_op jit(solution)/shard_map/ppermute | solution.py:23
  64.0 5.9 %collective-permute-done.8 = f32[96,7,128]{2,1,0:T(8,128)S(1)} collective-permute-done((f32[96,7,128]{2,1,0:T(8,128)S(1)}, f32[96,7,128]{2,1,0:T(8,128)S(1)}, u32[]{:S(2)}, u32[]{:S(2)}) %collective-permute-start.8) | collective-permute-done | bytes 344096 | tf_op jit(solution)/shard_map/ppermute | solution.py:23
  69.9 1.0 %gather_fusion.1 = f32[256,7,128]{2,1,0:T(8,128)S(1)} fusion(f32[288,7,128]{2,1,0:T(8,128)S(1)} %constant_dynamic-update-slice_fusion.11, s32[1024]{0:T(1024)S(1)} %pad_clamp_fusion.2), kind=kCustom, calls=%fused_computation.1 | custom fusion | bytes 1836032 | tf_op jit(solution)/shard_map/gather | solution.py:188
  71.9 17.7 %multiply_reduce_fusion.3 = (f32[32,128]{1,0:T(8,128)S(1)}, f32[32,128]{1,0:T(8,128)S(1)}, f32[32,128]{1,0:T(8,128)S(1)}, f32[32,128]{1,0:T(8,128)S(1)}, f32[32,128]{1,0:T(8,128)S(1)}, /*index=5*/f32[32,128]{1,0:T(8,128)S(1)}) fusion(f32[32,8,128]{2,1,0:T(8,128)S(1)} %get-tuple-element.40, f32[32,8,128]{2,1,0:T(8,128)S(1)} %get-tuple-element.41, ...), kind=kLoop, calls=%fused_computation.8 | loop fusion | flops 96444416 | bytes 1458176 | tf_op jit(solution)/shard_map/vmap()/reduce_sum | solution.py:53
  (135 shorter events, 13.3 us)
Async XLA Ops:
  0.0 21.1 %copy-start = (s32[1024]{0:T(1024)S(1)}, s32[1024]{0:T(1024)}, u32[]{:S(2)}) copy-start(s32[1024]{0:T(1024)} %param.12) | copy-start | bytes 12292
  0.0 20.8 %copy-start.1 = (s32[1,1,32,8]{2,3,1,0:T(8,128)S(1)}, s32[1,1,32,8]{2,3,1,0:T(8,128)}, u32[]{:S(2)}) copy-start(s32[1,1,32,8]{2,3,1,0:T(8,128)} %param.14) | copy-start | bytes 3076
  15.4 11.1 %collective-permute-start = (f32[9,7,128]{2,1,0:T(8,128)S(1)}, f32[9,7,128]{2,1,0:T(8,128)S(1)}, u32[]{:S(2)}, u32[]{:S(2)}) collective-permute-start(f32[9,7,128]{2,1,0:T(8,128)S(1)} %pad_maximum_fusion.5), channel_id=1, source_target_pairs={{0,16},{4,20},{8,24},{12,28},{16,0},{20,4},{24,8},{28,12},{1,17},{... | collective-permute-start | bytes 96776 | tf_op jit(solution)/shard_map/ppermute | solution.py:16
  21.1 5.3 %copy-start.2 = (s32[1,1,32,8]{2,3,1,0:T(8,128)S(1)}, s32[1,1,32,8]{2,3,1,0:T(8,128)}, u32[]{:S(2)}) copy-start(s32[1,1,32,8]{2,3,1,0:T(8,128)} %param.13) | copy-start | bytes 3076
  26.5 2.9 %collective-permute-start.1 = (f32[10,7,128]{2,1,0:T(8,128)S(1)}, f32[10,7,128]{2,1,0:T(8,128)S(1)}, u32[]{:S(2)}, u32[]{:S(2)}) collective-permute-start(f32[10,7,128]{2,1,0:T(8,128)S(1)} %pad_maximum_fusion.4), channel_id=1, source_target_pairs={{0,8},{4,12},{8,0},{12,4},{16,24},{20,28},{24,16},{28,20},{1,9},{5... | collective-permute-start | bytes 107528 | tf_op jit(solution)/shard_map/ppermute | solution.py:16
  29.4 4.0 %collective-permute-start.2 = (f32[12,7,128]{2,1,0:T(8,128)S(1)}, f32[12,7,128]{2,1,0:T(8,128)S(1)}, u32[]{:S(2)}, u32[]{:S(2)}) collective-permute-start(f32[12,7,128]{2,1,0:T(8,128)S(1)} %pad_maximum_fusion.3), channel_id=1, source_target_pairs={{0,4},{4,0},{8,12},{12,8},{16,20},{20,16},{24,28},{28,24},{1,5},{5... | collective-permute-start | bytes 129032 | tf_op jit(solution)/shard_map/ppermute | solution.py:16
  33.6 3.2 %collective-permute-start.3 = (f32[16,7,128]{2,1,0:T(8,128)S(1)}, f32[16,7,128]{2,1,0:T(8,128)S(1)}, u32[]{:S(2)}, u32[]{:S(2)}) collective-permute-start(f32[16,7,128]{2,1,0:T(8,128)S(1)} %constant_dynamic-update-slice_fusion), channel_id=1, source_target_pairs={{0,2},{1,3},{2,0},{3,1},{4,6},{5,7},{6,4},{7,5},{8,10},{9,11},{10,... | collective-permute-start | bytes 172040 | tf_op jit(solution)/shard_map/ppermute | solution.py:16
  36.8 4.5 %collective-permute-start.4 = (f32[24,7,128]{2,1,0:T(8,128)S(1)}, f32[24,7,128]{2,1,0:T(8,128)S(1)}, u32[]{:S(2)}, u32[]{:S(2)}) collective-permute-start(f32[24,7,128]{2,1,0:T(8,128)S(1)} %get-tuple-element.57), channel_id=1, source_target_pairs={{0,1},{1,0},{2,3},{3,2},{4,5},{5,4},{6,7},{7,6},{8,9},{9,8},{10,11... | collective-permute-start | bytes 258056 | tf_op jit(solution)/shard_map/ppermute | solution.py:16
  44.9 6.6 %collective-permute-start.5 = (f32[32,7,128]{2,1,0:T(8,128)S(1)}, f32[32,7,128]{2,1,0:T(8,128)S(1)}, u32[]{:S(2)}, u32[]{:S(2)}) collective-permute-start(f32[32,7,128]{2,1,0:T(8,128)S(1)} %slice.250), channel_id=1, source_target_pairs={{4,12},{8,0},{12,20},{16,8},{20,28},{24,16},{5,13},{9,1},{13,21},{... | collective-permute-start | bytes 344072 | tf_op jit(solution)/shard_map/ppermute | solution.py:29
  51.5 6.7 %collective-permute-start.6 = (f32[64,7,128]{2,1,0:T(8,128)S(1)}, f32[64,7,128]{2,1,0:T(8,128)S(1)}, u32[]{:S(2)}, u32[]{:S(2)}) collective-permute-start(f32[64,7,128]{2,1,0:T(8,128)S(1)} %pad_maximum_fusion.2), channel_id=1, source_target_pairs={{0,4},{4,0},{8,12},{12,8},{16,20},{20,16},{24,28},{28,24},{1,5},{5... | collective-permute-start | bytes 688136 | tf_op jit(solution)/shard_map/ppermute | solution.py:30
  58.3 5.6 %collective-permute-start.7 = (f32[96,7,128]{2,1,0:T(8,128)S(1)}, f32[96,7,128]{2,1,0:T(8,128)S(1)}, u32[]{:S(2)}, u32[]{:S(2)}) collective-permute-start(f32[96,7,128]{2,1,0:T(8,128)S(1)} %pad_maximum_fusion.1), channel_id=1, source_target_pairs={{0,1},{1,0},{2,3},{3,2},{4,5},{5,4},{6,7},{7,6},{8,9},{9,8},{10,11... | collective-permute-start | bytes 1032200 | tf_op jit(solution)/shard_map/ppermute | solution.py:23
  60.8 9.1 %collective-permute-start.8 = (f32[96,7,128]{2,1,0:T(8,128)S(1)}, f32[96,7,128]{2,1,0:T(8,128)S(1)}, u32[]{:S(2)}, u32[]{:S(2)}) collective-permute-start(f32[96,7,128]{2,1,0:T(8,128)S(1)} %pad_maximum_fusion.1), channel_id=1, source_target_pairs={{1,2},{2,1},{5,6},{6,5},{9,10},{10,9},{13,14},{14,13},{17,18},{18,... | collective-permute-start | bytes 1032200 | tf_op jit(solution)/shard_map/ppermute | solution.py:23

commit v13 on v11

--- a/solution.py
+++ b/solution.py
@@ -24,10 +24,16 @@
 
 
 def slot_multipoles(pos, stren, core):
-    centre = jnp.mean(pos, axis=2)
-    total = jnp.sum(stren, axis=2)
+    lanes = pos.shape[-1]
+    ones = jnp.ones((lanes,), jnp.float32)
+    exact = lax.Precision.HIGHEST
+    centre = jnp.einsum("scl,l->sc", pos, ones, precision=exact) / lanes
+    total = jnp.einsum("scl,l->sc", stren, ones, precision=exact)
     offset = pos - centre[:, :, None]
-    spread = jnp.mean(core * core, axis=1) + jnp.mean(jnp.sum(offset * offset, axis=1), axis=1)
+    spread = (
+        jnp.einsum("sl,l->s", core * core, ones, precision=exact) / lanes
+        + jnp.einsum("scl,l->s", offset * offset, ones, precision=exact) / lanes
+    )
     return jnp.concatenate([centre, total, spread[:, None]], axis=1)
 
 

time: 83.5 us -> 79.4 us (0.951)
  other arithmetic: 26.9 us -> 22.5 us
  matrix products: 0 us -> 1.71 us
  local copies, waits for them, and re-layouts: 15.4 us -> 14.1 us
    reduce_sum x4 -> x1, other arithmetic: 4.91 us -> 1.08 us  [slot_multipoles(): jnp.einsum('scl,l->s', offset * offset, ones, precision=exact) / lanes]
    dot_general x0 -> x4, matrix products: none -> 1.71 us  [the longest x1 0.93 us: slot_multipoles(): jnp.einsum('sl,l->s', core * core, ones, precision=exact) / lanes]
  transfers between devices with their start and end apart: 9 -> 9, of which waited for: 6 -> 6; matrix products, arithmetic and copies ran while one was open for 16% -> 14% of each run, Pallas kernels for 0% -> 0%
where the time goes in v13:
time: 79.4 us; the launch traced here: 78.9 us
  other arithmetic  22.5 us (28%)
  starting transfers between devices  15.4 us (19%)
  local copies, waits for them, and re-layouts  14.1 us (18%)
  waiting for transfers between devices  12.8 us (16%)
  between operations  12.4 us (16%)
  matrix products  1.71 us (2%)
    reduce_sum x1, other arithmetic, evaluate(): arm_x = jnp.sum(extra[:, 1][:, None, :] * weight, axis=(0, 2))  17.7 us
    ppermute x5, starting transfers between devices, from_partner(): lax.ppermute(shard, axis, [(i, i ^ 1 << apart) for i in range(lax.axis_si...  8.78 us
    ppermute x2, waiting for transfers between devices, swapped(): lax.ppermute(shard, axis, second)  6.64 us
    ppermute x2, starting transfers between devices, swapped(): lax.ppermute(shard, axis, second)  5.9 us
    ppermute x2, waiting for transfers between devices, swapped(): lax.ppermute(shard, axis, first)  3.46 us
    ppermute x5, waiting for transfers between devices, from_partner(): lax.ppermute(shard, axis, [(i, i ^ 1 << apart) for i in range(lax.axis_si...  2.68 us
  transfers between devices with their start and end apart: 9, of which 6 were waited for; matrix products, arithmetic and copies ran while one was open for 14% of the time, Pallas kernels for 0%

profile of v13, /device:TPU:9, one launch (start us, length us, event | category | flops | bytes accessed | tf_op | source)
XLA Modules:
  0.0 78.9 jit_solution(14133361140373628398)
XLA Ops:
  0.0 0.9 %convolution_bitcast_fusion.1 = f32[72]{0:T(128)S(1)} fusion(f32[1,1,72,128]{3,2,1,0:T(8,128)} %param.10), kind=kOutput, calls=%fused_computation.13 | convolution fusion | flops 119808 | bytes 37152 | tf_op jit(solution)/shard_map/sl,l->s/dot_general | solution.py:34
  1.0 1.1 %copy_bitcast_fusion = (f32[72,3,128]{2,1,0:T(4,128)S(1)}, f32[72,3,128]{2,1,0:T(4,128)S(1)}) fusion(f32[1,1,72,3,128]{4,2,3,1,0:T(8,128)} %param.9, f32[1,1,72,3,128]{4,2,3,1,0:T(8,128)} %param.8), kind=kLoop, calls=%fused_computation.31 | loop fusion | bytes 442368 | tf_op jit(solution)/shard_map/squeeze | solution.py:133
  2.7 0.9 %select_maximum_fusion = f32[80,7,128]{2,1,0:T(8,128)S(1)} fusion(f32[72,1,128]{2,1,0:T(1,128)} %bitcast.221, f32[72,3,128]{2,1,0:T(4,128)S(1)} %get-tuple-element.92, f32[72,3,128]{2,1,0:T(4,128)S(1)} %get-tuple-element.93), kind=kLoop, calls=%fused_computation.18 | loop fusion | flops 430080 | bytes 544768 | tf_op jit(solution)/shard_map/concatenate | solution.py:133
  3.6 1.5 %constant_dynamic-slice_fusion.11 = (s32[1,1,1]{1,2,0:T(1,128)}, s32[1,1,1]{1,2,0:T(1,128)}, s32[1,1,1]{1,2,0:T(1,128)}, s32[1,1,1]{1,2,0:T(1,128)}, s32[1,1,1]{...) fusion(s32[5,8,4]{1,2,0:T(4,128)} %param.11, ...), kind=kLoop, calls=%fused_computation.270 | loop fusion | bytes 108 | tf_op jit(solution)/shard_map/dynamic_slice | solution.py:150
  12.1 1.1 %multiply_reduce_fusion.6 = f32[72,128]{1,0:T(8,128)S(1)} fusion(f32[72,3]{1,0:T(8,128)S(1)} %copy.199, f32[1,1,72,3,128]{4,2,3,1,0:T(8,128)} %param.8), kind=kLoop, calls=%fused_computation.33 | loop fusion | flops 73728 | bytes 148320 | tf_op jit(solution)/shard_map/scl,l->s/reduce_sum | solution.py:35
  13.5 2.4 %collective-permute-start = (f32[9,7,128]{2,1,0:T(8,128)S(1)}, f32[9,7,128]{2,1,0:T(8,128)S(1)}, u32[]{:S(2)}, u32[]{:S(2)}) collective-permute-start(f32[9,7,128]{2,1,0:T(8,128)S(1)} %pad_maximum_fusion.4), channel_id=1, source_target_pairs={{0,16},{4,20},{8,24},{12,28},{16,0},{20,4},{24,8},{28,12},{1,17},{... | collective-permute-start | bytes 96776 | tf_op jit(solution)/shard_map/ppermute | solution.py:16
  17.1 1.4 %gather_fusion.2 = s32[256]{0:T(256)S(1)} fusion(s32[1024]{0:T(1024)S(1)} %copy-done, s32[1024]{0:T(1024)S(1)} %pad_clamp_fusion.1), kind=kCustom, calls=%fused_computation.2 | custom fusion | bytes 3072 | tf_op jit(solution)/shard_map/gather | solution.py:138
  24.2 1.3 %collective-permute-done.1 = f32[10,7,128]{2,1,0:T(8,128)S(1)} collective-permute-done((f32[10,7,128]{2,1,0:T(8,128)S(1)}, f32[10,7,128]{2,1,0:T(8,128)S(1)}, u32[]{:S(2)}, u32[]{:S(2)}) %collective-permute-start.1) | collective-permute-done | bytes 35872 | tf_op jit(solution)/shard_map/ppermute | solution.py:16
  25.5 1.3 %collective-permute-start.2 = (f32[12,7,128]{2,1,0:T(8,128)S(1)}, f32[12,7,128]{2,1,0:T(8,128)S(1)}, u32[]{:S(2)}, u32[]{:S(2)}) collective-permute-start(f32[12,7,128]{2,1,0:T(8,128)S(1)} %pad_maximum_fusion.2), channel_id=1, source_target_pairs={{0,4},{4,0},{8,12},{12,8},{16,20},{20,16},{24,28},{28,24},{1,5},{5... | collective-permute-start | bytes 129032 | tf_op jit(solution)/shard_map/ppermute | solution.py:16
  28.1 1.4 %gather_fusion = s32[256]{0:T(256)S(1)} fusion(s32[1024]{0:T(1024)S(1)} %copy-done, s32[1024]{0:T(1024)S(1)} %get-tuple-element.95), kind=kCustom, calls=%fused_computation | custom fusion | bytes 3072 | tf_op jit(solution)/shard_map/gather | solution.py:176
  29.6 1.3 %collective-permute-start.3 = (f32[16,7,128]{2,1,0:T(8,128)S(1)}, f32[16,7,128]{2,1,0:T(8,128)S(1)}, u32[]{:S(2)}, u32[]{:S(2)}) collective-permute-start(f32[16,7,128]{2,1,0:T(8,128)S(1)} %constant_dynamic-update-slice_fusion), channel_id=1, source_target_pairs={{0,2},{1,3},{2,0},{3,1},{4,6},{5,7},{6,4},{7,5},{8,10},{9,11},{10,... | collective-permute-start | bytes 172040 | tf_op jit(solution)/shard_map/ppermute | solution.py:16
  32.9 3.6 %collective-permute-start.4 = (f32[24,7,128]{2,1,0:T(8,128)S(1)}, f32[24,7,128]{2,1,0:T(8,128)S(1)}, u32[]{:S(2)}, u32[]{:S(2)}) collective-permute-start(f32[24,7,128]{2,1,0:T(8,128)S(1)} %get-tuple-element.55), channel_id=1, source_target_pairs={{0,1},{1,0},{2,3},{3,2},{4,5},{5,4},{6,7},{7,6},{8,9},{9,8},{10,11... | collective-permute-start | bytes 258056 | tf_op jit(solution)/shard_map/ppermute | solution.py:16
  36.5 0.9 %collective-permute-done.4 = f32[24,7,128]{2,1,0:T(8,128)S(1)} collective-permute-done((f32[24,7,128]{2,1,0:T(8,128)S(1)}, f32[24,7,128]{2,1,0:T(8,128)S(1)}, u32[]{:S(2)}, u32[]{:S(2)}) %collective-permute-start.4) | collective-permute-done | bytes 86048 | tf_op jit(solution)/shard_map/ppermute | solution.py:16
  37.4 2.8 %collective-permute-start.6 = (f32[32,7,128]{2,1,0:T(8,128)S(1)}, f32[32,7,128]{2,1,0:T(8,128)S(1)}, u32[]{:S(2)}, u32[]{:S(2)}) collective-permute-start(f32[32,7,128]{2,1,0:T(8,128)S(1)} %slice.242), channel_id=1, source_target_pairs={{4,8},{8,4},{12,16},{16,12},{20,24},{24,20},{5,9},{9,5},{13,17},{1... | collective-permute-start | bytes 344072 | tf_op jit(solution)/shard_map/ppermute | solution.py:23
  40.6 0.6 copy.220
  41.2 0.7 gather_fusion.3
  44.3 0.7 collective-permute-done.6
  45.0 3.5 %collective-permute-done.5 = f32[32,7,128]{2,1,0:T(8,128)S(1)} collective-permute-done((f32[32,7,128]{2,1,0:T(8,128)S(1)}, f32[32,7,128]{2,1,0:T(8,128)S(1)}, u32[]{:S(2)}, u32[]{:S(2)}) %collective-permute-start.5) | collective-permute-done | bytes 114720 | tf_op jit(solution)/shard_map/ppermute | solution.py:23
  49.4 3.1 %collective-permute-start.8 = (f32[96,7,128]{2,1,0:T(8,128)S(1)}, f32[96,7,128]{2,1,0:T(8,128)S(1)}, u32[]{:S(2)}, u32[]{:S(2)}) collective-permute-start(f32[96,7,128]{2,1,0:T(8,128)S(1)} %pad_maximum_fusion.1), channel_id=1, source_target_pairs={{1,2},{2,1},{5,6},{6,5},{9,10},{10,9},{13,14},{14,13},{17,18},{18,... | collective-permute-start | bytes 1032200 | tf_op jit(solution)/shard_map/ppermute | solution.py:23
  52.6 5.9 %collective-permute-done.8 = f32[96,7,128]{2,1,0:T(8,128)S(1)} collective-permute-done((f32[96,7,128]{2,1,0:T(8,128)S(1)}, f32[96,7,128]{2,1,0:T(8,128)S(1)}, u32[]{:S(2)}, u32[]{:S(2)}) %collective-permute-start.8) | collective-permute-done | bytes 344096 | tf_op jit(solution)/shard_map/ppermute | solution.py:23
  58.5 1.0 %gather_fusion.1 = f32[256,7,128]{2,1,0:T(8,128)S(1)} fusion(f32[288,7,128]{2,1,0:T(8,128)S(1)} %constant_dynamic-update-slice_fusion.11, s32[1024]{0:T(1024)S(1)} %pad_clamp_fusion.2), kind=kCustom, calls=%fused_computation.1 | custom fusion | bytes 1836032 | tf_op jit(solution)/shard_map/gather | solution.py:185
  59.6 0.6 fusion.72
  60.5 17.7 %multiply_reduce_fusion.3 = (f32[32,128]{1,0:T(8,128)S(1)}, f32[32,128]{1,0:T(8,128)S(1)}, f32[32,128]{1,0:T(8,128)S(1)}, f32[32,128]{1,0:T(8,128)S(1)}, f32[32,128]{1,0:T(8,128)S(1)}, /*index=5*/f32[32,128]{1,0:T(8,128)S(1)}) fusion(f32[32,8,128]{2,1,0:T(8,128)S(1)} %get-tuple-element.40, f32[32,8,128]{2,1,0:T(8,128)S(1)} %get-tuple-element.41, ...), kind=kLoop, calls=%fused_computation.8 | loop fusion | flops 96444416 | bytes 1458176 | tf_op jit(solution)/shard_map/vmap()/reduce_sum | solution.py:50
  78.3 0.6 fusion.17
  (139 shorter events, 10.2 us)
Async XLA Ops:
  0.0 17.1 %copy-start = (s32[1024]{0:T(1024)S(1)}, s32[1024]{0:T(1024)}, u32[]{:S(2)}) copy-start(s32[1024]{0:T(1024)} %param.12) | copy-start | bytes 12292
  0.0 16.1 %copy-start.4 = (s32[5]{0:T(128)S(1)}, s32[5]{0:T(128)}, u32[]{:S(2)}) copy-start(s32[5]{0:T(128)} %constant.216) | copy-start | bytes 64
  0.0 15.9 %copy-start.1 = (s32[5,8,4]{1,2,0:T(4,128)S(1)}, s32[5,8,4]{1,2,0:T(4,128)}, u32[]{:S(2)}) copy-start(s32[5,8,4]{1,2,0:T(4,128)} %param.11) | copy-start | bytes 1924
  0.0 16.9 %copy-start.2 = (s32[1,1,32,8]{2,3,1,0:T(8,128)S(1)}, s32[1,1,32,8]{2,3,1,0:T(8,128)}, u32[]{:S(2)}) copy-start(s32[1,1,32,8]{2,3,1,0:T(8,128)} %param.14) | copy-start | bytes 3076
  13.5 9.0 %collective-permute-start = (f32[9,7,128]{2,1,0:T(8,128)S(1)}, f32[9,7,128]{2,1,0:T(8,128)S(1)}, u32[]{:S(2)}, u32[]{:S(2)}) collective-permute-start(f32[9,7,128]{2,1,0:T(8,128)S(1)} %pad_maximum_fusion.4), channel_id=1, source_target_pairs={{0,16},{4,20},{8,24},{12,28},{16,0},{20,4},{24,8},{28,12},{1,17},{... | collective-permute-start | bytes 96776 | tf_op jit(solution)/shard_map/ppermute | solution.py:16
  17.1 5.3 %copy-start.3 = (s32[1,1,32,8]{2,3,1,0:T(8,128)S(1)}, s32[1,1,32,8]{2,3,1,0:T(8,128)}, u32[]{:S(2)}) copy-start(s32[1,1,32,8]{2,3,1,0:T(8,128)} %param.13) | copy-start | bytes 3076
  22.5 2.9 %collective-permute-start.1 = (f32[10,7,128]{2,1,0:T(8,128)S(1)}, f32[10,7,128]{2,1,0:T(8,128)S(1)}, u32[]{:S(2)}, u32[]{:S(2)}) collective-permute-start(f32[10,7,128]{2,1,0:T(8,128)S(1)} %pad_maximum_fusion.3), channel_id=1, source_target_pairs={{0,8},{4,12},{8,0},{12,4},{16,24},{20,28},{24,16},{28,20},{1,9},{5... | collective-permute-start | bytes 107528 | tf_op jit(solution)/shard_map/ppermute | solution.py:16
  25.5 4.0 %collective-permute-start.2 = (f32[12,7,128]{2,1,0:T(8,128)S(1)}, f32[12,7,128]{2,1,0:T(8,128)S(1)}, u32[]{:S(2)}, u32[]{:S(2)}) collective-permute-start(f32[12,7,128]{2,1,0:T(8,128)S(1)} %pad_maximum_fusion.2), channel_id=1, source_target_pairs={{0,4},{4,0},{8,12},{12,8},{16,20},{20,16},{24,28},{28,24},{1,5},{5... | collective-permute-start | bytes 129032 | tf_op jit(solution)/shard_map/ppermute | solution.py:16
  29.6 3.2 %collective-permute-start.3 = (f32[16,7,128]{2,1,0:T(8,128)S(1)}, f32[16,7,128]{2,1,0:T(8,128)S(1)}, u32[]{:S(2)}, u32[]{:S(2)}) collective-permute-start(f32[16,7,128]{2,1,0:T(8,128)S(1)} %constant_dynamic-update-slice_fusion), channel_id=1, source_target_pairs={{0,2},{1,3},{2,0},{3,1},{4,6},{5,7},{6,4},{7,5},{8,10},{9,11},{10,... | collective-permute-start | bytes 172040 | tf_op jit(solution)/shard_map/ppermute | solution.py:16
  32.9 4.5 %collective-permute-start.4 = (f32[24,7,128]{2,1,0:T(8,128)S(1)}, f32[24,7,128]{2,1,0:T(8,128)S(1)}, u32[]{:S(2)}, u32[]{:S(2)}) collective-permute-start(f32[24,7,128]{2,1,0:T(8,128)S(1)} %get-tuple-element.55), channel_id=1, source_target_pairs={{0,1},{1,0},{2,3},{3,2},{4,5},{5,4},{6,7},{7,6},{8,9},{9,8},{10,11... | collective-permute-start | bytes 258056 | tf_op jit(solution)/shard_map/ppermute | solution.py:16
  37.4 7.6 %collective-permute-start.6 = (f32[32,7,128]{2,1,0:T(8,128)S(1)}, f32[32,7,128]{2,1,0:T(8,128)S(1)}, u32[]{:S(2)}, u32[]{:S(2)}) collective-permute-start(f32[32,7,128]{2,1,0:T(8,128)S(1)} %slice.242), channel_id=1, source_target_pairs={{4,8},{8,4},{12,16},{16,12},{20,24},{24,20},{5,9},{9,5},{13,17},{1... | collective-permute-start | bytes 344072 | tf_op jit(solution)/shard_map/ppermute | solution.py:23
  40.3 8.2 %collective-permute-start.5 = (f32[32,7,128]{2,1,0:T(8,128)S(1)}, f32[32,7,128]{2,1,0:T(8,128)S(1)}, u32[]{:S(2)}, u32[]{:S(2)}) collective-permute-start(f32[32,7,128]{2,1,0:T(8,128)S(1)} %slice.242), channel_id=1, source_target_pairs={{0,4},{4,0},{8,12},{12,8},{16,20},{20,16},{24,28},{28,24},{1,5},{5... | collective-permute-start | bytes 344072 | tf_op jit(solution)/shard_map/ppermute | solution.py:23
  48.5 4.0 %collective-permute-start.7 = (f32[96,7,128]{2,1,0:T(8,128)S(1)}, f32[96,7,128]{2,1,0:T(8,128)S(1)}, u32[]{:S(2)}, u32[]{:S(2)}) collective-permute-start(f32[96,7,128]{2,1,0:T(8,128)S(1)} %pad_maximum_fusion.1), channel_id=1, source_target_pairs={{0,1},{1,0},{2,3},{3,2},{4,5},{5,4},{6,7},{7,6},{8,9},{9,8},{10,11... | collective-permute-start | bytes 1032200 | tf_op jit(solution)/shard_map/ppermute | solution.py:23
  49.4 9.1 %collective-permute-start.8 = (f32[96,7,128]{2,1,0:T(8,128)S(1)}, f32[96,7,128]{2,1,0:T(8,128)S(1)}, u32[]{:S(2)}, u32[]{:S(2)}) collective-permute-start(f32[96,7,128]{2,1,0:T(8,128)S(1)} %pad_maximum_fusion.1), channel_id=1, source_target_pairs={{1,2},{2,1},{5,6},{6,5},{9,10},{10,9},{13,14},{14,13},{17,18},{18,... | collective-permute-start | bytes 1032200 | tf_op jit(solution)/shard_map/ppermute | solution.py:23

commit v14 on v13

--- a/solution.py
+++ b/solution.py
@@ -32,7 +32,7 @@
     offset = pos - centre[:, :, None]
     spread = (
         jnp.einsum("sl,l->s", core * core, ones, precision=exact) / lanes
-        + jnp.einsum("scl,l->s", offset * offset, ones, precision=exact) / lanes
+        + jnp.sum(jnp.einsum("scl,l->sc", offset * offset, ones, precision=exact), axis=1) / lanes
     )
     return jnp.concatenate([centre, total, spread[:, None]], axis=1)
 

time: 79.4 us -> 78.8 us (level)
    reduce_sum x1 -> x0, other arithmetic: 1.08 us -> none  [slot_multipoles(): jnp.einsum('scl,l->s', offset * offset, ones, precision=exact) / lanes]
    mul x0 -> x1, other arithmetic: none -> 1.05 us  [slot_multipoles(): offset * offset]
where the time goes in v14:
time: 78.8 us; the launch traced here: 78.3 us
  other arithmetic  22.4 us (28%)
  starting transfers between devices  15.4 us (20%)
  local copies, waits for them, and re-layouts  14.2 us (18%)
  waiting for transfers between devices  12.8 us (16%)
  between operations  12.4 us (16%)
  matrix products  1.08 us (1%)
    reduce_sum x1, other arithmetic, evaluate(): arm_x = jnp.sum(extra[:, 1][:, None, :] * weight, axis=(0, 2))  17.7 us
    ppermute x5, starting transfers between devices, from_partner(): lax.ppermute(shard, axis, [(i, i ^ 1 << apart) for i in range(lax.axis_si...  8.79 us
    ppermute x2, waiting for transfers between devices, swapped(): lax.ppermute(shard, axis, second)  6.65 us
    ppermute x2, starting transfers between devices, swapped(): lax.ppermute(shard, axis, second)  5.87 us
    ppermute x2, waiting for transfers between devices, swapped(): lax.ppermute(shard, axis, first)  3.46 us
    ppermute x5, waiting for transfers between devices, from_partner(): lax.ppermute(shard, axis, [(i, i ^ 1 << apart) for i in range(lax.axis_si...  2.68 us
  transfers between devices with their start and end apart: 9, of which 6 were waited for; matrix products, arithmetic and copies ran while one was open for 14% of the time, Pallas kernels for 0%

profile of v14, /device:TPU:9, one launch (start us, length us, event | category | flops | bytes accessed | tf_op | source)
XLA Modules:
  0.0 78.3 jit_solution(5315846990841858409)
XLA Ops:
  0.1 1.0 %copy_bitcast_fusion = (f32[72,3,128]{2,1,0:T(4,128)S(1)}, f32[72,3,128]{2,1,0:T(4,128)S(1)}) fusion(f32[1,1,72,3,128]{4,2,3,1,0:T(8,128)} %param.9, f32[1,1,72,3,128]{4,2,3,1,0:T(8,128)} %param.8), kind=kLoop, calls=%fused_computation.31 | loop fusion | bytes 442368 | tf_op jit(solution)/shard_map/squeeze | solution.py:133
  1.7 0.9 %select_maximum_fusion = f32[80,7,128]{2,1,0:T(8,128)S(1)} fusion(f32[72,1,128]{2,1,0:T(1,128)} %bitcast.221, f32[72,3,128]{2,1,0:T(4,128)S(1)} %get-tuple-element.92, f32[72,3,128]{2,1,0:T(4,128)S(1)} %get-tuple-element.93), kind=kLoop, calls=%fused_computation.18 | loop fusion | flops 430080 | bytes 544768 | tf_op jit(solution)/shard_map/concatenate | solution.py:133
  2.6 1.5 %constant_dynamic-slice_fusion.11 = (s32[1,1,1]{1,2,0:T(1,128)}, s32[1,1,1]{1,2,0:T(1,128)}, s32[1,1,1]{1,2,0:T(1,128)}, s32[1,1,1]{1,2,0:T(1,128)}, s32[1,1,1]{...) fusion(s32[5,8,4]{1,2,0:T(4,128)} %param.11, ...), kind=kLoop, calls=%fused_computation.271 | loop fusion | bytes 108 | tf_op jit(solution)/shard_map/dynamic_slice | solution.py:150
  11.1 1.0 %subtract_multiply_fusion.9 = f32[72,3,128]{2,1,0:T(4,128)S(1)} fusion(f32[72,3]{1,0:T(8,128)S(1)} %copy.199, f32[1,1,72,3,128]{4,2,3,1,0:T(8,128)} %param.8), kind=kLoop, calls=%fused_computation.33 | loop fusion | flops 55296 | bytes 222048 | tf_op jit(solution)/shard_map/mul | solution.py:35
  12.9 2.4 %collective-permute-start = (f32[9,7,128]{2,1,0:T(8,128)S(1)}, f32[9,7,128]{2,1,0:T(8,128)S(1)}, u32[]{:S(2)}, u32[]{:S(2)}) collective-permute-start(f32[9,7,128]{2,1,0:T(8,128)S(1)} %pad_maximum_fusion.4), channel_id=1, source_target_pairs={{0,16},{4,20},{8,24},{12,28},{16,0},{20,4},{24,8},{28,12},{1,17},{... | collective-permute-start | bytes 96776 | tf_op jit(solution)/shard_map/ppermute | solution.py:16
  16.5 1.4 %gather_fusion.2 = s32[256]{0:T(256)S(1)} fusion(s32[1024]{0:T(1024)S(1)} %copy-done, s32[1024]{0:T(1024)S(1)} %pad_clamp_fusion.1), kind=kCustom, calls=%fused_computation.2 | custom fusion | bytes 3072 | tf_op jit(solution)/shard_map/gather | solution.py:138
  23.6 1.3 %collective-permute-done.1 = f32[10,7,128]{2,1,0:T(8,128)S(1)} collective-permute-done((f32[10,7,128]{2,1,0:T(8,128)S(1)}, f32[10,7,128]{2,1,0:T(8,128)S(1)}, u32[]{:S(2)}, u32[]{:S(2)}) %collective-permute-start.1) | collective-permute-done | bytes 35872 | tf_op jit(solution)/shard_map/ppermute | solution.py:16
  24.9 1.3 %collective-permute-start.2 = (f32[12,7,128]{2,1,0:T(8,128)S(1)}, f32[12,7,128]{2,1,0:T(8,128)S(1)}, u32[]{:S(2)}, u32[]{:S(2)}) collective-permute-start(f32[12,7,128]{2,1,0:T(8,128)S(1)} %pad_maximum_fusion.2), channel_id=1, source_target_pairs={{0,4},{4,0},{8,12},{12,8},{16,20},{20,16},{24,28},{28,24},{1,5},{5... | collective-permute-start | bytes 129032 | tf_op jit(solution)/shard_map/ppermute | solution.py:16
  27.5 1.4 %gather_fusion = s32[256]{0:T(256)S(1)} fusion(s32[1024]{0:T(1024)S(1)} %copy-done, s32[1024]{0:T(1024)S(1)} %get-tuple-element.95), kind=kCustom, calls=%fused_computation | custom fusion | bytes 3072 | tf_op jit(solution)/shard_map/gather | solution.py:176
  29.0 1.3 %collective-permute-start.3 = (f32[16,7,128]{2,1,0:T(8,128)S(1)}, f32[16,7,128]{2,1,0:T(8,128)S(1)}, u32[]{:S(2)}, u32[]{:S(2)}) collective-permute-start(f32[16,7,128]{2,1,0:T(8,128)S(1)} %constant_dynamic-update-slice_fusion), channel_id=1, source_target_pairs={{0,2},{1,3},{2,0},{3,1},{4,6},{5,7},{6,4},{7,5},{8,10},{9,11},{10,... | collective-permute-start | bytes 172040 | tf_op jit(solution)/shard_map/ppermute | solution.py:16
  32.3 3.6 %collective-permute-start.4 = (f32[24,7,128]{2,1,0:T(8,128)S(1)}, f32[24,7,128]{2,1,0:T(8,128)S(1)}, u32[]{:S(2)}, u32[]{:S(2)}) collective-permute-start(f32[24,7,128]{2,1,0:T(8,128)S(1)} %get-tuple-element.55), channel_id=1, source_target_pairs={{0,1},{1,0},{2,3},{3,2},{4,5},{5,4},{6,7},{7,6},{8,9},{9,8},{10,11... | collective-permute-start | bytes 258056 | tf_op jit(solution)/shard_map/ppermute | solution.py:16
  35.9 0.9 %collective-permute-done.4 = f32[24,7,128]{2,1,0:T(8,128)S(1)} collective-permute-done((f32[24,7,128]{2,1,0:T(8,128)S(1)}, f32[24,7,128]{2,1,0:T(8,128)S(1)}, u32[]{:S(2)}, u32[]{:S(2)}) %collective-permute-start.4) | collective-permute-done | bytes 86048 | tf_op jit(solution)/shard_map/ppermute | solution.py:16
  36.9 2.8 %collective-permute-start.6 = (f32[32,7,128]{2,1,0:T(8,128)S(1)}, f32[32,7,128]{2,1,0:T(8,128)S(1)}, u32[]{:S(2)}, u32[]{:S(2)}) collective-permute-start(f32[32,7,128]{2,1,0:T(8,128)S(1)} %slice.242), channel_id=1, source_target_pairs={{4,8},{8,4},{12,16},{16,12},{20,24},{24,20},{5,9},{9,5},{13,17},{1... | collective-permute-start | bytes 344072 | tf_op jit(solution)/shard_map/ppermute | solution.py:23
  40.0 0.6 copy.220
  40.6 0.7 gather_fusion.3
  43.7 0.7 collective-permute-done.6
  44.4 3.5 %collective-permute-done.5 = f32[32,7,128]{2,1,0:T(8,128)S(1)} collective-permute-done((f32[32,7,128]{2,1,0:T(8,128)S(1)}, f32[32,7,128]{2,1,0:T(8,128)S(1)}, u32[]{:S(2)}, u32[]{:S(2)}) %collective-permute-start.5) | collective-permute-done | bytes 114720 | tf_op jit(solution)/shard_map/ppermute | solution.py:23
  47.9 0.6 collective-permute-start.7
  48.8 3.1 %collective-permute-start.8 = (f32[96,7,128]{2,1,0:T(8,128)S(1)}, f32[96,7,128]{2,1,0:T(8,128)S(1)}, u32[]{:S(2)}, u32[]{:S(2)}) collective-permute-start(f32[96,7,128]{2,1,0:T(8,128)S(1)} %pad_maximum_fusion.1), channel_id=1, source_target_pairs={{1,2},{2,1},{5,6},{6,5},{9,10},{10,9},{13,14},{14,13},{17,18},{18,... | collective-permute-start | bytes 1032200 | tf_op jit(solution)/shard_map/ppermute | solution.py:23
  52.0 5.9 %collective-permute-done.8 = f32[96,7,128]{2,1,0:T(8,128)S(1)} collective-permute-done((f32[96,7,128]{2,1,0:T(8,128)S(1)}, f32[96,7,128]{2,1,0:T(8,128)S(1)}, u32[]{:S(2)}, u32[]{:S(2)}) %collective-permute-start.8) | collective-permute-done | bytes 344096 | tf_op jit(solution)/shard_map/ppermute | solution.py:23
  58.0 1.0 %gather_fusion.1 = f32[256,7,128]{2,1,0:T(8,128)S(1)} fusion(f32[288,7,128]{2,1,0:T(8,128)S(1)} %constant_dynamic-update-slice_fusion.11, s32[1024]{0:T(1024)S(1)} %pad_clamp_fusion.2), kind=kCustom, calls=%fused_computation.1 | custom fusion | bytes 1836032 | tf_op jit(solution)/shard_map/gather | solution.py:185
  59.0 0.6 fusion.73
  59.9 17.7 %multiply_reduce_fusion.3 = (f32[32,128]{1,0:T(8,128)S(1)}, f32[32,128]{1,0:T(8,128)S(1)}, f32[32,128]{1,0:T(8,128)S(1)}, f32[32,128]{1,0:T(8,128)S(1)}, f32[32,128]{1,0:T(8,128)S(1)}, /*index=5*/f32[32,128]{1,0:T(8,128)S(1)}) fusion(f32[32,8,128]{2,1,0:T(8,128)S(1)} %get-tuple-element.40, f32[32,8,128]{2,1,0:T(8,128)S(1)} %get-tuple-element.41, ...), kind=kLoop, calls=%fused_computation.8 | loop fusion | flops 96444416 | bytes 1458176 | tf_op jit(solution)/shard_map/vmap()/reduce_sum | solution.py:50
  77.7 0.6 fusion.18
  (142 shorter events, 10.1 us)
Async XLA Ops:
  0.0 16.5 %copy-start = (s32[1024]{0:T(1024)S(1)}, s32[1024]{0:T(1024)}, u32[]{:S(2)}) copy-start(s32[1024]{0:T(1024)} %param.12) | copy-start | bytes 12292
  0.0 15.5 %copy-start.5 = (s32[5]{0:T(128)S(1)}, s32[5]{0:T(128)}, u32[]{:S(2)}) copy-start(s32[5]{0:T(128)} %constant.216) | copy-start | bytes 64
  0.0 12.6 %copy-start.1 = (f32[1,1,72,128]{3,2,1,0:T(8,128)S(1)}, f32[1,1,72,128]{3,2,1,0:T(8,128)}, u32[]{:S(2)}) copy-start(f32[1,1,72,128]{3,2,1,0:T(8,128)} %param.10) | copy-start | bytes 110596
  0.0 15.3 %copy-start.2 = (s32[5,8,4]{1,2,0:T(4,128)S(1)}, s32[5,8,4]{1,2,0:T(4,128)}, u32[]{:S(2)}) copy-start(s32[5,8,4]{1,2,0:T(4,128)} %param.11) | copy-start | bytes 1924
  0.0 16.3 %copy-start.3 = (s32[1,1,32,8]{2,3,1,0:T(8,128)S(1)}, s32[1,1,32,8]{2,3,1,0:T(8,128)}, u32[]{:S(2)}) copy-start(s32[1,1,32,8]{2,3,1,0:T(8,128)} %param.14) | copy-start | bytes 3076
  12.9 9.0 %collective-permute-start = (f32[9,7,128]{2,1,0:T(8,128)S(1)}, f32[9,7,128]{2,1,0:T(8,128)S(1)}, u32[]{:S(2)}, u32[]{:S(2)}) collective-permute-start(f32[9,7,128]{2,1,0:T(8,128)S(1)} %pad_maximum_fusion.4), channel_id=1, source_target_pairs={{0,16},{4,20},{8,24},{12,28},{16,0},{20,4},{24,8},{28,12},{1,17},{... | collective-permute-start | bytes 96776 | tf_op jit(solution)/shard_map/ppermute | solution.py:16
  16.5 5.3 %copy-start.4 = (s32[1,1,32,8]{2,3,1,0:T(8,128)S(1)}, s32[1,1,32,8]{2,3,1,0:T(8,128)}, u32[]{:S(2)}) copy-start(s32[1,1,32,8]{2,3,1,0:T(8,128)} %param.13) | copy-start | bytes 3076
  22.0 2.9 %collective-permute-start.1 = (f32[10,7,128]{2,1,0:T(8,128)S(1)}, f32[10,7,128]{2,1,0:T(8,128)S(1)}, u32[]{:S(2)}, u32[]{:S(2)}) collective-permute-start(f32[10,7,128]{2,1,0:T(8,128)S(1)} %pad_maximum_fusion.3), channel_id=1, source_target_pairs={{0,8},{4,12},{8,0},{12,4},{16,24},{20,28},{24,16},{28,20},{1,9},{5... | collective-permute-start | bytes 107528 | tf_op jit(solution)/shard_map/ppermute | solution.py:16
  24.9 4.0 %collective-permute-start.2 = (f32[12,7,128]{2,1,0:T(8,128)S(1)}, f32[12,7,128]{2,1,0:T(8,128)S(1)}, u32[]{:S(2)}, u32[]{:S(2)}) collective-permute-start(f32[12,7,128]{2,1,0:T(8,128)S(1)} %pad_maximum_fusion.2), channel_id=1, source_target_pairs={{0,4},{4,0},{8,12},{12,8},{16,20},{20,16},{24,28},{28,24},{1,5},{5... | collective-permute-start | bytes 129032 | tf_op jit(solution)/shard_map/ppermute | solution.py:16
  29.0 3.2 %collective-permute-start.3 = (f32[16,7,128]{2,1,0:T(8,128)S(1)}, f32[16,7,128]{2,1,0:T(8,128)S(1)}, u32[]{:S(2)}, u32[]{:S(2)}) collective-permute-start(f32[16,7,128]{2,1,0:T(8,128)S(1)} %constant_dynamic-update-slice_fusion), channel_id=1, source_target_pairs={{0,2},{1,3},{2,0},{3,1},{4,6},{5,7},{6,4},{7,5},{8,10},{9,11},{10,... | collective-permute-start | bytes 172040 | tf_op jit(solution)/shard_map/ppermute | solution.py:16
  32.3 4.5 %collective-permute-start.4 = (f32[24,7,128]{2,1,0:T(8,128)S(1)}, f32[24,7,128]{2,1,0:T(8,128)S(1)}, u32[]{:S(2)}, u32[]{:S(2)}) collective-permute-start(f32[24,7,128]{2,1,0:T(8,128)S(1)} %get-tuple-element.55), channel_id=1, source_target_pairs={{0,1},{1,0},{2,3},{3,2},{4,5},{5,4},{6,7},{7,6},{8,9},{9,8},{10,11... | collective-permute-start | bytes 258056 | tf_op jit(solution)/shard_map/ppermute | solution.py:16
  36.9 7.6 %collective-permute-start.6 = (f32[32,7,128]{2,1,0:T(8,128)S(1)}, f32[32,7,128]{2,1,0:T(8,128)S(1)}, u32[]{:S(2)}, u32[]{:S(2)}) collective-permute-start(f32[32,7,128]{2,1,0:T(8,128)S(1)} %slice.242), channel_id=1, source_target_pairs={{4,8},{8,4},{12,16},{16,12},{20,24},{24,20},{5,9},{9,5},{13,17},{1... | collective-permute-start | bytes 344072 | tf_op jit(solution)/shard_map/ppermute | solution.py:23
  39.7 8.2 %collective-permute-start.5 = (f32[32,7,128]{2,1,0:T(8,128)S(1)}, f32[32,7,128]{2,1,0:T(8,128)S(1)}, u32[]{:S(2)}, u32[]{:S(2)}) collective-permute-start(f32[32,7,128]{2,1,0:T(8,128)S(1)} %slice.242), channel_id=1, source_target_pairs={{0,4},{4,0},{8,12},{12,8},{16,20},{20,16},{24,28},{28,24},{1,5},{5... | collective-permute-start | bytes 344072 | tf_op jit(solution)/shard_map/ppermute | solution.py:23
  47.9 4.0 %collective-permute-start.7 = (f32[96,7,128]{2,1,0:T(8,128)S(1)}, f32[96,7,128]{2,1,0:T(8,128)S(1)}, u32[]{:S(2)}, u32[]{:S(2)}) collective-permute-start(f32[96,7,128]{2,1,0:T(8,128)S(1)} %pad_maximum_fusion.1), channel_id=1, source_target_pairs={{0,1},{1,0},{2,3},{3,2},{4,5},{5,4},{6,7},{7,6},{8,9},{9,8},{10,11... | collective-permute-start | bytes 1032200 | tf_op jit(solution)/shard_map/ppermute | solution.py:23
  48.8 9.1 %collective-permute-start.8 = (f32[96,7,128]{2,1,0:T(8,128)S(1)}, f32[96,7,128]{2,1,0:T(8,128)S(1)}, u32[]{:S(2)}, u32[]{:S(2)}) collective-permute-start(f32[96,7,128]{2,1,0:T(8,128)S(1)} %pad_maximum_fusion.1), channel_id=1, source_target_pairs={{1,2},{2,1},{5,6},{6,5},{9,10},{10,9},{13,14},{14,13},{17,18},{18,... | collective-permute-start | bytes 1032200 | tf_op jit(solution)/shard_map/ppermute | solution.py:23

commit v15 on v14

--- a/solution.py
+++ b/solution.py
@@ -27,7 +27,8 @@
     lanes = pos.shape[-1]
     ones = jnp.ones((lanes,), jnp.float32)
     exact = lax.Precision.HIGHEST
-    centre = jnp.einsum("scl,l->sc", pos, ones, precision=exact) / lanes
+    rough = jnp.einsum("scl,l->sc", pos, ones, precision=exact) / lanes
+    centre = rough + jnp.einsum("scl,l->sc", pos - rough[:, :, None], ones, precision=exact) / lanes
     total = jnp.einsum("scl,l->sc", stren, ones, precision=exact)
     offset = pos - centre[:, :, None]
     spread = (

time: 78.8 us -> 79.5 us (level)
    sub x0 -> x1, other arithmetic: none -> 1.05 us  [slot_multipoles(): pos - rough[:, :, None]]
    mul x1, other arithmetic: 1.05 us -> 0.14 us  [slot_multipoles(): offset * offset]
where the time goes in v15:
time: 79.5 us; the launch traced here: 79.1 us
  other arithmetic  22.6 us (28%)
  starting transfers between devices  15.4 us (19%)
  local copies, waits for them, and re-layouts  14.4 us (18%)
  waiting for transfers between devices  12.8 us (16%)
  between operations  12.5 us (16%)
  matrix products  1.39 us (2%)
    reduce_sum x1, other arithmetic, evaluate(): arm_x = jnp.sum(extra[:, 1][:, None, :] * weight, axis=(0, 2))  17.7 us
    ppermute x5, starting transfers between devices, from_partner(): lax.ppermute(shard, axis, [(i, i ^ 1 << apart) for i in range(lax.axis_si...  8.79 us
    ppermute x2, waiting for transfers between devices, swapped(): lax.ppermute(shard, axis, second)  6.64 us
    ppermute x2, starting transfers between devices, swapped(): lax.ppermute(shard, axis, second)  5.89 us
    ppermute x2, waiting for transfers between devices, swapped(): lax.ppermute(shard, axis, first)  3.46 us
    ppermute x5, waiting for transfers between devices, from_partner(): lax.ppermute(shard, axis, [(i, i ^ 1 << apart) for i in range(lax.axis_si...  2.68 us
  transfers between devices with their start and end apart: 9, of which 6 were waited for; matrix products, arithmetic and copies ran while one was open for 14% of the time, Pallas kernels for 0%

profile of v15, /device:TPU:9, one launch (start us, length us, event | category | flops | bytes accessed | tf_op | source)
XLA Modules:
  0.0 79.1 jit_solution(6245211924347058854)
XLA Ops:
  0.1 1.1 %copy_bitcast_fusion = (f32[72,3,128]{2,1,0:T(4,128)S(1)}, f32[72,3,128]{2,1,0:T(4,128)S(1)}) fusion(f32[1,1,72,3,128]{4,2,3,1,0:T(8,128)} %param.9, f32[1,1,72,3,128]{4,2,3,1,0:T(8,128)} %param.8), kind=kLoop, calls=%fused_computation.31 | loop fusion | bytes 442368 | tf_op jit(solution)/shard_map/squeeze | solution.py:134
  1.8 0.9 %select_maximum_fusion = f32[80,7,128]{2,1,0:T(8,128)S(1)} fusion(f32[72,1,128]{2,1,0:T(1,128)} %bitcast.229, f32[72,3,128]{2,1,0:T(4,128)S(1)} %get-tuple-element.92, f32[72,3,128]{2,1,0:T(4,128)S(1)} %get-tuple-element.93), kind=kLoop, calls=%fused_computation.18 | loop fusion | flops 430080 | bytes 544768 | tf_op jit(solution)/shard_map/concatenate | solution.py:134
  2.7 1.5 %constant_dynamic-slice_fusion.11 = (s32[1,1,1]{1,2,0:T(1,128)}, s32[1,1,1]{1,2,0:T(1,128)}, s32[1,1,1]{1,2,0:T(1,128)}, s32[1,1,1]{1,2,0:T(1,128)}, s32[1,1,1]{...) fusion(s32[5,8,4]{1,2,0:T(4,128)} %param.11, ...), kind=kLoop, calls=%fused_computation.276 | loop fusion | bytes 108 | tf_op jit(solution)/shard_map/dynamic_slice | solution.py:151
  11.2 1.0 %broadcast_subtract_fusion = f32[72,3,128]{2,1,0:T(4,128)S(1)} fusion(f32[72,3]{1,0:T(8,128)S(1)} %copy.205, f32[1,1,72,3,128]{4,2,3,1,0:T(8,128)} %param.8), kind=kLoop, calls=%fused_computation.61 | loop fusion | flops 27648 | bytes 222048 | tf_op jit(solution)/shard_map/sub | solution.py:31
  13.7 2.4 %collective-permute-start = (f32[9,7,128]{2,1,0:T(8,128)S(1)}, f32[9,7,128]{2,1,0:T(8,128)S(1)}, u32[]{:S(2)}, u32[]{:S(2)}) collective-permute-start(f32[9,7,128]{2,1,0:T(8,128)S(1)} %pad_maximum_fusion.4), channel_id=1, source_target_pairs={{0,16},{4,20},{8,24},{12,28},{16,0},{20,4},{24,8},{28,12},{1,17},{... | collective-permute-start | bytes 96776 | tf_op jit(solution)/shard_map/ppermute | solution.py:16
  17.3 1.4 %gather_fusion.2 = s32[256]{0:T(256)S(1)} fusion(s32[1024]{0:T(1024)S(1)} %copy-done, s32[1024]{0:T(1024)S(1)} %pad_clamp_fusion.1), kind=kCustom, calls=%fused_computation.2 | custom fusion | bytes 3072 | tf_op jit(solution)/shard_map/gather | solution.py:139
  24.3 1.3 %collective-permute-done.1 = f32[10,7,128]{2,1,0:T(8,128)S(1)} collective-permute-done((f32[10,7,128]{2,1,0:T(8,128)S(1)}, f32[10,7,128]{2,1,0:T(8,128)S(1)}, u32[]{:S(2)}, u32[]{:S(2)}) %collective-permute-start.1) | collective-permute-done | bytes 35872 | tf_op jit(solution)/shard_map/ppermute | solution.py:16
  25.7 1.3 %collective-permute-start.2 = (f32[12,7,128]{2,1,0:T(8,128)S(1)}, f32[12,7,128]{2,1,0:T(8,128)S(1)}, u32[]{:S(2)}, u32[]{:S(2)}) collective-permute-start(f32[12,7,128]{2,1,0:T(8,128)S(1)} %pad_maximum_fusion.2), channel_id=1, source_target_pairs={{0,4},{4,0},{8,12},{12,8},{16,20},{20,16},{24,28},{28,24},{1,5},{5... | collective-permute-start | bytes 129032 | tf_op jit(solution)/shard_map/ppermute | solution.py:16
  28.2 1.4 %gather_fusion = s32[256]{0:T(256)S(1)} fusion(s32[1024]{0:T(1024)S(1)} %copy-done, s32[1024]{0:T(1024)S(1)} %get-tuple-element.95), kind=kCustom, calls=%fused_computation | custom fusion | bytes 3072 | tf_op jit(solution)/shard_map/gather | solution.py:177
  29.8 1.3 %collective-permute-start.3 = (f32[16,7,128]{2,1,0:T(8,128)S(1)}, f32[16,7,128]{2,1,0:T(8,128)S(1)}, u32[]{:S(2)}, u32[]{:S(2)}) collective-permute-start(f32[16,7,128]{2,1,0:T(8,128)S(1)} %constant_dynamic-update-slice_fusion), channel_id=1, source_target_pairs={{0,2},{1,3},{2,0},{3,1},{4,6},{5,7},{6,4},{7,5},{8,10},{9,11},{10,... | collective-permute-start | bytes 172040 | tf_op jit(solution)/shard_map/ppermute | solution.py:16
  33.0 3.6 %collective-permute-start.4 = (f32[24,7,128]{2,1,0:T(8,128)S(1)}, f32[24,7,128]{2,1,0:T(8,128)S(1)}, u32[]{:S(2)}, u32[]{:S(2)}) collective-permute-start(f32[24,7,128]{2,1,0:T(8,128)S(1)} %get-tuple-element.55), channel_id=1, source_target_pairs={{0,1},{1,0},{2,3},{3,2},{4,5},{5,4},{6,7},{7,6},{8,9},{9,8},{10,11... | collective-permute-start | bytes 258056 | tf_op jit(solution)/shard_map/ppermute | solution.py:16
  36.6 0.9 %collective-permute-done.4 = f32[24,7,128]{2,1,0:T(8,128)S(1)} collective-permute-done((f32[24,7,128]{2,1,0:T(8,128)S(1)}, f32[24,7,128]{2,1,0:T(8,128)S(1)}, u32[]{:S(2)}, u32[]{:S(2)}) %collective-permute-start.4) | collective-permute-done | bytes 86048 | tf_op jit(solution)/shard_map/ppermute | solution.py:16
  37.6 2.8 %collective-permute-start.6 = (f32[32,7,128]{2,1,0:T(8,128)S(1)}, f32[32,7,128]{2,1,0:T(8,128)S(1)}, u32[]{:S(2)}, u32[]{:S(2)}) collective-permute-start(f32[32,7,128]{2,1,0:T(8,128)S(1)} %slice.242), channel_id=1, source_target_pairs={{4,8},{8,4},{12,16},{16,12},{20,24},{24,20},{5,9},{9,5},{13,17},{1... | collective-permute-start | bytes 344072 | tf_op jit(solution)/shard_map/ppermute | solution.py:23
  40.7 0.6 copy.227
  41.4 0.7 gather_fusion.3
  44.4 0.7 collective-permute-done.6
  45.2 3.5 %collective-permute-done.5 = f32[32,7,128]{2,1,0:T(8,128)S(1)} collective-permute-done((f32[32,7,128]{2,1,0:T(8,128)S(1)}, f32[32,7,128]{2,1,0:T(8,128)S(1)}, u32[]{:S(2)}, u32[]{:S(2)}) %collective-permute-start.5) | collective-permute-done | bytes 114720 | tf_op jit(solution)/shard_map/ppermute | solution.py:23
  48.7 0.6 collective-permute-start.7
  49.6 3.1 %collective-permute-start.8 = (f32[96,7,128]{2,1,0:T(8,128)S(1)}, f32[96,7,128]{2,1,0:T(8,128)S(1)}, u32[]{:S(2)}, u32[]{:S(2)}) collective-permute-start(f32[96,7,128]{2,1,0:T(8,128)S(1)} %pad_maximum_fusion.1), channel_id=1, source_target_pairs={{1,2},{2,1},{5,6},{6,5},{9,10},{10,9},{13,14},{14,13},{17,18},{18,... | collective-permute-start | bytes 1032200 | tf_op jit(solution)/shard_map/ppermute | solution.py:23
  52.8 5.9 %collective-permute-done.8 = f32[96,7,128]{2,1,0:T(8,128)S(1)} collective-permute-done((f32[96,7,128]{2,1,0:T(8,128)S(1)}, f32[96,7,128]{2,1,0:T(8,128)S(1)}, u32[]{:S(2)}, u32[]{:S(2)}) %collective-permute-start.8) | collective-permute-done | bytes 344096 | tf_op jit(solution)/shard_map/ppermute | solution.py:23
  58.7 1.0 %gather_fusion.1 = f32[256,7,128]{2,1,0:T(8,128)S(1)} fusion(f32[288,7,128]{2,1,0:T(8,128)S(1)} %constant_dynamic-update-slice_fusion.11, s32[1024]{0:T(1024)S(1)} %pad_clamp_fusion.2), kind=kCustom, calls=%fused_computation.1 | custom fusion | bytes 1836032 | tf_op jit(solution)/shard_map/gather | solution.py:186
  59.7 0.6 fusion.78
  60.7 17.7 %multiply_reduce_fusion.3 = (f32[32,128]{1,0:T(8,128)S(1)}, f32[32,128]{1,0:T(8,128)S(1)}, f32[32,128]{1,0:T(8,128)S(1)}, f32[32,128]{1,0:T(8,128)S(1)}, f32[32,128]{1,0:T(8,128)S(1)}, /*index=5*/f32[32,128]{1,0:T(8,128)S(1)}) fusion(f32[32,8,128]{2,1,0:T(8,128)S(1)} %get-tuple-element.40, f32[32,8,128]{2,1,0:T(8,128)S(1)} %get-tuple-element.41, ...), kind=kLoop, calls=%fused_computation.8 | loop fusion | flops 96444416 | bytes 1458176 | tf_op jit(solution)/shard_map/vmap()/reduce_sum | solution.py:51
  78.4 0.6 fusion.20
  (149 shorter events, 10.7 us)
Async XLA Ops:
  0.0 17.3 %copy-start = (s32[1024]{0:T(1024)S(1)}, s32[1024]{0:T(1024)}, u32[]{:S(2)}) copy-start(s32[1024]{0:T(1024)} %param.12) | copy-start | bytes 12292
  0.0 16.2 %copy-start.6 = (s32[5]{0:T(128)S(1)}, s32[5]{0:T(128)}, u32[]{:S(2)}) copy-start(s32[5]{0:T(128)} %constant.217) | copy-start | bytes 64
  0.0 12.7 %copy-start.1 = (f32[1,1,72,3,128]{4,2,3,1,0:T(8,128)S(1)}, f32[1,1,72,3,128]{4,2,3,1,0:T(8,128)}, u32[]{:S(2)}) copy-start(f32[1,1,72,3,128]{4,2,3,1,0:T(8,128)} %param.8) | copy-start | bytes 331780
  0.0 13.3 %copy-start.2 = (f32[1,1,72,128]{3,2,1,0:T(8,128)S(1)}, f32[1,1,72,128]{3,2,1,0:T(8,128)}, u32[]{:S(2)}) copy-start(f32[1,1,72,128]{3,2,1,0:T(8,128)} %param.10) | copy-start | bytes 110596
  0.0 16.0 %copy-start.3 = (s32[5,8,4]{1,2,0:T(4,128)S(1)}, s32[5,8,4]{1,2,0:T(4,128)}, u32[]{:S(2)}) copy-start(s32[5,8,4]{1,2,0:T(4,128)} %param.11) | copy-start | bytes 1924
  0.0 17.0 %copy-start.4 = (s32[1,1,32,8]{2,3,1,0:T(8,128)S(1)}, s32[1,1,32,8]{2,3,1,0:T(8,128)}, u32[]{:S(2)}) copy-start(s32[1,1,32,8]{2,3,1,0:T(8,128)} %param.14) | copy-start | bytes 3076
  13.7 9.0 %collective-permute-start = (f32[9,7,128]{2,1,0:T(8,128)S(1)}, f32[9,7,128]{2,1,0:T(8,128)S(1)}, u32[]{:S(2)}, u32[]{:S(2)}) collective-permute-start(f32[9,7,128]{2,1,0:T(8,128)S(1)} %pad_maximum_fusion.4), channel_id=1, source_target_pairs={{0,16},{4,20},{8,24},{12,28},{16,0},{20,4},{24,8},{28,12},{1,17},{... | collective-permute-start | bytes 96776 | tf_op jit(solution)/shard_map/ppermute | solution.py:16
  17.3 5.3 %copy-start.5 = (s32[1,1,32,8]{2,3,1,0:T(8,128)S(1)}, s32[1,1,32,8]{2,3,1,0:T(8,128)}, u32[]{:S(2)}) copy-start(s32[1,1,32,8]{2,3,1,0:T(8,128)} %param.13) | copy-start | bytes 3076
  22.7 2.9 %collective-permute-start.1 = (f32[10,7,128]{2,1,0:T(8,128)S(1)}, f32[10,7,128]{2,1,0:T(8,128)S(1)}, u32[]{:S(2)}, u32[]{:S(2)}) collective-permute-start(f32[10,7,128]{2,1,0:T(8,128)S(1)} %pad_maximum_fusion.3), channel_id=1, source_target_pairs={{0,8},{4,12},{8,0},{12,4},{16,24},{20,28},{24,16},{28,20},{1,9},{5... | collective-permute-start | bytes 107528 | tf_op jit(solution)/shard_map/ppermute | solution.py:16
  25.7 4.0 %collective-permute-start.2 = (f32[12,7,128]{2,1,0:T(8,128)S(1)}, f32[12,7,128]{2,1,0:T(8,128)S(1)}, u32[]{:S(2)}, u32[]{:S(2)}) collective-permute-start(f32[12,7,128]{2,1,0:T(8,128)S(1)} %pad_maximum_fusion.2), channel_id=1, source_target_pairs={{0,4},{4,0},{8,12},{12,8},{16,20},{20,16},{24,28},{28,24},{1,5},{5... | collective-permute-start | bytes 129032 | tf_op jit(solution)/shard_map/ppermute | solution.py:16
  29.8 3.2 %collective-permute-start.3 = (f32[16,7,128]{2,1,0:T(8,128)S(1)}, f32[16,7,128]{2,1,0:T(8,128)S(1)}, u32[]{:S(2)}, u32[]{:S(2)}) collective-permute-start(f32[16,7,128]{2,1,0:T(8,128)S(1)} %constant_dynamic-update-slice_fusion), channel_id=1, source_target_pairs={{0,2},{1,3},{2,0},{3,1},{4,6},{5,7},{6,4},{7,5},{8,10},{9,11},{10,... | collective-permute-start | bytes 172040 | tf_op jit(solution)/shard_map/ppermute | solution.py:16
  33.0 4.5 %collective-permute-start.4 = (f32[24,7,128]{2,1,0:T(8,128)S(1)}, f32[24,7,128]{2,1,0:T(8,128)S(1)}, u32[]{:S(2)}, u32[]{:S(2)}) collective-permute-start(f32[24,7,128]{2,1,0:T(8,128)S(1)} %get-tuple-element.55), channel_id=1, source_target_pairs={{0,1},{1,0},{2,3},{3,2},{4,5},{5,4},{6,7},{7,6},{8,9},{9,8},{10,11... | collective-permute-start | bytes 258056 | tf_op jit(solution)/shard_map/ppermute | solution.py:16
  37.6 7.6 %collective-permute-start.6 = (f32[32,7,128]{2,1,0:T(8,128)S(1)}, f32[32,7,128]{2,1,0:T(8,128)S(1)}, u32[]{:S(2)}, u32[]{:S(2)}) collective-permute-start(f32[32,7,128]{2,1,0:T(8,128)S(1)} %slice.242), channel_id=1, source_target_pairs={{4,8},{8,4},{12,16},{16,12},{20,24},{24,20},{5,9},{9,5},{13,17},{1... | collective-permute-start | bytes 344072 | tf_op jit(solution)/shard_map/ppermute | solution.py:23
  40.4 8.2 %collective-permute-start.5 = (f32[32,7,128]{2,1,0:T(8,128)S(1)}, f32[32,7,128]{2,1,0:T(8,128)S(1)}, u32[]{:S(2)}, u32[]{:S(2)}) collective-permute-start(f32[32,7,128]{2,1,0:T(8,128)S(1)} %slice.242), channel_id=1, source_target_pairs={{0,4},{4,0},{8,12},{12,8},{16,20},{20,16},{24,28},{28,24},{1,5},{5... | collective-permute-start | bytes 344072 | tf_op jit(solution)/shard_map/ppermute | solution.py:23
  48.7 4.0 %collective-permute-start.7 = (f32[96,7,128]{2,1,0:T(8,128)S(1)}, f32[96,7,128]{2,1,0:T(8,128)S(1)}, u32[]{:S(2)}, u32[]{:S(2)}) collective-permute-start(f32[96,7,128]{2,1,0:T(8,128)S(1)} %pad_maximum_fusion.1), channel_id=1, source_target_pairs={{0,1},{1,0},{2,3},{3,2},{4,5},{5,4},{6,7},{7,6},{8,9},{9,8},{10,11... | collective-permute-start | bytes 1032200 | tf_op jit(solution)/shard_map/ppermute | solution.py:23
  49.6 9.1 %collective-permute-start.8 = (f32[96,7,128]{2,1,0:T(8,128)S(1)}, f32[96,7,128]{2,1,0:T(8,128)S(1)}, u32[]{:S(2)}, u32[]{:S(2)}) collective-permute-start(f32[96,7,128]{2,1,0:T(8,128)S(1)} %pad_maximum_fusion.1), channel_id=1, source_target_pairs={{1,2},{2,1},{5,6},{6,5},{9,10},{10,9},{13,14},{14,13},{17,18},{18,... | collective-permute-start | bytes 1032200 | tf_op jit(solution)/shard_map/ppermute | solution.py:23

commit v16 on v15

--- a/solution.py
+++ b/solution.py
@@ -82,7 +82,7 @@
     return lax.optimization_barrier(extra)
 
 
-def trace_back(loc, moves, levels, bits_x, nbd):
+def level_tables(moves, levels, bits_x, nbd):
     size_x, size_y = moves.shape[1], moves.shape[2]
     devices = size_x * size_y
     level_bit = np.array(
@@ -101,6 +101,12 @@
         before = before - delta[level]
     kept = jnp.stack(kept, axis=0)
     kept_mate = jnp.sum(jnp.where(swap, kept[:, None, :], 0), axis=2)
+    return kept, kept_mate, level_bit
+
+
+def trace_back(loc, kept, kept_mate, level_bit, nbd):
+    levels, devices = kept.shape
+    every = jnp.arange(devices, dtype=jnp.int32)
     device = loc.reshape(-1) // nbd
     slot = loc.reshape(-1) % nbd
     for level in reversed(range(levels)):
@@ -136,37 +142,42 @@
     width = slot_table.shape[1]
     gathered = table_blocks(slot_table, lanes)
     pieces = gathered.shape[0]
-    far_where = owner[far_list[0, 0]]
-    far_device, far_slot = trace_back(far_where, moves, levels, bits_x, nbd)
     held = jnp.pad(held, ((0, MOVE), (0, 0), (0, 0)))
-    plans = []
     level_bits = []
     for level in range(levels):
         if level < bits_x:
-            bit_at = bits_x - 1 - level
-            mate_moves = moves[level, jnp.bitwise_xor(column_index, 1 << bit_at), row_index]
-            level_bits.append((1 << bit_at) * size_y)
+            level_bits.append((1 << bits_x - 1 - level) * size_y)
         else:
-            bit_at = levels - 1 - level
-            mate_moves = moves[level, column_index, jnp.bitwise_xor(row_index, 1 << bit_at)]
-            level_bits.append(1 << bit_at)
-        plans.append((bit_at, moves[level, column_index, row_index], mate_moves))
-    count = jnp.int32(nbd)
-    for plan_item in plans:
-        count = count + plan_item[1] - plan_item[2]
-    for level in range(levels):
-        bit_at, own_moves, mate_moves = plans[level]
-        leaving = lax.dynamic_slice_in_dim(held, count - own_moves, MOVE, 0)
+            level_bits.append(1 << levels - 1 - level)
+    devices = size_x * size_y
+    flat_moves = moves.reshape(levels, devices)
+    every = jnp.arange(devices, dtype=jnp.int32)
+    mates = jnp.bitwise_xor(me, jnp.array(level_bits, jnp.int32))
+    own = jnp.sum(jnp.where(every[None, :] == me, flat_moves, 0), axis=1)
+    mate_own = jnp.sum(jnp.where(every[None, :] == mates[:, None], flat_moves, 0), axis=1)
+    count = nbd + jnp.sum(own - mate_own, keepdims=True)
+    slot_ids = jnp.arange(held.shape[0], dtype=jnp.int32)
+    move_ids = jnp.arange(MOVE, dtype=jnp.int32)
+    exact = lax.Precision.HIGHEST
+    for level in range(levels):
+        if level < bits_x:
+            axis_name, bit_at = "gx", bits_x - 1 - level
+        else:
+            axis_name, bit_at = "gy", levels - 1 - level
+        count = count - own[level : level + 1]
+        take = (slot_ids[None, :] == (count + move_ids)[:, None]).astype(jnp.float32)
+        leaving = jnp.einsum("ms,scl->mcl", take, held, precision=exact)
         payload = jnp.concatenate([leaving, gathered], axis=0)
-        if level < bits_x:
-            got = from_partner(payload, "gx", bit_at)
-        else:
-            got = from_partner(payload, "gy", bit_at)
+        got = from_partner(payload, axis_name, bit_at)
         arriving = got[:MOVE]
         gathered = jnp.concatenate([gathered, got[MOVE:]], axis=0)
-        count = count - own_moves
-        held = lax.dynamic_update_slice_in_dim(held, arriving, count, 0)
-        count = count + mate_moves
+        put = slot_ids[:, None] == (count + move_ids)[None, :]
+        placed = jnp.einsum("sm,mcl->scl", put.astype(jnp.float32), arriving, precision=exact)
+        held = jnp.where(jnp.any(put, axis=1)[:, None, None], placed, held)
+        count = count + mate_own[level : level + 1]
+    far_where = owner[far_list[0, 0]]
+    kept, kept_mate, level_bit = level_tables(moves, levels, bits_x, nbd)
+    far_device, far_slot = trace_back(far_where, kept, kept_mate, level_bit, nbd)
     blocks = held[:nbd]
     relative = jnp.bitwise_xor(far_device, me)
     entry = jnp.zeros_like(relative)

time: 79.5 us -> 84.8 us (1.067)
  matrix products: 1.39 us -> 10 us
  between operations: 12.5 us -> 6.87 us
  waiting for transfers between devices: 12.8 us -> 14.8 us
  local copies, waits for them, and re-layouts: 14.4 us -> 12.6 us
  starting transfers between devices: 15.4 us -> 16.5 us
  other arithmetic: 22.6 us -> 23.5 us
    dot_general x0 -> x10, matrix products: none -> 4.09 us  [the longest x5 2.14 us: local(): leaving = jnp.einsum('ms,scl->mcl', take, held, precision=exact)]
    ppermute x5, waiting for transfers between devices: 2.68 us -> 5.87 us  [from_partner(): lax.ppermute(shard, axis, [(i, i ^ 1 << apart) for i in range(lax.axis_si...]
    reduce_sum x3 -> x5, other arithmetic: 0.52 us -> 2.2 us  [the longest x1 1.04 us: local(): jnp.sum(jnp.where(every[None, :] == mates[:, None], flat_moves, 0), axis=1)]
    dynamic_slice x4 -> x0, local copies, waits for them, and re-layouts: 1.56 us -> none  [the longest x1 1.53 us: local(): moves[level, column_index, jnp.bitwise_xor(row_index, 1 << bit_at)]]
    squeeze x7 -> x6, local copies, waits for them, and re-layouts: 1.56 us -> 0.49 us  [level_tables(): kept.append(before - flat[level])]
    sub x5 -> x4, other arithmetic: 1.08 us -> 0.04 us  [the longest x3 0.03 us: level_tables(): kept.append(before - flat[level])]
    dot_general x1, matrix products: 0.31 us -> 1.3 us  [slot_multipoles(): jnp.einsum('scl,l->sc', pos - rough[:, :, None], ones, precision=exact)]
    dot_general x1, matrix products: 0.31 us -> 1.3 us  [slot_multipoles(): jnp.einsum('scl,l->sc', offset * offset, ones, precision=exact)]
  transfers between devices with their start and end apart: 9 -> 9, of which waited for: 6 -> 7; matrix products, arithmetic and copies ran while one was open for 14% -> 14% of each run, Pallas kernels for 0% -> 0%
where the time goes in v16:
time: 84.8 us; the launch traced here: 84.3 us
  other arithmetic  23.5 us (28%)
  starting transfers between devices  16.5 us (19%)
  waiting for transfers between devices  14.8 us (17%)
  local copies, waits for them, and re-layouts  12.6 us (15%)
  matrix products  10 us (12%)
  between operations  6.87 us (8%)
    reduce_sum x1, other arithmetic, evaluate(): arm_x = jnp.sum(extra[:, 1][:, None, :] * weight, axis=(0, 2))  17.9 us
    ppermute x5, starting transfers between devices, from_partner(): lax.ppermute(shard, axis, [(i, i ^ 1 << apart) for i in range(lax.axis_si...  9.65 us
    ppermute x2, starting transfers between devices, swapped(): lax.ppermute(shard, axis, second)  6.07 us
    ppermute x5, waiting for transfers between devices, from_partner(): lax.ppermute(shard, axis, [(i, i ^ 1 << apart) for i in range(lax.axis_si...  5.87 us
    ppermute x2, waiting for transfers between devices, swapped(): lax.ppermute(shard, axis, second)  5.74 us
    ppermute x2, waiting for transfers between devices, swapped(): lax.ppermute(shard, axis, first)  3.15 us
    dot_general x5, matrix products, local(): leaving = jnp.einsum('ms,scl->mcl', take, held, precision=exact)  2.14 us
    dot_general x5, matrix products, local(): jnp.einsum('sm,mcl->scl', put.astype(jnp.float32), arriving, precision=ex...  1.95 us
  transfers between devices with their start and end apart: 9, of which 7 were waited for; matrix products, arithmetic and copies ran while one was open for 14% of the time, Pallas kernels for 0%

profile of v16, /device:TPU:9, one launch (start us, length us, event | category | flops | bytes accessed | tf_op | source)
XLA Modules:
  0.0 84.3 jit_solution(3865892939808847975)
XLA Ops:
  0.7 1.0 %select_reduce_fusion.12 = (s32[5]{0:T(128)S(1)}, s32[5]{0:T(128)S(1)}) fusion(s32[5,8,4]{1,2,0:T(4,128)} %param.12, s32[8,4]{0,1:T(4,128)S(1)} %multiply_add_fusion, s32[5]{0:T(128)S(1)} %broadcast_xor_fusion, pred[8,4]{0,1:T(4,128)(4,1)S(1)} %broadcast_compare_fusion), kind=kLoop, calls=%fused_computation.217 | loop fusion | flops 790 | bytes 860 | tf_op jit(solution)/shard_map/reduce_sum | solution.py:157
  3.1 1.2 %fusion.117 = f32[1,72,3]{0,1,2:T(8,128)S(1)} fusion(f32[1,1,72,3,128]{4,2,3,1,0:T(8,128)} %param.9), kind=kOutput, calls=%fused_computation.307 | convolution fusion | flops 331776 | bytes 111456 | tf_op jit(solution)/shard_map/scl,l->sc/dot_general | solution.py:30
  4.4 1.3 %fusion.18 = f32[1,72,3]{0,1,2:T(8,128)S(1)} fusion(f32[72,3]{0,1:T(4,128)S(1)} %bitcast_multiply_fusion.7, f32[1,1,72,3,128]{4,2,3,1,0:T(8,128)} %param.9), kind=kOutput, calls=%fused_computation.58 | convolution fusion | flops 359424 | bytes 112320 | tf_op jit(solution)/shard_map/scl,l->sc/dot_general | solution.py:31
  5.8 1.3 %convolution_reduce_fusion = f32[1,72]{0,1:T(8,128)S(1)} fusion(f32[72,3]{0,1:T(4,128)S(1)} %fusion.101, f32[1,1,72,3,128]{4,2,3,1,0:T(8,128)} %param.9), kind=kOutput, calls=%fused_computation.16 | convolution fusion | flops 387216 | bytes 111744 | tf_op jit(solution)/shard_map/scl,l->sc/dot_general | solution.py:36
  7.2 1.2 %fusion.114 = f32[1,72,3]{0,1,2:T(8,128)S(1)} fusion(f32[1,1,72,3,128]{4,2,3,1,0:T(8,128)} %param.10), kind=kOutput, calls=%fused_computation.304 | convolution fusion | flops 331776 | bytes 111456 | tf_op jit(solution)/shard_map/scl,l->sc/dot_general | solution.py:32
  8.5 0.9 %fusion.2 = f32[72,1]{0,1:T(1,128)S(1)} fusion(f32[1,1,72,128]{3,2,1,0:T(8,128)} %param.11, f32[1,72]{1,0:T(1,128)S(1)} %copy.135), kind=kOutput, calls=%fused_computation.20 | convolution fusion | flops 119952 | bytes 37440 | tf_op jit(solution)/shard_map/sl,l->s/dot_general | solution.py:35
  10.8 1.2 %fusion.3 = f32[8,7,128]{2,0,1:T(8,128)S(1)} fusion(f32[72,1,128]{2,0,1:T(8,128)} %bitcast.270, f32[72,3,128]{2,0,1:T(8,128)} %bitcast.261, f32[72,3,128]{2,0,1:T(8,128)} %bitcast.246, s32[8]{0:T(128)S(1)} %iota_add_fusion), kind=kOutput, calls=%fused_computation.36 | convolution fusion | flops 7312000 | bytes 286752 | tf_op jit(solution)/shard_map/ms,scl->mcl/dot_general | solution.py:169
  12.0 2.4 %collective-permute-start = (f32[9,7,128]{2,0,1:T(8,128)S(1)}, f32[9,7,128]{2,0,1:T(8,128)S(1)}, u32[]{:S(2)}, u32[]{:S(2)}) collective-permute-start(f32[9,7,128]{2,0,1:T(8,128)S(1)} %pad_maximum_fusion.2), channel_id=1, source_target_pairs={{0,16},{4,20},{8,24},{12,28},{16,0},{20,4},{24,8},{28,12},{1,17},{... | collective-permute-start | bytes 96776 | tf_op jit(solution)/shard_map/ppermute | solution.py:16
  15.7 1.4 %gather_fusion.2 = s32[256]{0:T(256)S(1)} fusion(s32[1024]{0:T(1024)S(1)} %copy-done, s32[1024]{0:T(1024)S(1)} %pad_clamp_fusion.1), kind=kCustom, calls=%fused_computation.2 | custom fusion | bytes 3072 | tf_op jit(solution)/shard_map/gather | solution.py:178
  23.4 1.4 %gather_fusion = s32[256]{0:T(256)S(1)} fusion(s32[1024]{0:T(1024)S(1)} %copy-done, s32[1024]{0:T(1024)S(1)} %get-tuple-element.88), kind=kCustom, calls=%fused_computation | custom fusion | bytes 3072 | tf_op jit(solution)/shard_map/gather | solution.py:188
  27.7 1.5 %collective-permute-done.1 = f32[10,7,128]{2,0,1:T(8,128)S(1)} collective-permute-done((f32[10,7,128]{2,0,1:T(8,128)S(1)}, f32[10,7,128]{2,0,1:T(8,128)S(1)}, u32[]{:S(2)}, u32[]{:S(2)}) %collective-permute-start.1) | collective-permute-done | bytes 35872 | tf_op jit(solution)/shard_map/ppermute | solution.py:16
  29.9 1.3 %collective-permute-start.2 = (f32[12,7,128]{2,0,1:T(8,128)S(1)}, f32[12,7,128]{2,0,1:T(8,128)S(1)}, u32[]{:S(2)}, u32[]{:S(2)}) collective-permute-start(f32[12,7,128]{2,0,1:T(8,128)S(1)} %pad_maximum_fusion.4), channel_id=1, source_target_pairs={{0,4},{4,0},{8,12},{12,8},{16,20},{20,16},{24,28},{28,24},{1,5},{5... | collective-permute-start | bytes 129032 | tf_op jit(solution)/shard_map/ppermute | solution.py:16
  31.3 1.7 %collective-permute-done.2 = f32[12,7,128]{2,0,1:T(8,128)S(1)} collective-permute-done((f32[12,7,128]{2,0,1:T(8,128)S(1)}, f32[12,7,128]{2,0,1:T(8,128)S(1)}, u32[]{:S(2)}, u32[]{:S(2)}) %collective-permute-start.2) | collective-permute-done | bytes 43040 | tf_op jit(solution)/shard_map/ppermute | solution.py:16
  33.7 1.3 %collective-permute-start.3 = (f32[16,7,128]{2,0,1:T(8,128)S(1)}, f32[16,7,128]{2,0,1:T(8,128)S(1)}, u32[]{:S(2)}, u32[]{:S(2)}) collective-permute-start(f32[16,7,128]{2,0,1:T(8,128)S(1)} %concatenate.48), channel_id=1, source_target_pairs={{0,2},{1,3},{2,0},{3,1},{4,6},{5,7},{6,4},{7,5},{8,10},{9,11},{10,... | collective-permute-start | bytes 172040 | tf_op jit(solution)/shard_map/ppermute | solution.py:16
  35.1 1.7 %collective-permute-done.3 = f32[16,7,128]{2,0,1:T(8,128)S(1)} collective-permute-done((f32[16,7,128]{2,0,1:T(8,128)S(1)}, f32[16,7,128]{2,0,1:T(8,128)S(1)}, u32[]{:S(2)}, u32[]{:S(2)}) %collective-permute-start.3) | collective-permute-done | bytes 57376 | tf_op jit(solution)/shard_map/ppermute | solution.py:16
  37.5 4.5 %collective-permute-start.4 = (f32[24,7,128]{2,0,1:T(8,128)S(1)}, f32[24,7,128]{2,0,1:T(8,128)S(1)}, u32[]{:S(2)}, u32[]{:S(2)}) collective-permute-start(f32[24,7,128]{2,0,1:T(8,128)S(1)} %concatenate.49), channel_id=1, source_target_pairs={{0,1},{1,0},{2,3},{3,2},{4,5},{5,4},{6,7},{7,6},{8,9},{9,8},{10,11... | collective-permute-start | bytes 258056 | tf_op jit(solution)/shard_map/ppermute | solution.py:16
  42.0 0.9 %collective-permute-done.4 = f32[24,7,128]{2,0,1:T(8,128)S(1)} collective-permute-done((f32[24,7,128]{2,0,1:T(8,128)S(1)}, f32[24,7,128]{2,0,1:T(8,128)S(1)}, u32[]{:S(2)}, u32[]{:S(2)}) %collective-permute-start.4) | collective-permute-done | bytes 86048 | tf_op jit(solution)/shard_map/ppermute | solution.py:16
  43.3 3.0 %collective-permute-start.6 = (f32[32,7,128]{2,0,1:T(8,128)S(1)}, f32[32,7,128]{2,0,1:T(8,128)S(1)}, u32[]{:S(2)}, u32[]{:S(2)}) collective-permute-start(f32[32,7,128]{2,0,1:T(8,128)S(1)} %slice.278), channel_id=1, source_target_pairs={{4,8},{8,4},{12,16},{16,12},{20,24},{24,20},{5,9},{9,5},{13,17},{1... | collective-permute-start | bytes 344072 | tf_op jit(solution)/shard_map/ppermute | solution.py:23
  47.3 0.7 gather_fusion.3
  50.5 3.1 %collective-permute-done.5 = f32[32,7,128]{2,0,1:T(8,128)S(1)} collective-permute-done((f32[32,7,128]{2,0,1:T(8,128)S(1)}, f32[32,7,128]{2,0,1:T(8,128)S(1)}, u32[]{:S(2)}, u32[]{:S(2)}) %collective-permute-start.5) | collective-permute-done | bytes 114720 | tf_op jit(solution)/shard_map/ppermute | solution.py:23
  54.5 3.1 %collective-permute-start.8 = (f32[96,7,128]{2,0,1:T(8,128)S(1)}, f32[96,7,128]{2,0,1:T(8,128)S(1)}, u32[]{:S(2)}, u32[]{:S(2)}) collective-permute-start(f32[96,7,128]{2,0,1:T(8,128)S(1)} %pad_maximum_fusion.1), channel_id=1, source_target_pairs={{1,2},{2,1},{5,6},{6,5},{9,10},{10,9},{13,14},{14,13},{17,18},{18,... | collective-permute-start | bytes 1032200 | tf_op jit(solution)/shard_map/ppermute | solution.py:23
  57.7 5.4 %collective-permute-done.8 = f32[96,7,128]{2,0,1:T(8,128)S(1)} collective-permute-done((f32[96,7,128]{2,0,1:T(8,128)S(1)}, f32[96,7,128]{2,0,1:T(8,128)S(1)}, u32[]{:S(2)}, u32[]{:S(2)}) %collective-permute-start.8) | collective-permute-done | bytes 344096 | tf_op jit(solution)/shard_map/ppermute | solution.py:23
  63.8 1.0 %gather_fusion.1 = f32[256,7,128]{2,1,0:T(8,128)S(1)} fusion(f32[288,7,128]{2,1,0:T(8,128)S(1)} %copy.98, s32[1024]{0:T(1024)S(1)} %pad_clamp_fusion.2), kind=kCustom, calls=%fused_computation.1 | custom fusion | bytes 1836032 | tf_op jit(solution)/shard_map/gather | solution.py:197
  65.7 17.9 %multiply_reduce_fusion.3 = (f32[32,128]{1,0:T(8,128)S(1)}, f32[32,128]{1,0:T(8,128)S(1)}, f32[32,128]{1,0:T(8,128)S(1)}, f32[32,128]{1,0:T(8,128)S(1)}, f32[32,128]{1,0:T(8,128)S(1)}, /*index=5*/f32[32,128]{1,0:T(8,128)S(1)}) fusion(f32[32,8,128]{2,1,0:T(8,128)S(1)} %get-tuple-element.39, f32[32,8,128]{2,1,0:T(8,128)S(1)} %get-tuple-element.40, ...), kind=kLoop, calls=%fused_computation.8 | loop fusion | flops 96444416 | bytes 1458176 | tf_op jit(solution)/shard_map/vmap()/reduce_sum | solution.py:51
  (158 shorter events, 17.0 us)
Async XLA Ops:
  0.0 15.7 %copy-start = (s32[1024]{0:T(1024)S(1)}, s32[1024]{0:T(1024)}, u32[]{:S(2)}) copy-start(s32[1024]{0:T(1024)} %param.13) | copy-start | bytes 12292
  0.0 14.5 %copy-start.7 = (s32[5]{0:T(128)S(1)}, s32[5]{0:T(128)}, u32[]{:S(2)}) copy-start(s32[5]{0:T(128)} %constant.212.clone) | copy-start | bytes 64
  0.0 14.4 %copy-start.3 = (s32[5,8,4]{1,2,0:T(4,128)S(1)}, s32[5,8,4]{1,2,0:T(4,128)}, u32[]{:S(2)}) copy-start(s32[5,8,4]{1,2,0:T(4,128)} %param.12) | copy-start | bytes 1924
  0.0 15.5 %copy-start.5 = (s32[1,1,32,8]{2,3,1,0:T(8,128)S(1)}, s32[1,1,32,8]{2,3,1,0:T(8,128)}, u32[]{:S(2)}) copy-start(s32[1,1,32,8]{2,3,1,0:T(8,128)} %param.15) | copy-start | bytes 3076
  12.0 13.5 %collective-permute-start = (f32[9,7,128]{2,0,1:T(8,128)S(1)}, f32[9,7,128]{2,0,1:T(8,128)S(1)}, u32[]{:S(2)}, u32[]{:S(2)}) collective-permute-start(f32[9,7,128]{2,0,1:T(8,128)S(1)} %pad_maximum_fusion.2), channel_id=1, source_target_pairs={{0,16},{4,20},{8,24},{12,28},{16,0},{20,4},{24,8},{28,12},{1,17},{... | collective-permute-start | bytes 96776 | tf_op jit(solution)/shard_map/ppermute | solution.py:16
  15.7 7.5 %copy-start.6 = (s32[1,1,32,8]{2,3,1,0:T(8,128)S(1)}, s32[1,1,32,8]{2,3,1,0:T(8,128)}, u32[]{:S(2)}) copy-start(s32[1,1,32,8]{2,3,1,0:T(8,128)} %param.14) | copy-start | bytes 3076
  23.3 2.1 %copy-start.1 = (f32[1,1,72,3,128]{4,2,3,1,0:T(8,128)S(1)}, f32[1,1,72,3,128]{4,2,3,1,0:T(8,128)}, u32[]{:S(2)}) copy-start(f32[1,1,72,3,128]{4,2,3,1,0:T(8,128)} %param.9) | copy-start | bytes 331780
  23.4 2.1 %copy-start.2 = (f32[1,1,72,3,128]{4,2,3,1,0:T(8,128)S(1)}, f32[1,1,72,3,128]{4,2,3,1,0:T(8,128)}, u32[]{:S(2)}) copy-start(f32[1,1,72,3,128]{4,2,3,1,0:T(8,128)} %param.10) | copy-start | bytes 331780
  23.4 2.1 %copy-start.4 = (f32[1,1,72,128]{3,2,1,0:T(8,128)S(1)}, f32[1,1,72,128]{3,2,1,0:T(8,128)}, u32[]{:S(2)}) copy-start(f32[1,1,72,128]{3,2,1,0:T(8,128)} %param.11) | copy-start | bytes 110596
  26.2 3.1 %collective-permute-start.1 = (f32[10,7,128]{2,0,1:T(8,128)S(1)}, f32[10,7,128]{2,0,1:T(8,128)S(1)}, u32[]{:S(2)}, u32[]{:S(2)}) collective-permute-start(f32[10,7,128]{2,0,1:T(8,128)S(1)} %pad_maximum_fusion.3), channel_id=1, source_target_pairs={{0,8},{4,12},{8,0},{12,4},{16,24},{20,28},{24,16},{28,20},{1,9},{5... | collective-permute-start | bytes 107528 | tf_op jit(solution)/shard_map/ppermute | solution.py:16
  29.9 3.1 %collective-permute-start.2 = (f32[12,7,128]{2,0,1:T(8,128)S(1)}, f32[12,7,128]{2,0,1:T(8,128)S(1)}, u32[]{:S(2)}, u32[]{:S(2)}) collective-permute-start(f32[12,7,128]{2,0,1:T(8,128)S(1)} %pad_maximum_fusion.4), channel_id=1, source_target_pairs={{0,4},{4,0},{8,12},{12,8},{16,20},{20,16},{24,28},{28,24},{1,5},{5... | collective-permute-start | bytes 129032 | tf_op jit(solution)/shard_map/ppermute | solution.py:16
  33.7 3.1 %collective-permute-start.3 = (f32[16,7,128]{2,0,1:T(8,128)S(1)}, f32[16,7,128]{2,0,1:T(8,128)S(1)}, u32[]{:S(2)}, u32[]{:S(2)}) collective-permute-start(f32[16,7,128]{2,0,1:T(8,128)S(1)} %concatenate.48), channel_id=1, source_target_pairs={{0,2},{1,3},{2,0},{3,1},{4,6},{5,7},{6,4},{7,5},{8,10},{9,11},{10,... | collective-permute-start | bytes 172040 | tf_op jit(solution)/shard_map/ppermute | solution.py:16
  37.5 5.4 %collective-permute-start.4 = (f32[24,7,128]{2,0,1:T(8,128)S(1)}, f32[24,7,128]{2,0,1:T(8,128)S(1)}, u32[]{:S(2)}, u32[]{:S(2)}) collective-permute-start(f32[24,7,128]{2,0,1:T(8,128)S(1)} %concatenate.49), channel_id=1, source_target_pairs={{0,1},{1,0},{2,3},{3,2},{4,5},{5,4},{6,7},{7,6},{8,9},{9,8},{10,11... | collective-permute-start | bytes 258056 | tf_op jit(solution)/shard_map/ppermute | solution.py:16
  43.3 7.2 %collective-permute-start.6 = (f32[32,7,128]{2,0,1:T(8,128)S(1)}, f32[32,7,128]{2,0,1:T(8,128)S(1)}, u32[]{:S(2)}, u32[]{:S(2)}) collective-permute-start(f32[32,7,128]{2,0,1:T(8,128)S(1)} %slice.278), channel_id=1, source_target_pairs={{4,8},{8,4},{12,16},{16,12},{20,24},{24,20},{5,9},{9,5},{13,17},{1... | collective-permute-start | bytes 344072 | tf_op jit(solution)/shard_map/ppermute | solution.py:23
  46.3 7.3 %collective-permute-start.5 = (f32[32,7,128]{2,0,1:T(8,128)S(1)}, f32[32,7,128]{2,0,1:T(8,128)S(1)}, u32[]{:S(2)}, u32[]{:S(2)}) collective-permute-start(f32[32,7,128]{2,0,1:T(8,128)S(1)} %slice.278), channel_id=1, source_target_pairs={{0,4},{4,0},{8,12},{12,8},{16,20},{20,16},{24,28},{28,24},{1,5},{5... | collective-permute-start | bytes 344072 | tf_op jit(solution)/shard_map/ppermute | solution.py:23
  53.6 4.0 %collective-permute-start.7 = (f32[96,7,128]{2,0,1:T(8,128)S(1)}, f32[96,7,128]{2,0,1:T(8,128)S(1)}, u32[]{:S(2)}, u32[]{:S(2)}) collective-permute-start(f32[96,7,128]{2,0,1:T(8,128)S(1)} %pad_maximum_fusion.1), channel_id=1, source_target_pairs={{0,1},{1,0},{2,3},{3,2},{4,5},{5,4},{6,7},{7,6},{8,9},{9,8},{10,11... | collective-permute-start | bytes 1032200 | tf_op jit(solution)/shard_map/ppermute | solution.py:23
  54.5 8.6 %collective-permute-start.8 = (f32[96,7,128]{2,0,1:T(8,128)S(1)}, f32[96,7,128]{2,0,1:T(8,128)S(1)}, u32[]{:S(2)}, u32[]{:S(2)}) collective-permute-start(f32[96,7,128]{2,0,1:T(8,128)S(1)} %pad_maximum_fusion.1), channel_id=1, source_target_pairs={{1,2},{2,1},{5,6},{6,5},{9,10},{10,9},{13,14},{14,13},{17,18},{18,... | collective-permute-start | bytes 1032200 | tf_op jit(solution)/shard_map/ppermute | solution.py:23

commit v17 on v16

--- a/solution.py
+++ b/solution.py
@@ -175,9 +175,14 @@
         placed = jnp.einsum("sm,mcl->scl", put.astype(jnp.float32), arriving, precision=exact)
         held = jnp.where(jnp.any(put, axis=1)[:, None, None], placed, held)
         count = count + mate_own[level : level + 1]
-    far_where = owner[far_list[0, 0]]
-    kept, kept_mate, level_bit = level_tables(moves, levels, bits_x, nbd)
-    far_device, far_slot = trace_back(far_where, kept, kept_mate, level_bit, nbd)
+        if level == min(1, levels - 1):
+            moves_late, near_late, _ = lax.optimization_barrier((moves, near_list[0, 0], held))
+            kept, kept_mate, level_bit = level_tables(moves_late, levels, bits_x, nbd)
+            near_where = owner[near_late]
+        if level == min(2, levels - 1):
+            far_late, _ = lax.optimization_barrier((far_list[0, 0], held))
+            far_where = owner[far_late]
+            far_device, far_slot = trace_back(far_where, kept, kept_mate, level_bit, nbd)
     blocks = held[:nbd]
     relative = jnp.bitwise_xor(far_device, me)
     entry = jnp.zeros_like(relative)
@@ -185,7 +190,6 @@
         entry = entry + ((relative // level_bits[level]) % 2) * (1 << level)
     all_table = gathered.reshape(-1, pieces, width, lanes).transpose(0, 1, 3, 2).reshape(-1, width)
     moments = all_table[entry * (pieces * lanes) + far_slot]
-    near_where = owner[near_list[0, 0]]
     source_device = near_where // nbd
     source_slot = near_where % nbd
     delta_x = source_device // size_y - column_index

time: 84.8 us -> 86 us (1.014)
  waiting for transfers between devices: 14.8 us -> 15.9 us
    ppermute x5, waiting for transfers between devices: 5.87 us -> 6.93 us  [from_partner(): lax.ppermute(shard, axis, [(i, i ^ 1 << apart) for i in range(lax.axis_si...]
  transfers between devices with their start and end apart: 9 -> 9, of which waited for: 7 -> 7; matrix products, arithmetic and copies ran while one was open for 14% -> 6% of each run, Pallas kernels for 0% -> 0%
where the time goes in v17:
time: 86 us; the launch traced here: 85.6 us
  other arithmetic  23.6 us (27%)
  starting transfers between devices  16.5 us (19%)
  waiting for transfers between devices  15.9 us (18%)
  local copies, waits for them, and re-layouts  12.6 us (15%)
  matrix products  10.1 us (12%)
  between operations  6.86 us (8%)
    reduce_sum x1, other arithmetic, evaluate(): arm_x = jnp.sum(extra[:, 1][:, None, :] * weight, axis=(0, 2))  17.9 us
    ppermute x5, starting transfers between devices, from_partner(): lax.ppermute(shard, axis, [(i, i ^ 1 << apart) for i in range(lax.axis_si...  9.65 us
    ppermute x5, waiting for transfers between devices, from_partner(): lax.ppermute(shard, axis, [(i, i ^ 1 << apart) for i in range(lax.axis_si...  6.93 us
    ppermute x2, starting transfers between devices, swapped(): lax.ppermute(shard, axis, second)  6.06 us
    ppermute x2, waiting for transfers between devices, swapped(): lax.ppermute(shard, axis, second)  5.84 us
    ppermute x2, waiting for transfers between devices, swapped(): lax.ppermute(shard, axis, first)  3.15 us
    dot_general x5, matrix products, local(): leaving = jnp.einsum('ms,scl->mcl', take, held, precision=exact)  2.15 us
    dot_general x5, matrix products, local(): jnp.einsum('sm,mcl->scl', put.astype(jnp.float32), arriving, precision=ex...  1.96 us
  transfers between devices with their start and end apart: 9, of which 7 were waited for; matrix products, arithmetic and copies ran while one was open for 6% of the time, Pallas kernels for 0%

profile of v17, /device:TPU:9, one launch (start us, length us, event | category | flops | bytes accessed | tf_op | source)
XLA Modules:
  0.0 85.6 jit_solution(11570833519197043315)
XLA Ops:
  0.1 0.7 broadcast_xor_fusion
  0.8 1.0 %select_reduce_fusion.12 = (s32[5]{0:T(128)S(1)}, s32[5]{0:T(128)S(1)}) fusion(s32[5,8,4]{1,2,0:T(4,128)} %param.12, s32[8,4]{0,1:T(4,128)S(1)} %multiply_add_fusion, s32[5]{0:T(128)S(1)} %broadcast_xor_fusion, pred[8,4]{0,1:T(4,128)(4,1)S(1)} %broadcast_compare_fusion), kind=kLoop, calls=%fused_computation.217 | loop fusion | flops 790 | bytes 860 | tf_op jit(solution)/shard_map/reduce_sum | solution.py:157
  4.4 1.2 %fusion.114 = f32[1,72,3]{0,1,2:T(8,128)S(1)} fusion(f32[1,1,72,3,128]{4,2,3,1,0:T(8,128)} %param.10), kind=kOutput, calls=%fused_computation.304 | convolution fusion | flops 331776 | bytes 111456 | tf_op jit(solution)/shard_map/scl,l->sc/dot_general | solution.py:32
  5.7 1.2 %fusion.117 = f32[1,72,3]{0,1,2:T(8,128)S(1)} fusion(f32[1,1,72,3,128]{4,2,3,1,0:T(8,128)} %param.9), kind=kOutput, calls=%fused_computation.307 | convolution fusion | flops 331776 | bytes 111456 | tf_op jit(solution)/shard_map/scl,l->sc/dot_general | solution.py:30
  7.0 1.3 %fusion.18 = f32[1,72,3]{0,1,2:T(8,128)S(1)} fusion(f32[72,3]{0,1:T(4,128)S(1)} %bitcast_multiply_fusion.7, f32[1,1,72,3,128]{4,2,3,1,0:T(8,128)} %param.9), kind=kOutput, calls=%fused_computation.58 | convolution fusion | flops 359424 | bytes 112320 | tf_op jit(solution)/shard_map/scl,l->sc/dot_general | solution.py:31
  8.4 1.3 %convolution_reduce_fusion = f32[1,72]{0,1:T(8,128)S(1)} fusion(f32[72,3]{0,1:T(4,128)S(1)} %fusion.101, f32[1,1,72,3,128]{4,2,3,1,0:T(8,128)} %param.9), kind=kOutput, calls=%fused_computation.16 | convolution fusion | flops 387216 | bytes 111744 | tf_op jit(solution)/shard_map/scl,l->sc/dot_general | solution.py:36
  9.8 0.9 %fusion.2 = f32[72,1]{0,1:T(1,128)S(1)} fusion(f32[1,1,72,128]{3,2,1,0:T(8,128)} %param.11, f32[1,72]{1,0:T(1,128)S(1)} %copy.135), kind=kOutput, calls=%fused_computation.20 | convolution fusion | flops 119952 | bytes 37440 | tf_op jit(solution)/shard_map/sl,l->s/dot_general | solution.py:35
  10.8 1.2 %fusion.3 = f32[8,7,128]{2,0,1:T(8,128)S(1)} fusion(f32[72,1,128]{2,0,1:T(8,128)} %bitcast.264, f32[72,3,128]{2,0,1:T(8,128)} %bitcast.255, f32[72,3,128]{2,0,1:T(8,128)} %bitcast.240, s32[8]{0:T(128)S(1)} %iota_add_fusion), kind=kOutput, calls=%fused_computation.36 | convolution fusion | flops 7312000 | bytes 286752 | tf_op jit(solution)/shard_map/ms,scl->mcl/dot_general | solution.py:169
  12.0 2.4 %collective-permute-start = (f32[9,7,128]{2,0,1:T(8,128)S(1)}, f32[9,7,128]{2,0,1:T(8,128)S(1)}, u32[]{:S(2)}, u32[]{:S(2)}) collective-permute-start(f32[9,7,128]{2,0,1:T(8,128)S(1)} %pad_maximum_fusion.2), channel_id=1, source_target_pairs={{0,16},{4,20},{8,24},{12,28},{16,0},{20,4},{24,8},{28,12},{1,17},{... | collective-permute-start | bytes 96776 | tf_op jit(solution)/shard_map/ppermute | solution.py:16
  20.9 2.8 %collective-permute-done.1 = f32[10,7,128]{2,0,1:T(8,128)S(1)} collective-permute-done((f32[10,7,128]{2,0,1:T(8,128)S(1)}, f32[10,7,128]{2,0,1:T(8,128)S(1)}, u32[]{:S(2)}, u32[]{:S(2)}) %collective-permute-start.1) | collective-permute-done | bytes 35872 | tf_op jit(solution)/shard_map/ppermute | solution.py:16
  25.9 1.4 %gather_fusion = s32[256]{0:T(256)S(1)} fusion(s32[1024]{0:T(1024)S(1)} %copy-done, s32[1024]{0:T(1024)S(1)} %pad_clamp_fusion.3), kind=kCustom, calls=%fused_computation | custom fusion | bytes 3072 | tf_op jit(solution)/shard_map/gather | solution.py:181
  28.0 1.3 %collective-permute-start.2 = (f32[12,7,128]{2,0,1:T(8,128)S(1)}, f32[12,7,128]{2,0,1:T(8,128)S(1)}, u32[]{:S(2)}, u32[]{:S(2)}) collective-permute-start(f32[12,7,128]{2,0,1:T(8,128)S(1)} %pad_maximum_fusion.4), channel_id=1, source_target_pairs={{0,4},{4,0},{8,12},{12,8},{16,20},{20,16},{24,28},{28,24},{1,5},{5... | collective-permute-start | bytes 129032 | tf_op jit(solution)/shard_map/ppermute | solution.py:16
  29.4 1.6 %collective-permute-done.2 = f32[12,7,128]{2,0,1:T(8,128)S(1)} collective-permute-done((f32[12,7,128]{2,0,1:T(8,128)S(1)}, f32[12,7,128]{2,0,1:T(8,128)S(1)}, u32[]{:S(2)}, u32[]{:S(2)}) %collective-permute-start.2) | collective-permute-done | bytes 43040 | tf_op jit(solution)/shard_map/ppermute | solution.py:16
  31.7 1.4 %gather_fusion.2 = s32[256]{0:T(256)S(1)} fusion(s32[1024]{0:T(1024)S(1)} %copy-done, s32[1024]{0:T(1024)S(1)} %pad_clamp_fusion.1), kind=kCustom, calls=%fused_computation.2 | custom fusion | bytes 3072 | tf_op jit(solution)/shard_map/gather | solution.py:184
  34.8 1.3 %collective-permute-start.3 = (f32[16,7,128]{2,0,1:T(8,128)S(1)}, f32[16,7,128]{2,0,1:T(8,128)S(1)}, u32[]{:S(2)}, u32[]{:S(2)}) collective-permute-start(f32[16,7,128]{2,0,1:T(8,128)S(1)} %concatenate.48), channel_id=1, source_target_pairs={{0,2},{1,3},{2,0},{3,1},{4,6},{5,7},{6,4},{7,5},{8,10},{9,11},{10,... | collective-permute-start | bytes 172040 | tf_op jit(solution)/shard_map/ppermute | solution.py:16
  36.3 1.6 %collective-permute-done.3 = f32[16,7,128]{2,0,1:T(8,128)S(1)} collective-permute-done((f32[16,7,128]{2,0,1:T(8,128)S(1)}, f32[16,7,128]{2,0,1:T(8,128)S(1)}, u32[]{:S(2)}, u32[]{:S(2)}) %collective-permute-start.3) | collective-permute-done | bytes 57376 | tf_op jit(solution)/shard_map/ppermute | solution.py:16
  38.6 4.5 %collective-permute-start.4 = (f32[24,7,128]{2,0,1:T(8,128)S(1)}, f32[24,7,128]{2,0,1:T(8,128)S(1)}, u32[]{:S(2)}, u32[]{:S(2)}) collective-permute-start(f32[24,7,128]{2,0,1:T(8,128)S(1)} %concatenate.49), channel_id=1, source_target_pairs={{0,1},{1,0},{2,3},{3,2},{4,5},{5,4},{6,7},{7,6},{8,9},{9,8},{10,11... | collective-permute-start | bytes 258056 | tf_op jit(solution)/shard_map/ppermute | solution.py:16
  43.1 0.9 %collective-permute-done.4 = f32[24,7,128]{2,0,1:T(8,128)S(1)} collective-permute-done((f32[24,7,128]{2,0,1:T(8,128)S(1)}, f32[24,7,128]{2,0,1:T(8,128)S(1)}, u32[]{:S(2)}, u32[]{:S(2)}) %collective-permute-start.4) | collective-permute-done | bytes 86048 | tf_op jit(solution)/shard_map/ppermute | solution.py:16
  44.5 3.0 %collective-permute-start.6 = (f32[32,7,128]{2,0,1:T(8,128)S(1)}, f32[32,7,128]{2,0,1:T(8,128)S(1)}, u32[]{:S(2)}, u32[]{:S(2)}) collective-permute-start(f32[32,7,128]{2,0,1:T(8,128)S(1)} %slice.278), channel_id=1, source_target_pairs={{4,8},{8,4},{12,16},{16,12},{20,24},{24,20},{5,9},{9,5},{13,17},{1... | collective-permute-start | bytes 344072 | tf_op jit(solution)/shard_map/ppermute | solution.py:23
  51.7 3.1 %collective-permute-done.5 = f32[32,7,128]{2,0,1:T(8,128)S(1)} collective-permute-done((f32[32,7,128]{2,0,1:T(8,128)S(1)}, f32[32,7,128]{2,0,1:T(8,128)S(1)}, u32[]{:S(2)}, u32[]{:S(2)}) %collective-permute-start.5) | collective-permute-done | bytes 114720 | tf_op jit(solution)/shard_map/ppermute | solution.py:23
  55.8 3.1 %collective-permute-start.8 = (f32[96,7,128]{2,0,1:T(8,128)S(1)}, f32[96,7,128]{2,0,1:T(8,128)S(1)}, u32[]{:S(2)}, u32[]{:S(2)}) collective-permute-start(f32[96,7,128]{2,0,1:T(8,128)S(1)} %pad_maximum_fusion.1), channel_id=1, source_target_pairs={{1,2},{2,1},{5,6},{6,5},{9,10},{10,9},{13,14},{14,13},{17,18},{18,... | collective-permute-start | bytes 1032200 | tf_op jit(solution)/shard_map/ppermute | solution.py:23
  58.9 5.4 %collective-permute-done.8 = f32[96,7,128]{2,0,1:T(8,128)S(1)} collective-permute-done((f32[96,7,128]{2,0,1:T(8,128)S(1)}, f32[96,7,128]{2,0,1:T(8,128)S(1)}, u32[]{:S(2)}, u32[]{:S(2)}) %collective-permute-start.8) | collective-permute-done | bytes 344096 | tf_op jit(solution)/shard_map/ppermute | solution.py:23
  65.0 1.0 %gather_fusion.1 = f32[256,7,128]{2,1,0:T(8,128)S(1)} fusion(f32[288,7,128]{2,1,0:T(8,128)S(1)} %copy.98, s32[1024]{0:T(1024)S(1)} %pad_clamp_fusion.2), kind=kCustom, calls=%fused_computation.1 | custom fusion | bytes 1836032 | tf_op jit(solution)/shard_map/gather | solution.py:201
  67.0 17.9 %multiply_reduce_fusion.3 = (f32[32,128]{1,0:T(8,128)S(1)}, f32[32,128]{1,0:T(8,128)S(1)}, f32[32,128]{1,0:T(8,128)S(1)}, f32[32,128]{1,0:T(8,128)S(1)}, f32[32,128]{1,0:T(8,128)S(1)}, /*index=5*/f32[32,128]{1,0:T(8,128)S(1)}) fusion(f32[32,8,128]{2,1,0:T(8,128)S(1)} %get-tuple-element.45, f32[32,8,128]{2,1,0:T(8,128)S(1)} %get-tuple-element.46, ...), kind=kLoop, calls=%fused_computation.8 | loop fusion | flops 96444416 | bytes 1458176 | tf_op jit(solution)/shard_map/vmap()/reduce_sum | solution.py:51
  (159 shorter events, 17.1 us)
Async XLA Ops:
  0.0 25.9 %copy-start = (s32[1024]{0:T(1024)S(1)}, s32[1024]{0:T(1024)}, u32[]{:S(2)}) copy-start(s32[1024]{0:T(1024)} %param.13) | copy-start | bytes 12292
  0.0 14.5 %copy-start.7 = (s32[5]{0:T(128)S(1)}, s32[5]{0:T(128)}, u32[]{:S(2)}) copy-start(s32[5]{0:T(128)} %constant.212.clone) | copy-start | bytes 64
  0.0 19.9 %copy-start.2 = (f32[1,1,72,3,128]{4,2,3,1,0:T(8,128)S(1)}, f32[1,1,72,3,128]{4,2,3,1,0:T(8,128)}, u32[]{:S(2)}) copy-start(f32[1,1,72,3,128]{4,2,3,1,0:T(8,128)} %param.10) | copy-start | bytes 331780
  0.0 19.9 %copy-start.1 = (f32[1,1,72,3,128]{4,2,3,1,0:T(8,128)S(1)}, f32[1,1,72,3,128]{4,2,3,1,0:T(8,128)}, u32[]{:S(2)}) copy-start(f32[1,1,72,3,128]{4,2,3,1,0:T(8,128)} %param.9) | copy-start | bytes 331780
  0.0 19.9 %copy-start.4 = (f32[1,1,72,128]{3,2,1,0:T(8,128)S(1)}, f32[1,1,72,128]{3,2,1,0:T(8,128)}, u32[]{:S(2)}) copy-start(f32[1,1,72,128]{3,2,1,0:T(8,128)} %param.11) | copy-start | bytes 110596
  4.4 19.7 %copy-start.3 = (s32[5,8,4]{1,2,0:T(4,128)S(1)}, s32[5,8,4]{1,2,0:T(4,128)}, u32[]{:S(2)}) copy-start(s32[5,8,4]{1,2,0:T(4,128)} %param.12) | copy-start | bytes 1924
  6.9 17.9 %copy-start.5 = (s32[1,1,32,8]{2,3,1,0:T(8,128)S(1)}, s32[1,1,32,8]{2,3,1,0:T(8,128)}, u32[]{:S(2)}) copy-start(s32[1,1,32,8]{2,3,1,0:T(8,128)} %param.14) | copy-start | bytes 3076
  12.0 7.8 %collective-permute-start = (f32[9,7,128]{2,0,1:T(8,128)S(1)}, f32[9,7,128]{2,0,1:T(8,128)S(1)}, u32[]{:S(2)}, u32[]{:S(2)}) collective-permute-start(f32[9,7,128]{2,0,1:T(8,128)S(1)} %pad_maximum_fusion.2), channel_id=1, source_target_pairs={{0,16},{4,20},{8,24},{12,28},{16,0},{20,4},{24,8},{28,12},{1,17},{... | collective-permute-start | bytes 96776 | tf_op jit(solution)/shard_map/ppermute | solution.py:16
  20.6 3.1 %collective-permute-start.1 = (f32[10,7,128]{2,0,1:T(8,128)S(1)}, f32[10,7,128]{2,0,1:T(8,128)S(1)}, u32[]{:S(2)}, u32[]{:S(2)}) collective-permute-start(f32[10,7,128]{2,0,1:T(8,128)S(1)} %pad_maximum_fusion.3), channel_id=1, source_target_pairs={{0,8},{4,12},{8,0},{12,4},{16,24},{20,28},{24,16},{28,20},{1,9},{5... | collective-permute-start | bytes 107528 | tf_op jit(solution)/shard_map/ppermute | solution.py:16
  25.9 5.6 %copy-start.6 = (s32[1,1,32,8]{2,3,1,0:T(8,128)S(1)}, s32[1,1,32,8]{2,3,1,0:T(8,128)}, u32[]{:S(2)}) copy-start(s32[1,1,32,8]{2,3,1,0:T(8,128)} %param.15) | copy-start | bytes 3076
  28.0 3.1 %collective-permute-start.2 = (f32[12,7,128]{2,0,1:T(8,128)S(1)}, f32[12,7,128]{2,0,1:T(8,128)S(1)}, u32[]{:S(2)}, u32[]{:S(2)}) collective-permute-start(f32[12,7,128]{2,0,1:T(8,128)S(1)} %pad_maximum_fusion.4), channel_id=1, source_target_pairs={{0,4},{4,0},{8,12},{12,8},{16,20},{20,16},{24,28},{28,24},{1,5},{5... | collective-permute-start | bytes 129032 | tf_op jit(solution)/shard_map/ppermute | solution.py:16
  34.8 3.1 %collective-permute-start.3 = (f32[16,7,128]{2,0,1:T(8,128)S(1)}, f32[16,7,128]{2,0,1:T(8,128)S(1)}, u32[]{:S(2)}, u32[]{:S(2)}) collective-permute-start(f32[16,7,128]{2,0,1:T(8,128)S(1)} %concatenate.48), channel_id=1, source_target_pairs={{0,2},{1,3},{2,0},{3,1},{4,6},{5,7},{6,4},{7,5},{8,10},{9,11},{10,... | collective-permute-start | bytes 172040 | tf_op jit(solution)/shard_map/ppermute | solution.py:16
  38.6 5.4 %collective-permute-start.4 = (f32[24,7,128]{2,0,1:T(8,128)S(1)}, f32[24,7,128]{2,0,1:T(8,128)S(1)}, u32[]{:S(2)}, u32[]{:S(2)}) collective-permute-start(f32[24,7,128]{2,0,1:T(8,128)S(1)} %concatenate.49), channel_id=1, source_target_pairs={{0,1},{1,0},{2,3},{3,2},{4,5},{5,4},{6,7},{7,6},{8,9},{9,8},{10,11... | collective-permute-start | bytes 258056 | tf_op jit(solution)/shard_map/ppermute | solution.py:16
  44.5 7.2 %collective-permute-start.6 = (f32[32,7,128]{2,0,1:T(8,128)S(1)}, f32[32,7,128]{2,0,1:T(8,128)S(1)}, u32[]{:S(2)}, u32[]{:S(2)}) collective-permute-start(f32[32,7,128]{2,0,1:T(8,128)S(1)} %slice.278), channel_id=1, source_target_pairs={{4,8},{8,4},{12,16},{16,12},{20,24},{24,20},{5,9},{9,5},{13,17},{1... | collective-permute-start | bytes 344072 | tf_op jit(solution)/shard_map/ppermute | solution.py:23
  47.5 7.3 %collective-permute-start.5 = (f32[32,7,128]{2,0,1:T(8,128)S(1)}, f32[32,7,128]{2,0,1:T(8,128)S(1)}, u32[]{:S(2)}, u32[]{:S(2)}) collective-permute-start(f32[32,7,128]{2,0,1:T(8,128)S(1)} %slice.278), channel_id=1, source_target_pairs={{0,4},{4,0},{8,12},{12,8},{16,20},{20,16},{24,28},{28,24},{1,5},{5... | collective-permute-start | bytes 344072 | tf_op jit(solution)/shard_map/ppermute | solution.py:23
  54.9 4.0 %collective-permute-start.7 = (f32[96,7,128]{2,0,1:T(8,128)S(1)}, f32[96,7,128]{2,0,1:T(8,128)S(1)}, u32[]{:S(2)}, u32[]{:S(2)}) collective-permute-start(f32[96,7,128]{2,0,1:T(8,128)S(1)} %pad_maximum_fusion.1), channel_id=1, source_target_pairs={{0,1},{1,0},{2,3},{3,2},{4,5},{5,4},{6,7},{7,6},{8,9},{9,8},{10,11... | collective-permute-start | bytes 1032200 | tf_op jit(solution)/shard_map/ppermute | solution.py:23
  55.8 8.6 %collective-permute-start.8 = (f32[96,7,128]{2,0,1:T(8,128)S(1)}, f32[96,7,128]{2,0,1:T(8,128)S(1)}, u32[]{:S(2)}, u32[]{:S(2)}) collective-permute-start(f32[96,7,128]{2,0,1:T(8,128)S(1)} %pad_maximum_fusion.1), channel_id=1, source_target_pairs={{1,2},{2,1},{5,6},{6,5},{9,10},{10,9},{13,14},{14,13},{17,18},{18,... | collective-permute-start | bytes 1032200 | tf_op jit(solution)/shard_map/ppermute | solution.py:23

commit v18 on v15

--- a/solution.py
+++ b/solution.py
@@ -132,6 +132,7 @@
     lanes = positions.shape[4]
     me = column_index * size_y + row_index
     held = jnp.concatenate([positions[0, 0], strength[0, 0], core[0, 0][:, None, :]], axis=1)
+    held = lax.optimization_barrier(held)
     slot_table = slot_multipoles(held[:, 0:3], held[:, 3:6], held[:, 6])
     width = slot_table.shape[1]
     gathered = table_blocks(slot_table, lanes)

time: 79.5 us -> 78.7 us (0.990)
  other arithmetic: 22.6 us -> 21.8 us
    sub x1 -> x0, other arithmetic: 1.05 us -> none  [slot_multipoles(): pos - rough[:, :, None]]
where the time goes in v18:
time: 78.7 us; the launch traced here: 78.3 us
  other arithmetic  21.8 us (28%)
  starting transfers between devices  15.4 us (20%)
  local copies, waits for them, and re-layouts  14.4 us (18%)
  waiting for transfers between devices  12.8 us (16%)
  between operations  12.5 us (16%)
  matrix products  1.43 us (2%)
    reduce_sum x1, other arithmetic, evaluate(): arm_x = jnp.sum(extra[:, 1][:, None, :] * weight, axis=(0, 2))  17.7 us
    ppermute x5, starting transfers between devices, from_partner(): lax.ppermute(shard, axis, [(i, i ^ 1 << apart) for i in range(lax.axis_si...  8.79 us
    ppermute x2, waiting for transfers between devices, swapped(): lax.ppermute(shard, axis, second)  6.65 us
    ppermute x2, starting transfers between devices, swapped(): lax.ppermute(shard, axis, second)  5.87 us
    ppermute x2, waiting for transfers between devices, swapped(): lax.ppermute(shard, axis, first)  3.46 us
    ppermute x5, waiting for transfers between devices, from_partner(): lax.ppermute(shard, axis, [(i, i ^ 1 << apart) for i in range(lax.axis_si...  2.68 us
  transfers between devices with their start and end apart: 9, of which 6 were waited for; matrix products, arithmetic and copies ran while one was open for 14% of the time, Pallas kernels for 0%

profile of v18, /device:TPU:9, one launch (start us, length us, event | category | flops | bytes accessed | tf_op | source)
XLA Modules:
  0.0 78.3 jit_solution(1245395583104648289)
XLA Ops:
  0.0 1.1 %copy_bitcast_fusion = (f32[72,3,128]{2,1,0:T(4,128)S(1)}, f32[72,3,128]{2,1,0:T(4,128)S(1)}) fusion(f32[1,1,72,3,128]{4,2,3,1,0:T(8,128)} %param.9, f32[1,1,72,3,128]{4,2,3,1,0:T(8,128)} %param.8), kind=kLoop, calls=%fused_computation.29 | loop fusion | bytes 442368 | tf_op jit(solution)/shard_map/squeeze | solution.py:134
  1.1 0.9 %pad_maximum_fusion.2 = f32[72,7,128]{2,1,0:T(8,128)S(1)} fusion(f32[72,1,128]{2,1,0:T(1,128)} %bitcast.242, f32[72,3,128]{2,1,0:T(4,128)S(1)} %get-tuple-element.94, f32[72,3,128]{2,1,0:T(4,128)S(1)} %get-tuple-element.95), kind=kLoop, calls=%fused_computation.18 | loop fusion | flops 129024 | bytes 516096 | tf_op jit(solution)/shard_map/concatenate | solution.py:134
  2.1 1.5 %constant_dynamic-slice_fusion.11 = (s32[1,1,1]{1,2,0:T(1,128)}, s32[1,1,1]{1,2,0:T(1,128)}, s32[1,1,1]{1,2,0:T(1,128)}, s32[1,1,1]{1,2,0:T(1,128)}, s32[1,1,1]{...) fusion(s32[5,8,4]{1,2,0:T(4,128)} %param.11, ...), kind=kLoop, calls=%fused_computation.273 | loop fusion | bytes 108 | tf_op jit(solution)/shard_map/dynamic_slice | solution.py:152
  12.8 2.4 %collective-permute-start = (f32[9,7,128]{2,1,0:T(8,128)S(1)}, f32[9,7,128]{2,1,0:T(8,128)S(1)}, u32[]{:S(2)}, u32[]{:S(2)}) collective-permute-start(f32[9,7,128]{2,1,0:T(8,128)S(1)} %pad_maximum_fusion.5), channel_id=1, source_target_pairs={{0,16},{4,20},{8,24},{12,28},{16,0},{20,4},{24,8},{28,12},{1,17},{... | collective-permute-start | bytes 96776 | tf_op jit(solution)/shard_map/ppermute | solution.py:16
  16.4 1.4 %gather_fusion.2 = s32[256]{0:T(256)S(1)} fusion(s32[1024]{0:T(1024)S(1)} %copy-done, s32[1024]{0:T(1024)S(1)} %pad_clamp_fusion.1), kind=kCustom, calls=%fused_computation.2 | custom fusion | bytes 3072 | tf_op jit(solution)/shard_map/gather | solution.py:140
  23.6 1.3 %collective-permute-done.1 = f32[10,7,128]{2,1,0:T(8,128)S(1)} collective-permute-done((f32[10,7,128]{2,1,0:T(8,128)S(1)}, f32[10,7,128]{2,1,0:T(8,128)S(1)}, u32[]{:S(2)}, u32[]{:S(2)}) %collective-permute-start.1) | collective-permute-done | bytes 35872 | tf_op jit(solution)/shard_map/ppermute | solution.py:16
  24.9 1.3 %collective-permute-start.2 = (f32[12,7,128]{2,1,0:T(8,128)S(1)}, f32[12,7,128]{2,1,0:T(8,128)S(1)}, u32[]{:S(2)}, u32[]{:S(2)}) collective-permute-start(f32[12,7,128]{2,1,0:T(8,128)S(1)} %pad_maximum_fusion.3), channel_id=1, source_target_pairs={{0,4},{4,0},{8,12},{12,8},{16,20},{20,16},{24,28},{28,24},{1,5},{5... | collective-permute-start | bytes 129032 | tf_op jit(solution)/shard_map/ppermute | solution.py:16
  27.4 1.4 %gather_fusion = s32[256]{0:T(256)S(1)} fusion(s32[1024]{0:T(1024)S(1)} %copy-done, s32[1024]{0:T(1024)S(1)} %get-tuple-element.97), kind=kCustom, calls=%fused_computation | custom fusion | bytes 3072 | tf_op jit(solution)/shard_map/gather | solution.py:178
  29.0 1.3 %collective-permute-start.3 = (f32[16,7,128]{2,1,0:T(8,128)S(1)}, f32[16,7,128]{2,1,0:T(8,128)S(1)}, u32[]{:S(2)}, u32[]{:S(2)}) collective-permute-start(f32[16,7,128]{2,1,0:T(8,128)S(1)} %constant_dynamic-update-slice_fusion), channel_id=1, source_target_pairs={{0,2},{1,3},{2,0},{3,1},{4,6},{5,7},{6,4},{7,5},{8,10},{9,11},{10,... | collective-permute-start | bytes 172040 | tf_op jit(solution)/shard_map/ppermute | solution.py:16
  31.7 0.5 collective-permute-done.3
  32.2 3.6 %collective-permute-start.4 = (f32[24,7,128]{2,1,0:T(8,128)S(1)}, f32[24,7,128]{2,1,0:T(8,128)S(1)}, u32[]{:S(2)}, u32[]{:S(2)}) collective-permute-start(f32[24,7,128]{2,1,0:T(8,128)S(1)} %get-tuple-element.57), channel_id=1, source_target_pairs={{0,1},{1,0},{2,3},{3,2},{4,5},{5,4},{6,7},{7,6},{8,9},{9,8},{10,11... | collective-permute-start | bytes 258056 | tf_op jit(solution)/shard_map/ppermute | solution.py:16
  35.8 0.9 %collective-permute-done.4 = f32[24,7,128]{2,1,0:T(8,128)S(1)} collective-permute-done((f32[24,7,128]{2,1,0:T(8,128)S(1)}, f32[24,7,128]{2,1,0:T(8,128)S(1)}, u32[]{:S(2)}, u32[]{:S(2)}) %collective-permute-start.4) | collective-permute-done | bytes 86048 | tf_op jit(solution)/shard_map/ppermute | solution.py:16
  36.8 2.8 %collective-permute-start.6 = (f32[32,7,128]{2,1,0:T(8,128)S(1)}, f32[32,7,128]{2,1,0:T(8,128)S(1)}, u32[]{:S(2)}, u32[]{:S(2)}) collective-permute-start(f32[32,7,128]{2,1,0:T(8,128)S(1)} %slice.257), channel_id=1, source_target_pairs={{4,8},{8,4},{12,16},{16,12},{20,24},{24,20},{5,9},{9,5},{13,17},{1... | collective-permute-start | bytes 344072 | tf_op jit(solution)/shard_map/ppermute | solution.py:23
  39.9 0.6 copy.227
  40.6 0.7 gather_fusion.3
  43.6 0.7 collective-permute-done.6
  44.4 3.5 %collective-permute-done.5 = f32[32,7,128]{2,1,0:T(8,128)S(1)} collective-permute-done((f32[32,7,128]{2,1,0:T(8,128)S(1)}, f32[32,7,128]{2,1,0:T(8,128)S(1)}, u32[]{:S(2)}, u32[]{:S(2)}) %collective-permute-start.5) | collective-permute-done | bytes 114720 | tf_op jit(solution)/shard_map/ppermute | solution.py:23
  47.9 0.6 collective-permute-start.7
  48.8 3.1 %collective-permute-start.8 = (f32[96,7,128]{2,1,0:T(8,128)S(1)}, f32[96,7,128]{2,1,0:T(8,128)S(1)}, u32[]{:S(2)}, u32[]{:S(2)}) collective-permute-start(f32[96,7,128]{2,1,0:T(8,128)S(1)} %pad_maximum_fusion.1), channel_id=1, source_target_pairs={{1,2},{2,1},{5,6},{6,5},{9,10},{10,9},{13,14},{14,13},{17,18},{18,... | collective-permute-start | bytes 1032200 | tf_op jit(solution)/shard_map/ppermute | solution.py:23
  51.9 5.9 %collective-permute-done.8 = f32[96,7,128]{2,1,0:T(8,128)S(1)} collective-permute-done((f32[96,7,128]{2,1,0:T(8,128)S(1)}, f32[96,7,128]{2,1,0:T(8,128)S(1)}, u32[]{:S(2)}, u32[]{:S(2)}) %collective-permute-start.8) | collective-permute-done | bytes 344096 | tf_op jit(solution)/shard_map/ppermute | solution.py:23
  57.9 1.0 %gather_fusion.1 = f32[256,7,128]{2,1,0:T(8,128)S(1)} fusion(f32[288,7,128]{2,1,0:T(8,128)S(1)} %constant_dynamic-update-slice_fusion.11, s32[1024]{0:T(1024)S(1)} %pad_clamp_fusion.2), kind=kCustom, calls=%fused_computation.1 | custom fusion | bytes 1836032 | tf_op jit(solution)/shard_map/gather | solution.py:187
  58.9 0.6 fusion.76
  59.9 17.7 %multiply_reduce_fusion.3 = (f32[32,128]{1,0:T(8,128)S(1)}, f32[32,128]{1,0:T(8,128)S(1)}, f32[32,128]{1,0:T(8,128)S(1)}, f32[32,128]{1,0:T(8,128)S(1)}, f32[32,128]{1,0:T(8,128)S(1)}, /*index=5*/f32[32,128]{1,0:T(8,128)S(1)}) fusion(f32[32,8,128]{2,1,0:T(8,128)S(1)} %get-tuple-element.40, f32[32,8,128]{2,1,0:T(8,128)S(1)} %get-tuple-element.41, ...), kind=kLoop, calls=%fused_computation.8 | loop fusion | flops 96444416 | bytes 1458176 | tf_op jit(solution)/shard_map/vmap()/reduce_sum | solution.py:51
  77.6 0.6 fusion.20
  (148 shorter events, 10.5 us)
Async XLA Ops:
  0.0 16.4 %copy-start = (s32[1024]{0:T(1024)S(1)}, s32[1024]{0:T(1024)}, u32[]{:S(2)}) copy-start(s32[1024]{0:T(1024)} %param.12) | copy-start | bytes 12292
  0.0 15.2 %copy-start.1 = (s32[5,8,4]{1,2,0:T(4,128)S(1)}, s32[5,8,4]{1,2,0:T(4,128)}, u32[]{:S(2)}) copy-start(s32[5,8,4]{1,2,0:T(4,128)} %param.11) | copy-start | bytes 1924
  0.0 15.4 %copy-start.4 = (s32[5]{0:T(128)S(1)}, s32[5]{0:T(128)}, u32[]{:S(2)}) copy-start(s32[5]{0:T(128)} %constant.217) | copy-start | bytes 64
  1.1 15.1 %copy-start.2 = (s32[1,1,32,8]{2,3,1,0:T(8,128)S(1)}, s32[1,1,32,8]{2,3,1,0:T(8,128)}, u32[]{:S(2)}) copy-start(s32[1,1,32,8]{2,3,1,0:T(8,128)} %param.14) | copy-start | bytes 3076
  12.8 9.0 %collective-permute-start = (f32[9,7,128]{2,1,0:T(8,128)S(1)}, f32[9,7,128]{2,1,0:T(8,128)S(1)}, u32[]{:S(2)}, u32[]{:S(2)}) collective-permute-start(f32[9,7,128]{2,1,0:T(8,128)S(1)} %pad_maximum_fusion.5), channel_id=1, source_target_pairs={{0,16},{4,20},{8,24},{12,28},{16,0},{20,4},{24,8},{28,12},{1,17},{... | collective-permute-start | bytes 96776 | tf_op jit(solution)/shard_map/ppermute | solution.py:16
  16.4 5.3 %copy-start.3 = (s32[1,1,32,8]{2,3,1,0:T(8,128)S(1)}, s32[1,1,32,8]{2,3,1,0:T(8,128)}, u32[]{:S(2)}) copy-start(s32[1,1,32,8]{2,3,1,0:T(8,128)} %param.13) | copy-start | bytes 3076
  21.9 2.9 %collective-permute-start.1 = (f32[10,7,128]{2,1,0:T(8,128)S(1)}, f32[10,7,128]{2,1,0:T(8,128)S(1)}, u32[]{:S(2)}, u32[]{:S(2)}) collective-permute-start(f32[10,7,128]{2,1,0:T(8,128)S(1)} %pad_maximum_fusion.4), channel_id=1, source_target_pairs={{0,8},{4,12},{8,0},{12,4},{16,24},{20,28},{24,16},{28,20},{1,9},{5... | collective-permute-start | bytes 107528 | tf_op jit(solution)/shard_map/ppermute | solution.py:16
  24.9 4.0 %collective-permute-start.2 = (f32[12,7,128]{2,1,0:T(8,128)S(1)}, f32[12,7,128]{2,1,0:T(8,128)S(1)}, u32[]{:S(2)}, u32[]{:S(2)}) collective-permute-start(f32[12,7,128]{2,1,0:T(8,128)S(1)} %pad_maximum_fusion.3), channel_id=1, source_target_pairs={{0,4},{4,0},{8,12},{12,8},{16,20},{20,16},{24,28},{28,24},{1,5},{5... | collective-permute-start | bytes 129032 | tf_op jit(solution)/shard_map/ppermute | solution.py:16
  29.0 3.2 %collective-permute-start.3 = (f32[16,7,128]{2,1,0:T(8,128)S(1)}, f32[16,7,128]{2,1,0:T(8,128)S(1)}, u32[]{:S(2)}, u32[]{:S(2)}) collective-permute-start(f32[16,7,128]{2,1,0:T(8,128)S(1)} %constant_dynamic-update-slice_fusion), channel_id=1, source_target_pairs={{0,2},{1,3},{2,0},{3,1},{4,6},{5,7},{6,4},{7,5},{8,10},{9,11},{10,... | collective-permute-start | bytes 172040 | tf_op jit(solution)/shard_map/ppermute | solution.py:16
  32.2 4.5 %collective-permute-start.4 = (f32[24,7,128]{2,1,0:T(8,128)S(1)}, f32[24,7,128]{2,1,0:T(8,128)S(1)}, u32[]{:S(2)}, u32[]{:S(2)}) collective-permute-start(f32[24,7,128]{2,1,0:T(8,128)S(1)} %get-tuple-element.57), channel_id=1, source_target_pairs={{0,1},{1,0},{2,3},{3,2},{4,5},{5,4},{6,7},{7,6},{8,9},{9,8},{10,11... | collective-permute-start | bytes 258056 | tf_op jit(solution)/shard_map/ppermute | solution.py:16
  36.8 7.6 %collective-permute-start.6 = (f32[32,7,128]{2,1,0:T(8,128)S(1)}, f32[32,7,128]{2,1,0:T(8,128)S(1)}, u32[]{:S(2)}, u32[]{:S(2)}) collective-permute-start(f32[32,7,128]{2,1,0:T(8,128)S(1)} %slice.257), channel_id=1, source_target_pairs={{4,8},{8,4},{12,16},{16,12},{20,24},{24,20},{5,9},{9,5},{13,17},{1... | collective-permute-start | bytes 344072 | tf_op jit(solution)/shard_map/ppermute | solution.py:23
  39.6 8.2 %collective-permute-start.5 = (f32[32,7,128]{2,1,0:T(8,128)S(1)}, f32[32,7,128]{2,1,0:T(8,128)S(1)}, u32[]{:S(2)}, u32[]{:S(2)}) collective-permute-start(f32[32,7,128]{2,1,0:T(8,128)S(1)} %slice.257), channel_id=1, source_target_pairs={{0,4},{4,0},{8,12},{12,8},{16,20},{20,16},{24,28},{28,24},{1,5},{5... | collective-permute-start | bytes 344072 | tf_op jit(solution)/shard_map/ppermute | solution.py:23
  47.9 4.0 %collective-permute-start.7 = (f32[96,7,128]{2,1,0:T(8,128)S(1)}, f32[96,7,128]{2,1,0:T(8,128)S(1)}, u32[]{:S(2)}, u32[]{:S(2)}) collective-permute-start(f32[96,7,128]{2,1,0:T(8,128)S(1)} %pad_maximum_fusion.1), channel_id=1, source_target_pairs={{0,1},{1,0},{2,3},{3,2},{4,5},{5,4},{6,7},{7,6},{8,9},{9,8},{10,11... | collective-permute-start | bytes 1032200 | tf_op jit(solution)/shard_map/ppermute | solution.py:23
  48.8 9.1 %collective-permute-start.8 = (f32[96,7,128]{2,1,0:T(8,128)S(1)}, f32[96,7,128]{2,1,0:T(8,128)S(1)}, u32[]{:S(2)}, u32[]{:S(2)}) collective-permute-start(f32[96,7,128]{2,1,0:T(8,128)S(1)} %pad_maximum_fusion.1), channel_id=1, source_target_pairs={{1,2},{2,1},{5,6},{6,5},{9,10},{10,9},{13,14},{14,13},{17,18},{18,... | collective-permute-start | bytes 1032200 | tf_op jit(solution)/shard_map/ppermute | solution.py:23

commit v19 on v16

--- a/solution.py
+++ b/solution.py
@@ -138,6 +138,7 @@
     lanes = positions.shape[4]
     me = column_index * size_y + row_index
     held = jnp.concatenate([positions[0, 0], strength[0, 0], core[0, 0][:, None, :]], axis=1)
+    held = lax.optimization_barrier(held)
     slot_table = slot_multipoles(held[:, 0:3], held[:, 3:6], held[:, 6])
     width = slot_table.shape[1]
     gathered = table_blocks(slot_table, lanes)

time: 84.8 us -> 80.3 us (0.947)
  matrix products: 10 us -> 4.72 us
  other arithmetic: 23.5 us -> 24.5 us
    concatenate x0 -> x1, other arithmetic: none -> 1.01 us  [local(): jnp.concatenate([positions[0, 0], strength[0, 0], core[0, 0][:, None, :]]...]
    dot_general x5, matrix products: 2.14 us -> 1.17 us  [local(): leaving = jnp.einsum('ms,scl->mcl', take, held, precision=exact)]
    dot_general x1, matrix products: 1.21 us -> 0.31 us  [slot_multipoles(): total = jnp.einsum('scl,l->sc', stren, ones, precision=exact)]
    dot_general x1, matrix products: 1.3 us -> 0.41 us  [slot_multipoles(): jnp.einsum('scl,l->sc', pos - rough[:, :, None], ones, precision=exact)]
    dot_general x1, matrix products: 1.3 us -> 0.41 us  [slot_multipoles(): jnp.einsum('scl,l->sc', offset * offset, ones, precision=exact)]
    dot_general x1, matrix products: 1.19 us -> 0.31 us  [slot_multipoles(): rough = jnp.einsum('scl,l->sc', pos, ones, precision=exact) / lanes]
where the time goes in v19:
time: 80.3 us; the launch traced here: 80 us
  other arithmetic  24.5 us (31%)
  starting transfers between devices  16.5 us (21%)
  waiting for transfers between devices  14.8 us (18%)
  local copies, waits for them, and re-layouts  12.7 us (16%)
  between operations  6.83 us (9%)
  matrix products  4.72 us (6%)
    reduce_sum x1, other arithmetic, evaluate(): arm_x = jnp.sum(extra[:, 1][:, None, :] * weight, axis=(0, 2))  17.9 us
    ppermute x5, starting transfers between devices, from_partner(): lax.ppermute(shard, axis, [(i, i ^ 1 << apart) for i in range(lax.axis_si...  9.67 us
    ppermute x2, starting transfers between devices, swapped(): lax.ppermute(shard, axis, second)  6.05 us
    ppermute x5, waiting for transfers between devices, from_partner(): lax.ppermute(shard, axis, [(i, i ^ 1 << apart) for i in range(lax.axis_si...  5.86 us
    ppermute x2, waiting for transfers between devices, swapped(): lax.ppermute(shard, axis, second)  5.75 us
    ppermute x2, waiting for transfers between devices, swapped(): lax.ppermute(shard, axis, first)  3.15 us
    dot_general x5, matrix products, local(): jnp.einsum('sm,mcl->scl', put.astype(jnp.float32), arriving, precision=ex...  1.95 us
  transfers between devices with their start and end apart: 9, of which 7 were waited for; matrix products, arithmetic and copies ran while one was open for 14% of the time, Pallas kernels for 0%

profile of v19, /device:TPU:9, one launch (start us, length us, event | category | flops | bytes accessed | tf_op | source)
XLA Modules:
  0.0 80.0 jit_solution(11809922234868860144)
XLA Ops:
  0.0 1.0 %pad_maximum_fusion.2 = f32[72,7,128]{2,0,1:T(8,128)S(1)} fusion(f32[72,1,128]{2,0,1:T(8,128)} %bitcast.258, f32[72,3,128]{2,0,1:T(8,128)} %bitcast.249, f32[72,3,128]{2,0,1:T(8,128)} %bitcast.250), kind=kLoop, calls=%fused_computation.25 | loop fusion | flops 129024 | bytes 516096 | tf_op jit(solution)/shard_map/concatenate | solution.py:140
  1.7 0.7 broadcast_xor_fusion
  2.4 1.0 %select_reduce_fusion.12 = (s32[5]{0:T(128)S(1)}, s32[5]{0:T(128)S(1)}) fusion(s32[5,8,4]{1,2,0:T(4,128)} %param.12, s32[8,4]{0,1:T(4,128)S(1)} %multiply_add_fusion, s32[5]{0:T(128)S(1)} %broadcast_xor_fusion, pred[8,4]{0,1:T(4,128)(4,1)S(1)} %broadcast_compare_fusion), kind=kLoop, calls=%fused_computation.216 | loop fusion | flops 790 | bytes 860 | tf_op jit(solution)/shard_map/reduce_sum | solution.py:158
  3.4 0.6 subtract_reduce_fusion.1
  4.1 0.7 fusion.131
  7.7 2.4 %collective-permute-start = (f32[9,7,128]{2,0,1:T(8,128)S(1)}, f32[9,7,128]{2,0,1:T(8,128)S(1)}, u32[]{:S(2)}, u32[]{:S(2)}) collective-permute-start(f32[9,7,128]{2,0,1:T(8,128)S(1)} %pad_maximum_fusion.3), channel_id=1, source_target_pairs={{0,16},{4,20},{8,24},{12,28},{16,0},{20,4},{24,8},{28,12},{1,17},{... | collective-permute-start | bytes 96776 | tf_op jit(solution)/shard_map/ppermute | solution.py:16
  11.4 1.4 %gather_fusion.2 = s32[256]{0:T(256)S(1)} fusion(s32[1024]{0:T(1024)S(1)} %copy-done, s32[1024]{0:T(1024)S(1)} %pad_clamp_fusion.1), kind=kCustom, calls=%fused_computation.2 | custom fusion | bytes 3072 | tf_op jit(solution)/shard_map/gather | solution.py:179
  19.0 1.4 %gather_fusion = s32[256]{0:T(256)S(1)} fusion(s32[1024]{0:T(1024)S(1)} %copy-done, s32[1024]{0:T(1024)S(1)} %get-tuple-element.88), kind=kCustom, calls=%fused_computation | custom fusion | bytes 3072 | tf_op jit(solution)/shard_map/gather | solution.py:189
  23.4 1.5 %collective-permute-done.1 = f32[10,7,128]{2,0,1:T(8,128)S(1)} collective-permute-done((f32[10,7,128]{2,0,1:T(8,128)S(1)}, f32[10,7,128]{2,0,1:T(8,128)S(1)}, u32[]{:S(2)}, u32[]{:S(2)}) %collective-permute-start.1) | collective-permute-done | bytes 35872 | tf_op jit(solution)/shard_map/ppermute | solution.py:16
  25.6 1.3 %collective-permute-start.2 = (f32[12,7,128]{2,0,1:T(8,128)S(1)}, f32[12,7,128]{2,0,1:T(8,128)S(1)}, u32[]{:S(2)}, u32[]{:S(2)}) collective-permute-start(f32[12,7,128]{2,0,1:T(8,128)S(1)} %pad_maximum_fusion.5), channel_id=1, source_target_pairs={{0,4},{4,0},{8,12},{12,8},{16,20},{20,16},{24,28},{28,24},{1,5},{5... | collective-permute-start | bytes 129032 | tf_op jit(solution)/shard_map/ppermute | solution.py:16
  26.9 1.7 %collective-permute-done.2 = f32[12,7,128]{2,0,1:T(8,128)S(1)} collective-permute-done((f32[12,7,128]{2,0,1:T(8,128)S(1)}, f32[12,7,128]{2,0,1:T(8,128)S(1)}, u32[]{:S(2)}, u32[]{:S(2)}) %collective-permute-start.2) | collective-permute-done | bytes 43040 | tf_op jit(solution)/shard_map/ppermute | solution.py:16
  29.3 1.3 %collective-permute-start.3 = (f32[16,7,128]{2,0,1:T(8,128)S(1)}, f32[16,7,128]{2,0,1:T(8,128)S(1)}, u32[]{:S(2)}, u32[]{:S(2)}) collective-permute-start(f32[16,7,128]{2,0,1:T(8,128)S(1)} %concatenate.48), channel_id=1, source_target_pairs={{0,2},{1,3},{2,0},{3,1},{4,6},{5,7},{6,4},{7,5},{8,10},{9,11},{10,... | collective-permute-start | bytes 172040 | tf_op jit(solution)/shard_map/ppermute | solution.py:16
  30.7 1.7 %collective-permute-done.3 = f32[16,7,128]{2,0,1:T(8,128)S(1)} collective-permute-done((f32[16,7,128]{2,0,1:T(8,128)S(1)}, f32[16,7,128]{2,0,1:T(8,128)S(1)}, u32[]{:S(2)}, u32[]{:S(2)}) %collective-permute-start.3) | collective-permute-done | bytes 57376 | tf_op jit(solution)/shard_map/ppermute | solution.py:16
  33.1 4.5 %collective-permute-start.4 = (f32[24,7,128]{2,0,1:T(8,128)S(1)}, f32[24,7,128]{2,0,1:T(8,128)S(1)}, u32[]{:S(2)}, u32[]{:S(2)}) collective-permute-start(f32[24,7,128]{2,0,1:T(8,128)S(1)} %concatenate.49), channel_id=1, source_target_pairs={{0,1},{1,0},{2,3},{3,2},{4,5},{5,4},{6,7},{7,6},{8,9},{9,8},{10,11... | collective-permute-start | bytes 258056 | tf_op jit(solution)/shard_map/ppermute | solution.py:16
  37.6 0.9 %collective-permute-done.4 = f32[24,7,128]{2,0,1:T(8,128)S(1)} collective-permute-done((f32[24,7,128]{2,0,1:T(8,128)S(1)}, f32[24,7,128]{2,0,1:T(8,128)S(1)}, u32[]{:S(2)}, u32[]{:S(2)}) %collective-permute-start.4) | collective-permute-done | bytes 86048 | tf_op jit(solution)/shard_map/ppermute | solution.py:16
  38.9 3.0 %collective-permute-start.6 = (f32[32,7,128]{2,0,1:T(8,128)S(1)}, f32[32,7,128]{2,0,1:T(8,128)S(1)}, u32[]{:S(2)}, u32[]{:S(2)}) collective-permute-start(f32[32,7,128]{2,0,1:T(8,128)S(1)} %slice.292), channel_id=1, source_target_pairs={{4,8},{8,4},{12,16},{16,12},{20,24},{24,20},{5,9},{9,5},{13,17},{1... | collective-permute-start | bytes 344072 | tf_op jit(solution)/shard_map/ppermute | solution.py:23
  42.3 0.7 copy.143
  43.0 0.7 gather_fusion.3
  46.1 3.1 %collective-permute-done.5 = f32[32,7,128]{2,0,1:T(8,128)S(1)} collective-permute-done((f32[32,7,128]{2,0,1:T(8,128)S(1)}, f32[32,7,128]{2,0,1:T(8,128)S(1)}, u32[]{:S(2)}, u32[]{:S(2)}) %collective-permute-start.5) | collective-permute-done | bytes 114720 | tf_op jit(solution)/shard_map/ppermute | solution.py:23
  50.2 3.0 %collective-permute-start.8 = (f32[96,7,128]{2,0,1:T(8,128)S(1)}, f32[96,7,128]{2,0,1:T(8,128)S(1)}, u32[]{:S(2)}, u32[]{:S(2)}) collective-permute-start(f32[96,7,128]{2,0,1:T(8,128)S(1)} %pad_maximum_fusion.1), channel_id=1, source_target_pairs={{1,2},{2,1},{5,6},{6,5},{9,10},{10,9},{13,14},{14,13},{17,18},{18,... | collective-permute-start | bytes 1032200 | tf_op jit(solution)/shard_map/ppermute | solution.py:23
  53.3 5.4 %collective-permute-done.8 = f32[96,7,128]{2,0,1:T(8,128)S(1)} collective-permute-done((f32[96,7,128]{2,0,1:T(8,128)S(1)}, f32[96,7,128]{2,0,1:T(8,128)S(1)}, u32[]{:S(2)}, u32[]{:S(2)}) %collective-permute-start.8) | collective-permute-done | bytes 344096 | tf_op jit(solution)/shard_map/ppermute | solution.py:23
  59.4 1.0 %gather_fusion.1 = f32[256,7,128]{2,1,0:T(8,128)S(1)} fusion(f32[288,7,128]{2,1,0:T(8,128)S(1)} %copy.98, s32[1024]{0:T(1024)S(1)} %pad_clamp_fusion.2), kind=kCustom, calls=%fused_computation.1 | custom fusion | bytes 1836032 | tf_op jit(solution)/shard_map/gather | solution.py:198
  60.4 0.6 fusion.128
  61.4 17.9 %multiply_reduce_fusion.3 = (f32[32,128]{1,0:T(8,128)S(1)}, f32[32,128]{1,0:T(8,128)S(1)}, f32[32,128]{1,0:T(8,128)S(1)}, f32[32,128]{1,0:T(8,128)S(1)}, f32[32,128]{1,0:T(8,128)S(1)}, /*index=5*/f32[32,128]{1,0:T(8,128)S(1)}) fusion(f32[32,8,128]{2,1,0:T(8,128)S(1)} %get-tuple-element.39, f32[32,8,128]{2,1,0:T(8,128)S(1)} %get-tuple-element.40, ...), kind=kLoop, calls=%fused_computation.8 | loop fusion | flops 96444416 | bytes 1458176 | tf_op jit(solution)/shard_map/vmap()/reduce_sum | solution.py:51
  (153 shorter events, 15.5 us)
Async XLA Ops:
  0.0 11.4 %copy-start = (s32[1024]{0:T(1024)S(1)}, s32[1024]{0:T(1024)}, u32[]{:S(2)}) copy-start(s32[1024]{0:T(1024)} %param.13) | copy-start | bytes 12292
  0.0 10.2 %copy-start.4 = (s32[5]{0:T(128)S(1)}, s32[5]{0:T(128)}, u32[]{:S(2)}) copy-start(s32[5]{0:T(128)} %constant.212.clone) | copy-start | bytes 64
  0.0 10.1 %copy-start.1 = (s32[5,8,4]{1,2,0:T(4,128)S(1)}, s32[5,8,4]{1,2,0:T(4,128)}, u32[]{:S(2)}) copy-start(s32[5,8,4]{1,2,0:T(4,128)} %param.12) | copy-start | bytes 1924
  0.0 11.1 %copy-start.2 = (s32[1,1,32,8]{2,3,1,0:T(8,128)S(1)}, s32[1,1,32,8]{2,3,1,0:T(8,128)}, u32[]{:S(2)}) copy-start(s32[1,1,32,8]{2,3,1,0:T(8,128)} %param.15) | copy-start | bytes 3076
  7.7 13.5 %collective-permute-start = (f32[9,7,128]{2,0,1:T(8,128)S(1)}, f32[9,7,128]{2,0,1:T(8,128)S(1)}, u32[]{:S(2)}, u32[]{:S(2)}) collective-permute-start(f32[9,7,128]{2,0,1:T(8,128)S(1)} %pad_maximum_fusion.3), channel_id=1, source_target_pairs={{0,16},{4,20},{8,24},{12,28},{16,0},{20,4},{24,8},{28,12},{1,17},{... | collective-permute-start | bytes 96776 | tf_op jit(solution)/shard_map/ppermute | solution.py:16
  11.4 7.5 %copy-start.3 = (s32[1,1,32,8]{2,3,1,0:T(8,128)S(1)}, s32[1,1,32,8]{2,3,1,0:T(8,128)}, u32[]{:S(2)}) copy-start(s32[1,1,32,8]{2,3,1,0:T(8,128)} %param.14) | copy-start | bytes 3076
  21.8 3.1 %collective-permute-start.1 = (f32[10,7,128]{2,0,1:T(8,128)S(1)}, f32[10,7,128]{2,0,1:T(8,128)S(1)}, u32[]{:S(2)}, u32[]{:S(2)}) collective-permute-start(f32[10,7,128]{2,0,1:T(8,128)S(1)} %pad_maximum_fusion.4), channel_id=1, source_target_pairs={{0,8},{4,12},{8,0},{12,4},{16,24},{20,28},{24,16},{28,20},{1,9},{5... | collective-permute-start | bytes 107528 | tf_op jit(solution)/shard_map/ppermute | solution.py:16
  25.6 3.1 %collective-permute-start.2 = (f32[12,7,128]{2,0,1:T(8,128)S(1)}, f32[12,7,128]{2,0,1:T(8,128)S(1)}, u32[]{:S(2)}, u32[]{:S(2)}) collective-permute-start(f32[12,7,128]{2,0,1:T(8,128)S(1)} %pad_maximum_fusion.5), channel_id=1, source_target_pairs={{0,4},{4,0},{8,12},{12,8},{16,20},{20,16},{24,28},{28,24},{1,5},{5... | collective-permute-start | bytes 129032 | tf_op jit(solution)/shard_map/ppermute | solution.py:16
  29.3 3.1 %collective-permute-start.3 = (f32[16,7,128]{2,0,1:T(8,128)S(1)}, f32[16,7,128]{2,0,1:T(8,128)S(1)}, u32[]{:S(2)}, u32[]{:S(2)}) collective-permute-start(f32[16,7,128]{2,0,1:T(8,128)S(1)} %concatenate.48), channel_id=1, source_target_pairs={{0,2},{1,3},{2,0},{3,1},{4,6},{5,7},{6,4},{7,5},{8,10},{9,11},{10,... | collective-permute-start | bytes 172040 | tf_op jit(solution)/shard_map/ppermute | solution.py:16
  33.1 5.4 %collective-permute-start.4 = (f32[24,7,128]{2,0,1:T(8,128)S(1)}, f32[24,7,128]{2,0,1:T(8,128)S(1)}, u32[]{:S(2)}, u32[]{:S(2)}) collective-permute-start(f32[24,7,128]{2,0,1:T(8,128)S(1)} %concatenate.49), channel_id=1, source_target_pairs={{0,1},{1,0},{2,3},{3,2},{4,5},{5,4},{6,7},{7,6},{8,9},{9,8},{10,11... | collective-permute-start | bytes 258056 | tf_op jit(solution)/shard_map/ppermute | solution.py:16
  38.9 7.2 %collective-permute-start.6 = (f32[32,7,128]{2,0,1:T(8,128)S(1)}, f32[32,7,128]{2,0,1:T(8,128)S(1)}, u32[]{:S(2)}, u32[]{:S(2)}) collective-permute-start(f32[32,7,128]{2,0,1:T(8,128)S(1)} %slice.292), channel_id=1, source_target_pairs={{4,8},{8,4},{12,16},{16,12},{20,24},{24,20},{5,9},{9,5},{13,17},{1... | collective-permute-start | bytes 344072 | tf_op jit(solution)/shard_map/ppermute | solution.py:23
  41.9 7.3 %collective-permute-start.5 = (f32[32,7,128]{2,0,1:T(8,128)S(1)}, f32[32,7,128]{2,0,1:T(8,128)S(1)}, u32[]{:S(2)}, u32[]{:S(2)}) collective-permute-start(f32[32,7,128]{2,0,1:T(8,128)S(1)} %slice.292), channel_id=1, source_target_pairs={{0,4},{4,0},{8,12},{12,8},{16,20},{20,16},{24,28},{28,24},{1,5},{5... | collective-permute-start | bytes 344072 | tf_op jit(solution)/shard_map/ppermute | solution.py:23
  49.3 4.0 %collective-permute-start.7 = (f32[96,7,128]{2,0,1:T(8,128)S(1)}, f32[96,7,128]{2,0,1:T(8,128)S(1)}, u32[]{:S(2)}, u32[]{:S(2)}) collective-permute-start(f32[96,7,128]{2,0,1:T(8,128)S(1)} %pad_maximum_fusion.1), channel_id=1, source_target_pairs={{0,1},{1,0},{2,3},{3,2},{4,5},{5,4},{6,7},{7,6},{8,9},{9,8},{10,11... | collective-permute-start | bytes 1032200 | tf_op jit(solution)/shard_map/ppermute | solution.py:23
  50.2 8.6 %collective-permute-start.8 = (f32[96,7,128]{2,0,1:T(8,128)S(1)}, f32[96,7,128]{2,0,1:T(8,128)S(1)}, u32[]{:S(2)}, u32[]{:S(2)}) collective-permute-start(f32[96,7,128]{2,0,1:T(8,128)S(1)} %pad_maximum_fusion.1), channel_id=1, source_target_pairs={{1,2},{2,1},{5,6},{6,5},{9,10},{10,9},{13,14},{14,13},{17,18},{18,... | collective-permute-start | bytes 1032200 | tf_op jit(solution)/shard_map/ppermute | solution.py:23

commit v20 on v18

--- a/solution.py
+++ b/solution.py
@@ -16,10 +16,12 @@
     return lax.ppermute(shard, axis, [(i, i ^ 1 << apart) for i in range(lax.axis_size(axis))])
 
 
-def swapped(shard, axis):
+def swapped(shard, axis, wrap=False):
     size = lax.axis_size(axis)
     first = [(i, i ^ 1) for i in range(size)]
     second = [(i, i + 1 - 2 * (i % 2 == 0)) for i in range(1, size - 1)]
+    if wrap and size > 2:
+        second = second + [(0, size - 1), (size - 1, 0)]
     return jnp.concatenate([lax.ppermute(shard, axis, first), shard, lax.ppermute(shard, axis, second)], axis=0)
 
 
@@ -182,7 +184,7 @@
     delta_y = source_device % size_y - row_index
     sign_x = 2 * (column_index % 2) - 1
     sign_y = 2 * (row_index % 2) - 1
-    source_pool = swapped(swapped(blocks, "gx"), "gy")
+    source_pool = swapped(swapped(blocks, "gx"), "gy", wrap=True)
     pool_index = ((1 + delta_y * sign_y) * 3 + (1 + delta_x * sign_x)) * nbd + source_slot
     sources_all = source_pool[pool_index]
     targets = blocks[:, 0:3]

time: 78.7 us -> 80.4 us (1.022)
  waiting for transfers between devices: 12.8 us -> 16.4 us
  starting transfers between devices: 15.4 us -> 13.6 us
    ppermute x2, waiting for transfers between devices: 6.65 us -> 10.2 us  [swapped(): lax.ppermute(shard, axis, second)]
    ppermute x2, starting transfers between devices: 5.87 us -> 4.03 us  [swapped(): lax.ppermute(shard, axis, second)]
where the time goes in v20:
time: 80.4 us; the launch traced here: 80 us
  other arithmetic  21.8 us (27%)
  waiting for transfers between devices  16.4 us (20%)
  local copies, waits for them, and re-layouts  14.4 us (18%)
  starting transfers between devices  13.6 us (17%)
  between operations  12.4 us (15%)
  matrix products  1.43 us (2%)
    reduce_sum x1, other arithmetic, evaluate(): arm_x = jnp.sum(extra[:, 1][:, None, :] * weight, axis=(0, 2))  17.7 us
    ppermute x2, waiting for transfers between devices, swapped(): lax.ppermute(shard, axis, second)  10.2 us
    ppermute x5, starting transfers between devices, from_partner(): lax.ppermute(shard, axis, [(i, i ^ 1 << apart) for i in range(lax.axis_si...  8.79 us
    ppermute x2, starting transfers between devices, swapped(): lax.ppermute(shard, axis, second)  4.03 us
    ppermute x2, waiting for transfers between devices, swapped(): lax.ppermute(shard, axis, first)  3.46 us
    ppermute x5, waiting for transfers between devices, from_partner(): lax.ppermute(shard, axis, [(i, i ^ 1 << apart) for i in range(lax.axis_si...  2.68 us
  transfers between devices with their start and end apart: 9, of which 6 were waited for; matrix products, arithmetic and copies ran while one was open for 14% of the time, Pallas kernels for 0%

profile of v20, /device:TPU:9, one launch (start us, length us, event | category | flops | bytes accessed | tf_op | source)
XLA Modules:
  0.0 80.0 jit_solution(15743868112994111704)
XLA Ops:
  0.0 1.1 %copy_bitcast_fusion = (f32[72,3,128]{2,1,0:T(4,128)S(1)}, f32[72,3,128]{2,1,0:T(4,128)S(1)}) fusion(f32[1,1,72,3,128]{4,2,3,1,0:T(8,128)} %param.9, f32[1,1,72,3,128]{4,2,3,1,0:T(8,128)} %param.8), kind=kLoop, calls=%fused_computation.29 | loop fusion | bytes 442368 | tf_op jit(solution)/shard_map/squeeze | solution.py:136
  1.1 0.9 %pad_maximum_fusion.2 = f32[72,7,128]{2,1,0:T(8,128)S(1)} fusion(f32[72,1,128]{2,1,0:T(1,128)} %bitcast.242, f32[72,3,128]{2,1,0:T(4,128)S(1)} %get-tuple-element.94, f32[72,3,128]{2,1,0:T(4,128)S(1)} %get-tuple-element.95), kind=kLoop, calls=%fused_computation.18 | loop fusion | flops 129024 | bytes 516096 | tf_op jit(solution)/shard_map/concatenate | solution.py:136
  2.1 1.5 %constant_dynamic-slice_fusion.11 = (s32[1,1,1]{1,2,0:T(1,128)}, s32[1,1,1]{1,2,0:T(1,128)}, s32[1,1,1]{1,2,0:T(1,128)}, s32[1,1,1]{1,2,0:T(1,128)}, s32[1,1,1]{...) fusion(s32[5,8,4]{1,2,0:T(4,128)} %param.11, ...), kind=kLoop, calls=%fused_computation.273 | loop fusion | bytes 108 | tf_op jit(solution)/shard_map/dynamic_slice | solution.py:154
  12.8 2.4 %collective-permute-start = (f32[9,7,128]{2,1,0:T(8,128)S(1)}, f32[9,7,128]{2,1,0:T(8,128)S(1)}, u32[]{:S(2)}, u32[]{:S(2)}) collective-permute-start(f32[9,7,128]{2,1,0:T(8,128)S(1)} %pad_maximum_fusion.5), channel_id=1, source_target_pairs={{0,16},{4,20},{8,24},{12,28},{16,0},{20,4},{24,8},{28,12},{1,17},{... | collective-permute-start | bytes 96776 | tf_op jit(solution)/shard_map/ppermute | solution.py:16
  16.4 1.4 %gather_fusion.2 = s32[256]{0:T(256)S(1)} fusion(s32[1024]{0:T(1024)S(1)} %copy-done, s32[1024]{0:T(1024)S(1)} %pad_clamp_fusion.1), kind=kCustom, calls=%fused_computation.2 | custom fusion | bytes 3072 | tf_op jit(solution)/shard_map/gather | solution.py:142
  23.6 1.3 %collective-permute-done.1 = f32[10,7,128]{2,1,0:T(8,128)S(1)} collective-permute-done((f32[10,7,128]{2,1,0:T(8,128)S(1)}, f32[10,7,128]{2,1,0:T(8,128)S(1)}, u32[]{:S(2)}, u32[]{:S(2)}) %collective-permute-start.1) | collective-permute-done | bytes 35872 | tf_op jit(solution)/shard_map/ppermute | solution.py:16
  24.9 1.3 %collective-permute-start.2 = (f32[12,7,128]{2,1,0:T(8,128)S(1)}, f32[12,7,128]{2,1,0:T(8,128)S(1)}, u32[]{:S(2)}, u32[]{:S(2)}) collective-permute-start(f32[12,7,128]{2,1,0:T(8,128)S(1)} %pad_maximum_fusion.3), channel_id=1, source_target_pairs={{0,4},{4,0},{8,12},{12,8},{16,20},{20,16},{24,28},{28,24},{1,5},{5... | collective-permute-start | bytes 129032 | tf_op jit(solution)/shard_map/ppermute | solution.py:16
  27.4 1.4 %gather_fusion = s32[256]{0:T(256)S(1)} fusion(s32[1024]{0:T(1024)S(1)} %copy-done, s32[1024]{0:T(1024)S(1)} %get-tuple-element.97), kind=kCustom, calls=%fused_computation | custom fusion | bytes 3072 | tf_op jit(solution)/shard_map/gather | solution.py:180
  29.0 1.3 %collective-permute-start.3 = (f32[16,7,128]{2,1,0:T(8,128)S(1)}, f32[16,7,128]{2,1,0:T(8,128)S(1)}, u32[]{:S(2)}, u32[]{:S(2)}) collective-permute-start(f32[16,7,128]{2,1,0:T(8,128)S(1)} %constant_dynamic-update-slice_fusion), channel_id=1, source_target_pairs={{0,2},{1,3},{2,0},{3,1},{4,6},{5,7},{6,4},{7,5},{8,10},{9,11},{10,... | collective-permute-start | bytes 172040 | tf_op jit(solution)/shard_map/ppermute | solution.py:16
  31.7 0.5 collective-permute-done.3
  32.2 3.6 %collective-permute-start.4 = (f32[24,7,128]{2,1,0:T(8,128)S(1)}, f32[24,7,128]{2,1,0:T(8,128)S(1)}, u32[]{:S(2)}, u32[]{:S(2)}) collective-permute-start(f32[24,7,128]{2,1,0:T(8,128)S(1)} %get-tuple-element.57), channel_id=1, source_target_pairs={{0,1},{1,0},{2,3},{3,2},{4,5},{5,4},{6,7},{7,6},{8,9},{9,8},{10,11... | collective-permute-start | bytes 258056 | tf_op jit(solution)/shard_map/ppermute | solution.py:16
  35.8 0.9 %collective-permute-done.4 = f32[24,7,128]{2,1,0:T(8,128)S(1)} collective-permute-done((f32[24,7,128]{2,1,0:T(8,128)S(1)}, f32[24,7,128]{2,1,0:T(8,128)S(1)}, u32[]{:S(2)}, u32[]{:S(2)}) %collective-permute-start.4) | collective-permute-done | bytes 86048 | tf_op jit(solution)/shard_map/ppermute | solution.py:16
  36.8 2.8 %collective-permute-start.6 = (f32[32,7,128]{2,1,0:T(8,128)S(1)}, f32[32,7,128]{2,1,0:T(8,128)S(1)}, u32[]{:S(2)}, u32[]{:S(2)}) collective-permute-start(f32[32,7,128]{2,1,0:T(8,128)S(1)} %slice.257), channel_id=1, source_target_pairs={{4,8},{8,4},{12,16},{16,12},{20,24},{24,20},{5,9},{9,5},{13,17},{1... | collective-permute-start | bytes 344072 | tf_op jit(solution)/shard_map/ppermute | solution.py:25
  39.9 0.6 copy.227
  40.6 0.7 gather_fusion.3
  43.6 0.7 collective-permute-done.6
  44.4 3.5 %collective-permute-done.5 = f32[32,7,128]{2,1,0:T(8,128)S(1)} collective-permute-done((f32[32,7,128]{2,1,0:T(8,128)S(1)}, f32[32,7,128]{2,1,0:T(8,128)S(1)}, u32[]{:S(2)}, u32[]{:S(2)}) %collective-permute-start.5) | collective-permute-done | bytes 114720 | tf_op jit(solution)/shard_map/ppermute | solution.py:25
  47.9 0.6 collective-permute-start.7
  48.8 1.2 %collective-permute-start.8 = (f32[96,7,128]{2,1,0:T(8,128)S(1)}, f32[96,7,128]{2,1,0:T(8,128)S(1)}, u32[]{:S(2)}, u32[]{:S(2)}) collective-permute-start(f32[96,7,128]{2,1,0:T(8,128)S(1)} %pad_maximum_fusion.1), channel_id=1, source_target_pairs={{1,2},{2,1},{0,3},{3,0},{5,6},{6,5},{4,7},{7,4},{9,10},{10,9},{8,1... | collective-permute-start | bytes 1032200 | tf_op jit(solution)/shard_map/ppermute | solution.py:25
  50.1 9.5 %collective-permute-done.8 = f32[96,7,128]{2,1,0:T(8,128)S(1)} collective-permute-done((f32[96,7,128]{2,1,0:T(8,128)S(1)}, f32[96,7,128]{2,1,0:T(8,128)S(1)}, u32[]{:S(2)}, u32[]{:S(2)}) %collective-permute-start.8) | collective-permute-done | bytes 344096 | tf_op jit(solution)/shard_map/ppermute | solution.py:25
  59.6 1.0 %gather_fusion.1 = f32[256,7,128]{2,1,0:T(8,128)S(1)} fusion(f32[288,7,128]{2,1,0:T(8,128)S(1)} %constant_dynamic-update-slice_fusion.11, s32[1024]{0:T(1024)S(1)} %pad_clamp_fusion.2), kind=kCustom, calls=%fused_computation.1 | custom fusion | bytes 1836032 | tf_op jit(solution)/shard_map/gather | solution.py:189
  60.7 0.6 fusion.76
  61.6 17.7 %multiply_reduce_fusion.3 = (f32[32,128]{1,0:T(8,128)S(1)}, f32[32,128]{1,0:T(8,128)S(1)}, f32[32,128]{1,0:T(8,128)S(1)}, f32[32,128]{1,0:T(8,128)S(1)}, f32[32,128]{1,0:T(8,128)S(1)}, /*index=5*/f32[32,128]{1,0:T(8,128)S(1)}) fusion(f32[32,8,128]{2,1,0:T(8,128)S(1)} %get-tuple-element.40, f32[32,8,128]{2,1,0:T(8,128)S(1)} %get-tuple-element.41, ...), kind=kLoop, calls=%fused_computation.8 | loop fusion | flops 96444416 | bytes 1458176 | tf_op jit(solution)/shard_map/vmap()/reduce_sum | solution.py:53
  79.4 0.6 fusion.20
  (148 shorter events, 10.5 us)
Async XLA Ops:
  0.0 16.4 %copy-start = (s32[1024]{0:T(1024)S(1)}, s32[1024]{0:T(1024)}, u32[]{:S(2)}) copy-start(s32[1024]{0:T(1024)} %param.12) | copy-start | bytes 12292
  0.0 15.2 %copy-start.1 = (s32[5,8,4]{1,2,0:T(4,128)S(1)}, s32[5,8,4]{1,2,0:T(4,128)}, u32[]{:S(2)}) copy-start(s32[5,8,4]{1,2,0:T(4,128)} %param.11) | copy-start | bytes 1924
  0.0 15.4 %copy-start.4 = (s32[5]{0:T(128)S(1)}, s32[5]{0:T(128)}, u32[]{:S(2)}) copy-start(s32[5]{0:T(128)} %constant.217) | copy-start | bytes 64
  1.1 15.1 %copy-start.2 = (s32[1,1,32,8]{2,3,1,0:T(8,128)S(1)}, s32[1,1,32,8]{2,3,1,0:T(8,128)}, u32[]{:S(2)}) copy-start(s32[1,1,32,8]{2,3,1,0:T(8,128)} %param.14) | copy-start | bytes 3076
  12.8 9.0 %collective-permute-start = (f32[9,7,128]{2,1,0:T(8,128)S(1)}, f32[9,7,128]{2,1,0:T(8,128)S(1)}, u32[]{:S(2)}, u32[]{:S(2)}) collective-permute-start(f32[9,7,128]{2,1,0:T(8,128)S(1)} %pad_maximum_fusion.5), channel_id=1, source_target_pairs={{0,16},{4,20},{8,24},{12,28},{16,0},{20,4},{24,8},{28,12},{1,17},{... | collective-permute-start | bytes 96776 | tf_op jit(solution)/shard_map/ppermute | solution.py:16
  16.4 5.3 %copy-start.3 = (s32[1,1,32,8]{2,3,1,0:T(8,128)S(1)}, s32[1,1,32,8]{2,3,1,0:T(8,128)}, u32[]{:S(2)}) copy-start(s32[1,1,32,8]{2,3,1,0:T(8,128)} %param.13) | copy-start | bytes 3076
  21.9 2.9 %collective-permute-start.1 = (f32[10,7,128]{2,1,0:T(8,128)S(1)}, f32[10,7,128]{2,1,0:T(8,128)S(1)}, u32[]{:S(2)}, u32[]{:S(2)}) collective-permute-start(f32[10,7,128]{2,1,0:T(8,128)S(1)} %pad_maximum_fusion.4), channel_id=1, source_target_pairs={{0,8},{4,12},{8,0},{12,4},{16,24},{20,28},{24,16},{28,20},{1,9},{5... | collective-permute-start | bytes 107528 | tf_op jit(solution)/shard_map/ppermute | solution.py:16
  24.9 4.0 %collective-permute-start.2 = (f32[12,7,128]{2,1,0:T(8,128)S(1)}, f32[12,7,128]{2,1,0:T(8,128)S(1)}, u32[]{:S(2)}, u32[]{:S(2)}) collective-permute-start(f32[12,7,128]{2,1,0:T(8,128)S(1)} %pad_maximum_fusion.3), channel_id=1, source_target_pairs={{0,4},{4,0},{8,12},{12,8},{16,20},{20,16},{24,28},{28,24},{1,5},{5... | collective-permute-start | bytes 129032 | tf_op jit(solution)/shard_map/ppermute | solution.py:16
  29.0 3.2 %collective-permute-start.3 = (f32[16,7,128]{2,1,0:T(8,128)S(1)}, f32[16,7,128]{2,1,0:T(8,128)S(1)}, u32[]{:S(2)}, u32[]{:S(2)}) collective-permute-start(f32[16,7,128]{2,1,0:T(8,128)S(1)} %constant_dynamic-update-slice_fusion), channel_id=1, source_target_pairs={{0,2},{1,3},{2,0},{3,1},{4,6},{5,7},{6,4},{7,5},{8,10},{9,11},{10,... | collective-permute-start | bytes 172040 | tf_op jit(solution)/shard_map/ppermute | solution.py:16
  32.2 4.5 %collective-permute-start.4 = (f32[24,7,128]{2,1,0:T(8,128)S(1)}, f32[24,7,128]{2,1,0:T(8,128)S(1)}, u32[]{:S(2)}, u32[]{:S(2)}) collective-permute-start(f32[24,7,128]{2,1,0:T(8,128)S(1)} %get-tuple-element.57), channel_id=1, source_target_pairs={{0,1},{1,0},{2,3},{3,2},{4,5},{5,4},{6,7},{7,6},{8,9},{9,8},{10,11... | collective-permute-start | bytes 258056 | tf_op jit(solution)/shard_map/ppermute | solution.py:16
  36.8 7.6 %collective-permute-start.6 = (f32[32,7,128]{2,1,0:T(8,128)S(1)}, f32[32,7,128]{2,1,0:T(8,128)S(1)}, u32[]{:S(2)}, u32[]{:S(2)}) collective-permute-start(f32[32,7,128]{2,1,0:T(8,128)S(1)} %slice.257), channel_id=1, source_target_pairs={{4,8},{8,4},{12,16},{16,12},{20,24},{24,20},{5,9},{9,5},{13,17},{1... | collective-permute-start | bytes 344072 | tf_op jit(solution)/shard_map/ppermute | solution.py:25
  39.6 8.2 %collective-permute-start.5 = (f32[32,7,128]{2,1,0:T(8,128)S(1)}, f32[32,7,128]{2,1,0:T(8,128)S(1)}, u32[]{:S(2)}, u32[]{:S(2)}) collective-permute-start(f32[32,7,128]{2,1,0:T(8,128)S(1)} %slice.257), channel_id=1, source_target_pairs={{0,4},{4,0},{8,12},{12,8},{16,20},{20,16},{24,28},{28,24},{1,5},{5... | collective-permute-start | bytes 344072 | tf_op jit(solution)/shard_map/ppermute | solution.py:25
  47.9 2.1 %collective-permute-start.7 = (f32[96,7,128]{2,1,0:T(8,128)S(1)}, f32[96,7,128]{2,1,0:T(8,128)S(1)}, u32[]{:S(2)}, u32[]{:S(2)}) collective-permute-start(f32[96,7,128]{2,1,0:T(8,128)S(1)} %pad_maximum_fusion.1), channel_id=1, source_target_pairs={{0,1},{1,0},{2,3},{3,2},{4,5},{5,4},{6,7},{7,6},{8,9},{9,8},{10,11... | collective-permute-start | bytes 1032200 | tf_op jit(solution)/shard_map/ppermute | solution.py:25
  48.8 10.8 %collective-permute-start.8 = (f32[96,7,128]{2,1,0:T(8,128)S(1)}, f32[96,7,128]{2,1,0:T(8,128)S(1)}, u32[]{:S(2)}, u32[]{:S(2)}) collective-permute-start(f32[96,7,128]{2,1,0:T(8,128)S(1)} %pad_maximum_fusion.1), channel_id=1, source_target_pairs={{1,2},{2,1},{0,3},{3,0},{5,6},{6,5},{4,7},{7,4},{9,10},{10,9},{8,1... | collective-permute-start | bytes 1032200 | tf_op jit(solution)/shard_map/ppermute | solution.py:25

commit v21 on v18

--- a/solution.py
+++ b/solution.py
@@ -182,8 +182,17 @@
     delta_y = source_device % size_y - row_index
     sign_x = 2 * (column_index % 2) - 1
     sign_y = 2 * (row_index % 2) - 1
-    source_pool = swapped(swapped(blocks, "gx"), "gy")
-    pool_index = ((1 + delta_y * sign_y) * 3 + (1 + delta_x * sign_x)) * nbd + source_slot
+    row = swapped(blocks, "gx")
+    column = swapped(blocks, "gy")
+    corners = swapped(jnp.concatenate([row[:nbd], row[2 * nbd :]], axis=0), "gy")
+    source_pool = jnp.concatenate([row, column, corners], axis=0)
+    pos_x = 1 + delta_x * sign_x
+    pos_y = 1 + delta_y * sign_y
+    pool_index = jnp.where(
+        delta_y == 0,
+        pos_x * nbd,
+        jnp.where(delta_x == 0, 3 * nbd + pos_y * nbd, 6 * nbd + pos_y * 2 * nbd + (pos_x // 2) * nbd),
+    ) + source_slot
     sources_all = source_pool[pool_index]
     targets = blocks[:, 0:3]
     centre = jnp.mean(targets, axis=2)

time: 78.7 us -> 81.7 us (1.038); the launches traced: 78.3 us -> 80.3 us
  waiting for transfers between devices: 12.8 us -> 3.83 us
  local copies, waits for them, and re-layouts: 14.4 us -> 22.2 us
  starting transfers between devices: 15.4 us -> 18.6 us
    ppermute x2 -> x3, waiting for transfers between devices: 6.65 us -> 1.15 us  [swapped(): lax.ppermute(shard, axis, second)]
    unnamed x27 -> x31, local copies, waits for them, and re-layouts: 0.46 us -> 5.73 us
    ppermute x2 -> x3, waiting for transfers between devices: 3.46 us -> 0.01 us  [swapped(): lax.ppermute(shard, axis, first)]
    ppermute x2 -> x3, starting transfers between devices: 5.87 us -> 7.76 us  [swapped(): lax.ppermute(shard, axis, second)]
    concatenate x1 -> x2, local copies, waits for them, and re-layouts: 0.03 us -> 1.41 us  [the longest x1 0.73 us: local(): source_pool = jnp.concatenate([row, column, corners], axis=0)]
    ppermute x2 -> x3, starting transfers between devices: 0.75 us -> 2.08 us  [swapped(): lax.ppermute(shard, axis, first)]
    gather x1, local copies, waits for them, and re-layouts: 1.03 us -> 2.16 us  [local(): sources_all = source_pool[pool_index]]
  transfers between devices with their start and end apart: 9 -> 11, of which waited for: 6 -> 4; matrix products, arithmetic and copies ran while one was open for 14% -> 21% of each run, Pallas kernels for 0% -> 0%
where the time goes in v21:
time: 81.7 us; the launch traced here: 80.3 us
  local copies, waits for them, and re-layouts  22.2 us (27%)
  other arithmetic  21.7 us (27%)
  starting transfers between devices  18.6 us (23%)
  between operations  12.4 us (15%)
  waiting for transfers between devices  3.83 us (5%)
  matrix products  1.43 us (2%)
    reduce_sum x1, other arithmetic, evaluate(): arm_x = jnp.sum(extra[:, 1][:, None, :] * weight, axis=(0, 2))  17.7 us
    ppermute x5, starting transfers between devices, from_partner(): lax.ppermute(shard, axis, [(i, i ^ 1 << apart) for i in range(lax.axis_si...  8.79 us
    ppermute x3, starting transfers between devices, swapped(): lax.ppermute(shard, axis, second)  7.76 us
    unnamed x31, local copies, waits for them, and re-layouts  5.73 us
    ppermute x5, waiting for transfers between devices, from_partner(): lax.ppermute(shard, axis, [(i, i ^ 1 << apart) for i in range(lax.axis_si...  2.67 us
    gather x1, local copies, waits for them, and re-layouts, local(): sources_all = source_pool[pool_index]  2.16 us
    ppermute x3, starting transfers between devices, swapped(): lax.ppermute(shard, axis, first)  2.08 us
  transfers between devices with their start and end apart: 11, of which 4 were waited for; matrix products, arithmetic and copies ran while one was open for 21% of the time, Pallas kernels for 0%

profile of v21, /device:TPU:9, one launch (start us, length us, event | category | flops | bytes accessed | tf_op | source)
XLA Modules:
  0.0 80.3 jit_solution(4301017662984410150)
XLA Ops:
  0.0 1.1 %copy_bitcast_fusion = (f32[72,3,128]{2,1,0:T(4,128)S(1)}, f32[72,3,128]{2,1,0:T(4,128)S(1)}) fusion(f32[1,1,72,3,128]{4,2,3,1,0:T(8,128)} %param.9, f32[1,1,72,3,128]{4,2,3,1,0:T(8,128)} %param.8), kind=kLoop, calls=%fused_computation.28 | loop fusion | bytes 442368 | tf_op jit(solution)/shard_map/squeeze | solution.py:134
  1.1 0.9 %pad_maximum_fusion.1 = f32[72,7,128]{2,1,0:T(8,128)S(1)} fusion(f32[72,1,128]{2,1,0:T(1,128)} %bitcast.242, f32[72,3,128]{2,1,0:T(4,128)S(1)} %get-tuple-element.98, f32[72,3,128]{2,1,0:T(4,128)S(1)} %get-tuple-element.99), kind=kLoop, calls=%fused_computation.17 | loop fusion | flops 129024 | bytes 516096 | tf_op jit(solution)/shard_map/concatenate | solution.py:134
  2.1 1.5 %constant_dynamic-slice_fusion.11 = (s32[1,1,1]{1,2,0:T(1,128)}, s32[1,1,1]{1,2,0:T(1,128)}, s32[1,1,1]{1,2,0:T(1,128)}, s32[1,1,1]{1,2,0:T(1,128)}, s32[1,1,1]{...) fusion(s32[5,8,4]{1,2,0:T(4,128)} %param.11, ...), kind=kLoop, calls=%fused_computation.281 | loop fusion | bytes 108 | tf_op jit(solution)/shard_map/dynamic_slice | solution.py:152
  12.8 2.4 %collective-permute-start = (f32[9,7,128]{2,1,0:T(8,128)S(1)}, f32[9,7,128]{2,1,0:T(8,128)S(1)}, u32[]{:S(2)}, u32[]{:S(2)}) collective-permute-start(f32[9,7,128]{2,1,0:T(8,128)S(1)} %pad_maximum_fusion.4), channel_id=1, source_target_pairs={{0,16},{4,20},{8,24},{12,28},{16,0},{20,4},{24,8},{28,12},{1,17},{... | collective-permute-start | bytes 96776 | tf_op jit(solution)/shard_map/ppermute | solution.py:16
  16.4 1.4 %gather_fusion.2 = s32[256]{0:T(256)S(1)} fusion(s32[1024]{0:T(1024)S(1)} %copy-done, s32[1024]{0:T(1024)S(1)} %pad_clamp_fusion.1), kind=kCustom, calls=%fused_computation.2 | custom fusion | bytes 3072 | tf_op jit(solution)/shard_map/gather | solution.py:140
  23.6 1.3 %collective-permute-done.1 = f32[10,7,128]{2,1,0:T(8,128)S(1)} collective-permute-done((f32[10,7,128]{2,1,0:T(8,128)S(1)}, f32[10,7,128]{2,1,0:T(8,128)S(1)}, u32[]{:S(2)}, u32[]{:S(2)}) %collective-permute-start.1) | collective-permute-done | bytes 35872 | tf_op jit(solution)/shard_map/ppermute | solution.py:16
  24.9 1.3 %collective-permute-start.2 = (f32[12,7,128]{2,1,0:T(8,128)S(1)}, f32[12,7,128]{2,1,0:T(8,128)S(1)}, u32[]{:S(2)}, u32[]{:S(2)}) collective-permute-start(f32[12,7,128]{2,1,0:T(8,128)S(1)} %pad_maximum_fusion.2), channel_id=1, source_target_pairs={{0,4},{4,0},{8,12},{12,8},{16,20},{20,16},{24,28},{28,24},{1,5},{5... | collective-permute-start | bytes 129032 | tf_op jit(solution)/shard_map/ppermute | solution.py:16
  27.4 1.4 %gather_fusion = s32[256]{0:T(256)S(1)} fusion(s32[1024]{0:T(1024)S(1)} %copy-done, s32[1024]{0:T(1024)S(1)} %get-tuple-element.101), kind=kCustom, calls=%fused_computation | custom fusion | bytes 3072 | tf_op jit(solution)/shard_map/gather | solution.py:178
  29.0 1.3 %collective-permute-start.3 = (f32[16,7,128]{2,1,0:T(8,128)S(1)}, f32[16,7,128]{2,1,0:T(8,128)S(1)}, u32[]{:S(2)}, u32[]{:S(2)}) collective-permute-start(f32[16,7,128]{2,1,0:T(8,128)S(1)} %constant_dynamic-update-slice_fusion), channel_id=1, source_target_pairs={{0,2},{1,3},{2,0},{3,1},{4,6},{5,7},{6,4},{7,5},{8,10},{9,11},{10,... | collective-permute-start | bytes 172040 | tf_op jit(solution)/shard_map/ppermute | solution.py:16
  32.2 3.6 %collective-permute-start.4 = (f32[24,7,128]{2,1,0:T(8,128)S(1)}, f32[24,7,128]{2,1,0:T(8,128)S(1)}, u32[]{:S(2)}, u32[]{:S(2)}) collective-permute-start(f32[24,7,128]{2,1,0:T(8,128)S(1)} %get-tuple-element.61), channel_id=1, source_target_pairs={{0,1},{1,0},{2,3},{3,2},{4,5},{5,4},{6,7},{7,6},{8,9},{9,8},{10,11... | collective-permute-start | bytes 258056 | tf_op jit(solution)/shard_map/ppermute | solution.py:16
  35.8 0.9 %collective-permute-done.4 = f32[24,7,128]{2,1,0:T(8,128)S(1)} collective-permute-done((f32[24,7,128]{2,1,0:T(8,128)S(1)}, f32[24,7,128]{2,1,0:T(8,128)S(1)}, u32[]{:S(2)}, u32[]{:S(2)}) %collective-permute-start.4) | collective-permute-done | bytes 86048 | tf_op jit(solution)/shard_map/ppermute | solution.py:16
  36.8 1.1 %collective-permute-start.5 = (f32[32,7,128]{2,1,0:T(8,128)S(1)}, f32[32,7,128]{2,1,0:T(8,128)S(1)}, u32[]{:S(2)}, u32[]{:S(2)}) collective-permute-start(f32[32,7,128]{2,1,0:T(8,128)S(1)} %slice.257), channel_id=1, source_target_pairs={{0,4},{4,0},{8,12},{12,8},{16,20},{20,16},{24,28},{28,24},{1,5},{5... | collective-permute-start | bytes 344072 | tf_op jit(solution)/shard_map/ppermute | solution.py:23
  37.9 2.2 %collective-permute-start.6 = (f32[32,7,128]{2,1,0:T(8,128)S(1)}, f32[32,7,128]{2,1,0:T(8,128)S(1)}, u32[]{:S(2)}, u32[]{:S(2)}) collective-permute-start(f32[32,7,128]{2,1,0:T(8,128)S(1)} %slice.257), channel_id=1, source_target_pairs={{4,8},{8,4},{12,16},{16,12},{20,24},{24,20},{5,9},{9,5},{13,17},{1... | collective-permute-start | bytes 344072 | tf_op jit(solution)/shard_map/ppermute | solution.py:23
  40.2 1.0 %collective-permute-start.7 = (f32[32,7,128]{2,1,0:T(8,128)S(1)}, f32[32,7,128]{2,1,0:T(8,128)S(1)}, u32[]{:S(2)}, u32[]{:S(2)}) collective-permute-start(f32[32,7,128]{2,1,0:T(8,128)S(1)} %slice.257), channel_id=1, source_target_pairs={{0,1},{1,0},{2,3},{3,2},{4,5},{5,4},{6,7},{7,6},{8,9},{9,8},{10,11... | collective-permute-start | bytes 344072 | tf_op jit(solution)/shard_map/ppermute | solution.py:23
  41.1 3.0 %collective-permute-start.8 = (f32[32,7,128]{2,1,0:T(8,128)S(1)}, f32[32,7,128]{2,1,0:T(8,128)S(1)}, u32[]{:S(2)}, u32[]{:S(2)}) collective-permute-start(f32[32,7,128]{2,1,0:T(8,128)S(1)} %slice.257), channel_id=1, source_target_pairs={{1,2},{2,1},{5,6},{6,5},{9,10},{10,9},{13,14},{14,13},{17,18},{18,... | collective-permute-start | bytes 344072 | tf_op jit(solution)/shard_map/ppermute | solution.py:23
  44.9 0.7 gather_fusion.3
  49.0 0.7 constant_dynamic-update-slice_fusion.21
  49.7 0.7 constant_dynamic-update-slice_fusion.11
  50.4 2.5 %collective-permute-start.10 = (f32[64,7,128]{2,1,0:T(8,128)S(1)}, f32[64,7,128]{2,1,0:T(8,128)S(1)}, u32[]{:S(2)}, u32[]{:S(2)}) collective-permute-start(f32[64,7,128]{2,1,0:T(8,128)S(1)} %get-tuple-element.50), channel_id=1, source_target_pairs={{1,2},{2,1},{5,6},{6,5},{9,10},{10,9},{13,14},{14,13},{17,18},{18,... | collective-permute-start | bytes 688136 | tf_op jit(solution)/shard_map/ppermute | solution.py:23
  54.8 0.7 constant_dynamic-update-slice_fusion.16
  56.9 1.1 %collective-permute-done.10 = f32[64,7,128]{2,1,0:T(8,128)S(1)} collective-permute-done((f32[64,7,128]{2,1,0:T(8,128)S(1)}, f32[64,7,128]{2,1,0:T(8,128)S(1)}, u32[]{:S(2)}, u32[]{:S(2)}) %collective-permute-start.10) | collective-permute-done | bytes 229408 | tf_op jit(solution)/shard_map/ppermute | solution.py:23
  58.0 0.7 constant_dynamic-update-slice_fusion.13
  58.8 2.2 %gather_fusion.1 = f32[256,7,128]{2,1,0:T(8,128)S(1)} fusion(f32[384,7,128]{2,1,0:T(8,128)} %constant_dynamic-update-slice_fusion.13, s32[1024]{0:T(1024)S(1)} %pad_clamp_fusion.2), kind=kCustom, calls=%fused_computation.1 | custom fusion | bytes 1836032 | tf_op jit(solution)/shard_map/gather | solution.py:196
  61.9 17.7 %multiply_reduce_fusion.3 = (f32[32,128]{1,0:T(8,128)S(1)}, f32[32,128]{1,0:T(8,128)S(1)}, f32[32,128]{1,0:T(8,128)S(1)}, f32[32,128]{1,0:T(8,128)S(1)}, f32[32,128]{1,0:T(8,128)S(1)}, /*index=5*/f32[32,128]{1,0:T(8,128)S(1)}) fusion(f32[32,8,128]{2,1,0:T(8,128)S(1)} %get-tuple-element.40, f32[32,8,128]{2,1,0:T(8,128)S(1)} %get-tuple-element.41, ...), kind=kLoop, calls=%fused_computation.8 | loop fusion | flops 96444416 | bytes 1458176 | tf_op jit(solution)/shard_map/vmap()/reduce_sum | solution.py:51
  (156 shorter events, 16.5 us)
Async XLA Ops:
  0.0 16.4 %copy-start = (s32[1024]{0:T(1024)S(1)}, s32[1024]{0:T(1024)}, u32[]{:S(2)}) copy-start(s32[1024]{0:T(1024)} %param.12) | copy-start | bytes 12292
  0.0 15.2 %copy-start.1 = (s32[5,8,4]{1,2,0:T(4,128)S(1)}, s32[5,8,4]{1,2,0:T(4,128)}, u32[]{:S(2)}) copy-start(s32[5,8,4]{1,2,0:T(4,128)} %param.11) | copy-start | bytes 1924
  0.0 15.4 %copy-start.4 = (s32[5]{0:T(128)S(1)}, s32[5]{0:T(128)}, u32[]{:S(2)}) copy-start(s32[5]{0:T(128)} %constant.229) | copy-start | bytes 64
  1.1 15.1 %copy-start.2 = (s32[1,1,32,8]{2,3,1,0:T(8,128)S(1)}, s32[1,1,32,8]{2,3,1,0:T(8,128)}, u32[]{:S(2)}) copy-start(s32[1,1,32,8]{2,3,1,0:T(8,128)} %param.14) | copy-start | bytes 3076
  12.8 9.0 %collective-permute-start = (f32[9,7,128]{2,1,0:T(8,128)S(1)}, f32[9,7,128]{2,1,0:T(8,128)S(1)}, u32[]{:S(2)}, u32[]{:S(2)}) collective-permute-start(f32[9,7,128]{2,1,0:T(8,128)S(1)} %pad_maximum_fusion.4), channel_id=1, source_target_pairs={{0,16},{4,20},{8,24},{12,28},{16,0},{20,4},{24,8},{28,12},{1,17},{... | collective-permute-start | bytes 96776 | tf_op jit(solution)/shard_map/ppermute | solution.py:16
  16.4 5.3 %copy-start.3 = (s32[1,1,32,8]{2,3,1,0:T(8,128)S(1)}, s32[1,1,32,8]{2,3,1,0:T(8,128)}, u32[]{:S(2)}) copy-start(s32[1,1,32,8]{2,3,1,0:T(8,128)} %param.13) | copy-start | bytes 3076
  21.9 2.9 %collective-permute-start.1 = (f32[10,7,128]{2,1,0:T(8,128)S(1)}, f32[10,7,128]{2,1,0:T(8,128)S(1)}, u32[]{:S(2)}, u32[]{:S(2)}) collective-permute-start(f32[10,7,128]{2,1,0:T(8,128)S(1)} %pad_maximum_fusion.3), channel_id=1, source_target_pairs={{0,8},{4,12},{8,0},{12,4},{16,24},{20,28},{24,16},{28,20},{1,9},{5... | collective-permute-start | bytes 107528 | tf_op jit(solution)/shard_map/ppermute | solution.py:16
  24.9 4.0 %collective-permute-start.2 = (f32[12,7,128]{2,1,0:T(8,128)S(1)}, f32[12,7,128]{2,1,0:T(8,128)S(1)}, u32[]{:S(2)}, u32[]{:S(2)}) collective-permute-start(f32[12,7,128]{2,1,0:T(8,128)S(1)} %pad_maximum_fusion.2), channel_id=1, source_target_pairs={{0,4},{4,0},{8,12},{12,8},{16,20},{20,16},{24,28},{28,24},{1,5},{5... | collective-permute-start | bytes 129032 | tf_op jit(solution)/shard_map/ppermute | solution.py:16
  29.0 3.2 %collective-permute-start.3 = (f32[16,7,128]{2,1,0:T(8,128)S(1)}, f32[16,7,128]{2,1,0:T(8,128)S(1)}, u32[]{:S(2)}, u32[]{:S(2)}) collective-permute-start(f32[16,7,128]{2,1,0:T(8,128)S(1)} %constant_dynamic-update-slice_fusion), channel_id=1, source_target_pairs={{0,2},{1,3},{2,0},{3,1},{4,6},{5,7},{6,4},{7,5},{8,10},{9,11},{10,... | collective-permute-start | bytes 172040 | tf_op jit(solution)/shard_map/ppermute | solution.py:16
  32.2 4.5 %collective-permute-start.4 = (f32[24,7,128]{2,1,0:T(8,128)S(1)}, f32[24,7,128]{2,1,0:T(8,128)S(1)}, u32[]{:S(2)}, u32[]{:S(2)}) collective-permute-start(f32[24,7,128]{2,1,0:T(8,128)S(1)} %get-tuple-element.61), channel_id=1, source_target_pairs={{0,1},{1,0},{2,3},{3,2},{4,5},{5,4},{6,7},{7,6},{8,9},{9,8},{10,11... | collective-permute-start | bytes 258056 | tf_op jit(solution)/shard_map/ppermute | solution.py:16
  36.8 11.5 %collective-permute-start.5 = (f32[32,7,128]{2,1,0:T(8,128)S(1)}, f32[32,7,128]{2,1,0:T(8,128)S(1)}, u32[]{:S(2)}, u32[]{:S(2)}) collective-permute-start(f32[32,7,128]{2,1,0:T(8,128)S(1)} %slice.257), channel_id=1, source_target_pairs={{0,4},{4,0},{8,12},{12,8},{16,20},{20,16},{24,28},{28,24},{1,5},{5... | collective-permute-start | bytes 344072 | tf_op jit(solution)/shard_map/ppermute | solution.py:23
  37.9 11.7 %collective-permute-start.6 = (f32[32,7,128]{2,1,0:T(8,128)S(1)}, f32[32,7,128]{2,1,0:T(8,128)S(1)}, u32[]{:S(2)}, u32[]{:S(2)}) collective-permute-start(f32[32,7,128]{2,1,0:T(8,128)S(1)} %slice.257), channel_id=1, source_target_pairs={{4,8},{8,4},{12,16},{16,12},{20,24},{24,20},{5,9},{9,5},{13,17},{1... | collective-permute-start | bytes 344072 | tf_op jit(solution)/shard_map/ppermute | solution.py:23
  40.2 12.7 %collective-permute-start.7 = (f32[32,7,128]{2,1,0:T(8,128)S(1)}, f32[32,7,128]{2,1,0:T(8,128)S(1)}, u32[]{:S(2)}, u32[]{:S(2)}) collective-permute-start(f32[32,7,128]{2,1,0:T(8,128)S(1)} %slice.257), channel_id=1, source_target_pairs={{0,1},{1,0},{2,3},{3,2},{4,5},{5,4},{6,7},{7,6},{8,9},{9,8},{10,11... | collective-permute-start | bytes 344072 | tf_op jit(solution)/shard_map/ppermute | solution.py:23
  41.1 13.1 %collective-permute-start.8 = (f32[32,7,128]{2,1,0:T(8,128)S(1)}, f32[32,7,128]{2,1,0:T(8,128)S(1)}, u32[]{:S(2)}, u32[]{:S(2)}) collective-permute-start(f32[32,7,128]{2,1,0:T(8,128)S(1)} %slice.257), channel_id=1, source_target_pairs={{1,2},{2,1},{5,6},{6,5},{9,10},{10,9},{13,14},{14,13},{17,18},{18,... | collective-permute-start | bytes 344072 | tf_op jit(solution)/shard_map/ppermute | solution.py:23
  50.3 4.5 %collective-permute-start.9 = (f32[64,7,128]{2,1,0:T(8,128)S(1)}, f32[64,7,128]{2,1,0:T(8,128)S(1)}, u32[]{:S(2)}, u32[]{:S(2)}) collective-permute-start(f32[64,7,128]{2,1,0:T(8,128)S(1)} %get-tuple-element.50), channel_id=1, source_target_pairs={{0,1},{1,0},{2,3},{3,2},{4,5},{5,4},{6,7},{7,6},{8,9},{9,8},{10,11... | collective-permute-start | bytes 688136 | tf_op jit(solution)/shard_map/ppermute | solution.py:23
  50.4 7.7 %collective-permute-start.10 = (f32[64,7,128]{2,1,0:T(8,128)S(1)}, f32[64,7,128]{2,1,0:T(8,128)S(1)}, u32[]{:S(2)}, u32[]{:S(2)}) collective-permute-start(f32[64,7,128]{2,1,0:T(8,128)S(1)} %get-tuple-element.50), channel_id=1, source_target_pairs={{1,2},{2,1},{5,6},{6,5},{9,10},{10,9},{13,14},{14,13},{17,18},{18,... | collective-permute-start | bytes 688136 | tf_op jit(solution)/shard_map/ppermute | solution.py:23

commit v22 on v18

--- a/solution.py
+++ b/solution.py
@@ -181,9 +181,12 @@
     delta_x = source_device // size_y - column_index
     delta_y = source_device % size_y - row_index
     sign_x = 2 * (column_index % 2) - 1
-    sign_y = 2 * (row_index % 2) - 1
-    source_pool = swapped(swapped(blocks, "gx"), "gy")
-    pool_index = ((1 + delta_y * sign_y) * 3 + (1 + delta_x * sign_x)) * nbd + source_slot
+    row = swapped(blocks, "gx")
+    size_y_axis = lax.axis_size("gy")
+    from_below = lax.ppermute(row, "gy", [(i, i + 1) for i in range(size_y_axis - 1)])
+    from_above = lax.ppermute(row, "gy", [(i + 1, i) for i in range(size_y_axis - 1)])
+    source_pool = jnp.concatenate([from_below, row, from_above], axis=0)
+    pool_index = ((1 + delta_y) * 3 + (1 + delta_x * sign_x)) * nbd + source_slot
     sources_all = source_pool[pool_index]
     targets = blocks[:, 0:3]
     centre = jnp.mean(targets, axis=2)

time: 78.7 us -> 81.7 us (1.038)
  starting transfers between devices: 15.4 us -> 17.3 us
  waiting for transfers between devices: 12.8 us -> 13.9 us
    ppermute x0 -> x2, waiting for transfers between devices: none -> 7.08 us  [the longest x1 4.68 us: local(): lax.ppermute(row, 'gy', [(i + 1, i) for i in range(size_y_axis - 1)])]
    ppermute x2 -> x1, waiting for transfers between devices: 6.65 us -> 0.71 us  [swapped(): lax.ppermute(shard, axis, second)]
    ppermute x0 -> x2, starting transfers between devices: none -> 5.45 us  [the longest x1 3.53 us: local(): lax.ppermute(row, 'gy', [(i, i + 1) for i in range(size_y_axis - 1)])]
    ppermute x2 -> x1, starting transfers between devices: 5.87 us -> 2.83 us  [swapped(): lax.ppermute(shard, axis, second)]
    ppermute x2 -> x1, waiting for transfers between devices: 3.46 us -> 3.46 us  [swapped(): lax.ppermute(shard, axis, first)]
  transfers between devices with their start and end apart: 9 -> 9, of which waited for: 6 -> 7; matrix products, arithmetic and copies ran while one was open for 14% -> 14% of each run, Pallas kernels for 0% -> 0%
where the time goes in v22:
time: 81.7 us; the launch traced here: 81.2 us
  other arithmetic  21.8 us (27%)
  starting transfers between devices  17.3 us (21%)
  local copies, waits for them, and re-layouts  14.4 us (18%)
  waiting for transfers between devices  13.9 us (17%)
  between operations  12.5 us (15%)
  matrix products  1.43 us (2%)
    reduce_sum x1, other arithmetic, evaluate(): arm_x = jnp.sum(extra[:, 1][:, None, :] * weight, axis=(0, 2))  17.7 us
    ppermute x5, starting transfers between devices, from_partner(): lax.ppermute(shard, axis, [(i, i ^ 1 << apart) for i in range(lax.axis_si...  8.79 us
    ppermute x1, waiting for transfers between devices, local(): lax.ppermute(row, 'gy', [(i + 1, i) for i in range(size_y_axis - 1)])  4.68 us
    ppermute x1, starting transfers between devices, local(): lax.ppermute(row, 'gy', [(i, i + 1) for i in range(size_y_axis - 1)])  3.53 us
    ppermute x1, waiting for transfers between devices, swapped(): lax.ppermute(shard, axis, first)  3.46 us
    ppermute x1, starting transfers between devices, swapped(): lax.ppermute(shard, axis, second)  2.83 us
    ppermute x5, waiting for transfers between devices, from_partner(): lax.ppermute(shard, axis, [(i, i ^ 1 << apart) for i in range(lax.axis_si...  2.69 us
    ppermute x1, waiting for transfers between devices, local(): lax.ppermute(row, 'gy', [(i, i + 1) for i in range(size_y_axis - 1)])  2.4 us
  transfers between devices with their start and end apart: 9, of which 7 were waited for; matrix products, arithmetic and copies ran while one was open for 14% of the time, Pallas kernels for 0%

profile of v22, /device:TPU:9, one launch (start us, length us, event | category | flops | bytes accessed | tf_op | source)
XLA Modules:
  0.0 81.2 jit_solution(6876018632373817403)
XLA Ops:
  0.0 1.1 %copy_bitcast_fusion = (f32[72,3,128]{2,1,0:T(4,128)S(1)}, f32[72,3,128]{2,1,0:T(4,128)S(1)}) fusion(f32[1,1,72,3,128]{4,2,3,1,0:T(8,128)} %param.9, f32[1,1,72,3,128]{4,2,3,1,0:T(8,128)} %param.8), kind=kLoop, calls=%fused_computation.29 | loop fusion | bytes 442368 | tf_op jit(solution)/shard_map/squeeze | solution.py:134
  1.1 0.9 %pad_maximum_fusion.2 = f32[72,7,128]{2,1,0:T(8,128)S(1)} fusion(f32[72,1,128]{2,1,0:T(1,128)} %bitcast.242, f32[72,3,128]{2,1,0:T(4,128)S(1)} %get-tuple-element.94, f32[72,3,128]{2,1,0:T(4,128)S(1)} %get-tuple-element.95), kind=kLoop, calls=%fused_computation.18 | loop fusion | flops 129024 | bytes 516096 | tf_op jit(solution)/shard_map/concatenate | solution.py:134
  2.1 1.5 %constant_dynamic-slice_fusion.11 = (s32[1,1,1]{1,2,0:T(1,128)}, s32[1,1,1]{1,2,0:T(1,128)}, s32[1,1,1]{1,2,0:T(1,128)}, s32[1,1,1]{1,2,0:T(1,128)}, s32[1,1,1]{...) fusion(s32[5,8,4]{1,2,0:T(4,128)} %param.11, ...), kind=kLoop, calls=%fused_computation.272 | loop fusion | bytes 108 | tf_op jit(solution)/shard_map/dynamic_slice | solution.py:152
  12.8 2.4 %collective-permute-start = (f32[9,7,128]{2,1,0:T(8,128)S(1)}, f32[9,7,128]{2,1,0:T(8,128)S(1)}, u32[]{:S(2)}, u32[]{:S(2)}) collective-permute-start(f32[9,7,128]{2,1,0:T(8,128)S(1)} %pad_maximum_fusion.5), channel_id=1, source_target_pairs={{0,16},{4,20},{8,24},{12,28},{16,0},{20,4},{24,8},{28,12},{1,17},{... | collective-permute-start | bytes 96776 | tf_op jit(solution)/shard_map/ppermute | solution.py:16
  16.4 1.4 %gather_fusion.2 = s32[256]{0:T(256)S(1)} fusion(s32[1024]{0:T(1024)S(1)} %copy-done, s32[1024]{0:T(1024)S(1)} %pad_clamp_fusion.1), kind=kCustom, calls=%fused_computation.2 | custom fusion | bytes 3072 | tf_op jit(solution)/shard_map/gather | solution.py:140
  23.6 1.3 %collective-permute-done.1 = f32[10,7,128]{2,1,0:T(8,128)S(1)} collective-permute-done((f32[10,7,128]{2,1,0:T(8,128)S(1)}, f32[10,7,128]{2,1,0:T(8,128)S(1)}, u32[]{:S(2)}, u32[]{:S(2)}) %collective-permute-start.1) | collective-permute-done | bytes 35872 | tf_op jit(solution)/shard_map/ppermute | solution.py:16
  24.9 1.3 %collective-permute-start.2 = (f32[12,7,128]{2,1,0:T(8,128)S(1)}, f32[12,7,128]{2,1,0:T(8,128)S(1)}, u32[]{:S(2)}, u32[]{:S(2)}) collective-permute-start(f32[12,7,128]{2,1,0:T(8,128)S(1)} %pad_maximum_fusion.3), channel_id=1, source_target_pairs={{0,4},{4,0},{8,12},{12,8},{16,20},{20,16},{24,28},{28,24},{1,5},{5... | collective-permute-start | bytes 129032 | tf_op jit(solution)/shard_map/ppermute | solution.py:16
  27.4 1.4 %gather_fusion = s32[256]{0:T(256)S(1)} fusion(s32[1024]{0:T(1024)S(1)} %copy-done, s32[1024]{0:T(1024)S(1)} %get-tuple-element.97), kind=kCustom, calls=%fused_computation | custom fusion | bytes 3072 | tf_op jit(solution)/shard_map/gather | solution.py:178
  29.0 1.3 %collective-permute-start.3 = (f32[16,7,128]{2,1,0:T(8,128)S(1)}, f32[16,7,128]{2,1,0:T(8,128)S(1)}, u32[]{:S(2)}, u32[]{:S(2)}) collective-permute-start(f32[16,7,128]{2,1,0:T(8,128)S(1)} %constant_dynamic-update-slice_fusion), channel_id=1, source_target_pairs={{0,2},{1,3},{2,0},{3,1},{4,6},{5,7},{6,4},{7,5},{8,10},{9,11},{10,... | collective-permute-start | bytes 172040 | tf_op jit(solution)/shard_map/ppermute | solution.py:16
  32.2 3.6 %collective-permute-start.4 = (f32[24,7,128]{2,1,0:T(8,128)S(1)}, f32[24,7,128]{2,1,0:T(8,128)S(1)}, u32[]{:S(2)}, u32[]{:S(2)}) collective-permute-start(f32[24,7,128]{2,1,0:T(8,128)S(1)} %get-tuple-element.57), channel_id=1, source_target_pairs={{0,1},{1,0},{2,3},{3,2},{4,5},{5,4},{6,7},{7,6},{8,9},{9,8},{10,11... | collective-permute-start | bytes 258056 | tf_op jit(solution)/shard_map/ppermute | solution.py:16
  35.8 0.9 %collective-permute-done.4 = f32[24,7,128]{2,1,0:T(8,128)S(1)} collective-permute-done((f32[24,7,128]{2,1,0:T(8,128)S(1)}, f32[24,7,128]{2,1,0:T(8,128)S(1)}, u32[]{:S(2)}, u32[]{:S(2)}) %collective-permute-start.4) | collective-permute-done | bytes 86048 | tf_op jit(solution)/shard_map/ppermute | solution.py:16
  36.8 2.8 %collective-permute-start.6 = (f32[32,7,128]{2,1,0:T(8,128)S(1)}, f32[32,7,128]{2,1,0:T(8,128)S(1)}, u32[]{:S(2)}, u32[]{:S(2)}) collective-permute-start(f32[32,7,128]{2,1,0:T(8,128)S(1)} %slice.257), channel_id=1, source_target_pairs={{4,8},{8,4},{12,16},{16,12},{20,24},{24,20},{5,9},{9,5},{13,17},{1... | collective-permute-start | bytes 344072 | tf_op jit(solution)/shard_map/ppermute | solution.py:23
  39.9 0.6 copy.227
  40.6 0.7 gather_fusion.3
  43.6 0.7 collective-permute-done.6
  44.3 3.5 %collective-permute-done.5 = f32[32,7,128]{2,1,0:T(8,128)S(1)} collective-permute-done((f32[32,7,128]{2,1,0:T(8,128)S(1)}, f32[32,7,128]{2,1,0:T(8,128)S(1)}, u32[]{:S(2)}, u32[]{:S(2)}) %collective-permute-start.5) | collective-permute-done | bytes 114720 | tf_op jit(solution)/shard_map/ppermute | solution.py:23
  47.8 3.5 %collective-permute-start.7 = (f32[96,7,128]{2,1,0:T(8,128)S(1)}, f32[96,7,128]{2,1,0:T(8,128)S(1)}, u32[]{:S(2)}, u32[]{:S(2)}) collective-permute-start(f32[96,7,128]{2,1,0:T(8,128)S(1)} %pad_maximum_fusion.1), channel_id=1, source_target_pairs={{0,1},{1,2},{2,3},{4,5},{5,6},{6,7},{8,9},{9,10},{10,11},{12,13},{... | collective-permute-start | bytes 1032200 | tf_op jit(solution)/shard_map/ppermute | solution.py:186
  51.8 1.9 %collective-permute-start.8 = (f32[96,7,128]{2,1,0:T(8,128)S(1)}, f32[96,7,128]{2,1,0:T(8,128)S(1)}, u32[]{:S(2)}, u32[]{:S(2)}) collective-permute-start(f32[96,7,128]{2,1,0:T(8,128)S(1)} %pad_maximum_fusion.1), channel_id=1, source_target_pairs={{1,0},{2,1},{3,2},{5,4},{6,5},{7,6},{9,8},{10,9},{11,10},{13,12},{... | collective-permute-start | bytes 1032200 | tf_op jit(solution)/shard_map/ppermute | solution.py:187
  53.7 2.4 %collective-permute-done.7 = f32[96,7,128]{2,1,0:T(8,128)S(1)} collective-permute-done((f32[96,7,128]{2,1,0:T(8,128)S(1)}, f32[96,7,128]{2,1,0:T(8,128)S(1)}, u32[]{:S(2)}, u32[]{:S(2)}) %collective-permute-start.7) | collective-permute-done | bytes 344096 | tf_op jit(solution)/shard_map/ppermute | solution.py:186
  56.2 4.7 %collective-permute-done.8 = f32[96,7,128]{2,1,0:T(8,128)S(1)} collective-permute-done((f32[96,7,128]{2,1,0:T(8,128)S(1)}, f32[96,7,128]{2,1,0:T(8,128)S(1)}, u32[]{:S(2)}, u32[]{:S(2)}) %collective-permute-start.8) | collective-permute-done | bytes 344096 | tf_op jit(solution)/shard_map/ppermute | solution.py:187
  60.9 1.0 %gather_fusion.1 = f32[256,7,128]{2,1,0:T(8,128)S(1)} fusion(f32[288,7,128]{2,1,0:T(8,128)S(1)} %constant_dynamic-update-slice_fusion.11, s32[1024]{0:T(1024)S(1)} %pad_clamp_fusion.2), kind=kCustom, calls=%fused_computation.1 | custom fusion | bytes 1836032 | tf_op jit(solution)/shard_map/gather | solution.py:190
  61.9 0.6 fusion.75
  62.9 17.7 %multiply_reduce_fusion.3 = (f32[32,128]{1,0:T(8,128)S(1)}, f32[32,128]{1,0:T(8,128)S(1)}, f32[32,128]{1,0:T(8,128)S(1)}, f32[32,128]{1,0:T(8,128)S(1)}, f32[32,128]{1,0:T(8,128)S(1)}, /*index=5*/f32[32,128]{1,0:T(8,128)S(1)}) fusion(f32[32,8,128]{2,1,0:T(8,128)S(1)} %get-tuple-element.40, f32[32,8,128]{2,1,0:T(8,128)S(1)} %get-tuple-element.41, ...), kind=kLoop, calls=%fused_computation.8 | loop fusion | flops 96444416 | bytes 1458176 | tf_op jit(solution)/shard_map/vmap()/reduce_sum | solution.py:51
  80.6 0.6 fusion.20
  (148 shorter events, 11.0 us)
Async XLA Ops:
  0.0 16.4 %copy-start = (s32[1024]{0:T(1024)S(1)}, s32[1024]{0:T(1024)}, u32[]{:S(2)}) copy-start(s32[1024]{0:T(1024)} %param.12) | copy-start | bytes 12292
  0.0 15.2 %copy-start.1 = (s32[5,8,4]{1,2,0:T(4,128)S(1)}, s32[5,8,4]{1,2,0:T(4,128)}, u32[]{:S(2)}) copy-start(s32[5,8,4]{1,2,0:T(4,128)} %param.11) | copy-start | bytes 1924
  0.0 15.4 %copy-start.4 = (s32[5]{0:T(128)S(1)}, s32[5]{0:T(128)}, u32[]{:S(2)}) copy-start(s32[5]{0:T(128)} %constant.212) | copy-start | bytes 64
  1.1 15.1 %copy-start.2 = (s32[1,1,32,8]{2,3,1,0:T(8,128)S(1)}, s32[1,1,32,8]{2,3,1,0:T(8,128)}, u32[]{:S(2)}) copy-start(s32[1,1,32,8]{2,3,1,0:T(8,128)} %param.14) | copy-start | bytes 3076
  12.8 9.0 %collective-permute-start = (f32[9,7,128]{2,1,0:T(8,128)S(1)}, f32[9,7,128]{2,1,0:T(8,128)S(1)}, u32[]{:S(2)}, u32[]{:S(2)}) collective-permute-start(f32[9,7,128]{2,1,0:T(8,128)S(1)} %pad_maximum_fusion.5), channel_id=1, source_target_pairs={{0,16},{4,20},{8,24},{12,28},{16,0},{20,4},{24,8},{28,12},{1,17},{... | collective-permute-start | bytes 96776 | tf_op jit(solution)/shard_map/ppermute | solution.py:16
  16.4 5.3 %copy-start.3 = (s32[1,1,32,8]{2,3,1,0:T(8,128)S(1)}, s32[1,1,32,8]{2,3,1,0:T(8,128)}, u32[]{:S(2)}) copy-start(s32[1,1,32,8]{2,3,1,0:T(8,128)} %param.13) | copy-start | bytes 3076
  21.9 2.9 %collective-permute-start.1 = (f32[10,7,128]{2,1,0:T(8,128)S(1)}, f32[10,7,128]{2,1,0:T(8,128)S(1)}, u32[]{:S(2)}, u32[]{:S(2)}) collective-permute-start(f32[10,7,128]{2,1,0:T(8,128)S(1)} %pad_maximum_fusion.4), channel_id=1, source_target_pairs={{0,8},{4,12},{8,0},{12,4},{16,24},{20,28},{24,16},{28,20},{1,9},{5... | collective-permute-start | bytes 107528 | tf_op jit(solution)/shard_map/ppermute | solution.py:16
  24.9 4.0 %collective-permute-start.2 = (f32[12,7,128]{2,1,0:T(8,128)S(1)}, f32[12,7,128]{2,1,0:T(8,128)S(1)}, u32[]{:S(2)}, u32[]{:S(2)}) collective-permute-start(f32[12,7,128]{2,1,0:T(8,128)S(1)} %pad_maximum_fusion.3), channel_id=1, source_target_pairs={{0,4},{4,0},{8,12},{12,8},{16,20},{20,16},{24,28},{28,24},{1,5},{5... | collective-permute-start | bytes 129032 | tf_op jit(solution)/shard_map/ppermute | solution.py:16
  29.0 3.2 %collective-permute-start.3 = (f32[16,7,128]{2,1,0:T(8,128)S(1)}, f32[16,7,128]{2,1,0:T(8,128)S(1)}, u32[]{:S(2)}, u32[]{:S(2)}) collective-permute-start(f32[16,7,128]{2,1,0:T(8,128)S(1)} %constant_dynamic-update-slice_fusion), channel_id=1, source_target_pairs={{0,2},{1,3},{2,0},{3,1},{4,6},{5,7},{6,4},{7,5},{8,10},{9,11},{10,... | collective-permute-start | bytes 172040 | tf_op jit(solution)/shard_map/ppermute | solution.py:16
  32.2 4.5 %collective-permute-start.4 = (f32[24,7,128]{2,1,0:T(8,128)S(1)}, f32[24,7,128]{2,1,0:T(8,128)S(1)}, u32[]{:S(2)}, u32[]{:S(2)}) collective-permute-start(f32[24,7,128]{2,1,0:T(8,128)S(1)} %get-tuple-element.57), channel_id=1, source_target_pairs={{0,1},{1,0},{2,3},{3,2},{4,5},{5,4},{6,7},{7,6},{8,9},{9,8},{10,11... | collective-permute-start | bytes 258056 | tf_op jit(solution)/shard_map/ppermute | solution.py:16
  36.8 7.6 %collective-permute-start.6 = (f32[32,7,128]{2,1,0:T(8,128)S(1)}, f32[32,7,128]{2,1,0:T(8,128)S(1)}, u32[]{:S(2)}, u32[]{:S(2)}) collective-permute-start(f32[32,7,128]{2,1,0:T(8,128)S(1)} %slice.257), channel_id=1, source_target_pairs={{4,8},{8,4},{12,16},{16,12},{20,24},{24,20},{5,9},{9,5},{13,17},{1... | collective-permute-start | bytes 344072 | tf_op jit(solution)/shard_map/ppermute | solution.py:23
  39.6 8.2 %collective-permute-start.5 = (f32[32,7,128]{2,1,0:T(8,128)S(1)}, f32[32,7,128]{2,1,0:T(8,128)S(1)}, u32[]{:S(2)}, u32[]{:S(2)}) collective-permute-start(f32[32,7,128]{2,1,0:T(8,128)S(1)} %slice.257), channel_id=1, source_target_pairs={{0,4},{4,0},{8,12},{12,8},{16,20},{20,16},{24,28},{28,24},{1,5},{5... | collective-permute-start | bytes 344072 | tf_op jit(solution)/shard_map/ppermute | solution.py:23
  47.8 8.2 %collective-permute-start.7 = (f32[96,7,128]{2,1,0:T(8,128)S(1)}, f32[96,7,128]{2,1,0:T(8,128)S(1)}, u32[]{:S(2)}, u32[]{:S(2)}) collective-permute-start(f32[96,7,128]{2,1,0:T(8,128)S(1)} %pad_maximum_fusion.1), channel_id=1, source_target_pairs={{0,1},{1,2},{2,3},{4,5},{5,6},{6,7},{8,9},{9,10},{10,11},{12,13},{... | collective-permute-start | bytes 1032200 | tf_op jit(solution)/shard_map/ppermute | solution.py:186
  51.8 9.1 %collective-permute-start.8 = (f32[96,7,128]{2,1,0:T(8,128)S(1)}, f32[96,7,128]{2,1,0:T(8,128)S(1)}, u32[]{:S(2)}, u32[]{:S(2)}) collective-permute-start(f32[96,7,128]{2,1,0:T(8,128)S(1)} %pad_maximum_fusion.1), channel_id=1, source_target_pairs={{1,0},{2,1},{3,2},{5,4},{6,5},{7,6},{9,8},{10,9},{11,10},{13,12},{... | collective-permute-start | bytes 1032200 | tf_op jit(solution)/shard_map/ppermute | solution.py:187

commit v23 on v18

--- a/solution.py
+++ b/solution.py
@@ -4,6 +4,7 @@
 import jax.numpy as jnp
 import numpy as np
 from jax import lax
+from jax.experimental.layout import Layout, with_layout_constraint
 from jax.sharding import PartitionSpec as P
 
 MOVE = 8
@@ -16,11 +17,11 @@
     return lax.ppermute(shard, axis, [(i, i ^ 1 << apart) for i in range(lax.axis_size(axis))])
 
 
-def swapped(shard, axis):
+def swapped(shard, axis, dim=0):
     size = lax.axis_size(axis)
     first = [(i, i ^ 1) for i in range(size)]
     second = [(i, i + 1 - 2 * (i % 2 == 0)) for i in range(1, size - 1)]
-    return jnp.concatenate([lax.ppermute(shard, axis, first), shard, lax.ppermute(shard, axis, second)], axis=0)
+    return jnp.concatenate([lax.ppermute(shard, axis, first), shard, lax.ppermute(shard, axis, second)], axis=dim)
 
 
 def slot_multipoles(pos, stren, core):
@@ -182,9 +183,10 @@
     delta_y = source_device % size_y - row_index
     sign_x = 2 * (column_index % 2) - 1
     sign_y = 2 * (row_index % 2) - 1
-    source_pool = swapped(swapped(blocks, "gx"), "gy")
+    dense = with_layout_constraint(jnp.transpose(blocks, (1, 0, 2)), Layout(major_to_minor=(0, 1, 2)))
+    source_pool = swapped(swapped(dense, "gx", 1), "gy", 1)
     pool_index = ((1 + delta_y * sign_y) * 3 + (1 + delta_x * sign_x)) * nbd + source_slot
-    sources_all = source_pool[pool_index]
+    sources_all = jnp.transpose(source_pool[:, pool_index], (1, 2, 0, 3))
     targets = blocks[:, 0:3]
     centre = jnp.mean(targets, axis=2)
     extra = source_terms(sources_all, centre)

time: 78.7 us -> 77.6 us (0.986)
  waiting for transfers between devices: 12.8 us -> 11.8 us
    squeeze x1 -> x0, local copies, waits for them, and re-layouts: 1.06 us -> none  [local(): strength[0, 0]]
    ppermute x2, waiting for transfers between devices: 6.65 us -> 5.86 us  [swapped(): lax.ppermute(shard, axis, second)]
where the time goes in v23:
time: 77.6 us; the launch traced here: 77.3 us
  other arithmetic  21.7 us (28%)
  starting transfers between devices  15.5 us (20%)
  local copies, waits for them, and re-layouts  14.3 us (18%)
  between operations  12.4 us (16%)
  waiting for transfers between devices  11.8 us (15%)
  matrix products  1.6 us (2%)
    reduce_sum x1, other arithmetic, evaluate(): arm_x = jnp.sum(extra[:, 1][:, None, :] * weight, axis=(0, 2))  17.8 us
    ppermute x5, starting transfers between devices, from_partner(): lax.ppermute(shard, axis, [(i, i ^ 1 << apart) for i in range(lax.axis_si...  8.8 us
    ppermute x2, starting transfers between devices, swapped(): lax.ppermute(shard, axis, second)  5.94 us
    ppermute x2, waiting for transfers between devices, swapped(): lax.ppermute(shard, axis, second)  5.86 us
    ppermute x2, waiting for transfers between devices, swapped(): lax.ppermute(shard, axis, first)  3.15 us
    ppermute x5, waiting for transfers between devices, from_partner(): lax.ppermute(shard, axis, [(i, i ^ 1 << apart) for i in range(lax.axis_si...  2.76 us
  transfers between devices with their start and end apart: 9, of which 6 were waited for; matrix products, arithmetic and copies ran while one was open for 14% of the time, Pallas kernels for 0%

profile of v23, /device:TPU:9, one launch (start us, length us, event | category | flops | bytes accessed | tf_op | source)
XLA Modules:
  0.0 77.3 jit_solution(1697742521302765951)
XLA Ops:
  0.0 1.0 %pad_maximum_fusion.2 = f32[72,7,128]{2,0,1:T(8,128)S(1)} fusion(f32[72,1,128]{2,0,1:T(8,128)} %bitcast.232, f32[72,3,128]{2,0,1:T(8,128)} %bitcast.223, f32[72,3,128]{2,0,1:T(8,128)} %bitcast.224), kind=kLoop, calls=%fused_computation.18 | loop fusion | flops 129024 | bytes 516096 | tf_op jit(solution)/shard_map/concatenate | solution.py:135
  2.3 0.4 convolution_reduce_fusion
  3.1 1.5 %constant_dynamic-slice_fusion.13 = (s32[1,1,1]{1,2,0:T(1,128)}, s32[1,1,1]{1,2,0:T(1,128)}, s32[1,1,1]{1,2,0:T(1,128)}, s32[1,1,1]{1,2,0:T(1,128)}, s32[1,1,1]{...) fusion(s32[5,8,4]{1,2,0:T(4,128)} %param.11, ...), kind=kLoop, calls=%fused_computation.254 | loop fusion | bytes 108 | tf_op jit(solution)/shard_map/dynamic_slice | solution.py:153
  11.5 2.4 %collective-permute-start = (f32[9,7,128]{2,0,1:T(8,128)S(1)}, f32[9,7,128]{2,0,1:T(8,128)S(1)}, u32[]{:S(2)}, u32[]{:S(2)}) collective-permute-start(f32[9,7,128]{2,0,1:T(8,128)S(1)} %pad_maximum_fusion.3), channel_id=1, source_target_pairs={{0,16},{4,20},{8,24},{12,28},{16,0},{20,4},{24,8},{28,12},{1,17},{... | collective-permute-start | bytes 96776 | tf_op jit(solution)/shard_map/ppermute | solution.py:17
  15.1 1.4 %gather_fusion.2 = s32[256]{0:T(256)S(1)} fusion(s32[1024]{0:T(1024)S(1)} %copy-done, s32[1024]{0:T(1024)S(1)} %pad_clamp_fusion.1), kind=kCustom, calls=%fused_computation.2 | custom fusion | bytes 3072 | tf_op jit(solution)/shard_map/gather | solution.py:141
  22.4 1.4 %collective-permute-done.1 = f32[10,7,128]{2,0,1:T(8,128)S(1)} collective-permute-done((f32[10,7,128]{2,0,1:T(8,128)S(1)}, f32[10,7,128]{2,0,1:T(8,128)S(1)}, u32[]{:S(2)}, u32[]{:S(2)}) %collective-permute-start.1) | collective-permute-done | bytes 35872 | tf_op jit(solution)/shard_map/ppermute | solution.py:17
  24.0 1.3 %collective-permute-start.2 = (f32[12,7,128]{2,0,1:T(8,128)S(1)}, f32[12,7,128]{2,0,1:T(8,128)S(1)}, u32[]{:S(2)}, u32[]{:S(2)}) collective-permute-start(f32[12,7,128]{2,0,1:T(8,128)S(1)} %pad_maximum_fusion.5), channel_id=1, source_target_pairs={{0,4},{4,0},{8,12},{12,8},{16,20},{20,16},{24,28},{28,24},{1,5},{5... | collective-permute-start | bytes 129032 | tf_op jit(solution)/shard_map/ppermute | solution.py:17
  26.6 1.4 %gather_fusion = s32[256]{0:T(256)S(1)} fusion(s32[1024]{0:T(1024)S(1)} %copy-done, s32[1024]{0:T(1024)S(1)} %get-tuple-element.85), kind=kCustom, calls=%fused_computation | custom fusion | bytes 3072 | tf_op jit(solution)/shard_map/gather | solution.py:179
  28.3 1.3 %collective-permute-start.3 = (f32[16,7,128]{2,0,1:T(8,128)S(1)}, f32[16,7,128]{2,0,1:T(8,128)S(1)}, u32[]{:S(2)}, u32[]{:S(2)}) collective-permute-start(f32[16,7,128]{2,0,1:T(8,128)S(1)} %concatenate.48), channel_id=1, source_target_pairs={{0,2},{1,3},{2,0},{3,1},{4,6},{5,7},{6,4},{7,5},{8,10},{9,11},{10,... | collective-permute-start | bytes 172040 | tf_op jit(solution)/shard_map/ppermute | solution.py:17
  31.6 3.6 %collective-permute-start.4 = (f32[24,7,128]{2,0,1:T(8,128)S(1)}, f32[24,7,128]{2,0,1:T(8,128)S(1)}, u32[]{:S(2)}, u32[]{:S(2)}) collective-permute-start(f32[24,7,128]{2,0,1:T(8,128)S(1)} %concatenate.49), channel_id=1, source_target_pairs={{0,1},{1,0},{2,3},{3,2},{4,5},{5,4},{6,7},{7,6},{8,9},{9,8},{10,11... | collective-permute-start | bytes 258056 | tf_op jit(solution)/shard_map/ppermute | solution.py:17
  35.2 0.9 %collective-permute-done.4 = f32[24,7,128]{2,0,1:T(8,128)S(1)} collective-permute-done((f32[24,7,128]{2,0,1:T(8,128)S(1)}, f32[24,7,128]{2,0,1:T(8,128)S(1)}, u32[]{:S(2)}, u32[]{:S(2)}) %collective-permute-start.4) | collective-permute-done | bytes 86048 | tf_op jit(solution)/shard_map/ppermute | solution.py:17
  36.3 2.9 %collective-permute-start.6 = (f32[7,32,128]{2,1,0:T(8,128)S(1)}, f32[7,32,128]{2,1,0:T(8,128)S(1)}, u32[]{:S(2)}, u32[]{:S(2)}) collective-permute-start(f32[7,32,128]{2,1,0:T(8,128)S(1)} %slice_bitcast_fusion.4), channel_id=1, source_target_pairs={{4,8},{8,4},{12,16},{16,12},{20,24},{24,20},{5,9},{9,5},{13,17},{1... | collective-permute-start | bytes 344072 | tf_op jit(solution)/shard_map/ppermute | solution.py:24
  39.5 0.7 copy.142
  40.2 0.7 gather_fusion.3
  43.0 0.4 collective-permute-done.6
  43.5 3.1 %collective-permute-done.5 = f32[7,32,128]{2,1,0:T(8,128)S(1)} collective-permute-done((f32[7,32,128]{2,1,0:T(8,128)S(1)}, f32[7,32,128]{2,1,0:T(8,128)S(1)}, u32[]{:S(2)}, u32[]{:S(2)}) %collective-permute-start.5) | collective-permute-done | bytes 114720 | tf_op jit(solution)/shard_map/ppermute | solution.py:24
  46.7 0.6 collective-permute-start.7
  47.6 3.1 %collective-permute-start.8 = (f32[7,96,128]{2,1,0:T(8,128)S(1)}, f32[7,96,128]{2,1,0:T(8,128)S(1)}, u32[]{:S(2)}, u32[]{:S(2)}) collective-permute-start(f32[7,96,128]{2,1,0:T(8,128)S(1)} %pad_maximum_fusion.1), channel_id=1, source_target_pairs={{1,2},{2,1},{5,6},{6,5},{9,10},{10,9},{13,14},{14,13},{17,18},{18,... | collective-permute-start | bytes 1032200 | tf_op jit(solution)/shard_map/ppermute | solution.py:24
  50.7 5.4 %collective-permute-done.8 = f32[7,96,128]{2,1,0:T(8,128)S(1)} collective-permute-done((f32[7,96,128]{2,1,0:T(8,128)S(1)}, f32[7,96,128]{2,1,0:T(8,128)S(1)}, u32[]{:S(2)}, u32[]{:S(2)}) %collective-permute-start.8) | collective-permute-done | bytes 344096 | tf_op jit(solution)/shard_map/ppermute | solution.py:24
  56.2 0.6 copy.97
  56.8 1.0 %gather_fusion.1 = f32[256,7,128]{2,1,0:T(8,128)S(1)} fusion(f32[7,288,128]{2,0,1:T(8,128)S(1)} %copy.97, s32[1024]{0:T(1024)S(1)} %pad_clamp_fusion.2), kind=kCustom, calls=%fused_computation.1 | custom fusion | bytes 1836032 | tf_op jit(solution)/shard_map/gather | solution.py:189
  57.8 0.6 fusion.81
  58.7 17.8 %multiply_reduce_fusion.3 = (f32[32,128]{1,0:T(8,128)S(1)}, f32[32,128]{1,0:T(8,128)S(1)}, f32[32,128]{1,0:T(8,128)S(1)}, f32[32,128]{1,0:T(8,128)S(1)}, f32[32,128]{1,0:T(8,128)S(1)}, /*index=5*/f32[32,128]{1,0:T(8,128)S(1)}) fusion(f32[32,8,128]{2,1,0:T(8,128)S(1)} %get-tuple-element.37, f32[32,8,128]{2,1,0:T(8,128)S(1)} %get-tuple-element.38, ...), kind=kLoop, calls=%fused_computation.8 | loop fusion | flops 96444416 | bytes 1458176 | tf_op jit(solution)/shard_map/vmap()/reduce_sum | solution.py:52
  76.7 0.6 fusion.21
  (143 shorter events, 10.6 us)
Async XLA Ops:
  0.0 15.1 %copy-start = (s32[1024]{0:T(1024)S(1)}, s32[1024]{0:T(1024)}, u32[]{:S(2)}) copy-start(s32[1024]{0:T(1024)} %param.12) | copy-start | bytes 12292
  0.0 14.0 %copy-start.4 = (s32[5]{0:T(128)S(1)}, s32[5]{0:T(128)}, u32[]{:S(2)}) copy-start(s32[5]{0:T(128)} %constant.217) | copy-start | bytes 64
  0.0 13.8 %copy-start.1 = (s32[5,8,4]{1,2,0:T(4,128)S(1)}, s32[5,8,4]{1,2,0:T(4,128)}, u32[]{:S(2)}) copy-start(s32[5,8,4]{1,2,0:T(4,128)} %param.11) | copy-start | bytes 1924
  0.0 14.9 %copy-start.2 = (s32[1,1,32,8]{2,3,1,0:T(8,128)S(1)}, s32[1,1,32,8]{2,3,1,0:T(8,128)}, u32[]{:S(2)}) copy-start(s32[1,1,32,8]{2,3,1,0:T(8,128)} %param.14) | copy-start | bytes 3076
  11.5 9.0 %collective-permute-start = (f32[9,7,128]{2,0,1:T(8,128)S(1)}, f32[9,7,128]{2,0,1:T(8,128)S(1)}, u32[]{:S(2)}, u32[]{:S(2)}) collective-permute-start(f32[9,7,128]{2,0,1:T(8,128)S(1)} %pad_maximum_fusion.3), channel_id=1, source_target_pairs={{0,16},{4,20},{8,24},{12,28},{16,0},{20,4},{24,8},{28,12},{1,17},{... | collective-permute-start | bytes 96776 | tf_op jit(solution)/shard_map/ppermute | solution.py:17
  15.1 5.3 %copy-start.3 = (s32[1,1,32,8]{2,3,1,0:T(8,128)S(1)}, s32[1,1,32,8]{2,3,1,0:T(8,128)}, u32[]{:S(2)}) copy-start(s32[1,1,32,8]{2,3,1,0:T(8,128)} %param.13) | copy-start | bytes 3076
  20.7 3.1 %collective-permute-start.1 = (f32[10,7,128]{2,0,1:T(8,128)S(1)}, f32[10,7,128]{2,0,1:T(8,128)S(1)}, u32[]{:S(2)}, u32[]{:S(2)}) collective-permute-start(f32[10,7,128]{2,0,1:T(8,128)S(1)} %pad_maximum_fusion.4), channel_id=1, source_target_pairs={{0,8},{4,12},{8,0},{12,4},{16,24},{20,28},{24,16},{28,20},{1,9},{5... | collective-permute-start | bytes 107528 | tf_op jit(solution)/shard_map/ppermute | solution.py:17
  24.0 4.0 %collective-permute-start.2 = (f32[12,7,128]{2,0,1:T(8,128)S(1)}, f32[12,7,128]{2,0,1:T(8,128)S(1)}, u32[]{:S(2)}, u32[]{:S(2)}) collective-permute-start(f32[12,7,128]{2,0,1:T(8,128)S(1)} %pad_maximum_fusion.5), channel_id=1, source_target_pairs={{0,4},{4,0},{8,12},{12,8},{16,20},{20,16},{24,28},{28,24},{1,5},{5... | collective-permute-start | bytes 129032 | tf_op jit(solution)/shard_map/ppermute | solution.py:17
  28.3 3.1 %collective-permute-start.3 = (f32[16,7,128]{2,0,1:T(8,128)S(1)}, f32[16,7,128]{2,0,1:T(8,128)S(1)}, u32[]{:S(2)}, u32[]{:S(2)}) collective-permute-start(f32[16,7,128]{2,0,1:T(8,128)S(1)} %concatenate.48), channel_id=1, source_target_pairs={{0,2},{1,3},{2,0},{3,1},{4,6},{5,7},{6,4},{7,5},{8,10},{9,11},{10,... | collective-permute-start | bytes 172040 | tf_op jit(solution)/shard_map/ppermute | solution.py:17
  31.6 4.5 %collective-permute-start.4 = (f32[24,7,128]{2,0,1:T(8,128)S(1)}, f32[24,7,128]{2,0,1:T(8,128)S(1)}, u32[]{:S(2)}, u32[]{:S(2)}) collective-permute-start(f32[24,7,128]{2,0,1:T(8,128)S(1)} %concatenate.49), channel_id=1, source_target_pairs={{0,1},{1,0},{2,3},{3,2},{4,5},{5,4},{6,7},{7,6},{8,9},{9,8},{10,11... | collective-permute-start | bytes 258056 | tf_op jit(solution)/shard_map/ppermute | solution.py:17
  36.3 7.2 %collective-permute-start.6 = (f32[7,32,128]{2,1,0:T(8,128)S(1)}, f32[7,32,128]{2,1,0:T(8,128)S(1)}, u32[]{:S(2)}, u32[]{:S(2)}) collective-permute-start(f32[7,32,128]{2,1,0:T(8,128)S(1)} %slice_bitcast_fusion.4), channel_id=1, source_target_pairs={{4,8},{8,4},{12,16},{16,12},{20,24},{24,20},{5,9},{9,5},{13,17},{1... | collective-permute-start | bytes 344072 | tf_op jit(solution)/shard_map/ppermute | solution.py:24
  39.2 7.4 %collective-permute-start.5 = (f32[7,32,128]{2,1,0:T(8,128)S(1)}, f32[7,32,128]{2,1,0:T(8,128)S(1)}, u32[]{:S(2)}, u32[]{:S(2)}) collective-permute-start(f32[7,32,128]{2,1,0:T(8,128)S(1)} %slice_bitcast_fusion.4), channel_id=1, source_target_pairs={{0,4},{4,0},{8,12},{12,8},{16,20},{20,16},{24,28},{28,24},{1,5},{5... | collective-permute-start | bytes 344072 | tf_op jit(solution)/shard_map/ppermute | solution.py:24
  46.7 4.0 %collective-permute-start.7 = (f32[7,96,128]{2,1,0:T(8,128)S(1)}, f32[7,96,128]{2,1,0:T(8,128)S(1)}, u32[]{:S(2)}, u32[]{:S(2)}) collective-permute-start(f32[7,96,128]{2,1,0:T(8,128)S(1)} %pad_maximum_fusion.1), channel_id=1, source_target_pairs={{0,1},{1,0},{2,3},{3,2},{4,5},{5,4},{6,7},{7,6},{8,9},{9,8},{10,11... | collective-permute-start | bytes 1032200 | tf_op jit(solution)/shard_map/ppermute | solution.py:24
  47.6 8.6 %collective-permute-start.8 = (f32[7,96,128]{2,1,0:T(8,128)S(1)}, f32[7,96,128]{2,1,0:T(8,128)S(1)}, u32[]{:S(2)}, u32[]{:S(2)}) collective-permute-start(f32[7,96,128]{2,1,0:T(8,128)S(1)} %pad_maximum_fusion.1), channel_id=1, source_target_pairs={{1,2},{2,1},{5,6},{6,5},{9,10},{10,9},{13,14},{14,13},{17,18},{18,... | collective-permute-start | bytes 1032200 | tf_op jit(solution)/shard_map/ppermute | solution.py:24

commit v24 on v23

--- a/solution.py
+++ b/solution.py
@@ -160,10 +160,12 @@
         bit_at, own_moves, mate_moves = plans[level]
         leaving = lax.dynamic_slice_in_dim(held, count - own_moves, MOVE, 0)
         payload = jnp.concatenate([leaving, gathered], axis=0)
+        payload = with_layout_constraint(jnp.transpose(payload, (1, 0, 2)), Layout(major_to_minor=(0, 1, 2)))
         if level < bits_x:
             got = from_partner(payload, "gx", bit_at)
         else:
             got = from_partner(payload, "gy", bit_at)
+        got = jnp.transpose(got, (1, 0, 2))
         arriving = got[:MOVE]
         gathered = jnp.concatenate([gathered, got[MOVE:]], axis=0)
         count = count - own_moves

time: 77.6 us -> 77.7 us (level)
  no operation moved by 1% of the time
where the time goes in v24:
time: 77.7 us; the launch traced here: 77.4 us
  other arithmetic  21.7 us (28%)
  starting transfers between devices  15.5 us (20%)
  local copies, waits for them, and re-layouts  14.4 us (19%)
  between operations  12.4 us (16%)
  waiting for transfers between devices  11.8 us (15%)
  matrix products  1.6 us (2%)
    reduce_sum x1, other arithmetic, evaluate(): arm_x = jnp.sum(extra[:, 1][:, None, :] * weight, axis=(0, 2))  17.8 us
    ppermute x5, starting transfers between devices, from_partner(): lax.ppermute(shard, axis, [(i, i ^ 1 << apart) for i in range(lax.axis_si...  8.8 us
    ppermute x2, starting transfers between devices, swapped(): lax.ppermute(shard, axis, second)  5.96 us
    ppermute x2, waiting for transfers between devices, swapped(): lax.ppermute(shard, axis, second)  5.84 us
    ppermute x2, waiting for transfers between devices, swapped(): lax.ppermute(shard, axis, first)  3.15 us
    ppermute x5, waiting for transfers between devices, from_partner(): lax.ppermute(shard, axis, [(i, i ^ 1 << apart) for i in range(lax.axis_si...  2.76 us
  transfers between devices with their start and end apart: 9, of which 6 were waited for; matrix products, arithmetic and copies ran while one was open for 14% of the time, Pallas kernels for 0%

profile of v24, /device:TPU:9, one launch (start us, length us, event | category | flops | bytes accessed | tf_op | source)
XLA Modules:
  0.0 77.4 jit_solution(8378109457656702435)
XLA Ops:
  0.0 1.0 %pad_maximum_fusion.2 = f32[72,7,128]{2,0,1:T(8,128)S(1)} fusion(f32[72,1,128]{2,0,1:T(8,128)} %bitcast.250, f32[72,3,128]{2,0,1:T(8,128)} %bitcast.236, f32[72,3,128]{2,0,1:T(8,128)} %bitcast.237), kind=kLoop, calls=%fused_computation.18 | loop fusion | flops 129024 | bytes 516096 | tf_op jit(solution)/shard_map/concatenate | solution.py:135
  2.3 0.4 convolution_reduce_fusion
  3.1 1.5 %constant_dynamic-slice_fusion.13 = (s32[1,1,1]{1,2,0:T(1,128)}, s32[1,1,1]{1,2,0:T(1,128)}, s32[1,1,1]{1,2,0:T(1,128)}, s32[1,1,1]{1,2,0:T(1,128)}, s32[1,1,1]{...) fusion(s32[5,8,4]{1,2,0:T(4,128)} %param.11, ...), kind=kLoop, calls=%fused_computation.254 | loop fusion | bytes 108 | tf_op jit(solution)/shard_map/dynamic_slice | solution.py:153
  11.5 2.4 %collective-permute-start = (f32[7,9,128]{2,1,0:T(8,128)S(1)}, f32[7,9,128]{2,1,0:T(8,128)S(1)}, u32[]{:S(2)}, u32[]{:S(2)}) collective-permute-start(f32[7,9,128]{2,1,0:T(8,128)S(1)} %maximum_bitcast_fusion), channel_id=1, source_target_pairs={{0,16},{4,20},{8,24},{12,28},{16,0},{20,4},{24,8},{28,12},{1,17},{... | collective-permute-start | bytes 96776 | tf_op jit(solution)/shard_map/ppermute | solution.py:17
  15.1 1.4 %gather_fusion.2 = s32[256]{0:T(256)S(1)} fusion(s32[1024]{0:T(1024)S(1)} %copy-done, s32[1024]{0:T(1024)S(1)} %pad_clamp_fusion.1), kind=kCustom, calls=%fused_computation.2 | custom fusion | bytes 3072 | tf_op jit(solution)/shard_map/gather | solution.py:141
  22.4 1.4 %collective-permute-done.1 = f32[7,10,128]{2,1,0:T(8,128)S(1)} collective-permute-done((f32[7,10,128]{2,1,0:T(8,128)S(1)}, f32[7,10,128]{2,1,0:T(8,128)S(1)}, u32[]{:S(2)}, u32[]{:S(2)}) %collective-permute-start.1) | collective-permute-done | bytes 35872 | tf_op jit(solution)/shard_map/ppermute | solution.py:17
  24.0 1.3 %collective-permute-start.2 = (f32[7,12,128]{2,1,0:T(8,128)S(1)}, f32[7,12,128]{2,1,0:T(8,128)S(1)}, u32[]{:S(2)}, u32[]{:S(2)}) collective-permute-start(f32[7,12,128]{2,1,0:T(8,128)S(1)} %maximum_bitcast_fusion.2), channel_id=1, source_target_pairs={{0,4},{4,0},{8,12},{12,8},{16,20},{20,16},{24,28},{28,24},{1,5},{5... | collective-permute-start | bytes 129032 | tf_op jit(solution)/shard_map/ppermute | solution.py:17
  26.6 1.4 %gather_fusion = s32[256]{0:T(256)S(1)} fusion(s32[1024]{0:T(1024)S(1)} %copy-done, s32[1024]{0:T(1024)S(1)} %get-tuple-element.85), kind=kCustom, calls=%fused_computation | custom fusion | bytes 3072 | tf_op jit(solution)/shard_map/gather | solution.py:181
  28.3 1.3 %collective-permute-start.3 = (f32[7,16,128]{2,1,0:T(8,128)S(1)}, f32[7,16,128]{2,1,0:T(8,128)S(1)}, u32[]{:S(2)}, u32[]{:S(2)}) collective-permute-start(f32[7,16,128]{2,1,0:T(8,128)S(1)} %bitcast.249), channel_id=1, source_target_pairs={{0,2},{1,3},{2,0},{3,1},{4,6},{5,7},{6,4},{7,5},{8,10},{9,11},{10,... | collective-permute-start | bytes 172040 | tf_op jit(solution)/shard_map/ppermute | solution.py:17
  31.6 3.6 %collective-permute-start.4 = (f32[7,24,128]{2,1,0:T(8,128)S(1)}, f32[7,24,128]{2,1,0:T(8,128)S(1)}, u32[]{:S(2)}, u32[]{:S(2)}) collective-permute-start(f32[7,24,128]{2,1,0:T(8,128)S(1)} %bitcast.240), channel_id=1, source_target_pairs={{0,1},{1,0},{2,3},{3,2},{4,5},{5,4},{6,7},{7,6},{8,9},{9,8},{10,11... | collective-permute-start | bytes 258056 | tf_op jit(solution)/shard_map/ppermute | solution.py:17
  35.2 0.9 %collective-permute-done.4 = f32[7,24,128]{2,1,0:T(8,128)S(1)} collective-permute-done((f32[7,24,128]{2,1,0:T(8,128)S(1)}, f32[7,24,128]{2,1,0:T(8,128)S(1)}, u32[]{:S(2)}, u32[]{:S(2)}) %collective-permute-start.4) | collective-permute-done | bytes 86048 | tf_op jit(solution)/shard_map/ppermute | solution.py:17
  36.4 2.9 %collective-permute-start.6 = (f32[7,32,128]{2,1,0:T(8,128)S(1)}, f32[7,32,128]{2,1,0:T(8,128)S(1)}, u32[]{:S(2)}, u32[]{:S(2)}) collective-permute-start(f32[7,32,128]{2,1,0:T(8,128)S(1)} %slice_bitcast_fusion.4), channel_id=1, source_target_pairs={{4,8},{8,4},{12,16},{16,12},{20,24},{24,20},{5,9},{9,5},{13,17},{1... | collective-permute-start | bytes 344072 | tf_op jit(solution)/shard_map/ppermute | solution.py:24
  39.6 0.7 copy.142
  40.3 0.7 gather_fusion.3
  43.1 0.4 collective-permute-done.6
  43.6 3.1 %collective-permute-done.5 = f32[7,32,128]{2,1,0:T(8,128)S(1)} collective-permute-done((f32[7,32,128]{2,1,0:T(8,128)S(1)}, f32[7,32,128]{2,1,0:T(8,128)S(1)}, u32[]{:S(2)}, u32[]{:S(2)}) %collective-permute-start.5) | collective-permute-done | bytes 114720 | tf_op jit(solution)/shard_map/ppermute | solution.py:24
  46.7 0.6 collective-permute-start.7
  47.6 3.1 %collective-permute-start.8 = (f32[7,96,128]{2,1,0:T(8,128)S(1)}, f32[7,96,128]{2,1,0:T(8,128)S(1)}, u32[]{:S(2)}, u32[]{:S(2)}) collective-permute-start(f32[7,96,128]{2,1,0:T(8,128)S(1)} %pad_maximum_fusion.1), channel_id=1, source_target_pairs={{1,2},{2,1},{5,6},{6,5},{9,10},{10,9},{13,14},{14,13},{17,18},{18,... | collective-permute-start | bytes 1032200 | tf_op jit(solution)/shard_map/ppermute | solution.py:24
  50.8 5.4 %collective-permute-done.8 = f32[7,96,128]{2,1,0:T(8,128)S(1)} collective-permute-done((f32[7,96,128]{2,1,0:T(8,128)S(1)}, f32[7,96,128]{2,1,0:T(8,128)S(1)}, u32[]{:S(2)}, u32[]{:S(2)}) %collective-permute-start.8) | collective-permute-done | bytes 344096 | tf_op jit(solution)/shard_map/ppermute | solution.py:24
  56.2 0.6 copy.97
  56.8 1.0 %gather_fusion.1 = f32[256,7,128]{2,1,0:T(8,128)S(1)} fusion(f32[7,288,128]{2,0,1:T(8,128)S(1)} %copy.97, s32[1024]{0:T(1024)S(1)} %pad_clamp_fusion.2), kind=kCustom, calls=%fused_computation.1 | custom fusion | bytes 1836032 | tf_op jit(solution)/shard_map/gather | solution.py:191
  57.9 0.6 fusion.81
  58.8 17.8 %multiply_reduce_fusion.3 = (f32[32,128]{1,0:T(8,128)S(1)}, f32[32,128]{1,0:T(8,128)S(1)}, f32[32,128]{1,0:T(8,128)S(1)}, f32[32,128]{1,0:T(8,128)S(1)}, f32[32,128]{1,0:T(8,128)S(1)}, /*index=5*/f32[32,128]{1,0:T(8,128)S(1)}) fusion(f32[32,8,128]{2,1,0:T(8,128)S(1)} %get-tuple-element.37, f32[32,8,128]{2,1,0:T(8,128)S(1)} %get-tuple-element.38, ...), kind=kLoop, calls=%fused_computation.8 | loop fusion | flops 96444416 | bytes 1458176 | tf_op jit(solution)/shard_map/vmap()/reduce_sum | solution.py:52
  76.7 0.6 fusion.21
  (143 shorter events, 10.7 us)
Async XLA Ops:
  0.0 15.1 %copy-start = (s32[1024]{0:T(1024)S(1)}, s32[1024]{0:T(1024)}, u32[]{:S(2)}) copy-start(s32[1024]{0:T(1024)} %param.12) | copy-start | bytes 12292
  0.0 14.0 %copy-start.4 = (s32[5]{0:T(128)S(1)}, s32[5]{0:T(128)}, u32[]{:S(2)}) copy-start(s32[5]{0:T(128)} %constant.217) | copy-start | bytes 64
  0.0 13.8 %copy-start.1 = (s32[5,8,4]{1,2,0:T(4,128)S(1)}, s32[5,8,4]{1,2,0:T(4,128)}, u32[]{:S(2)}) copy-start(s32[5,8,4]{1,2,0:T(4,128)} %param.11) | copy-start | bytes 1924
  0.0 14.9 %copy-start.2 = (s32[1,1,32,8]{2,3,1,0:T(8,128)S(1)}, s32[1,1,32,8]{2,3,1,0:T(8,128)}, u32[]{:S(2)}) copy-start(s32[1,1,32,8]{2,3,1,0:T(8,128)} %param.14) | copy-start | bytes 3076
  11.5 9.0 %collective-permute-start = (f32[7,9,128]{2,1,0:T(8,128)S(1)}, f32[7,9,128]{2,1,0:T(8,128)S(1)}, u32[]{:S(2)}, u32[]{:S(2)}) collective-permute-start(f32[7,9,128]{2,1,0:T(8,128)S(1)} %maximum_bitcast_fusion), channel_id=1, source_target_pairs={{0,16},{4,20},{8,24},{12,28},{16,0},{20,4},{24,8},{28,12},{1,17},{... | collective-permute-start | bytes 96776 | tf_op jit(solution)/shard_map/ppermute | solution.py:17
  15.1 5.3 %copy-start.3 = (s32[1,1,32,8]{2,3,1,0:T(8,128)S(1)}, s32[1,1,32,8]{2,3,1,0:T(8,128)}, u32[]{:S(2)}) copy-start(s32[1,1,32,8]{2,3,1,0:T(8,128)} %param.13) | copy-start | bytes 3076
  20.7 3.1 %collective-permute-start.1 = (f32[7,10,128]{2,1,0:T(8,128)S(1)}, f32[7,10,128]{2,1,0:T(8,128)S(1)}, u32[]{:S(2)}, u32[]{:S(2)}) collective-permute-start(f32[7,10,128]{2,1,0:T(8,128)S(1)} %maximum_bitcast_fusion.1), channel_id=1, source_target_pairs={{0,8},{4,12},{8,0},{12,4},{16,24},{20,28},{24,16},{28,20},{1,9},{5... | collective-permute-start | bytes 107528 | tf_op jit(solution)/shard_map/ppermute | solution.py:17
  24.0 4.0 %collective-permute-start.2 = (f32[7,12,128]{2,1,0:T(8,128)S(1)}, f32[7,12,128]{2,1,0:T(8,128)S(1)}, u32[]{:S(2)}, u32[]{:S(2)}) collective-permute-start(f32[7,12,128]{2,1,0:T(8,128)S(1)} %maximum_bitcast_fusion.2), channel_id=1, source_target_pairs={{0,4},{4,0},{8,12},{12,8},{16,20},{20,16},{24,28},{28,24},{1,5},{5... | collective-permute-start | bytes 129032 | tf_op jit(solution)/shard_map/ppermute | solution.py:17
  28.3 3.1 %collective-permute-start.3 = (f32[7,16,128]{2,1,0:T(8,128)S(1)}, f32[7,16,128]{2,1,0:T(8,128)S(1)}, u32[]{:S(2)}, u32[]{:S(2)}) collective-permute-start(f32[7,16,128]{2,1,0:T(8,128)S(1)} %bitcast.249), channel_id=1, source_target_pairs={{0,2},{1,3},{2,0},{3,1},{4,6},{5,7},{6,4},{7,5},{8,10},{9,11},{10,... | collective-permute-start | bytes 172040 | tf_op jit(solution)/shard_map/ppermute | solution.py:17
  31.6 4.5 %collective-permute-start.4 = (f32[7,24,128]{2,1,0:T(8,128)S(1)}, f32[7,24,128]{2,1,0:T(8,128)S(1)}, u32[]{:S(2)}, u32[]{:S(2)}) collective-permute-start(f32[7,24,128]{2,1,0:T(8,128)S(1)} %bitcast.240), channel_id=1, source_target_pairs={{0,1},{1,0},{2,3},{3,2},{4,5},{5,4},{6,7},{7,6},{8,9},{9,8},{10,11... | collective-permute-start | bytes 258056 | tf_op jit(solution)/shard_map/ppermute | solution.py:17
  36.4 7.2 %collective-permute-start.6 = (f32[7,32,128]{2,1,0:T(8,128)S(1)}, f32[7,32,128]{2,1,0:T(8,128)S(1)}, u32[]{:S(2)}, u32[]{:S(2)}) collective-permute-start(f32[7,32,128]{2,1,0:T(8,128)S(1)} %slice_bitcast_fusion.4), channel_id=1, source_target_pairs={{4,8},{8,4},{12,16},{16,12},{20,24},{24,20},{5,9},{9,5},{13,17},{1... | collective-permute-start | bytes 344072 | tf_op jit(solution)/shard_map/ppermute | solution.py:24
  39.3 7.4 %collective-permute-start.5 = (f32[7,32,128]{2,1,0:T(8,128)S(1)}, f32[7,32,128]{2,1,0:T(8,128)S(1)}, u32[]{:S(2)}, u32[]{:S(2)}) collective-permute-start(f32[7,32,128]{2,1,0:T(8,128)S(1)} %slice_bitcast_fusion.4), channel_id=1, source_target_pairs={{0,4},{4,0},{8,12},{12,8},{16,20},{20,16},{24,28},{28,24},{1,5},{5... | collective-permute-start | bytes 344072 | tf_op jit(solution)/shard_map/ppermute | solution.py:24
  46.7 4.0 %collective-permute-start.7 = (f32[7,96,128]{2,1,0:T(8,128)S(1)}, f32[7,96,128]{2,1,0:T(8,128)S(1)}, u32[]{:S(2)}, u32[]{:S(2)}) collective-permute-start(f32[7,96,128]{2,1,0:T(8,128)S(1)} %pad_maximum_fusion.1), channel_id=1, source_target_pairs={{0,1},{1,0},{2,3},{3,2},{4,5},{5,4},{6,7},{7,6},{8,9},{9,8},{10,11... | collective-permute-start | bytes 1032200 | tf_op jit(solution)/shard_map/ppermute | solution.py:24
  47.6 8.6 %collective-permute-start.8 = (f32[7,96,128]{2,1,0:T(8,128)S(1)}, f32[7,96,128]{2,1,0:T(8,128)S(1)}, u32[]{:S(2)}, u32[]{:S(2)}) collective-permute-start(f32[7,96,128]{2,1,0:T(8,128)S(1)} %pad_maximum_fusion.1), channel_id=1, source_target_pairs={{1,2},{2,1},{5,6},{6,5},{9,10},{10,9},{13,14},{14,13},{17,18},{18,... | collective-permute-start | bytes 1032200 | tf_op jit(solution)/shard_map/ppermute | solution.py:24

commit v25 on v23

--- a/solution.py
+++ b/solution.py
@@ -40,18 +40,18 @@
 
 
 def evaluate(target, centre, sources, extra, moments):
-    sep_x = target[0][None, :, None] - sources[:, 0][:, None, :]
-    sep_y = target[1][None, :, None] - sources[:, 1][:, None, :]
-    sep_z = target[2][None, :, None] - sources[:, 2][:, None, :]
-    radius_sq = sep_x * sep_x + sep_y * sep_y + sep_z * sep_z + extra[:, 0][:, None, :]
+    sep_x = target[0][None, :, None] - sources[0][:, None, :]
+    sep_y = target[1][None, :, None] - sources[1][:, None, :]
+    sep_z = target[2][None, :, None] - sources[2][:, None, :]
+    radius_sq = sep_x * sep_x + sep_y * sep_y + sep_z * sep_z + extra[0][:, None, :]
     inverse = lax.rsqrt(radius_sq)
     weight = inverse * inverse * inverse
-    sum_x = jnp.sum(sources[:, 3][:, None, :] * weight, axis=(0, 2))
-    sum_y = jnp.sum(sources[:, 4][:, None, :] * weight, axis=(0, 2))
-    sum_z = jnp.sum(sources[:, 5][:, None, :] * weight, axis=(0, 2))
-    arm_x = jnp.sum(extra[:, 1][:, None, :] * weight, axis=(0, 2))
-    arm_y = jnp.sum(extra[:, 2][:, None, :] * weight, axis=(0, 2))
-    arm_z = jnp.sum(extra[:, 3][:, None, :] * weight, axis=(0, 2))
+    sum_x = jnp.sum(sources[3][:, None, :] * weight, axis=(0, 2))
+    sum_y = jnp.sum(sources[4][:, None, :] * weight, axis=(0, 2))
+    sum_z = jnp.sum(sources[5][:, None, :] * weight, axis=(0, 2))
+    arm_x = jnp.sum(extra[1][:, None, :] * weight, axis=(0, 2))
+    arm_y = jnp.sum(extra[2][:, None, :] * weight, axis=(0, 2))
+    arm_z = jnp.sum(extra[3][:, None, :] * weight, axis=(0, 2))
     rel_x = target[0] - centre[0]
     rel_y = target[1] - centre[1]
     rel_z = target[2] - centre[2]
@@ -74,12 +74,12 @@
 
 
 def source_terms(sources_all, centre):
-    px = sources_all[:, :, 0] - centre[:, 0][:, None, None]
-    py = sources_all[:, :, 1] - centre[:, 1][:, None, None]
-    pz = sources_all[:, :, 2] - centre[:, 2][:, None, None]
-    sx, sy, sz = sources_all[:, :, 3], sources_all[:, :, 4], sources_all[:, :, 5]
-    core_sq = sources_all[:, :, 6] * sources_all[:, :, 6]
-    extra = jnp.stack([core_sq, sy * pz - sz * py, sz * px - sx * pz, sx * py - sy * px], axis=2)
+    px = sources_all[0] - centre[:, 0][:, None, None]
+    py = sources_all[1] - centre[:, 1][:, None, None]
+    pz = sources_all[2] - centre[:, 2][:, None, None]
+    sx, sy, sz = sources_all[3], sources_all[4], sources_all[5]
+    core_sq = sources_all[6] * sources_all[6]
+    extra = jnp.stack([core_sq, sy * pz - sz * py, sz * px - sx * pz, sx * py - sy * px], axis=0)
     return lax.optimization_barrier(extra)
 
 
@@ -186,11 +186,11 @@
     dense = with_layout_constraint(jnp.transpose(blocks, (1, 0, 2)), Layout(major_to_minor=(0, 1, 2)))
     source_pool = swapped(swapped(dense, "gx", 1), "gy", 1)
     pool_index = ((1 + delta_y * sign_y) * 3 + (1 + delta_x * sign_x)) * nbd + source_slot
-    sources_all = jnp.transpose(source_pool[:, pool_index], (1, 2, 0, 3))
+    sources_all = source_pool[:, pool_index]
     targets = blocks[:, 0:3]
     centre = jnp.mean(targets, axis=2)
     extra = source_terms(sources_all, centre)
-    velocity = jax.vmap(evaluate)(targets, centre, sources_all, extra, moments)
+    velocity = jax.vmap(evaluate, in_axes=(0, 0, 1, 1, 0))(targets, centre, sources_all, extra, moments)
     return velocity[None, None]
 
 

time: 77.6 us -> 77.3 us (level)
  no operation moved by 1% of the time
where the time goes in v25:
time: 77.3 us; the launch traced here: 76.9 us
  other arithmetic  21.7 us (28%)
  starting transfers between devices  15.5 us (20%)
  local copies, waits for them, and re-layouts  13.9 us (18%)
  between operations  12.4 us (16%)
  waiting for transfers between devices  11.8 us (15%)
  matrix products  1.6 us (2%)
    reduce_sum x1, other arithmetic, evaluate(): arm_x = jnp.sum(extra[1][:, None, :] * weight, axis=(0, 2))  17.9 us
    ppermute x5, starting transfers between devices, from_partner(): lax.ppermute(shard, axis, [(i, i ^ 1 << apart) for i in range(lax.axis_si...  8.8 us
    ppermute x2, starting transfers between devices, swapped(): lax.ppermute(shard, axis, second)  5.94 us
    ppermute x2, waiting for transfers between devices, swapped(): lax.ppermute(shard, axis, second)  5.86 us
    ppermute x2, waiting for transfers between devices, swapped(): lax.ppermute(shard, axis, first)  3.15 us
    ppermute x5, waiting for transfers between devices, from_partner(): lax.ppermute(shard, axis, [(i, i ^ 1 << apart) for i in range(lax.axis_si...  2.76 us
  transfers between devices with their start and end apart: 9, of which 6 were waited for; matrix products, arithmetic and copies ran while one was open for 14% of the time, Pallas kernels for 0%

profile of v25, /device:TPU:9, one launch (start us, length us, event | category | flops | bytes accessed | tf_op | source)
XLA Modules:
  0.0 76.9 jit_solution(6103741832165582958)
XLA Ops:
  0.0 1.0 %pad_maximum_fusion.2 = f32[72,7,128]{2,0,1:T(8,128)S(1)} fusion(f32[72,1,128]{2,0,1:T(8,128)} %bitcast.209, f32[72,3,128]{2,0,1:T(8,128)} %bitcast.200, f32[72,3,128]{2,0,1:T(8,128)} %bitcast.201), kind=kLoop, calls=%fused_computation.19 | loop fusion | flops 129024 | bytes 516096 | tf_op jit(solution)/shard_map/concatenate | solution.py:135
  1.8 0.4 fusion.15
  2.3 0.4 convolution_reduce_fusion
  3.1 1.5 %constant_dynamic-slice_fusion.13 = (s32[1,1,1]{1,2,0:T(1,128)}, s32[1,1,1]{1,2,0:T(1,128)}, s32[1,1,1]{1,2,0:T(1,128)}, s32[1,1,1]{1,2,0:T(1,128)}, s32[1,1,1]{...) fusion(s32[5,8,4]{1,2,0:T(4,128)} %param.11, ...), kind=kLoop, calls=%fused_computation.265 | loop fusion | bytes 108 | tf_op jit(solution)/shard_map/dynamic_slice | solution.py:153
  11.5 2.4 %collective-permute-start = (f32[9,7,128]{2,0,1:T(8,128)S(1)}, f32[9,7,128]{2,0,1:T(8,128)S(1)}, u32[]{:S(2)}, u32[]{:S(2)}) collective-permute-start(f32[9,7,128]{2,0,1:T(8,128)S(1)} %pad_maximum_fusion.3), channel_id=1, source_target_pairs={{0,16},{4,20},{8,24},{12,28},{16,0},{20,4},{24,8},{28,12},{1,17},{... | collective-permute-start | bytes 96776 | tf_op jit(solution)/shard_map/ppermute | solution.py:17
  15.1 1.4 %gather_fusion.2 = s32[256]{0:T(256)S(1)} fusion(s32[1024]{0:T(1024)S(1)} %copy-done, s32[1024]{0:T(1024)S(1)} %pad_clamp_fusion.1), kind=kCustom, calls=%fused_computation.2 | custom fusion | bytes 3072 | tf_op jit(solution)/shard_map/gather | solution.py:141
  22.4 1.4 %collective-permute-done.1 = f32[10,7,128]{2,0,1:T(8,128)S(1)} collective-permute-done((f32[10,7,128]{2,0,1:T(8,128)S(1)}, f32[10,7,128]{2,0,1:T(8,128)S(1)}, u32[]{:S(2)}, u32[]{:S(2)}) %collective-permute-start.1) | collective-permute-done | bytes 35872 | tf_op jit(solution)/shard_map/ppermute | solution.py:17
  24.0 1.3 %collective-permute-start.2 = (f32[12,7,128]{2,0,1:T(8,128)S(1)}, f32[12,7,128]{2,0,1:T(8,128)S(1)}, u32[]{:S(2)}, u32[]{:S(2)}) collective-permute-start(f32[12,7,128]{2,0,1:T(8,128)S(1)} %pad_maximum_fusion.5), channel_id=1, source_target_pairs={{0,4},{4,0},{8,12},{12,8},{16,20},{20,16},{24,28},{28,24},{1,5},{5... | collective-permute-start | bytes 129032 | tf_op jit(solution)/shard_map/ppermute | solution.py:17
  26.6 1.4 %gather_fusion = s32[256]{0:T(256)S(1)} fusion(s32[1024]{0:T(1024)S(1)} %copy-done, s32[1024]{0:T(1024)S(1)} %get-tuple-element.85), kind=kCustom, calls=%fused_computation | custom fusion | bytes 3072 | tf_op jit(solution)/shard_map/gather | solution.py:179
  28.3 1.3 %collective-permute-start.3 = (f32[16,7,128]{2,0,1:T(8,128)S(1)}, f32[16,7,128]{2,0,1:T(8,128)S(1)}, u32[]{:S(2)}, u32[]{:S(2)}) collective-permute-start(f32[16,7,128]{2,0,1:T(8,128)S(1)} %concatenate.48), channel_id=1, source_target_pairs={{0,2},{1,3},{2,0},{3,1},{4,6},{5,7},{6,4},{7,5},{8,10},{9,11},{10,... | collective-permute-start | bytes 172040 | tf_op jit(solution)/shard_map/ppermute | solution.py:17
  31.6 3.6 %collective-permute-start.4 = (f32[24,7,128]{2,0,1:T(8,128)S(1)}, f32[24,7,128]{2,0,1:T(8,128)S(1)}, u32[]{:S(2)}, u32[]{:S(2)}) collective-permute-start(f32[24,7,128]{2,0,1:T(8,128)S(1)} %concatenate.49), channel_id=1, source_target_pairs={{0,1},{1,0},{2,3},{3,2},{4,5},{5,4},{6,7},{7,6},{8,9},{9,8},{10,11... | collective-permute-start | bytes 258056 | tf_op jit(solution)/shard_map/ppermute | solution.py:17
  35.2 0.9 %collective-permute-done.4 = f32[24,7,128]{2,0,1:T(8,128)S(1)} collective-permute-done((f32[24,7,128]{2,0,1:T(8,128)S(1)}, f32[24,7,128]{2,0,1:T(8,128)S(1)}, u32[]{:S(2)}, u32[]{:S(2)}) %collective-permute-start.4) | collective-permute-done | bytes 86048 | tf_op jit(solution)/shard_map/ppermute | solution.py:17
  36.3 2.9 %collective-permute-start.6 = (f32[7,32,128]{2,1,0:T(8,128)S(1)}, f32[7,32,128]{2,1,0:T(8,128)S(1)}, u32[]{:S(2)}, u32[]{:S(2)}) collective-permute-start(f32[7,32,128]{2,1,0:T(8,128)S(1)} %slice_bitcast_fusion.10), channel_id=1, source_target_pairs={{4,8},{8,4},{12,16},{16,12},{20,24},{24,20},{5,9},{9,5},{13,17},{1... | collective-permute-start | bytes 344072 | tf_op jit(solution)/shard_map/ppermute | solution.py:24
  39.5 0.7 copy.102
  40.2 0.7 gather_fusion.3
  43.0 0.5 collective-permute-done.6
  43.5 3.1 %collective-permute-done.5 = f32[7,32,128]{2,1,0:T(8,128)S(1)} collective-permute-done((f32[7,32,128]{2,1,0:T(8,128)S(1)}, f32[7,32,128]{2,1,0:T(8,128)S(1)}, u32[]{:S(2)}, u32[]{:S(2)}) %collective-permute-start.5) | collective-permute-done | bytes 114720 | tf_op jit(solution)/shard_map/ppermute | solution.py:24
  46.7 0.6 collective-permute-start.7
  47.6 3.1 %collective-permute-start.8 = (f32[7,96,128]{2,1,0:T(8,128)S(1)}, f32[7,96,128]{2,1,0:T(8,128)S(1)}, u32[]{:S(2)}, u32[]{:S(2)}) collective-permute-start(f32[7,96,128]{2,1,0:T(8,128)S(1)} %pad_maximum_fusion.1), channel_id=1, source_target_pairs={{1,2},{2,1},{5,6},{6,5},{9,10},{10,9},{13,14},{14,13},{17,18},{18,... | collective-permute-start | bytes 1032200 | tf_op jit(solution)/shard_map/ppermute | solution.py:24
  50.7 5.4 %collective-permute-done.8 = f32[7,96,128]{2,1,0:T(8,128)S(1)} collective-permute-done((f32[7,96,128]{2,1,0:T(8,128)S(1)}, f32[7,96,128]{2,1,0:T(8,128)S(1)}, u32[]{:S(2)}, u32[]{:S(2)}) %collective-permute-start.8) | collective-permute-done | bytes 344096 | tf_op jit(solution)/shard_map/ppermute | solution.py:24
  56.2 0.6 copy.71
  56.8 1.0 %gather_fusion.1 = f32[256,7,128]{2,1,0:T(8,128)S(1)} fusion(f32[7,288,128]{2,0,1:T(8,128)S(1)} %copy.71, s32[1024]{0:T(1024)S(1)} %pad_clamp_fusion.2), kind=kCustom, calls=%fused_computation.1 | custom fusion | bytes 1836032 | tf_op jit(solution)/shard_map/gather | solution.py:189
  58.3 17.9 %multiply_reduce_fusion.3 = (f32[32,128]{1,0:T(8,128)S(1)}, f32[32,128]{1,0:T(8,128)S(1)}, f32[32,128]{1,0:T(8,128)S(1)}, f32[32,128]{1,0:T(8,128)S(1)}, f32[32,128]{1,0:T(8,128)S(1)}, /*index=5*/f32[32,128]{1,0:T(8,128)S(1)}) fusion(f32[32,8,128]{2,1,0:T(8,128)S(1)} %get-tuple-element.40, f32[32,8,128]{2,1,0:T(8,128)S(1)} %get-tuple-element.41, ...), kind=kLoop, calls=%fused_computation.8 | loop fusion | flops 96444416 | bytes 1458176 | tf_op jit(solution)/shard_map/vmap()/reduce_sum | solution.py:52
  76.3 0.6 fusion.21
  (143 shorter events, 10.4 us)
Async XLA Ops:
  0.0 15.1 %copy-start = (s32[1024]{0:T(1024)S(1)}, s32[1024]{0:T(1024)}, u32[]{:S(2)}) copy-start(s32[1024]{0:T(1024)} %param.12) | copy-start | bytes 12292
  0.0 14.0 %copy-start.4 = (s32[5]{0:T(128)S(1)}, s32[5]{0:T(128)}, u32[]{:S(2)}) copy-start(s32[5]{0:T(128)} %constant.217) | copy-start | bytes 64
  0.0 13.8 %copy-start.1 = (s32[5,8,4]{1,2,0:T(4,128)S(1)}, s32[5,8,4]{1,2,0:T(4,128)}, u32[]{:S(2)}) copy-start(s32[5,8,4]{1,2,0:T(4,128)} %param.11) | copy-start | bytes 1924
  0.0 14.9 %copy-start.2 = (s32[1,1,32,8]{2,3,1,0:T(8,128)S(1)}, s32[1,1,32,8]{2,3,1,0:T(8,128)}, u32[]{:S(2)}) copy-start(s32[1,1,32,8]{2,3,1,0:T(8,128)} %param.14) | copy-start | bytes 3076
  11.5 9.0 %collective-permute-start = (f32[9,7,128]{2,0,1:T(8,128)S(1)}, f32[9,7,128]{2,0,1:T(8,128)S(1)}, u32[]{:S(2)}, u32[]{:S(2)}) collective-permute-start(f32[9,7,128]{2,0,1:T(8,128)S(1)} %pad_maximum_fusion.3), channel_id=1, source_target_pairs={{0,16},{4,20},{8,24},{12,28},{16,0},{20,4},{24,8},{28,12},{1,17},{... | collective-permute-start | bytes 96776 | tf_op jit(solution)/shard_map/ppermute | solution.py:17
  15.1 5.3 %copy-start.3 = (s32[1,1,32,8]{2,3,1,0:T(8,128)S(1)}, s32[1,1,32,8]{2,3,1,0:T(8,128)}, u32[]{:S(2)}) copy-start(s32[1,1,32,8]{2,3,1,0:T(8,128)} %param.13) | copy-start | bytes 3076
  20.7 3.1 %collective-permute-start.1 = (f32[10,7,128]{2,0,1:T(8,128)S(1)}, f32[10,7,128]{2,0,1:T(8,128)S(1)}, u32[]{:S(2)}, u32[]{:S(2)}) collective-permute-start(f32[10,7,128]{2,0,1:T(8,128)S(1)} %pad_maximum_fusion.4), channel_id=1, source_target_pairs={{0,8},{4,12},{8,0},{12,4},{16,24},{20,28},{24,16},{28,20},{1,9},{5... | collective-permute-start | bytes 107528 | tf_op jit(solution)/shard_map/ppermute | solution.py:17
  24.0 4.0 %collective-permute-start.2 = (f32[12,7,128]{2,0,1:T(8,128)S(1)}, f32[12,7,128]{2,0,1:T(8,128)S(1)}, u32[]{:S(2)}, u32[]{:S(2)}) collective-permute-start(f32[12,7,128]{2,0,1:T(8,128)S(1)} %pad_maximum_fusion.5), channel_id=1, source_target_pairs={{0,4},{4,0},{8,12},{12,8},{16,20},{20,16},{24,28},{28,24},{1,5},{5... | collective-permute-start | bytes 129032 | tf_op jit(solution)/shard_map/ppermute | solution.py:17
  28.3 3.1 %collective-permute-start.3 = (f32[16,7,128]{2,0,1:T(8,128)S(1)}, f32[16,7,128]{2,0,1:T(8,128)S(1)}, u32[]{:S(2)}, u32[]{:S(2)}) collective-permute-start(f32[16,7,128]{2,0,1:T(8,128)S(1)} %concatenate.48), channel_id=1, source_target_pairs={{0,2},{1,3},{2,0},{3,1},{4,6},{5,7},{6,4},{7,5},{8,10},{9,11},{10,... | collective-permute-start | bytes 172040 | tf_op jit(solution)/shard_map/ppermute | solution.py:17
  31.6 4.5 %collective-permute-start.4 = (f32[24,7,128]{2,0,1:T(8,128)S(1)}, f32[24,7,128]{2,0,1:T(8,128)S(1)}, u32[]{:S(2)}, u32[]{:S(2)}) collective-permute-start(f32[24,7,128]{2,0,1:T(8,128)S(1)} %concatenate.49), channel_id=1, source_target_pairs={{0,1},{1,0},{2,3},{3,2},{4,5},{5,4},{6,7},{7,6},{8,9},{9,8},{10,11... | collective-permute-start | bytes 258056 | tf_op jit(solution)/shard_map/ppermute | solution.py:17
  36.3 7.2 %collective-permute-start.6 = (f32[7,32,128]{2,1,0:T(8,128)S(1)}, f32[7,32,128]{2,1,0:T(8,128)S(1)}, u32[]{:S(2)}, u32[]{:S(2)}) collective-permute-start(f32[7,32,128]{2,1,0:T(8,128)S(1)} %slice_bitcast_fusion.10), channel_id=1, source_target_pairs={{4,8},{8,4},{12,16},{16,12},{20,24},{24,20},{5,9},{9,5},{13,17},{1... | collective-permute-start | bytes 344072 | tf_op jit(solution)/shard_map/ppermute | solution.py:24
  39.2 7.4 %collective-permute-start.5 = (f32[7,32,128]{2,1,0:T(8,128)S(1)}, f32[7,32,128]{2,1,0:T(8,128)S(1)}, u32[]{:S(2)}, u32[]{:S(2)}) collective-permute-start(f32[7,32,128]{2,1,0:T(8,128)S(1)} %slice_bitcast_fusion.10), channel_id=1, source_target_pairs={{0,4},{4,0},{8,12},{12,8},{16,20},{20,16},{24,28},{28,24},{1,5},{5... | collective-permute-start | bytes 344072 | tf_op jit(solution)/shard_map/ppermute | solution.py:24
  46.7 4.0 %collective-permute-start.7 = (f32[7,96,128]{2,1,0:T(8,128)S(1)}, f32[7,96,128]{2,1,0:T(8,128)S(1)}, u32[]{:S(2)}, u32[]{:S(2)}) collective-permute-start(f32[7,96,128]{2,1,0:T(8,128)S(1)} %pad_maximum_fusion.1), channel_id=1, source_target_pairs={{0,1},{1,0},{2,3},{3,2},{4,5},{5,4},{6,7},{7,6},{8,9},{9,8},{10,11... | collective-permute-start | bytes 1032200 | tf_op jit(solution)/shard_map/ppermute | solution.py:24
  47.6 8.6 %collective-permute-start.8 = (f32[7,96,128]{2,1,0:T(8,128)S(1)}, f32[7,96,128]{2,1,0:T(8,128)S(1)}, u32[]{:S(2)}, u32[]{:S(2)}) collective-permute-start(f32[7,96,128]{2,1,0:T(8,128)S(1)} %pad_maximum_fusion.1), channel_id=1, source_target_pairs={{1,2},{2,1},{5,6},{6,5},{9,10},{10,9},{13,14},{14,13},{17,18},{18,... | collective-permute-start | bytes 1032200 | tf_op jit(solution)/shard_map/ppermute | solution.py:24
